TPU v7x, 32 devices: a whole 2x2x4 slice. The times are simulated.
32 devices in a mesh: lat: 8 (over y, x, core), lon: 4 (over z).
Axes of the slice: x: 2, y: 2, z: 4, core: 2. Of those that a mesh axis runs over, the one named last changes fastest.
Arguments:
- tracers: float32 [5, 4, 64, 2880], P(None, None, 'lat', 'lon'), may hold values from -6 to 6
- courant_x: float32 [4, 64, 2880], P(None, 'lat', 'lon'), may hold values from -0.3 to 0.3
- courant_y: float32 [4, 64, 2880], P(None, 'lat', 'lon'), may hold values from -0.3 to 0.3
- cutoffs: int32 [64], replicated, may hold values from 1 to 720, as said below
Outputs:
- advected: float32 [5, 4, 64, 2880], P(None, None, 'lat', 'lon')
Inputs may be any that keep to these rules, and one draw needn't show every extreme that they name: `cutoffs`: some row poleward of 45 degrees keeps exactly 720 wavenumbers.
All inputs are finite; a program needn't handle non-finite values.
Results may differ from a plain program's by a relative error of at most 0.0003.
Values sent between devices are 32-bit elements; how exact they have to be, the bound alone decides.
No kernel may reach another device: no remote copies, remote signals or barrier semaphores. Data moves between devices by JAX's collectives and lax.ppermute only.
A program may use at most 64 MiB of HBM per device.

v0:
```python
import math

import jax
import jax.numpy as jnp
from jax import lax
from jax.sharding import PartitionSpec as P

KMAX = 720
SUBSTEPS = 2


def extended_2(cells, sides, width):
    for axis, dim in sides:
        count = lax.axis_size(axis)
        head = lax.slice_in_dim(cells, 0, width, axis=dim)
        tail = lax.slice_in_dim(cells, cells.shape[dim] - width, cells.shape[dim], axis=dim)
        cells = jnp.concatenate(
            [
                lax.ppermute(tail, axis, [(i, (i + 1) % count) for i in range(count)]),
                cells,
                lax.ppermute(head, axis, [((i + 1) % count, i) for i in range(count)]),
            ],
            axis=dim,
        )
    return cells


def from_behind(x, axis, by):
    size = lax.axis_size(axis)
    return lax.ppermute(x, axis, [(i, (i + by) % size) for i in range(size)])


def window(values, first_cell, last_cell, dim_at):
    return lax.slice_in_dim(values, first_cell, last_cell, axis=dim_at)


def ppm_flux(padded, courant, dim_at, cell_count):
    edge_values = 7.0 / 12.0 * (
        window(padded, 1, cell_count + 4, dim_at) + window(padded, 2, cell_count + 5, dim_at)
    ) - 1.0 / 12.0 * (
        window(padded, 0, cell_count + 3, dim_at) + window(padded, 3, cell_count + 6, dim_at)
    )
    left_edge = window(edge_values, 0, cell_count + 1, dim_at)
    mid_edge = window(edge_values, 1, cell_count + 2, dim_at)
    right_edge = window(edge_values, 2, cell_count + 3, dim_at)
    left_cell = window(padded, 2, cell_count + 3, dim_at)
    right_cell = window(padded, 3, cell_count + 4, dim_at)
    magnitude = jnp.abs(courant)
    six_left = 6.0 * left_cell - 3.0 * (left_edge + mid_edge)
    six_right = 6.0 * right_cell - 3.0 * (mid_edge + right_edge)
    from_left = mid_edge - 0.5 * magnitude * (
        mid_edge - left_edge - (1.0 - magnitude * (2.0 / 3.0)) * six_left
    )
    from_right = mid_edge + 0.5 * magnitude * (
        right_edge - mid_edge + (1.0 - magnitude * (2.0 / 3.0)) * six_right
    )
    return courant * jnp.where(courant >= 0.0, from_left, from_right)


def dft_basis(first_col, column_count, circle):
    position = first_col + jnp.arange(column_count, dtype=jnp.int32)
    wavenumber = jnp.arange(KMAX, dtype=jnp.int32)
    phase_index = position[:, None] * wavenumber[None, :] % circle
    phase_angle = phase_index.astype(jnp.float32) * (2.0 * math.pi / circle)
    return jnp.concatenate([jnp.cos(phase_angle), jnp.sin(phase_angle)], axis=1)


def mode_weights(cut_rows, circle):
    wavenumber = jnp.arange(KMAX, dtype=jnp.int32)
    mode_scale = jnp.where(wavenumber == 0, 1.0 / circle, 2.0 / circle).astype(jnp.float32)
    weights = jnp.where(wavenumber[None, :] < cut_rows[:, None], mode_scale[None, :], 0.0)
    return jnp.concatenate([weights, weights], axis=1)


def on_device(tracers, courant_x, courant_y, cutoffs):
    tracer_count, level_count, lat_rows, lon_cols = tracers.shape
    field_count = tracer_count * level_count
    lat_devices = lax.axis_size("lat")
    lon_devices = lax.axis_size("lon")
    lat_index = lax.axis_index("lat")
    lon_index = lax.axis_index("lon")
    circle = lon_cols * lon_devices
    total_rows = lat_rows * lat_devices
    row_global = lat_index * lat_rows + jnp.arange(lat_rows, dtype=jnp.int32)
    face_global = lat_index * lat_rows + jnp.arange(lat_rows + 1, dtype=jnp.int32)
    face_angle = (face_global.astype(jnp.float32) / total_rows - 0.5) * math.pi
    face_weight = jnp.where(
        (face_global == 0) | (face_global == total_rows), 0.0, jnp.cos(face_angle)
    )
    center_weight = jnp.cos(((row_global.astype(jnp.float32) + 0.5) / total_rows - 0.5) * math.pi)
    polar_rows = (row_global < total_rows // 4) | (row_global >= total_rows - total_rows // 4)
    basis_tile = dft_basis(lon_index * lon_cols, lon_cols, circle)
    state = tracers
    for substep in range(SUBSTEPS):
        flat_rows = state.reshape(field_count, lat_rows, lon_cols)
        stacked = jnp.concatenate([flat_rows, courant_x, courant_y], axis=0)
        padded = extended_2(stacked, (("lat", 1), ("lon", 2)), 3)
        pad_tracer = padded[:field_count].reshape(
            tracer_count, level_count, lat_rows + 6, lon_cols + 6
        )
        pad_east = padded[field_count : field_count + level_count]
        pad_north = padded[field_count + level_count :]
        east_courant = pad_east[:, 3 : 3 + lat_rows, 2 : lon_cols + 3]
        zonal = ppm_flux(pad_tracer[:, :, 3 : 3 + lat_rows, :], east_courant, 3, lon_cols)
        edge_rows = jnp.concatenate([state[:, :, :3], state[:, :, lat_rows - 3 :]], axis=2)
        antipodal = from_behind(edge_rows, "lon", lon_devices // 2)
        south_rows = jnp.where(
            lat_index == 0, antipodal[:, :, 2::-1], pad_tracer[:, :, :3, 3 : 3 + lon_cols]
        )
        north_rows = jnp.where(
            lat_index == lat_devices - 1,
            antipodal[:, :, 5:2:-1],
            pad_tracer[:, :, lat_rows + 3 :, 3 : 3 + lon_cols],
        )
        extended = jnp.concatenate(
            [south_rows, pad_tracer[:, :, 3 : 3 + lat_rows, 3 : 3 + lon_cols], north_rows], axis=2
        )
        north_courant = pad_north[:, 3 : lat_rows + 4, 3 : 3 + lon_cols]
        meridional = ppm_flux(extended, north_courant, 2, lat_rows) * face_weight[:, None]
        change = (
            zonal[..., 1:]
            - zonal[..., :-1]
            + (meridional[:, :, 1:] - meridional[:, :, :-1]) / center_weight[:, None]
        )
        state = state - change
        flat_rows = state.reshape(field_count * lat_rows, lon_cols)
        band_cuts = lax.dynamic_slice_in_dim(cutoffs, lat_index * lat_rows, lat_rows)
        cut_rows = jnp.tile(band_cuts, field_count)
        partial_value = jnp.dot(flat_rows, basis_tile, precision=lax.Precision.HIGHEST)
        spectra = lax.psum(partial_value, "lon")
        weighted = spectra * mode_weights(cut_rows, circle)
        smooth = jnp.dot(weighted, basis_tile.T, precision=lax.Precision.HIGHEST)
        polar_flat = jnp.tile(polar_rows, field_count)
        filtered_rows = jnp.where(polar_flat[:, None], smooth, flat_rows)
        state = filtered_rows.reshape(tracer_count, level_count, lat_rows, lon_cols)
    return state


def solution(mesh):
    in_specs = (P(None, None, "lat", "lon"), P(None, "lat", "lon"), P(None, "lat", "lon"), P())
    out_specs = P(None, None, "lat", "lon")
    return jax.shard_map(
        on_device, mesh=mesh, in_specs=in_specs, out_specs=out_specs, check_vma=False
    )
```

profile of v0, /device:TPU:3, one launch (start us, length us, event | category | flops | bytes accessed | tf_op | source)
XLA Modules:
  0.0 246.5 jit_solution(7881026659669633347)
XLA Ops:
  6.5 1.3 fusion.126
  7.9 0.9 pad_maximum_fusion.28
  8.8 2.3 collective-permute-start.4
  11.1 1.0 pad_maximum_fusion.25
  12.1 0.9 fusion.122
  13.0 2.1 collective-permute-start
  15.2 10.8 %fusion.5 = (f32[720,720]{1,0:T(8,128)S(1)}, f32[720,720]{1,0:T(8,128)}) fusion(s32[720]{0:T(1024)S(1)} %iota_add_fusion), kind=kLoop, calls=%fused_computation.8 | loop fusion | flops 4665600 | bytes 4150080 | tf_op jit(solution)/shard_map/cos | solution.py:65
  26.0 1.4 fusion.12
  27.5 1.3 collective-permute-start.2
  28.9 2.0 collective-permute-start.3
  30.9 0.8 abs_multiply_fusion.1
  31.7 4.3 %collective-permute-done.2 = f32[28,14,3]{2,1,0:T(8,128)S(1)} collective-permute-done((f32[28,14,3]{2,1,0:T(8,128)S(1)}, f32[28,14,3]{2,1,0:T(8,128)S(1)}, u32[]{:S(2)}, u32[]{:S(2)}) %collective-permute-start.2) | collective-permute-done | bytes 4736 | tf_op jit(solution)/shard_map/ppermute | solution.py:19
  36.0 7.4 %collective-permute-done.3 = f32[28,14,3]{2,1,0:T(8,128)S(1)} collective-permute-done((f32[28,14,3]{2,1,0:T(8,128)S(1)}, f32[28,14,3]{2,1,0:T(8,128)S(1)}, u32[]{:S(2)}, u32[]{:S(2)}) %collective-permute-start.3) | collective-permute-done | bytes 4736 | tf_op jit(solution)/shard_map/ppermute | solution.py:21
  43.4 1.7 fusion.60
  45.6 0.9 broadcast_compare_fusion.3
  46.5 1.0 slice.329
  47.5 1.4 fusion.98
  48.9 2.1 fusion.125
  51.0 3.7 %rev.12 = f32[5,4,3,720]{3,2,1,0:T(4,128)} reverse(f32[5,4,3,720]{3,2,1,0:T(4,128)} %get-tuple-element.29), dimensions={2} | reverse | bytes 345600 | tf_op jit(solution)/shard_map/rev | solution.py:108
  54.7 3.7 %rev.13 = f32[5,4,3,720]{3,2,1,0:T(4,128)} reverse(f32[5,4,3,720]{3,2,1,0:T(4,128)} %get-tuple-element.30), dimensions={2} | reverse | bytes 345600 | tf_op jit(solution)/shard_map/rev | solution.py:112
  58.8 1.2 pad_maximum_fusion.21
  61.1 1.0 fusion.43
  62.5 1.4 copy-done
  63.9 4.2 %fusion.10 = f32[160,1440]{1,0:T(8,128)} fusion(f32[160,720]{1,0:T(8,128)S(1)} %bitcast.30, f32[720,720]{1,0:T(8,128)S(1)} %copy-done, f32[720,720]{1,0:T(8,128)S(1)} %get-tuple-element.41), kind=kOutput, calls=%fused_computation.13 | convolution fusion | flops 1991692800 | bytes 5529600 | tf_op jit(solution)/shard_map/dot_general | solution.py:129
  68.7 0.9 fusion.107
  69.6 50.3 %all-reduce.3.cloned.1.call-done = f32[160,1440]{1,0:T(8,128)} async-done(((f32[160,1440]{1,0:T(8,128)}), f32[160,1440]{1,0:T(8,128)}) %all-reduce.3.cloned.1.call-update) | async-done | bytes 921616 | tf_op jit(solution)/shard_map/psum | solution.py:130
  119.8 6.8 %fusion.15 = f32[160,720]{1,0:T(8,128)S(1)} fusion(f32[160,720]{1,0:T(8,128)S(1)} %bitcast.31, f32[720,720]{1,0:T(8,128)} %get-tuple-element.42, f32[720,720]{1,0:T(8,128)S(1)} %get-tuple-element.41, f32[160,1440]{1,0:T(8,128)} %all-reduce.3.cloned.1.call-done, f32[160,720]{1,0:T(8,128)} %fusion.107, pred[160]{0:T(512)(128)(4,1)S(1)} %broadcast_in_dim.83), kind=kOutput, calls=%fused_computation.34 | convolution fusion | flops 1992268800 | bytes 6451360 | tf_op jit(solution)/shard_map/dot_general | solution.py:132
  126.8 1.7 collective-permute-start.5
  128.7 1.4 collective-permute-start.9
  130.1 5.4 %collective-permute-done.5 = f32[28,3,720]{2,1,0:T(4,128)S(1)} collective-permute-done((f32[28,3,720]{2,1,0:T(4,128)S(1)}, f32[28,3,720]{2,1,0:T(4,128)S(1)}, u32[]{:S(2)}, u32[]{:S(2)}) %collective-permute-start.5) | collective-permute-done | bytes 241952 | tf_op jit(solution)/shard_map/ppermute | solution.py:19
  135.6 2.5 %collective-permute-done.6 = f32[28,3,720]{2,1,0:T(4,128)S(1)} collective-permute-done((f32[28,3,720]{2,1,0:T(4,128)S(1)}, f32[28,3,720]{2,1,0:T(4,128)S(1)}, u32[]{:S(2)}, u32[]{:S(2)}) %collective-permute-start.6) | collective-permute-done | bytes 241952 | tf_op jit(solution)/shard_map/ppermute | solution.py:21
  138.5 1.4 collective-permute-start.7
  139.8 2.0 collective-permute-start.8
  141.8 0.8 abs_multiply_fusion
  142.6 5.3 %collective-permute-done.7 = f32[28,14,3]{2,1,0:T(8,128)S(1)} collective-permute-done((f32[28,14,3]{2,1,0:T(8,128)S(1)}, f32[28,14,3]{2,1,0:T(8,128)S(1)}, u32[]{:S(2)}, u32[]{:S(2)}) %collective-permute-start.7) | collective-permute-done | bytes 4736 | tf_op jit(solution)/shard_map/ppermute | solution.py:19
  148.0 13.0 %collective-permute-done.8 = f32[28,14,3]{2,1,0:T(8,128)S(1)} collective-permute-done((f32[28,14,3]{2,1,0:T(8,128)S(1)}, f32[28,14,3]{2,1,0:T(8,128)S(1)}, u32[]{:S(2)}, u32[]{:S(2)}) %collective-permute-start.8) | collective-permute-done | bytes 4736 | tf_op jit(solution)/shard_map/ppermute | solution.py:21
  161.0 0.7 fusion.64
  162.3 1.0 slice.362
  163.2 1.4 fusion.80
  164.6 0.9 fusion.123
  165.5 3.8 %rev.14 = f32[5,4,3,720]{3,2,1,0:T(4,128)} reverse(f32[5,4,3,720]{3,2,1,0:T(4,128)} %get-tuple-element.25), dimensions={2} | reverse | bytes 345600 | tf_op jit(solution)/shard_map/rev | solution.py:108
  169.3 3.8 %rev.15 = f32[5,4,3,720]{3,2,1,0:T(4,128)} reverse(f32[5,4,3,720]{3,2,1,0:T(4,128)} %get-tuple-element.26), dimensions={2} | reverse | bytes 345600 | tf_op jit(solution)/shard_map/rev | solution.py:112
  173.0 1.5 slice_select_fusion.1
  175.9 1.0 fusion.26
  177.1 1.4 copy-done.1
  178.5 4.2 %fusion.8 = f32[160,1440]{1,0:T(8,128)} fusion(f32[160,720]{1,0:T(8,128)S(1)} %bitcast.32, f32[720,720]{1,0:T(8,128)S(1)} %copy-done.1, f32[720,720]{1,0:T(8,128)S(1)} %get-tuple-element.41), kind=kOutput, calls=%fused_computation.11 | convolution fusion | flops 1991692800 | bytes 5529600 | tf_op jit(solution)/shard_map/dot_general | solution.py:129
  182.7 49.6 %all-reduce.5.cloned.1.call-done = f32[160,1440]{1,0:T(8,128)} async-done(((f32[160,1440]{1,0:T(8,128)}), f32[160,1440]{1,0:T(8,128)}) %all-reduce.5.cloned.1.call-update) | async-done | bytes 921616 | tf_op jit(solution)/shard_map/psum | solution.py:130
  232.3 7.3 %fusion.16 = f32[160,720]{1,0:T(8,128)} fusion(f32[160,720]{1,0:T(8,128)S(1)} %bitcast.33, f32[720,720]{1,0:T(8,128)} %get-tuple-element.42, f32[720,720]{1,0:T(8,128)S(1)} %get-tuple-element.41, f32[160,1440]{1,0:T(8,128)} %all-reduce.5.cloned.1.call-done, f32[160,720]{1,0:T(8,128)S(1)} %copy-done.14, pred[160]{0:T(512)(128)(4,1)S(1)} %broadcast_in_dim.83), kind=kOutput, calls=%fused_computation.35 | convolution fusion | flops 1992268800 | bytes 6451360 | tf_op jit(solution)/shard_map/dot_general | solution.py:132
  (86 shorter events, 6.1 us)
Async XLA Ops:
  6.5 4.5 %copy-start.3 = (f32[5,4,8,720]{3,2,1,0:T(8,128)S(1)}, f32[5,4,8,720]{3,2,1,0:T(8,128)}, u32[]{:S(2)}) copy-start(f32[5,4,8,720]{3,2,1,0:T(8,128)} %param.4) | copy-start | bytes 1382404
  6.5 113.3 %all-reduce.3.cloned.1.call-start = ((), (), s32[]{:S(2)}) async-start(), calls=%async_computation | async-start | bytes 1966080 | tf_op jit(solution)/shard_map/psum | solution.py:130
  8.8 40.1 %collective-permute-start.4 = (f32[5,4,6,720]{3,2,1,0:T(8,128)}, f32[5,4,6,720]{3,2,1,0:T(8,128)}, u32[]{:S(2)}, u32[]{:S(2)}) collective-permute-start(f32[5,4,6,720]{3,2,1,0:T(8,128)} %pad_maximum_fusion.28), channel_id=1, source_target_pairs={{0,2},{1,3},{2,0},{3,1},{4,6},{5,7},{6,4},{7,5},{8,10},{9,11},{10,... | collective-permute-start | bytes 1036808 | tf_op jit(solution)/shard_map/ppermute | solution.py:30
  13.0 13.0 %collective-permute-start = (f32[28,3,720]{2,1,0:T(4,128)}, f32[28,3,720]{2,1,0:T(4,128)}, u32[]{:S(2)}, u32[]{:S(2)}) collective-permute-start(f32[28,3,720]{2,1,0:T(4,128)} %get-tuple-element.23), channel_id=1, source_target_pairs={{0,4},{4,8},{8,12},{12,16},{16,20},{20,24},{24,28},{28,0},{1,5},{5... | collective-permute-start | bytes 725768 | tf_op jit(solution)/shard_map/ppermute | solution.py:19
  15.1 10.9 %collective-permute-start.1 = (f32[28,3,720]{2,1,0:T(4,128)}, f32[28,3,720]{2,1,0:T(4,128)S(1)}, u32[]{:S(2)}, u32[]{:S(2)}) collective-permute-start(f32[28,3,720]{2,1,0:T(4,128)} %get-tuple-element.24), channel_id=1, source_target_pairs={{4,0},{8,4},{12,8},{16,12},{20,16},{24,20},{28,24},{0,28},{5,1},{9... | collective-permute-start | bytes 725768 | tf_op jit(solution)/shard_map/ppermute | solution.py:21
  15.2 10.8 %copy-start.6 = (f32[4,8,720]{2,1,0:T(8,128)S(1)}, f32[4,8,720]{2,1,0:T(8,128)}, u32[]{:S(2)}) copy-start(f32[4,8,720]{2,1,0:T(8,128)} %param.6) | copy-start | bytes 276484
  15.2 10.8 %copy-start.7 = (f32[4,8,720]{2,1,0:T(8,128)S(1)}, f32[4,8,720]{2,1,0:T(8,128)}, u32[]{:S(2)}) copy-start(f32[4,8,720]{2,1,0:T(8,128)} %param.5) | copy-start | bytes 276484
  26.0 17.4 %copy-start.4 = (f32[5,4,8,720]{3,2,1,0:T(8,128)S(1)}, f32[5,4,8,720]{3,2,1,0:T(8,128)}, u32[]{:S(2)}) copy-start(f32[5,4,8,720]{3,2,1,0:T(8,128)} %param.4) | copy-start | bytes 1382404
  26.0 4.9 %copy-start.10 = (f32[28,3,720]{2,1,0:T(4,128)}, f32[28,3,720]{2,1,0:T(4,128)S(1)}, u32[]{:S(2)}) copy-start(f32[28,3,720]{2,1,0:T(4,128)S(1)} %collective-permute-done.1) | copy-start | bytes 725764
  27.5 8.5 %collective-permute-start.2 = (f32[28,14,3]{2,1,0:T(8,128)S(1)}, f32[28,14,3]{2,1,0:T(8,128)S(1)}, u32[]{:S(2)}, u32[]{:S(2)}) collective-permute-start(f32[28,14,3]{2,1,0:T(8,128)S(1)} %get-tuple-element.15), channel_id=1, source_target_pairs={{0,1},{1,2},{2,3},{3,0},{4,5},{5,6},{6,7},{7,4},{8,9},{9,10},{10,1... | collective-permute-start | bytes 14120 | tf_op jit(solution)/shard_map/ppermute | solution.py:19
  28.9 14.5 %collective-permute-start.3 = (f32[28,14,3]{2,1,0:T(8,128)S(1)}, f32[28,14,3]{2,1,0:T(8,128)S(1)}, u32[]{:S(2)}, u32[]{:S(2)}) collective-permute-start(f32[28,14,3]{2,1,0:T(8,128)S(1)} %get-tuple-element.16), channel_id=1, source_target_pairs={{1,0},{2,1},{3,2},{0,3},{5,4},{6,5},{7,6},{4,7},{9,8},{10,9},{11,1... | collective-permute-start | bytes 14120 | tf_op jit(solution)/shard_map/ppermute | solution.py:21
  30.9 5.1 %copy-start.17 = (f32[4,9,720]{2,1,0:T(8,128)}, f32[4,9,720]{2,1,0:T(8,128)S(1)}, u32[]{:S(2)}) copy-start(f32[4,9,720]{2,1,0:T(8,128)S(1)} %get-tuple-element.12) | copy-start | bytes 311044
  31.7 13.9 %copy-start.11 = (f32[28,3,720]{2,1,0:T(4,128)S(1)}, f32[28,3,720]{2,1,0:T(4,128)}, u32[]{:S(2)}) copy-start(f32[28,3,720]{2,1,0:T(4,128)} %copy-done.10) | copy-start | bytes 725764
  58.4 1.6 copy-start.9
  60.0 0.9 copy-start.18
  60.0 1.0 copy-start.21
  60.0 1.1 copy-start.22
  61.1 1.0 copy-start.5
  61.1 1.2 copy-start.13
  62.3 1.6 copy-start
  63.9 4.6 %copy-start.23 = (s32[64]{0:T(128)S(1)}, s32[64]{0:T(128)}, u32[]{:S(2)}) copy-start(s32[64]{0:T(128)} %param.7) | copy-start | bytes 772
  68.2 164.2 %all-reduce.5.cloned.1.call-start = ((), (), s32[]{:S(2)}) async-start(), calls=%async_computation.1 | async-start | bytes 1966080 | tf_op jit(solution)/shard_map/psum | solution.py:130
  126.8 8.7 %collective-permute-start.5 = (f32[28,3,720]{2,1,0:T(4,128)S(1)}, f32[28,3,720]{2,1,0:T(4,128)S(1)}, u32[]{:S(2)}, u32[]{:S(2)}) collective-permute-start(f32[28,3,720]{2,1,0:T(4,128)S(1)} %get-tuple-element.21), channel_id=1, source_target_pairs={{0,4},{4,8},{8,12},{12,16},{16,20},{20,24},{24,28},{28,0},{1,5},{5... | collective-permute-start | bytes 725768 | tf_op jit(solution)/shard_map/ppermute | solution.py:19
  128.5 9.5 %collective-permute-start.6 = (f32[28,3,720]{2,1,0:T(4,128)S(1)}, f32[28,3,720]{2,1,0:T(4,128)S(1)}, u32[]{:S(2)}, u32[]{:S(2)}) collective-permute-start(f32[28,3,720]{2,1,0:T(4,128)S(1)} %get-tuple-element.22), channel_id=1, source_target_pairs={{4,0},{8,4},{12,8},{16,12},{20,16},{24,20},{28,24},{0,28},{5,1},{9... | collective-permute-start | bytes 725768 | tf_op jit(solution)/shard_map/ppermute | solution.py:21
  128.7 35.9 %collective-permute-start.9 = (f32[5,4,6,720]{3,2,1,0:T(8,128)S(1)}, f32[5,4,6,720]{3,2,1,0:T(8,128)S(1)}, u32[]{:S(2)}, u32[]{:S(2)}) collective-permute-start(f32[5,4,6,720]{3,2,1,0:T(8,128)S(1)} %pad_maximum_fusion.29), channel_id=1, source_target_pairs={{0,2},{1,3},{2,0},{3,1},{4,6},{5,7},{6,4},{7,5},{8,10},{9,11},{10,... | collective-permute-start | bytes 1036808 | tf_op jit(solution)/shard_map/ppermute | solution.py:30
  138.5 9.5 %collective-permute-start.7 = (f32[28,14,3]{2,1,0:T(8,128)S(1)}, f32[28,14,3]{2,1,0:T(8,128)S(1)}, u32[]{:S(2)}, u32[]{:S(2)}) collective-permute-start(f32[28,14,3]{2,1,0:T(8,128)S(1)} %get-tuple-element.13), channel_id=1, source_target_pairs={{0,1},{1,2},{2,3},{3,0},{4,5},{5,6},{6,7},{7,4},{8,9},{9,10},{10,1... | collective-permute-start | bytes 14120 | tf_op jit(solution)/shard_map/ppermute | solution.py:19
  139.8 21.2 %collective-permute-start.8 = (f32[28,14,3]{2,1,0:T(8,128)S(1)}, f32[28,14,3]{2,1,0:T(8,128)S(1)}, u32[]{:S(2)}, u32[]{:S(2)}) collective-permute-start(f32[28,14,3]{2,1,0:T(8,128)S(1)} %get-tuple-element.14), channel_id=1, source_target_pairs={{1,0},{2,1},{3,2},{0,3},{5,4},{6,5},{7,6},{4,7},{9,8},{10,9},{11,1... | collective-permute-start | bytes 14120 | tf_op jit(solution)/shard_map/ppermute | solution.py:21
  141.8 6.2 %copy-start.15 = (f32[4,9,720]{2,1,0:T(8,128)}, f32[4,9,720]{2,1,0:T(8,128)S(1)}, u32[]{:S(2)}) copy-start(f32[4,9,720]{2,1,0:T(8,128)S(1)} %get-tuple-element.8) | copy-start | bytes 311044
  161.6 1.6 copy-start.2
  164.6 9.9 %copy-start.8 = (f32[5,4,8,720]{3,2,1,0:T(8,128)S(1)}, f32[5,4,8,720]{3,2,1,0:T(8,128)}, u32[]{:S(2)}) copy-start(f32[5,4,8,720]{3,2,1,0:T(8,128)} %slice.362) | copy-start | bytes 1382404
  174.7 0.9 copy-start.16
  174.7 1.0 copy-start.19
  174.7 1.1 copy-start.20
  175.8 1.0 copy-start.12
  176.9 1.6 copy-start.1
  178.5 53.8 %copy-start.14 = (f32[160,720]{1,0:T(8,128)S(1)}, f32[160,720]{1,0:T(8,128)}, u32[]{:S(2)}) copy-start(f32[160,720]{1,0:T(8,128)} %fusion.107) | copy-start | bytes 1382404
Sparse Core Ops, SparseCore 0:
  68.3 51.5 all-reduce.2
  182.9 49.4 all-reduce.4
where the time goes:
time: 250 us; the launch traced here: 246 us
  waiting for transfers between devices  138 us (55%)
  other arithmetic  30.7 us (12%)
  local copies, waits for them, and re-layouts  27.3 us (11%)
  matrix products  22.5 us (9%)
  starting transfers between devices  14.3 us (6%)
  between operations  13.8 us (6%)
    psum x2, waiting for transfers between devices, on_device(): spectra = lax.psum(partial_value, 'lon')  99.8 us
    ppermute x4, waiting for transfers between devices, extended_2(): lax.ppermute(head, axis, [((i + 1) % count, i) for i in range(count)])  22.8 us
    ppermute x4, waiting for transfers between devices, extended_2(): lax.ppermute(tail, axis, [(i, (i + 1) % count) for i in range(count)])  15.1 us
    dot_general x2, matrix products, on_device(): smooth = jnp.dot(weighted, basis_tile.T, precision=lax.Precision.HIGHEST)  14.1 us
    cos x1, other arithmetic, dft_basis(): return jnp.concatenate([jnp.cos(phase_angle), jnp.sin(phase_angle)], axis=1)  10.8 us
    dot_general x2, matrix products, on_device(): jnp.dot(flat_rows, basis_tile, precision=lax.Precision.HIGHEST)  8.41 us
    rev x2, local copies, waits for them, and re-layouts, on_device(): antipodal[:, :, 2::-1]  7.49 us
    rev x2, local copies, waits for them, and re-layouts, on_device(): antipodal[:, :, 5:2:-1]  7.48 us
  transfers between devices with their start and end apart: 12, of which 8 were waited for; matrix products, arithmetic and copies ran while one was open for 11% of the time, Pallas kernels for 0%

commit v1 on v0

v1 whole, which is shorter than its diff:
```python
import math

import jax
import jax.numpy as jnp
from jax import lax
from jax.sharding import PartitionSpec as P

KMAX = 720
SUBSTEPS = 2
HALO = 3
HIGHEST = lax.Precision.HIGHEST


def shift(x, axis, by, wrap):
    size = lax.axis_size(axis)
    pairs = [(i, (i + by) % size) for i in range(size) if wrap or 0 <= i + by < size]
    return lax.ppermute(x, axis, pairs)


def window(values, first_cell, last_cell, dim_at):
    return lax.slice_in_dim(values, first_cell, last_cell, axis=dim_at)


def ppm_flux(padded, courant, dim_at, cell_count):
    edge_values = 7.0 / 12.0 * (
        window(padded, 1, cell_count + 4, dim_at) + window(padded, 2, cell_count + 5, dim_at)
    ) - 1.0 / 12.0 * (
        window(padded, 0, cell_count + 3, dim_at) + window(padded, 3, cell_count + 6, dim_at)
    )
    left_edge = window(edge_values, 0, cell_count + 1, dim_at)
    mid_edge = window(edge_values, 1, cell_count + 2, dim_at)
    right_edge = window(edge_values, 2, cell_count + 3, dim_at)
    left_cell = window(padded, 2, cell_count + 3, dim_at)
    right_cell = window(padded, 3, cell_count + 4, dim_at)
    magnitude = jnp.abs(courant)
    six_left = 6.0 * left_cell - 3.0 * (left_edge + mid_edge)
    six_right = 6.0 * right_cell - 3.0 * (mid_edge + right_edge)
    from_left = mid_edge - 0.5 * magnitude * (
        mid_edge - left_edge - (1.0 - magnitude * (2.0 / 3.0)) * six_left
    )
    from_right = mid_edge + 0.5 * magnitude * (
        right_edge - mid_edge + (1.0 - magnitude * (2.0 / 3.0)) * six_right
    )
    return courant * jnp.where(courant >= 0.0, from_left, from_right)


def root_table(count):
    d = jnp.arange(count, dtype=jnp.int32)
    angle = (d[:, None] * d[None, :] % count).astype(jnp.float32) * (2.0 * math.pi / count)
    cos_dr, sin_dr = jnp.cos(angle), jnp.sin(angle)
    cos_dr = jnp.where(jnp.abs(cos_dr) < 1e-6, 0.0, cos_dr)
    sin_dr = jnp.where(jnp.abs(sin_dr) < 1e-6, 0.0, sin_dr)
    return cos_dr, sin_dr


def class_basis(tiles, cols, circle):
    per_class = KMAX // tiles
    r = jnp.arange(tiles, dtype=jnp.int32)
    m = jnp.arange(per_class, dtype=jnp.int32)
    q = jnp.arange(-HALO, cols + HALO, dtype=jnp.int32) % circle
    k = tiles * m[None, :] + r[:, None]
    phase = (q[None, :, None] * k[:, None, :]) % circle
    angle = phase.astype(jnp.float32) * (2.0 * math.pi / circle)
    return jnp.concatenate([jnp.cos(angle), jnp.sin(angle)], axis=2)


def filter_rows(rows, basis, roots, weights, polar):
    tiles, count, cols = rows.shape
    cos_dr, sin_dr = roots
    z_re = jnp.sum(cos_dr[:, :, None, None] * rows[None], axis=1)
    z_im = -jnp.sum(sin_dr[:, :, None, None] * rows[None], axis=1)
    z = jnp.concatenate([z_re, z_im], axis=1)
    z = jnp.pad(z, ((0, 0), (0, 0), (HALO, HALO)))
    prod = lax.dot_general(z, basis, (((2,), (1,)), ((0,), (0,))), precision=HIGHEST)
    per_class = basis.shape[2] // 2
    zc, zs = prod[:, :count, :per_class], prod[:, :count, per_class:]
    wc, ws = prod[:, count:, :per_class], prod[:, count:, per_class:]
    real = (zc + ws) * weights
    imag = (zs - wc) * weights
    spec = jnp.concatenate(
        [jnp.concatenate([real, imag], axis=2), jnp.concatenate([-imag, real], axis=2)], axis=1
    )
    back = lax.dot_general(spec, basis, (((2,), (2,)), ((0,), (0,))), precision=HIGHEST)
    w_re, w_im = back[:, :count], back[:, count:]
    smooth = jnp.sum(
        cos_dr[:, :, None, None] * w_re[None] - sin_dr[:, :, None, None] * w_im[None], axis=1
    )
    left = jnp.roll(rows[:, :, cols - HALO :], 1, axis=0)
    right = jnp.roll(rows[:, :, :HALO], -1, axis=0)
    wide = jnp.concatenate([left, rows, right], axis=2)
    return jnp.where(polar[None, :, None], smooth, wide)


def on_device(tracers, courant_x, courant_y, cutoffs):
    tracer_count, level_count, lat_rows, lon_cols = tracers.shape
    field_count = tracer_count * level_count
    lat_devices = lax.axis_size("lat")
    lon_devices = lax.axis_size("lon")
    lat_index = lax.axis_index("lat")
    lon_index = lax.axis_index("lon")
    circle = lon_cols * lon_devices
    total_rows = lat_rows * lat_devices
    row_global = lat_index * lat_rows + jnp.arange(lat_rows, dtype=jnp.int32)
    face_global = lat_index * lat_rows + jnp.arange(lat_rows + 1, dtype=jnp.int32)
    face_angle = (face_global.astype(jnp.float32) / total_rows - 0.5) * math.pi
    face_weight = jnp.where(
        (face_global == 0) | (face_global == total_rows), 0.0, jnp.cos(face_angle)
    )
    center_weight = jnp.cos(((row_global.astype(jnp.float32) + 0.5) / total_rows - 0.5) * math.pi)
    is_south = lat_index == 0
    is_north = lat_index == lat_devices - 1

    count = field_count * lat_rows // lon_devices
    flat = lon_index * count + jnp.arange(count, dtype=jnp.int32)
    held_global = lat_index * lat_rows + flat % lat_rows
    polar = (held_global < total_rows // 4) | (held_global >= total_rows - total_rows // 4)
    cut = jnp.take(cutoffs, held_global)
    per_class = KMAX // lon_devices
    k = lon_devices * jnp.arange(per_class, dtype=jnp.int32)[None, :] + jnp.arange(
        lon_devices, dtype=jnp.int32
    )[:, None]
    scale = jnp.where(k == 0, 1.0 / circle, 2.0 / circle).astype(jnp.float32)
    weights = jnp.where(k[:, None, :] < cut[None, :, None], scale[:, None, :], 0.0)
    basis = class_basis(lon_devices, lon_cols, circle)
    roots = root_table(lon_devices)

    west_cx = shift(courant_x[:, :, lon_cols - 1 :], "lon", 1, True)
    north_cy = shift(courant_y[:, :1], "lat", -1, False)
    east_courant = jnp.concatenate([west_cx, courant_x], axis=2)
    north_courant = jnp.concatenate(
        [courant_y, jnp.where(is_north, 0.0, north_cy)], axis=1
    )

    def lat_halos(state):
        south_in = shift(state[:, :, lat_rows - HALO :], "lat", 1, False)
        north_in = shift(state[:, :, :HALO], "lat", -1, False)
        edge = jnp.where(is_south, state[:, :, :HALO], state[:, :, lat_rows - HALO :])
        far = shift(edge, "lon", lon_devices // 2, True)
        far_rev = jnp.concatenate([far[:, :, 2:3], far[:, :, 1:2], far[:, :, 0:1]], axis=2)
        south_rows = jnp.where(is_south, far_rev, south_in)
        north_rows = jnp.where(is_north, far_rev, north_in)
        return jnp.concatenate([south_rows, state, north_rows], axis=2)

    state = tracers
    west_in = shift(state[..., lon_cols - HALO :], "lon", 1, True)
    east_in = shift(state[..., :HALO], "lon", -1, True)
    wrapped = jnp.concatenate([west_in, state, east_in], axis=3)
    for substep in range(SUBSTEPS):
        extended = lat_halos(state)
        zonal = ppm_flux(wrapped, east_courant, 3, lon_cols)
        meridional = ppm_flux(extended, north_courant, 2, lat_rows) * face_weight[:, None]
        change = (
            zonal[..., 1:]
            - zonal[..., :-1]
            + (meridional[:, :, 1:] - meridional[:, :, :-1]) / center_weight[:, None]
        )
        state = state - change
        rows = state.reshape(lon_devices, count, lon_cols)
        rows = lax.all_to_all(rows, "lon", 0, 0)
        wide = filter_rows(rows, basis, roots, weights, polar)
        if substep == SUBSTEPS - 1:
            wide = wide[:, :, HALO : HALO + lon_cols]
        wide = lax.all_to_all(wide, "lon", 0, 0)
        wrapped = wide.reshape(tracer_count, level_count, lat_rows, wide.shape[2])
        state = wrapped if substep == SUBSTEPS - 1 else wrapped[..., HALO : HALO + lon_cols]
    return state


def solution(mesh):
    in_specs = (P(None, None, "lat", "lon"), P(None, "lat", "lon"), P(None, "lat", "lon"), P())
    out_specs = P(None, None, "lat", "lon")
    return jax.shard_map(
        on_device, mesh=mesh, in_specs=in_specs, out_specs=out_specs, check_vma=False
    )
```

time: 250 us -> 140 us (0.56)
  waiting for transfers between devices: 138 us -> 15.8 us
  blocking collectives: 0 us -> 47.2 us
  local copies, waits for them, and re-layouts: 27.3 us -> 6.75 us
  between operations: 13.8 us -> 0.59 us
  starting transfers between devices: 14.3 us -> 26.2 us
  matrix products: 22.5 us -> 14.7 us
  other arithmetic: 30.7 us -> 26 us
    psum x2 -> x0, waiting for transfers between devices: 99.8 us -> none  [on_device(): spectra = lax.psum(partial_value, 'lon')]
    all_to_all x0 -> x3, blocking collectives: none -> 47.2 us  [the longest x2 31.8 us: on_device(): wide = lax.all_to_all(wide, 'lon', 0, 0)]
    ppermute x10, waiting for transfers between devices: 37.9 us -> 14.4 us  [shift(): return lax.ppermute(x, axis, pairs)]
    rev x4 -> x0, local copies, waits for them, and re-layouts: 15 us -> none  [the longest x2 7.49 us: on_device(): antipodal[:, :, 2::-1]]
    ppermute x10, starting transfers between devices: 14.1 us -> 22.6 us  [shift(): return lax.ppermute(x, axis, pairs)]
    dot_general x4, matrix products: 22.5 us -> 14.7 us  [the longest x2 8.23 us: filter_rows(): lax.dot_general(z, basis, (((2,), (1,)), ((0,), (0,))), precision=HIGHEST)]
    concatenate x10 -> x4, other arithmetic: 7.47 us -> 0.62 us  [the longest x2 0.36 us: lat_halos(): return jnp.concatenate([south_rows, state, north_rows], axis=2)]
    slice x10 -> x12, local copies, waits for them, and re-layouts: 7.62 us -> 3.59 us  [the longest x1 1.01 us: on_device(): west_in = shift(state[..., lon_cols - HALO:], 'lon', 1, True)]
  transfers between devices with their start and end apart: 12 -> 11, of which waited for: 8 -> 4; matrix products, arithmetic and copies ran while one was open for 11% -> 15% of each run, Pallas kernels for 0% -> 0%
where the time goes in v1:
time: 140 us; the launch traced here: 137 us
  blocking collectives  47.2 us (34%)
  starting transfers between devices  26.2 us (19%)
  other arithmetic  26 us (19%)
  waiting for transfers between devices  15.8 us (11%)
  matrix products  14.7 us (10%)
  local copies, waits for them, and re-layouts  6.75 us (5%)
    all_to_all x2, blocking collectives, on_device(): wide = lax.all_to_all(wide, 'lon', 0, 0)  31.8 us
    ppermute x10, starting transfers between devices, shift(): return lax.ppermute(x, axis, pairs)  22.6 us
    all_to_all x1, blocking collectives, on_device(): rows = lax.all_to_all(rows, 'lon', 0, 0)  15.4 us
    ppermute x10, waiting for transfers between devices, shift(): return lax.ppermute(x, axis, pairs)  14.4 us
    cos x1, other arithmetic, class_basis(): return jnp.concatenate([jnp.cos(angle), jnp.sin(angle)], axis=2)  11.1 us
    dot_general x2, matrix products, filter_rows(): lax.dot_general(z, basis, (((2,), (1,)), ((0,), (0,))), precision=HIGHEST)  8.23 us
    dot_general x2, matrix products, filter_rows(): lax.dot_general(spec, basis, (((2,), (2,)), ((0,), (0,))), precision=HIGH...  6.47 us
    all_to_all x1, starting transfers between devices, on_device(): rows = lax.all_to_all(rows, 'lon', 0, 0)  3.65 us
  transfers between devices with their start and end apart: 11, of which 4 were waited for; matrix products, arithmetic and copies ran while one was open for 15% of the time, Pallas kernels for 0%

profile of v1, /device:TPU:3, one launch (start us, length us, event | category | flops | bytes accessed | tf_op | source)
XLA Modules:
  0.0 137.3 jit_solution(10465575918507018692)
XLA Ops:
  0.0 1.4 fusion.161
  1.4 3.7 %collective-permute-start.5 = (f32[5,4,3,720]{3,2,1,0:T(4,128)S(1)}, f32[5,4,3,720]{3,2,1,0:T(4,128)S(1)}, u32[]{:S(2)}, u32[]{:S(2)}) collective-permute-start(f32[5,4,3,720]{3,2,1,0:T(4,128)S(1)} %get-tuple-element.34), channel_id=1, source_target_pairs={{0,4},{4,8},{8,12},{12,16},{16,20},{20,24},{24,28},{1,5},{5,9},{9,... | collective-permute-start | bytes 518408 | tf_op jit(solution)/shard_map/ppermute | solution.py:17
  5.1 2.4 %collective-permute-start.4 = (f32[5,4,3,720]{3,2,1,0:T(4,128)S(1)}, f32[5,4,3,720]{3,2,1,0:T(4,128)S(1)}, u32[]{:S(2)}, u32[]{:S(2)}) collective-permute-start(f32[5,4,3,720]{3,2,1,0:T(4,128)S(1)} %get-tuple-element.35), channel_id=1, source_target_pairs={{0,2},{1,3},{2,0},{3,1},{4,6},{5,7},{6,4},{7,5},{8,10},{9,11},{10,... | collective-permute-start | bytes 518408 | tf_op jit(solution)/shard_map/ppermute | solution.py:17
  7.4 1.9 %collective-permute-start.6 = (f32[5,4,3,720]{3,2,1,0:T(4,128)S(1)}, f32[5,4,3,720]{3,2,1,0:T(4,128)S(1)}, u32[]{:S(2)}, u32[]{:S(2)}) collective-permute-start(f32[5,4,3,720]{3,2,1,0:T(4,128)S(1)} %get-tuple-element.36), channel_id=1, source_target_pairs={{4,0},{8,4},{12,8},{16,12},{20,16},{24,20},{28,24},{5,1},{9,5},{13... | collective-permute-start | bytes 518408 | tf_op jit(solution)/shard_map/ppermute | solution.py:17
  9.3 1.0 fusion.160
  10.4 1.1 collective-permute-start.2
  11.5 0.8 slice.262
  12.3 0.4 collective-permute-start
  12.7 0.6 add_select_fusion.1
  13.5 0.8 gather_fusion
  14.2 0.6 and_select_fusion.1
  14.8 0.9 slice.274
  15.7 1.1 collective-permute-done
  16.8 4.4 %collective-permute-start.1 = (f32[5,4,8,3]{3,2,1,0:T(8,128)S(1)}, f32[5,4,8,3]{3,2,1,0:T(8,128)S(1)}, u32[]{:S(2)}, u32[]{:S(2)}) collective-permute-start(f32[5,4,8,3]{3,2,1,0:T(8,128)S(1)} %get-tuple-element.32), channel_id=1, source_target_pairs={{0,1},{1,2},{2,3},{3,0},{4,5},{5,6},{6,7},{7,4},{8,9},{9,10},{10,1... | collective-permute-start | bytes 5768 | tf_op jit(solution)/shard_map/ppermute | solution.py:17
  21.2 1.0 broadcast_compare_fusion.1
  22.3 2.5 %collective-permute-start.3 = (f32[4,1,720]{2,1,0:T(1,128)S(1)}, f32[4,1,720]{2,1,0:T(1,128)S(1)}, u32[]{:S(2)}, u32[]{:S(2)}) collective-permute-start(f32[4,1,720]{2,1,0:T(1,128)S(1)} %slice.274), channel_id=1, source_target_pairs={{4,0},{8,4},{12,8},{16,12},{20,16},{24,20},{28,24},{5,1},{9,5},{13... | collective-permute-start | bytes 34568 | tf_op jit(solution)/shard_map/ppermute | solution.py:17
  25.0 0.5 fusion.64
  25.5 0.5 fusion.73
  26.1 2.2 %collective-permute-done.3 = f32[4,1,720]{2,1,0:T(1,128)S(1)} collective-permute-done((f32[4,1,720]{2,1,0:T(1,128)S(1)}, f32[4,1,720]{2,1,0:T(1,128)S(1)}, u32[]{:S(2)}, u32[]{:S(2)}) %collective-permute-start.3) | collective-permute-done | bytes 11552 | tf_op jit(solution)/shard_map/ppermute | solution.py:17
  29.0 0.4 fusion.50
  29.4 1.0 fusion.37
  30.4 1.0 fusion.108
  31.4 3.6 %all-to-all-start = ((f32[4,40,720]{2,1,0:T(8,128)}), f32[4,40,720]{2,1,0:T(8,128)S(1)}, u32[]{:S(2)}, u32[]{:S(2)}) async-start(f32[4,40,720]{2,1,0:T(8,128)} %bitcast), calls=%async_computation | async-start | bytes 983040 | tf_op jit(solution)/shard_map/all_to_all | solution.py:159
  35.0 0.5 compare_or_fusion
  35.6 0.6 compare_select_fusion
  36.2 11.1 %fusion.5 = (f32[4,726,180]{1,2,0:T(8,128)S(1)}, f32[4,726,180]{1,2,0:T(8,128)}) fusion(s32[4,180]{1,0:T(4,128)S(1)} %iota_add_fusion, s32[726]{0:T(1024)} %add_select_fusion.1), kind=kLoop, calls=%fused_computation.9 | loop fusion | flops 4704480 | bytes 4187544 | tf_op jit(solution)/shard_map/cos | solution.py:64
  47.3 1.4 %all-to-all-done = f32[4,40,720]{2,1,0:T(8,128)S(1)} async-done(((f32[4,40,720]{2,1,0:T(8,128)}), f32[4,40,720]{2,1,0:T(8,128)S(1)}, u32[]{:S(2)}, u32[]{:S(2)}) %all-to-all-start) | async-done | bytes 460832 | tf_op jit(solution)/shard_map/all_to_all | solution.py:159
  48.8 0.4 multiply_reduce_fusion.3
  49.2 1.2 copy-done.2
  50.4 4.1 %fusion.10 = f32[4,80,360]{2,1,0:T(8,128)S(1)} fusion(f32[4,726,180]{1,2,0:T(8,128)S(1)} %copy-done.2, f32[4,726,180]{1,2,0:T(8,128)S(1)} %get-tuple-element.52, f32[4,40,720]{2,1,0:T(8,128)S(1)} %neg.12, f32[4,40,720]{2,1,0:T(8,128)S(1)} %get-tuple-element.7), kind=kOutput, calls=%fused_computation.20 | convolution fusion | flops 1006061760 | bytes 5564160 | tf_op jit(solution)/shard_map/dot_general | solution.py:74
  54.7 3.2 %fusion.9 = f32[4,80,726]{2,1,0:T(8,128)S(1)} fusion(f32[4,726,180]{1,2,0:T(8,128)S(1)} %copy-done.2, f32[4,726,180]{1,2,0:T(8,128)S(1)} %get-tuple-element.52, f32[4,40,180]{2,1,0:T(8,128)S(1)} %get-tuple-element.20, f32[4,40,180]{2,1,0:T(8,128)S(1)} %get-tuple-element.11, f32[4,40,180]{2,1,0:T(8,128)S(1)} %get-tuple-element.12), kind=kOutput, calls=%fused_computation.19 | convolution fusion | flops 1005013440 | bytes 5456640 | tf_op jit(solution)/shard_map/dot_general | solution.py:83
  58.0 0.4 subtract_reduce_fusion.1
  58.8 15.8 %all_to_all.20 = f32[4,40,726]{2,1,0:T(8,128)S(1)} all-to-all(f32[4,40,726]{2,1,0:T(8,128)S(1)} %maximum_select_fusion), channel_id=1, replica_groups=mesh['lat'=8,'lon'=4] {'lon'}, dimensions={0} | all-to-all | bytes 929280 | tf_op jit(solution)/shard_map/all_to_all | solution.py:163
  75.2 0.4 fusion.102
  75.6 4.0 %collective-permute-start.8 = (f32[5,4,3,720]{3,2,1,0:T(4,128)S(1)}, f32[5,4,3,720]{3,2,1,0:T(4,128)S(1)}, u32[]{:S(2)}, u32[]{:S(2)}) collective-permute-start(f32[5,4,3,720]{3,2,1,0:T(4,128)S(1)} %get-tuple-element.25), channel_id=1, source_target_pairs={{0,4},{4,8},{8,12},{12,16},{16,20},{20,24},{24,28},{1,5},{5,9},{9,... | collective-permute-start | bytes 518408 | tf_op jit(solution)/shard_map/ppermute | solution.py:17
  79.7 2.1 %collective-permute-start.9 = (f32[5,4,3,720]{3,2,1,0:T(4,128)S(1)}, f32[5,4,3,720]{3,2,1,0:T(4,128)S(1)}, u32[]{:S(2)}, u32[]{:S(2)}) collective-permute-start(f32[5,4,3,720]{3,2,1,0:T(4,128)S(1)} %get-tuple-element.27), channel_id=1, source_target_pairs={{4,0},{8,4},{12,8},{16,12},{20,16},{24,20},{28,24},{5,1},{9,5},{13... | collective-permute-start | bytes 518408 | tf_op jit(solution)/shard_map/ppermute | solution.py:17
  81.9 0.6 fusion.95
  82.5 11.1 %collective-permute-done.7 = f32[5,4,3,720]{3,2,1,0:T(4,128)S(1)} collective-permute-done((f32[5,4,3,720]{3,2,1,0:T(4,128)S(1)}, f32[5,4,3,720]{3,2,1,0:T(4,128)S(1)}, u32[]{:S(2)}, u32[]{:S(2)}) %collective-permute-start.7) | collective-permute-done | bytes 172832 | tf_op jit(solution)/shard_map/ppermute | solution.py:17
  94.2 0.4 fusion.47
  94.6 0.3 copy-done.7
  94.9 1.0 fusion.20
  96.3 15.4 %all_to_all.21 = f32[4,40,720]{2,1,0:T(8,128)S(1)} all-to-all(f32[4,40,720]{2,1,0:T(8,128)S(1)} %bitcast.11), channel_id=1, replica_groups=mesh['lat'=8,'lon'=4] {'lon'}, dimensions={0} | all-to-all | bytes 921600 | tf_op jit(solution)/shard_map/all_to_all | solution.py:159
  111.7 0.4 multiply_reduce_fusion.1
  112.1 4.1 %fusion.8 = f32[4,80,360]{2,1,0:T(8,128)S(1)} fusion(f32[4,726,180]{1,2,0:T(8,128)S(1)} %copy-done.2, f32[4,726,180]{1,2,0:T(8,128)S(1)} %get-tuple-element.52, f32[4,40,720]{2,1,0:T(8,128)S(1)} %neg.14, f32[4,40,720]{2,1,0:T(8,128)S(1)} %get-tuple-element.5), kind=kOutput, calls=%fused_computation.18 | convolution fusion | flops 1006061760 | bytes 5564160 | tf_op jit(solution)/shard_map/dot_general | solution.py:74
  116.4 3.2 %fusion.7 = f32[4,80,726]{2,1,0:T(8,128)S(1)} fusion(f32[4,726,180]{1,2,0:T(8,128)S(1)} %copy-done.2, f32[4,726,180]{1,2,0:T(8,128)S(1)} %get-tuple-element.52, f32[4,40,180]{2,1,0:T(8,128)S(1)} %get-tuple-element.19, f32[4,40,180]{2,1,0:T(8,128)S(1)} %get-tuple-element.9, f32[4,40,180]{2,1,0:T(8,128)S(1)} %get-tuple-element.10), kind=kOutput, calls=%fused_computation.17 | convolution fusion | flops 1005013440 | bytes 5456640 | tf_op jit(solution)/shard_map/dot_general | solution.py:83
  119.7 0.4 subtract_reduce_fusion
  120.5 16.0 %all_to_all.22 = f32[4,40,720]{2,1,0:T(8,128)S(1)} all-to-all(f32[4,40,720]{2,1,0:T(8,128)S(1)} %slice_select_fusion), channel_id=1, replica_groups=mesh['lat'=8,'lon'=4] {'lon'}, dimensions={0} | all-to-all | bytes 921600 | tf_op jit(solution)/shard_map/all_to_all | solution.py:163
  136.5 0.8 copy.32
  (73 shorter events, 3.9 us)
Async XLA Ops:
  0.0 13.4 %copy-start = (s32[64]{0:T(128)S(1)}, s32[64]{0:T(128)}, u32[]{:S(2)}) copy-start(s32[64]{0:T(128)} %param.7) | copy-start | bytes 772
  0.0 24.8 %copy-start.1 = (f32[5,4,8,720]{3,2,1,0:T(8,128)S(1)}, f32[5,4,8,720]{3,2,1,0:T(8,128)}, u32[]{:S(2)}) copy-start(f32[5,4,8,720]{3,2,1,0:T(8,128)} %param.4) | copy-start | bytes 1382404
  1.4 27.1 %collective-permute-start.5 = (f32[5,4,3,720]{3,2,1,0:T(4,128)S(1)}, f32[5,4,3,720]{3,2,1,0:T(4,128)S(1)}, u32[]{:S(2)}, u32[]{:S(2)}) collective-permute-start(f32[5,4,3,720]{3,2,1,0:T(4,128)S(1)} %get-tuple-element.34), channel_id=1, source_target_pairs={{0,4},{4,8},{8,12},{12,16},{16,20},{20,24},{24,28},{1,5},{5,9},{9,... | collective-permute-start | bytes 518408 | tf_op jit(solution)/shard_map/ppermute | solution.py:17
  5.1 23.3 %collective-permute-start.4 = (f32[5,4,3,720]{3,2,1,0:T(4,128)S(1)}, f32[5,4,3,720]{3,2,1,0:T(4,128)S(1)}, u32[]{:S(2)}, u32[]{:S(2)}) collective-permute-start(f32[5,4,3,720]{3,2,1,0:T(4,128)S(1)} %get-tuple-element.35), channel_id=1, source_target_pairs={{0,2},{1,3},{2,0},{3,1},{4,6},{5,7},{6,4},{7,5},{8,10},{9,11},{10,... | collective-permute-start | bytes 518408 | tf_op jit(solution)/shard_map/ppermute | solution.py:17
  7.4 21.1 %collective-permute-start.6 = (f32[5,4,3,720]{3,2,1,0:T(4,128)S(1)}, f32[5,4,3,720]{3,2,1,0:T(4,128)S(1)}, u32[]{:S(2)}, u32[]{:S(2)}) collective-permute-start(f32[5,4,3,720]{3,2,1,0:T(4,128)S(1)} %get-tuple-element.36), channel_id=1, source_target_pairs={{4,0},{8,4},{12,8},{16,12},{20,16},{24,20},{28,24},{5,1},{9,5},{13... | collective-permute-start | bytes 518408 | tf_op jit(solution)/shard_map/ppermute | solution.py:17
  10.4 11.9 %collective-permute-start.2 = (f32[5,4,8,3]{3,2,1,0:T(8,128)S(1)}, f32[5,4,8,3]{3,2,1,0:T(8,128)S(1)}, u32[]{:S(2)}, u32[]{:S(2)}) collective-permute-start(f32[5,4,8,3]{3,2,1,0:T(8,128)S(1)} %get-tuple-element.33), channel_id=1, source_target_pairs={{0,3},{1,0},{2,1},{3,2},{4,7},{5,4},{6,5},{7,6},{8,11},{9,8},{10,9... | collective-permute-start | bytes 5768 | tf_op jit(solution)/shard_map/ppermute | solution.py:17
  12.3 4.5 %collective-permute-start = (f32[4,8,1]{2,1,0:T(8,128)S(1)}, f32[4,8,1]{2,1,0:T(8,128)S(1)}, u32[]{:S(2)}, u32[]{:S(2)}) collective-permute-start(f32[4,8,1]{2,1,0:T(8,128)S(1)} %slice.262), channel_id=1, source_target_pairs={{0,1},{1,2},{2,3},{3,0},{4,5},{5,6},{6,7},{7,4},{8,9},{9,10},{10,1... | collective-permute-start | bytes 392 | tf_op jit(solution)/shard_map/ppermute | solution.py:17
  13.3 16.0 %copy-start.14 = (f32[9]{0:T(128)}, f32[9]{0:T(128)S(1)}, u32[]{:S(2)}) copy-start(f32[9]{0:T(128)S(1)} %or_select_fusion) | copy-start | bytes 112
  13.4 17.0 %copy-start.12 = (f32[8]{0:T(128)}, f32[8]{0:T(128)S(1)}, u32[]{:S(2)}) copy-start(f32[8]{0:T(128)S(1)} %multiply_cosine_fusion) | copy-start | bytes 100
  16.8 7.9 %collective-permute-start.1 = (f32[5,4,8,3]{3,2,1,0:T(8,128)S(1)}, f32[5,4,8,3]{3,2,1,0:T(8,128)S(1)}, u32[]{:S(2)}, u32[]{:S(2)}) collective-permute-start(f32[5,4,8,3]{3,2,1,0:T(8,128)S(1)} %get-tuple-element.32), channel_id=1, source_target_pairs={{0,1},{1,2},{2,3},{3,0},{4,5},{5,6},{6,7},{7,4},{8,9},{9,10},{10,1... | collective-permute-start | bytes 5768 | tf_op jit(solution)/shard_map/ppermute | solution.py:17
  22.2 3.8 %copy-start.8 = (pred[4,8,721]{2,1,0:T(8,128)(4,1)}, pred[4,8,721]{2,1,0:T(8,128)(4,1)S(1)}, u32[]{:S(2)}) copy-start(pred[4,8,721]{2,1,0:T(8,128)(4,1)S(1)} %get-tuple-element.13) | copy-start | bytes 69220
  22.3 3.8 %copy-start.3 = (f32[4,8,721]{2,1,0:T(8,128)}, f32[4,8,721]{2,1,0:T(8,128)S(1)}, u32[]{:S(2)}) copy-start(f32[4,8,721]{2,1,0:T(8,128)S(1)} %get-tuple-element.51) | copy-start | bytes 276868
  22.3 5.9 %collective-permute-start.3 = (f32[4,1,720]{2,1,0:T(1,128)S(1)}, f32[4,1,720]{2,1,0:T(1,128)S(1)}, u32[]{:S(2)}, u32[]{:S(2)}) collective-permute-start(f32[4,1,720]{2,1,0:T(1,128)S(1)} %slice.274), channel_id=1, source_target_pairs={{4,0},{8,4},{12,8},{16,12},{20,16},{24,20},{28,24},{5,1},{9,5},{13... | collective-permute-start | bytes 34568 | tf_op jit(solution)/shard_map/ppermute | solution.py:17
  25.0 3.2 %copy-start.5 = (f32[4,8,720]{2,1,0:T(8,128)S(1)}, f32[4,8,720]{2,1,0:T(8,128)}, u32[]{:S(2)}) copy-start(f32[4,8,720]{2,1,0:T(8,128)} %param.6) | copy-start | bytes 276484
  28.3 1.1 copy-start.6
  31.4 17.4 %all-to-all-start = ((f32[4,40,720]{2,1,0:T(8,128)}), f32[4,40,720]{2,1,0:T(8,128)S(1)}, u32[]{:S(2)}, u32[]{:S(2)}) async-start(f32[4,40,720]{2,1,0:T(8,128)} %bitcast), calls=%async_computation | async-start | bytes 983040 | tf_op jit(solution)/shard_map/all_to_all | solution.py:159
  48.8 1.6 %copy-start.2 = (f32[4,726,180]{1,2,0:T(8,128)S(1)}, f32[4,726,180]{1,2,0:T(8,128)}, u32[]{:S(2)}) copy-start(f32[4,726,180]{1,2,0:T(8,128)} %get-tuple-element.53) | copy-start | bytes 6272644
  50.4 4.1 %copy-start.10 = (f32[4,180]{1,0:T(4,128)S(1)}, f32[4,180]{1,0:T(4,128)}, u32[]{:S(2)}) copy-start(f32[4,180]{1,0:T(4,128)} %compare_select_fusion) | copy-start | bytes 8644
  50.4 4.1 %copy-start.11 = (s32[40]{0:T(128)S(1)}, s32[40]{0:T(128)}, u32[]{:S(2)}) copy-start(s32[40]{0:T(128)} %and_select_fusion.1) | copy-start | bytes 484
  58.0 0.6 copy-start.16
  74.6 7.2 %copy-start.4 = (f32[4,8,721]{2,1,0:T(8,128)S(1)}, f32[4,8,721]{2,1,0:T(8,128)}, u32[]{:S(2)}) copy-start(f32[4,8,721]{2,1,0:T(8,128)} %copy-done.3) | copy-start | bytes 276868
  74.6 7.2 %copy-start.9 = (pred[4,8,721]{2,1,0:T(8,128)(4,1)S(1)}, pred[4,8,721]{2,1,0:T(8,128)(4,1)}, u32[]{:S(2)}) copy-start(pred[4,8,721]{2,1,0:T(8,128)(4,1)} %copy-done.8) | copy-start | bytes 69220
  75.6 18.1 %collective-permute-start.8 = (f32[5,4,3,720]{3,2,1,0:T(4,128)S(1)}, f32[5,4,3,720]{3,2,1,0:T(4,128)S(1)}, u32[]{:S(2)}, u32[]{:S(2)}) collective-permute-start(f32[5,4,3,720]{3,2,1,0:T(4,128)S(1)} %get-tuple-element.25), channel_id=1, source_target_pairs={{0,4},{4,8},{8,12},{12,16},{16,20},{20,24},{24,28},{1,5},{5,9},{9,... | collective-permute-start | bytes 518408 | tf_op jit(solution)/shard_map/ppermute | solution.py:17
  79.6 13.9 %collective-permute-start.7 = (f32[5,4,3,720]{3,2,1,0:T(4,128)S(1)}, f32[5,4,3,720]{3,2,1,0:T(4,128)S(1)}, u32[]{:S(2)}, u32[]{:S(2)}) collective-permute-start(f32[5,4,3,720]{3,2,1,0:T(4,128)S(1)} %get-tuple-element.26), channel_id=1, source_target_pairs={{0,2},{1,3},{2,0},{3,1},{4,6},{5,7},{6,4},{7,5},{8,10},{9,11},{10,... | collective-permute-start | bytes 518408 | tf_op jit(solution)/shard_map/ppermute | solution.py:17
  79.7 14.0 %collective-permute-start.9 = (f32[5,4,3,720]{3,2,1,0:T(4,128)S(1)}, f32[5,4,3,720]{3,2,1,0:T(4,128)S(1)}, u32[]{:S(2)}, u32[]{:S(2)}) collective-permute-start(f32[5,4,3,720]{3,2,1,0:T(4,128)S(1)} %get-tuple-element.27), channel_id=1, source_target_pairs={{4,0},{8,4},{12,8},{16,12},{20,16},{24,20},{28,24},{5,1},{9,5},{13... | collective-permute-start | bytes 518408 | tf_op jit(solution)/shard_map/ppermute | solution.py:17
  94.1 0.8 copy-start.7
  94.1 0.8 copy-start.15
  94.9 1.0 copy-start.13

commit v2 on v1

--- a/solution.py
+++ b/solution.py
@@ -53,11 +53,11 @@
     return cos_dr, sin_dr
 
 
-def class_basis(tiles, cols, circle):
+def class_basis(tiles, cols, circle, halo=HALO):
     per_class = KMAX // tiles
     r = jnp.arange(tiles, dtype=jnp.int32)
     m = jnp.arange(per_class, dtype=jnp.int32)
-    q = jnp.arange(-HALO, cols + HALO, dtype=jnp.int32) % circle
+    q = jnp.arange(-halo, cols + halo, dtype=jnp.int32) % circle
     k = tiles * m[None, :] + r[:, None]
     phase = (q[None, :, None] * k[:, None, :]) % circle
     angle = phase.astype(jnp.float32) * (2.0 * math.pi / circle)
@@ -91,7 +91,7 @@
     return jnp.where(polar[None, :, None], smooth, wide)
 
 
-def on_device(tracers, courant_x, courant_y, cutoffs):
+def tiled_path(tracers, courant_x, courant_y, cutoffs):
     tracer_count, level_count, lat_rows, lon_cols = tracers.shape
     field_count = tracer_count * level_count
     lat_devices = lax.axis_size("lat")
@@ -166,6 +166,113 @@
     return state
 
 
+def filter_full(rows, basis, roots, weights):
+    count, tiles, cols = rows.shape
+    cos_dr, sin_dr = roots
+    z_re = jnp.sum(cos_dr[:, None, :, None] * rows[None], axis=2)
+    z_im = -jnp.sum(sin_dr[:, None, :, None] * rows[None], axis=2)
+    z = jnp.concatenate([z_re, z_im], axis=1)
+    prod = lax.dot_general(z, basis, (((2,), (1,)), ((0,), (0,))), precision=HIGHEST)
+    per_class = basis.shape[2] // 2
+    zc, zs = prod[:, :count, :per_class], prod[:, :count, per_class:]
+    wc, ws = prod[:, count:, :per_class], prod[:, count:, per_class:]
+    real = (zc + ws) * weights
+    imag = (zs - wc) * weights
+    spec = jnp.concatenate(
+        [jnp.concatenate([real, imag], axis=2), jnp.concatenate([-imag, real], axis=2)], axis=1
+    )
+    back = lax.dot_general(spec, basis, (((2,), (2,)), ((0,), (0,))), precision=HIGHEST)
+    w_re = jnp.transpose(back[:, :count], (1, 0, 2))
+    w_im = jnp.transpose(back[:, count:], (1, 0, 2))
+    return jnp.sum(
+        cos_dr[None, :, :, None] * w_re[:, None] - sin_dr[None, :, :, None] * w_im[:, None], axis=2
+    )
+
+
+def transposed_path(tracers, courant_x, courant_y, cutoffs):
+    tracer_count, level_count, lat_rows, lon_cols = tracers.shape
+    field_count = tracer_count * level_count
+    lat_devices = lax.axis_size("lat")
+    lon_devices = lax.axis_size("lon")
+    lat_index = lax.axis_index("lat")
+    lon_index = lax.axis_index("lon")
+    circle = lon_cols * lon_devices
+    total_rows = lat_rows * lat_devices
+    per_device = field_count // lon_devices
+    row_global = lat_index * lat_rows + jnp.arange(lat_rows, dtype=jnp.int32)
+    face_global = lat_index * lat_rows + jnp.arange(lat_rows + 1, dtype=jnp.int32)
+    face_angle = (face_global.astype(jnp.float32) / total_rows - 0.5) * math.pi
+    face_weight = jnp.where(
+        (face_global == 0) | (face_global == total_rows), 0.0, jnp.cos(face_angle)
+    )
+    center_weight = jnp.cos(((row_global.astype(jnp.float32) + 0.5) / total_rows - 0.5) * math.pi)
+    is_south = lat_index == 0
+    is_north = lat_index == lat_devices - 1
+
+    tiles = tracers.reshape(lon_devices, per_device, lat_rows, lon_cols)
+    tiles = lax.all_to_all(tiles, "lon", 0, 0)
+    state = jnp.transpose(tiles, (1, 2, 0, 3)).reshape(per_device, lat_rows, circle)
+
+    north_cy = shift(courant_y[:, :1], "lat", -1, False)
+    north_cy = jnp.where(is_north, 0.0, north_cy)
+    own = jnp.concatenate([courant_x, courant_y, north_cy], axis=1)
+    pieces = jnp.stack([own] + [shift(own, "lon", s, True) for s in range(1, lon_devices)])
+    source = (lon_index - jnp.arange(lon_devices, dtype=jnp.int32)) % lon_devices
+    full = jnp.take(pieces, source, axis=0)
+    full = jnp.transpose(full, (1, 2, 0, 3)).reshape(level_count, 2 * lat_rows + 1, circle)
+    levels = (lon_index * per_device + jnp.arange(per_device, dtype=jnp.int32)) % level_count
+    held = jnp.take(full, levels, axis=0)
+    cx = held[:, :lat_rows]
+    north_courant = held[:, lat_rows:]
+    east_courant = jnp.concatenate([cx[..., circle - 1 :], cx], axis=2)
+
+    count = per_device * lat_rows
+    held_global = lat_index * lat_rows + jnp.arange(count, dtype=jnp.int32) % lat_rows
+    polar = (held_global < total_rows // 4) | (held_global >= total_rows - total_rows // 4)
+    cut = jnp.take(cutoffs, held_global)
+    per_class = KMAX // lon_devices
+    k = lon_devices * jnp.arange(per_class, dtype=jnp.int32)[None, :] + jnp.arange(
+        lon_devices, dtype=jnp.int32
+    )[:, None]
+    scale = jnp.where(k == 0, 1.0 / circle, 2.0 / circle).astype(jnp.float32)
+    weights = jnp.where(k[:, None, :] < cut[None, :, None], scale[:, None, :], 0.0)
+    basis = class_basis(lon_devices, lon_cols, circle, 0)
+    roots = root_table(lon_devices)
+
+    for substep in range(SUBSTEPS):
+        south_in = shift(state[:, lat_rows - HALO :], "lat", 1, False)
+        north_in = shift(state[:, :HALO], "lat", -1, False)
+        edge = jnp.where(is_south, state[:, :HALO], state[:, lat_rows - HALO :])
+        far = jnp.roll(edge, circle // 2, axis=2)
+        far_rev = jnp.concatenate([far[:, 2:3], far[:, 1:2], far[:, 0:1]], axis=1)
+        south_rows = jnp.where(is_south, far_rev, south_in)
+        north_rows = jnp.where(is_north, far_rev, north_in)
+        extended = jnp.concatenate([south_rows, state, north_rows], axis=1)
+        wrapped = jnp.concatenate([state[..., circle - HALO :], state, state[..., :HALO]], axis=2)
+        zonal = ppm_flux(wrapped, east_courant, 2, circle)
+        meridional = ppm_flux(extended, north_courant, 1, lat_rows) * face_weight[:, None]
+        change = (
+            zonal[..., 1:]
+            - zonal[..., :-1]
+            + (meridional[:, 1:] - meridional[:, :-1]) / center_weight[:, None]
+        )
+        state = state - change
+        rows = state.reshape(count, lon_devices, lon_cols)
+        smooth = filter_full(rows, basis, roots, weights)
+        state = jnp.where(polar[:, None, None], smooth, rows).reshape(per_device, lat_rows, circle)
+
+    tiles = jnp.transpose(state.reshape(per_device, lat_rows, lon_devices, lon_cols), (2, 0, 1, 3))
+    tiles = lax.all_to_all(tiles, "lon", 0, 0)
+    return tiles.reshape(tracer_count, level_count, lat_rows, lon_cols)
+
+
+def on_device(tracers, courant_x, courant_y, cutoffs):
+    field_count = tracers.shape[0] * tracers.shape[1]
+    if field_count % lax.axis_size("lon") == 0 and tracers.shape[2] >= HALO:
+        return transposed_path(tracers, courant_x, courant_y, cutoffs)
+    return tiled_path(tracers, courant_x, courant_y, cutoffs)
+
+
 def solution(mesh):
     in_specs = (P(None, None, "lat", "lon"), P(None, "lat", "lon"), P(None, "lat", "lon"), P())
     out_specs = P(None, None, "lat", "lon")

time: 140 us -> 163 us (1.16); the launches traced: 137 us -> 163 us
  blocking collectives: 47.2 us -> 20.9 us
  local copies, waits for them, and re-layouts: 6.75 us -> 32.5 us
  other arithmetic: 26 us -> 40.8 us
  waiting for transfers between devices: 15.8 us -> 27.9 us
  starting transfers between devices: 26.2 us -> 24.4 us
    all_to_all x3 -> x1, blocking collectives: 47.2 us -> 20.9 us  [transposed_path(): tiles = lax.all_to_all(tiles, 'lon', 0, 0)]
    ppermute x10 -> x8, waiting for transfers between devices: 14.4 us -> 27.9 us  [shift(): return lax.ppermute(x, axis, pairs)]
    reshape x0 -> x4, local copies, waits for them, and re-layouts: none -> 7.14 us  [the longest x2 4.36 us: transposed_path(): jnp.transpose(full, (1, 2, 0, 3))]
    gather x1 -> x3, local copies, waits for them, and re-layouts: 0.77 us -> 7.55 us  [the longest x1 3.1 us: transposed_path(): held = jnp.take(full, levels, axis=0)]
    mul x0 -> x4, local copies, waits for them, and re-layouts: none -> 5.07 us  [filter_full(): z_re = jnp.sum(cos_dr[:, None, :, None] * rows[None], axis=2)]
    select_n x10 -> x12, other arithmetic: 2.85 us -> 7.42 us  [the longest x2 1.53 us: transposed_path(): held = jnp.take(full, levels, axis=0)]
    unnamed x35 -> x39, local copies, waits for them, and re-layouts: 2.39 us -> 5.28 us
    ppermute x10 -> x8, starting transfers between devices: 22.6 us -> 19.7 us  [shift(): return lax.ppermute(x, axis, pairs)]
  transfers between devices with their start and end apart: 11 -> 9, of which waited for: 4 -> 6; matrix products, arithmetic and copies ran while one was open for 15% -> 25% of each run, Pallas kernels for 0% -> 0%
where the time goes in v2:
time: 163 us
  other arithmetic  40.8 us (25%)
  local copies, waits for them, and re-layouts  32.5 us (20%)
  waiting for transfers between devices  27.9 us (17%)
  starting transfers between devices  24.4 us (15%)
  blocking collectives  20.9 us (13%)
  matrix products  15.6 us (10%)
    ppermute x8, waiting for transfers between devices, shift(): return lax.ppermute(x, axis, pairs)  27.9 us
    all_to_all x1, blocking collectives, transposed_path(): tiles = lax.all_to_all(tiles, 'lon', 0, 0)  20.9 us
    ppermute x8, starting transfers between devices, shift(): return lax.ppermute(x, axis, pairs)  19.7 us
    cos x1, other arithmetic, class_basis(): return jnp.concatenate([jnp.cos(angle), jnp.sin(angle)], axis=2)  13.2 us
    dot_general x2, matrix products, filter_full(): lax.dot_general(spec, basis, (((2,), (2,)), ((0,), (0,))), precision=HIGH...  9.22 us
    dot_general x2, matrix products, filter_full(): lax.dot_general(z, basis, (((2,), (1,)), ((0,), (0,))), precision=HIGHEST)  6.38 us
    unnamed x39, local copies, waits for them, and re-layouts  5.28 us
    mul x4, local copies, waits for them, and re-layouts, filter_full(): z_re = jnp.sum(cos_dr[:, None, :, None] * rows[None], axis=2)  5.07 us
  transfers between devices with their start and end apart: 9, of which 6 were waited for; matrix products, arithmetic and copies ran while one was open for 25% of the time, Pallas kernels for 0%

profile of v2, /device:TPU:3, one launch (start us, length us, event | category | flops | bytes accessed | tf_op | source)
XLA Modules:
  0.0 162.5 jit_solution(11595144476542217874)
XLA Ops:
  0.0 4.7 %all-to-all-start = ((f32[4,5,8,720]{3,2,1,0:T(8,128)}), f32[4,5,8,720]{3,2,1,0:T(8,128)S(1)}, u32[]{:S(2)}, u32[]{:S(2)}) async-start(f32[4,5,8,720]{3,2,1,0:T(8,128)} %bitcast.30), calls=%async_computation | async-start | bytes 983040 | tf_op jit(solution)/shard_map/all_to_all | solution.py:213
  4.7 1.5 slice.241
  6.2 2.9 %collective-permute-start = (f32[4,1,720]{2,1,0:T(1,128)}, f32[4,1,720]{2,1,0:T(1,128)}, u32[]{:S(2)}, u32[]{:S(2)}) collective-permute-start(f32[4,1,720]{2,1,0:T(1,128)} %slice.241), channel_id=1, source_target_pairs={{4,0},{8,4},{12,8},{16,12},{20,16},{24,20},{28,24},{5,1},{9,5},{13... | collective-permute-start | bytes 34568 | tf_op jit(solution)/shard_map/ppermute | solution.py:17
  14.0 13.2 %fusion.5 = (f32[4,720,180]{2,1,0:T(8,128)S(1)}, f32[4,720,180]{2,1,0:T(8,128)}) fusion(s32[4,180]{1,0:T(4,128)S(1)} %iota_add_fusion), kind=kLoop, calls=%fused_computation.11 | loop fusion | flops 4665600 | bytes 4150080 | tf_op jit(solution)/shard_map/cos | solution.py:64
  27.7 1.4 gather_fusion.2
  29.8 0.9 fusion.151
  30.8 2.7 %collective-permute-start.2 = (f32[4,17,720]{2,1,0:T(8,128)S(1)}, f32[4,17,720]{2,1,0:T(8,128)S(1)}, u32[]{:S(2)}, u32[]{:S(2)}) collective-permute-start(f32[4,17,720]{2,1,0:T(8,128)S(1)} %get-tuple-element.40), channel_id=1, source_target_pairs={{0,2},{1,3},{2,0},{3,1},{4,6},{5,7},{6,4},{7,5},{8,10},{9,11},{10,... | collective-permute-start | bytes 587528 | tf_op jit(solution)/shard_map/ppermute | solution.py:17
  33.5 1.2 collective-permute-start.1
  34.7 2.1 %collective-permute-start.3 = (f32[4,17,720]{2,1,0:T(8,128)S(1)}, f32[4,17,720]{2,1,0:T(8,128)S(1)}, u32[]{:S(2)}, u32[]{:S(2)}) collective-permute-start(f32[4,17,720]{2,1,0:T(8,128)S(1)} %get-tuple-element.40), channel_id=1, source_target_pairs={{0,3},{1,0},{2,1},{3,2},{4,7},{5,4},{6,5},{7,6},{8,11},{9,8},{10,9... | collective-permute-start | bytes 587528 | tf_op jit(solution)/shard_map/ppermute | solution.py:17
  37.4 16.2 %collective-permute-done.2 = f32[4,17,720]{2,1,0:T(8,128)S(1)} collective-permute-done((f32[4,17,720]{2,1,0:T(8,128)S(1)}, f32[4,17,720]{2,1,0:T(8,128)S(1)}, u32[]{:S(2)}, u32[]{:S(2)}) %collective-permute-start.2) | collective-permute-done | bytes 195872 | tf_op jit(solution)/shard_map/ppermute | solution.py:17
  54.0 1.2 pad_maximum_fusion.5
  55.2 3.0 %gather_fusion = f32[4,4,17,720]{3,2,1,0:T(8,128)} fusion(f32[4,4,17,720]{3,2,1,0:T(8,128)} %pad_maximum_fusion.5, s32[1024]{0:T(1024)} %pad_clamp_fusion.2), kind=kCustom, calls=%fused_computation | custom fusion | bytes 1566736 | tf_op jit(solution)/shard_map/jit(_take)/gather | solution.py:221
  58.2 1.4 select_bitcast_fusion
  59.7 1.4 copy.39
  61.1 2.9 %reshape.387 = f32[4,17,2880]{2,1,0:T(8,128)} reshape(f32[4,17,4,720]{3,2,1,0:T(4,128)} %copy.39) | data formatting | bytes 1566720 | tf_op jit(solution)/shard_map/reshape | solution.py:222
  64.0 3.1 %gather_fusion.1 = f32[5,17,2880]{2,1,0:T(8,128)} fusion(f32[4,17,2880]{2,1,0:T(8,128)} %reshape.387, s32[1024]{0:T(1024)} %pad_clamp_fusion.1), kind=kCustom, calls=%fused_computation.1 | custom fusion | bytes 1958420 | tf_op jit(solution)/shard_map/jit(_take)/gather | solution.py:224
  67.1 1.5 broadcast_select_fusion
  68.7 1.0 copy-done.3
  70.6 1.0 copy.31
  71.6 1.3 reshape.359
  73.0 1.0 concatenate.92
  73.9 1.7 %fusion.95 = f32[5,8,2883]{2,1,0:T(8,128)S(1)} fusion(f32[5,8,3]{2,1,0:T(8,128)S(1)} %get-tuple-element.27, f32[5,8,3]{2,1,0:T(8,128)S(1)} %get-tuple-element.26, f32[5,8,2886]{2,1,0:T(8,128)} %concatenate.92, f32[5,8,2880]{2,1,0:T(8,128)S(1)} %reshape.359), kind=kLoop, calls=%fused_computation.141 | loop fusion | flops 807240 | bytes 1845600 | tf_op jit(solution)/shard_map/sub | solution.py:25
  75.8 4.4 %collective-permute-start.4 = (f32[5,3,2880]{2,1,0:T(4,128)S(1)}, f32[5,3,2880]{2,1,0:T(4,128)S(1)}, u32[]{:S(2)}, u32[]{:S(2)}) collective-permute-start(f32[5,3,2880]{2,1,0:T(4,128)S(1)} %get-tuple-element.28), channel_id=1, source_target_pairs={{0,4},{4,8},{8,12},{12,16},{16,20},{20,24},{24,28},{1,5},{5,9},{9,... | collective-permute-start | bytes 518408 | tf_op jit(solution)/shard_map/ppermute | solution.py:17
  80.2 2.1 %collective-permute-start.5 = (f32[5,3,2880]{2,1,0:T(4,128)S(1)}, f32[5,3,2880]{2,1,0:T(4,128)S(1)}, u32[]{:S(2)}, u32[]{:S(2)}) collective-permute-start(f32[5,3,2880]{2,1,0:T(4,128)S(1)} %get-tuple-element.30), channel_id=1, source_target_pairs={{4,0},{8,4},{12,8},{16,12},{20,16},{24,20},{28,24},{5,1},{9,5},{13... | collective-permute-start | bytes 518408 | tf_op jit(solution)/shard_map/ppermute | solution.py:17
  83.2 5.3 %collective-permute-done.5 = f32[5,3,2880]{2,1,0:T(4,128)S(1)} collective-permute-done((f32[5,3,2880]{2,1,0:T(4,128)S(1)}, f32[5,3,2880]{2,1,0:T(4,128)S(1)}, u32[]{:S(2)}, u32[]{:S(2)}) %collective-permute-start.5) | collective-permute-done | bytes 172832 | tf_op jit(solution)/shard_map/ppermute | solution.py:17
  89.4 0.9 copy-done.4
  90.4 1.9 %fusion.41 = (f32[5,9,2880]{2,1,0:T(8,128)S(1)}, pred[5,9,2880]{2,1,0:T(8,128)(4,1)}) fusion(f32[5,8,2880]{2,1,0:T(8,128)S(1)} %reshape.359, f32[5,3,2880]{2,1,0:T(4,128)S(1)} %get-tuple-element.34, f32[5,3,2880]{2,1,0:T(4,128)S(1)} %get-tuple-element.33, f32[5,11,2880]{2,1,0:T(8,128)S(1)} %fusion.54, f32[5,17,2880]{2,1,0:T(8,128)S(1)} %copy-done.4, ...), kind=kLoop, calls=%fused_computation.67 | loop fusion | flops 3628800 | bytes 3528036 | tf_op jit(solution)/shard_map/mul | solution.py:253
  92.2 1.0 fusion.118
  93.2 1.5 mul.488
  95.2 1.3 copy-done.1
  96.5 3.2 %fusion.7 = f32[4,80,360]{2,1,0:T(8,128)S(1)} fusion(f32[4,40,720]{2,1,0:T(8,128)S(1)} %neg.12, f32[4,40,720]{2,1,0:T(8,128)S(1)} %get-tuple-element.7, f32[4,720,180]{2,1,0:T(8,128)S(1)} %copy-done.1, f32[4,720,180]{2,1,0:T(8,128)S(1)} %get-tuple-element.41), kind=kOutput, calls=%fused_computation.33 | convolution fusion | flops 996595200 | bytes 5529600 | tf_op jit(solution)/shard_map/dot_general | solution.py:175
  99.9 4.6 %fusion.57 = f32[4,80,720]{2,1,0:T(8,128)S(1)} fusion(f32[4,40,180]{2,1,0:T(8,128)S(1)} %get-tuple-element.20, f32[4,40,180]{2,1,0:T(8,128)S(1)} %get-tuple-element.11, f32[4,40,180]{2,1,0:T(8,128)S(1)} %get-tuple-element.12, f32[4,720,180]{2,1,0:T(8,128)S(1)} %copy-done.1, f32[4,720,180]{2,1,0:T(8,128)S(1)} %get-tuple-element.41), kind=kOutput, calls=%fused_computation.102 | convolution fusion | flops 996710400 | bytes 5414400 | tf_op jit(solution)/shard_map/dot_general | solution.py:184
  105.2 1.1 reduce_sum.61
  106.2 1.3 broadcast_select_fusion.1
  107.6 0.9 fusion.155
  108.5 1.2 concatenate.105
  109.7 1.7 %fusion.76 = f32[5,8,2883]{2,1,0:T(8,128)S(1)} fusion(f32[5,8,3]{2,1,0:T(8,128)S(1)} %get-tuple-element.22, f32[5,8,3]{2,1,0:T(8,128)S(1)} %get-tuple-element.21, f32[5,8,2886]{2,1,0:T(8,128)} %concatenate.105, f32[5,8,2880]{2,1,0:T(8,128)S(1)} %broadcast_select_fusion.1), kind=kLoop, calls=%fused_computation.122 | loop fusion | flops 807240 | bytes 1845600 | tf_op jit(solution)/shard_map/sub | solution.py:25
  112.1 1.9 %collective-permute-start.6 = (f32[5,3,2880]{2,1,0:T(4,128)S(1)}, f32[5,3,2880]{2,1,0:T(4,128)S(1)}, u32[]{:S(2)}, u32[]{:S(2)}) collective-permute-start(f32[5,3,2880]{2,1,0:T(4,128)S(1)} %copy-done.11), channel_id=1, source_target_pairs={{0,4},{4,8},{8,12},{12,16},{16,20},{20,24},{24,28},{1,5},{5,9},{9,... | collective-permute-start | bytes 518408 | tf_op jit(solution)/shard_map/ppermute | solution.py:17
  114.0 2.4 %collective-permute-start.7 = (f32[5,3,2880]{2,1,0:T(4,128)S(1)}, f32[5,3,2880]{2,1,0:T(4,128)S(1)}, u32[]{:S(2)}, u32[]{:S(2)}) collective-permute-start(f32[5,3,2880]{2,1,0:T(4,128)S(1)} %copy-done.10), channel_id=1, source_target_pairs={{4,0},{8,4},{12,8},{16,12},{20,16},{24,20},{28,24},{5,1},{9,5},{13... | collective-permute-start | bytes 518408 | tf_op jit(solution)/shard_map/ppermute | solution.py:17
  117.0 5.3 %collective-permute-done.7 = f32[5,3,2880]{2,1,0:T(4,128)S(1)} collective-permute-done((f32[5,3,2880]{2,1,0:T(4,128)S(1)}, f32[5,3,2880]{2,1,0:T(4,128)S(1)}, u32[]{:S(2)}, u32[]{:S(2)}) %collective-permute-start.7) | collective-permute-done | bytes 172832 | tf_op jit(solution)/shard_map/ppermute | solution.py:17
  124.2 1.1 fusion.24
  125.3 1.0 fusion.114
  126.3 1.5 reshape.361
  127.8 2.2 %mul.529 = f32[40,4,720]{2,1,0:T(4,128)} reshape(f32[5,8,2880]{2,1,0:T(8,128)} %fusion.114) | data formatting | bytes 921600 | tf_op jit(solution)/shard_map/mul | solution.py:172
  130.0 1.3 copy.36
  132.0 3.2 %fusion.11 = f32[4,80,360]{2,1,0:T(8,128)S(1)} fusion(f32[4,40,720]{2,1,0:T(8,128)S(1)} %neg.14, f32[4,40,720]{2,1,0:T(8,128)S(1)} %get-tuple-element.5, f32[4,720,180]{2,1,0:T(8,128)S(1)} %copy-done.2, f32[4,720,180]{2,1,0:T(8,128)S(1)} %get-tuple-element.41), kind=kOutput, calls=%fused_computation.37 | convolution fusion | flops 996595200 | bytes 5529600 | tf_op jit(solution)/shard_map/dot_general | solution.py:175
  135.4 4.6 %fusion.65 = f32[4,80,720]{2,1,0:T(8,128)S(1)} fusion(f32[4,40,180]{2,1,0:T(8,128)S(1)} %get-tuple-element.19, f32[4,40,180]{2,1,0:T(8,128)S(1)} %get-tuple-element.9, f32[4,40,180]{2,1,0:T(8,128)S(1)} %get-tuple-element.10, f32[4,720,180]{2,1,0:T(8,128)S(1)} %copy-done.2, f32[4,720,180]{2,1,0:T(8,128)S(1)} %get-tuple-element.41), kind=kOutput, calls=%fused_computation.110 | convolution fusion | flops 996710400 | bytes 5414400 | tf_op jit(solution)/shard_map/dot_general | solution.py:184
  140.8 20.9 %all_to_all.10 = f32[4,5,8,720]{3,2,1,0:T(8,128)S(1)} all-to-all(f32[4,5,8,720]{3,2,1,0:T(8,128)S(1)} %copy.38), channel_id=1, replica_groups=mesh['lat'=8,'lon'=4] {'lon'}, dimensions={0} | all-to-all | bytes 921600 | tf_op jit(solution)/shard_map/all_to_all | solution.py:265
  (88 shorter events, 16.9 us)
Async XLA Ops:
  0.0 27.7 %copy-start = (s32[64]{0:T(128)S(1)}, s32[64]{0:T(128)}, u32[]{:S(2)}) copy-start(s32[64]{0:T(128)} %param.7) | copy-start | bytes 772
  0.0 70.6 %all-to-all-start = ((f32[4,5,8,720]{3,2,1,0:T(8,128)}), f32[4,5,8,720]{3,2,1,0:T(8,128)S(1)}, u32[]{:S(2)}, u32[]{:S(2)}) async-start(f32[4,5,8,720]{3,2,1,0:T(8,128)} %bitcast.30), calls=%async_computation | async-start | bytes 983040 | tf_op jit(solution)/shard_map/all_to_all | solution.py:213
  6.2 22.9 %collective-permute-start = (f32[4,1,720]{2,1,0:T(1,128)}, f32[4,1,720]{2,1,0:T(1,128)}, u32[]{:S(2)}, u32[]{:S(2)}) collective-permute-start(f32[4,1,720]{2,1,0:T(1,128)} %slice.241), channel_id=1, source_target_pairs={{4,0},{8,4},{12,8},{16,12},{20,16},{24,20},{28,24},{5,1},{9,5},{13... | collective-permute-start | bytes 34568 | tf_op jit(solution)/shard_map/ppermute | solution.py:17
  14.0 15.8 %copy-start.12 = (f32[4,8,720]{2,1,0:T(8,128)S(1)}, f32[4,8,720]{2,1,0:T(8,128)}, u32[]{:S(2)}) copy-start(f32[4,8,720]{2,1,0:T(8,128)} %param.6) | copy-start | bytes 276484
  30.8 22.8 %collective-permute-start.2 = (f32[4,17,720]{2,1,0:T(8,128)S(1)}, f32[4,17,720]{2,1,0:T(8,128)S(1)}, u32[]{:S(2)}, u32[]{:S(2)}) collective-permute-start(f32[4,17,720]{2,1,0:T(8,128)S(1)} %get-tuple-element.40), channel_id=1, source_target_pairs={{0,2},{1,3},{2,0},{3,1},{4,6},{5,7},{6,4},{7,5},{8,10},{9,11},{10,... | collective-permute-start | bytes 587528 | tf_op jit(solution)/shard_map/ppermute | solution.py:17
  33.5 20.1 %collective-permute-start.1 = (f32[4,17,720]{2,1,0:T(8,128)S(1)}, f32[4,17,720]{2,1,0:T(8,128)S(1)}, u32[]{:S(2)}, u32[]{:S(2)}) collective-permute-start(f32[4,17,720]{2,1,0:T(8,128)S(1)} %get-tuple-element.40), channel_id=1, source_target_pairs={{0,1},{1,2},{2,3},{3,0},{4,5},{5,6},{6,7},{7,4},{8,9},{9,10},{10,1... | collective-permute-start | bytes 587528 | tf_op jit(solution)/shard_map/ppermute | solution.py:17
  34.7 19.4 %collective-permute-start.3 = (f32[4,17,720]{2,1,0:T(8,128)S(1)}, f32[4,17,720]{2,1,0:T(8,128)S(1)}, u32[]{:S(2)}, u32[]{:S(2)}) collective-permute-start(f32[4,17,720]{2,1,0:T(8,128)S(1)} %get-tuple-element.40), channel_id=1, source_target_pairs={{0,3},{1,0},{2,1},{3,2},{4,7},{5,4},{6,5},{7,6},{8,11},{9,8},{10,9... | collective-permute-start | bytes 587528 | tf_op jit(solution)/shard_map/ppermute | solution.py:17
  54.0 4.2 %copy-start.18 = (pred[4]{0:T(512)(128)(4,1)S(1)}, pred[4]{0:T(512)(128)(4,1)}, u32[]{:S(2)}) copy-start(pred[4]{0:T(512)(128)(4,1)} %compare_and_fusion) | copy-start | bytes 16
  61.1 6.0 %copy-start.17 = (pred[5]{0:T(512)(128)(4,1)S(1)}, pred[5]{0:T(512)(128)(4,1)}, u32[]{:S(2)}) copy-start(pred[5]{0:T(512)(128)(4,1)} %compare_and_fusion.1) | copy-start | bytes 19
  68.7 1.1 copy-start.3
  73.9 8.4 %copy-start.6 = (f32[5,8,2880]{2,1,0:T(8,128)S(1)}, f32[5,8,2880]{2,1,0:T(8,128)}, u32[]{:S(2)}) copy-start(f32[5,8,2880]{2,1,0:T(8,128)} %slice.318) | copy-start | bytes 1382404
  75.8 7.5 %collective-permute-start.4 = (f32[5,3,2880]{2,1,0:T(4,128)S(1)}, f32[5,3,2880]{2,1,0:T(4,128)S(1)}, u32[]{:S(2)}, u32[]{:S(2)}) collective-permute-start(f32[5,3,2880]{2,1,0:T(4,128)S(1)} %get-tuple-element.28), channel_id=1, source_target_pairs={{0,4},{4,8},{8,12},{12,16},{16,20},{20,24},{24,28},{1,5},{5,9},{9,... | collective-permute-start | bytes 518408 | tf_op jit(solution)/shard_map/ppermute | solution.py:17
  80.2 8.3 %collective-permute-start.5 = (f32[5,3,2880]{2,1,0:T(4,128)S(1)}, f32[5,3,2880]{2,1,0:T(4,128)S(1)}, u32[]{:S(2)}, u32[]{:S(2)}) collective-permute-start(f32[5,3,2880]{2,1,0:T(4,128)S(1)} %get-tuple-element.30), channel_id=1, source_target_pairs={{4,0},{8,4},{12,8},{16,12},{20,16},{24,20},{28,24},{5,1},{9,5},{13... | collective-permute-start | bytes 518408 | tf_op jit(solution)/shard_map/ppermute | solution.py:17
  89.0 1.4 copy-start.4
  89.0 1.3 copy-start.16
  90.3 1.9 %copy-start.15 = (f32[8]{0:T(128)S(1)}, f32[8]{0:T(128)}, u32[]{:S(2)}) copy-start(f32[8]{0:T(128)} %multiply_cosine_fusion) | copy-start | bytes 100
  94.7 1.8 %copy-start.1 = (f32[4,720,180]{2,1,0:T(8,128)S(1)}, f32[4,720,180]{2,1,0:T(8,128)}, u32[]{:S(2)}) copy-start(f32[4,720,180]{2,1,0:T(8,128)} %get-tuple-element.42) | copy-start | bytes 6220804
  96.5 3.2 %copy-start.13 = (f32[4,180]{1,0:T(4,128)S(1)}, f32[4,180]{1,0:T(4,128)}, u32[]{:S(2)}) copy-start(f32[4,180]{1,0:T(4,128)} %compare_select_fusion) | copy-start | bytes 8644
  104.6 1.7 %copy-start.14 = (pred[5,8]{1,0:T(8,128)(4,1)S(1)}, pred[5,8]{1,0:T(8,128)(4,1)}, u32[]{:S(2)}) copy-start(pred[5,8]{1,0:T(8,128)(4,1)} %fusion.131) | copy-start | bytes 124
  109.7 1.8 %copy-start.7 = (f32[5,8,2880]{2,1,0:T(8,128)S(1)}, f32[5,8,2880]{2,1,0:T(8,128)}, u32[]{:S(2)}) copy-start(f32[5,8,2880]{2,1,0:T(8,128)} %slice.318) | copy-start | bytes 1382404
  109.7 2.4 %copy-start.11 = (f32[5,3,2880]{2,1,0:T(4,128)S(1)}, f32[5,3,2880]{2,1,0:T(4,128)}, u32[]{:S(2)}) copy-start(f32[5,3,2880]{2,1,0:T(4,128)} %get-tuple-element.23) | copy-start | bytes 518404
  109.7 4.3 %copy-start.10 = (f32[5,3,2880]{2,1,0:T(4,128)S(1)}, f32[5,3,2880]{2,1,0:T(4,128)}, u32[]{:S(2)}) copy-start(f32[5,3,2880]{2,1,0:T(4,128)} %get-tuple-element.25) | copy-start | bytes 518404
  109.7 6.7 %copy-start.8 = (f32[5,3,2880]{2,1,0:T(4,128)S(1)}, f32[5,3,2880]{2,1,0:T(4,128)}, u32[]{:S(2)}) copy-start(f32[5,3,2880]{2,1,0:T(4,128)} %get-tuple-element.24) | copy-start | bytes 518404
  112.1 4.9 %collective-permute-start.6 = (f32[5,3,2880]{2,1,0:T(4,128)S(1)}, f32[5,3,2880]{2,1,0:T(4,128)S(1)}, u32[]{:S(2)}, u32[]{:S(2)}) collective-permute-start(f32[5,3,2880]{2,1,0:T(4,128)S(1)} %copy-done.11), channel_id=1, source_target_pairs={{0,4},{4,8},{8,12},{12,16},{16,20},{20,24},{24,28},{1,5},{5,9},{9,... | collective-permute-start | bytes 518408 | tf_op jit(solution)/shard_map/ppermute | solution.py:17
  114.0 8.3 %collective-permute-start.7 = (f32[5,3,2880]{2,1,0:T(4,128)S(1)}, f32[5,3,2880]{2,1,0:T(4,128)S(1)}, u32[]{:S(2)}, u32[]{:S(2)}) collective-permute-start(f32[5,3,2880]{2,1,0:T(4,128)S(1)} %copy-done.10), channel_id=1, source_target_pairs={{4,0},{8,4},{12,8},{16,12},{20,16},{24,20},{28,24},{5,1},{9,5},{13... | collective-permute-start | bytes 518408 | tf_op jit(solution)/shard_map/ppermute | solution.py:17
  122.8 1.4 copy-start.5
  122.8 1.4 copy-start.9
  130.0 2.0 %copy-start.2 = (f32[4,720,180]{2,1,0:T(8,128)S(1)}, f32[4,720,180]{2,1,0:T(8,128)}, u32[]{:S(2)}) copy-start(f32[4,720,180]{2,1,0:T(8,128)} %get-tuple-element.42) | copy-start | bytes 6220804

commit v3 on v1

--- a/solution.py
+++ b/solution.py
@@ -53,24 +53,24 @@
     return cos_dr, sin_dr
 
 
-def class_basis(tiles, cols, circle):
+def class_basis(tiles, cols, circle, halo=HALO):
     per_class = KMAX // tiles
     r = jnp.arange(tiles, dtype=jnp.int32)
     m = jnp.arange(per_class, dtype=jnp.int32)
-    q = jnp.arange(-HALO, cols + HALO, dtype=jnp.int32) % circle
+    q = jnp.arange(-halo, cols + halo, dtype=jnp.int32) % circle
     k = tiles * m[None, :] + r[:, None]
     phase = (q[None, :, None] * k[:, None, :]) % circle
     angle = phase.astype(jnp.float32) * (2.0 * math.pi / circle)
     return jnp.concatenate([jnp.cos(angle), jnp.sin(angle)], axis=2)
 
 
-def filter_rows(rows, basis, roots, weights, polar):
+def filter_rows(rows, basis, roots, weights, polar, halo=HALO):
     tiles, count, cols = rows.shape
     cos_dr, sin_dr = roots
     z_re = jnp.sum(cos_dr[:, :, None, None] * rows[None], axis=1)
     z_im = -jnp.sum(sin_dr[:, :, None, None] * rows[None], axis=1)
     z = jnp.concatenate([z_re, z_im], axis=1)
-    z = jnp.pad(z, ((0, 0), (0, 0), (HALO, HALO)))
+    z = jnp.pad(z, ((0, 0), (0, 0), (halo, halo)))
     prod = lax.dot_general(z, basis, (((2,), (1,)), ((0,), (0,))), precision=HIGHEST)
     per_class = basis.shape[2] // 2
     zc, zs = prod[:, :count, :per_class], prod[:, :count, per_class:]
@@ -85,13 +85,15 @@
     smooth = jnp.sum(
         cos_dr[:, :, None, None] * w_re[None] - sin_dr[:, :, None, None] * w_im[None], axis=1
     )
-    left = jnp.roll(rows[:, :, cols - HALO :], 1, axis=0)
-    right = jnp.roll(rows[:, :, :HALO], -1, axis=0)
-    wide = jnp.concatenate([left, rows, right], axis=2)
+    wide = rows
+    if halo:
+        left = jnp.roll(rows[:, :, cols - halo :], 1, axis=0)
+        right = jnp.roll(rows[:, :, :halo], -1, axis=0)
+        wide = jnp.concatenate([left, rows, right], axis=2)
     return jnp.where(polar[None, :, None], smooth, wide)
 
 
-def on_device(tracers, courant_x, courant_y, cutoffs):
+def tiled_path(tracers, courant_x, courant_y, cutoffs):
     tracer_count, level_count, lat_rows, lon_cols = tracers.shape
     field_count = tracer_count * level_count
     lat_devices = lax.axis_size("lat")
@@ -166,6 +168,93 @@
     return state
 
 
+def transposed_path(tracers, courant_x, courant_y, cutoffs):
+    tracer_count, level_count, lat_rows, lon_cols = tracers.shape
+    lat_devices = lax.axis_size("lat")
+    lon_devices = lax.axis_size("lon")
+    lat_index = lax.axis_index("lat")
+    circle = lon_cols * lon_devices
+    total_rows = lat_rows * lat_devices
+    row_global = lat_index * lat_rows + jnp.arange(lat_rows, dtype=jnp.int32)
+    face_global = lat_index * lat_rows + jnp.arange(lat_rows + 1, dtype=jnp.int32)
+    face_angle = (face_global.astype(jnp.float32) / total_rows - 0.5) * math.pi
+    face_weight = jnp.where(
+        (face_global == 0) | (face_global == total_rows), 0.0, jnp.cos(face_angle)
+    )
+    center_weight = jnp.cos(((row_global.astype(jnp.float32) + 0.5) / total_rows - 0.5) * math.pi)
+    is_south = lat_index == 0
+    is_north = lat_index == lat_devices - 1
+
+    north_cy = shift(courant_y[:, :1], "lat", -1, False)
+    north_cy = jnp.where(is_north, 0.0, north_cy)
+    count = tracer_count * lat_rows
+    payload = jnp.concatenate(
+        [
+            jnp.transpose(tracers, (1, 0, 2, 3)).reshape(level_count, count, lon_cols),
+            courant_x,
+            courant_y,
+            north_cy,
+        ],
+        axis=1,
+    )
+    payload = lax.all_to_all(payload, "lon", 0, 0)
+    state = payload[:, :count].reshape(lon_devices, tracer_count, lat_rows, lon_cols)
+    cx = payload[:, None, count : count + lat_rows]
+    north_courant = payload[:, None, count + lat_rows :]
+    east_courant = jnp.concatenate([jnp.roll(cx[..., lon_cols - 1 :], 1, axis=0), cx], axis=3)
+
+    held_global = lat_index * lat_rows + jnp.arange(count, dtype=jnp.int32) % lat_rows
+    polar = (held_global < total_rows // 4) | (held_global >= total_rows - total_rows // 4)
+    cut = jnp.take(cutoffs, held_global)
+    per_class = KMAX // lon_devices
+    k = lon_devices * jnp.arange(per_class, dtype=jnp.int32)[None, :] + jnp.arange(
+        lon_devices, dtype=jnp.int32
+    )[:, None]
+    scale = jnp.where(k == 0, 1.0 / circle, 2.0 / circle).astype(jnp.float32)
+    weights = jnp.where(k[:, None, :] < cut[None, :, None], scale[:, None, :], 0.0)
+    basis = class_basis(lon_devices, lon_cols, circle, 0)
+    roots = root_table(lon_devices)
+
+    for substep in range(SUBSTEPS):
+        south_in = shift(state[:, :, lat_rows - HALO :], "lat", 1, False)
+        north_in = shift(state[:, :, :HALO], "lat", -1, False)
+        edge = jnp.where(is_south, state[:, :, :HALO], state[:, :, lat_rows - HALO :])
+        far = jnp.roll(edge, lon_devices // 2, axis=0)
+        far_rev = jnp.concatenate([far[:, :, 2:3], far[:, :, 1:2], far[:, :, 0:1]], axis=2)
+        south_rows = jnp.where(is_south, far_rev, south_in)
+        north_rows = jnp.where(is_north, far_rev, north_in)
+        extended = jnp.concatenate([south_rows, state, north_rows], axis=2)
+        wrapped = jnp.concatenate(
+            [
+                jnp.roll(state[..., lon_cols - HALO :], 1, axis=0),
+                state,
+                jnp.roll(state[..., :HALO], -1, axis=0),
+            ],
+            axis=3,
+        )
+        zonal = ppm_flux(wrapped, east_courant, 3, lon_cols)
+        meridional = ppm_flux(extended, north_courant, 2, lat_rows) * face_weight[:, None]
+        change = (
+            zonal[..., 1:]
+            - zonal[..., :-1]
+            + (meridional[:, :, 1:] - meridional[:, :, :-1]) / center_weight[:, None]
+        )
+        state = state - change
+        rows = state.reshape(lon_devices, count, lon_cols)
+        rows = filter_rows(rows, basis, roots, weights, polar, 0)
+        state = rows.reshape(lon_devices, tracer_count, lat_rows, lon_cols)
+
+    tiles = lax.all_to_all(state, "lon", 0, 0)
+    return jnp.transpose(tiles, (1, 0, 2, 3))
+
+
+def on_device(tracers, courant_x, courant_y, cutoffs):
+    field_count = tracers.shape[0] * tracers.shape[1]
+    if tracers.shape[1] == lax.axis_size("lon") and tracers.shape[2] >= HALO:
+        return transposed_path(tracers, courant_x, courant_y, cutoffs)
+    return tiled_path(tracers, courant_x, courant_y, cutoffs)
+
+
 def solution(mesh):
     in_specs = (P(None, None, "lat", "lon"), P(None, "lat", "lon"), P(None, "lat", "lon"), P())
     out_specs = P(None, None, "lat", "lon")

time: 140 us -> 98.1 us (0.70); the launches traced: 137 us -> 97.5 us
  blocking collectives: 47.2 us -> 14.8 us
  starting transfers between devices: 26.2 us -> 17.2 us
    all_to_all x3 -> x1, blocking collectives: 47.2 us -> 14.8 us  [transposed_path(): tiles = lax.all_to_all(state, 'lon', 0, 0)]
    ppermute x10 -> x5, starting transfers between devices: 22.6 us -> 12.6 us  [shift(): return lax.ppermute(x, axis, pairs)]
    ppermute x10 -> x5, waiting for transfers between devices: 14.4 us -> 9.03 us  [shift(): return lax.ppermute(x, axis, pairs)]
    all_to_all x1, waiting for transfers between devices: 1.43 us -> 6.59 us  [transposed_path(): payload = lax.all_to_all(payload, 'lon', 0, 0)]
    dot_general x2, matrix products: 6.47 us -> 9.31 us  [filter_rows(): lax.dot_general(spec, basis, (((2,), (2,)), ((0,), (0,))), precision=HIGH...]
    concatenate x4 -> x6, other arithmetic: 0.62 us -> 2.7 us  [the longest x1 1.9 us: transposed_path(): jnp.concatenate([jnp.transpose(tracers, (1, 0, 2, 3)).reshape(level_count...]
    cos x1, other arithmetic: 11.1 us -> 13.2 us  [class_basis(): return jnp.concatenate([jnp.cos(angle), jnp.sin(angle)], axis=2)]
    slice x10 -> x9, local copies, waits for them, and re-layouts: 3.45 us -> 1.45 us  [the longest x1 0.91 us: transposed_path(): north_cy = shift(courant_y[:, :1], 'lat', -1, False)]
  transfers between devices with their start and end apart: 11 -> 6, of which waited for: 4 -> 4; matrix products, arithmetic and copies ran while one was open for 15% -> 20% of each run, Pallas kernels for 0% -> 0%
where the time goes in v3:
time: 98.1 us; the launch traced here: 97.5 us
  other arithmetic  27.4 us (28%)
  starting transfers between devices  17.2 us (18%)
  matrix products  15.7 us (16%)
  waiting for transfers between devices  15.6 us (16%)
  blocking collectives  14.8 us (15%)
  local copies, waits for them, and re-layouts  6.38 us (7%)
    all_to_all x1, blocking collectives, transposed_path(): tiles = lax.all_to_all(state, 'lon', 0, 0)  14.8 us
    cos x1, other arithmetic, class_basis(): return jnp.concatenate([jnp.cos(angle), jnp.sin(angle)], axis=2)  13.2 us
    ppermute x5, starting transfers between devices, shift(): return lax.ppermute(x, axis, pairs)  12.6 us
    dot_general x2, matrix products, filter_rows(): lax.dot_general(spec, basis, (((2,), (2,)), ((0,), (0,))), precision=HIGH...  9.31 us
    ppermute x5, waiting for transfers between devices, shift(): return lax.ppermute(x, axis, pairs)  9.03 us
    all_to_all x1, waiting for transfers between devices, transposed_path(): payload = lax.all_to_all(payload, 'lon', 0, 0)  6.59 us
    dot_general x2, matrix products, filter_rows(): lax.dot_general(z, basis, (((2,), (1,)), ((0,), (0,))), precision=HIGHEST)  6.39 us
    all_to_all x1, starting transfers between devices, transposed_path(): payload = lax.all_to_all(payload, 'lon', 0, 0)  4.59 us
  transfers between devices with their start and end apart: 6, of which 4 were waited for; matrix products, arithmetic and copies ran while one was open for 20% of the time, Pallas kernels for 0%

profile of v3, /device:TPU:3, one launch (start us, length us, event | category | flops | bytes accessed | tf_op | source)
XLA Modules:
  0.0 97.5 jit_solution(18196530287360021411)
XLA Ops:
  0.0 0.9 slice.279
  0.9 2.6 %collective-permute-start = (f32[4,1,720]{2,1,0:T(1,128)S(1)}, f32[4,1,720]{2,1,0:T(1,128)S(1)}, u32[]{:S(2)}, u32[]{:S(2)}) collective-permute-start(f32[4,1,720]{2,1,0:T(1,128)S(1)} %slice.279), channel_id=1, source_target_pairs={{4,0},{8,4},{12,8},{16,12},{20,16},{24,20},{28,24},{5,1},{9,5},{13... | collective-permute-start | bytes 34568 | tf_op jit(solution)/shard_map/ppermute | solution.py:17
  3.6 0.8 gather_fusion
  4.4 1.1 %copy.48 = f32[5,4,8,720]{3,2,0,1:T(8,128)S(1)} copy(f32[5,4,8,720]{3,2,1,0:T(8,128)} %param.4) | data formatting | bytes 921600 | tf_op args[0]
  5.5 1.3 %collective-permute-done = f32[4,1,720]{2,1,0:T(1,128)S(1)} collective-permute-done((f32[4,1,720]{2,1,0:T(1,128)S(1)}, f32[4,1,720]{2,1,0:T(1,128)S(1)}, u32[]{:S(2)}, u32[]{:S(2)}) %collective-permute-start) | collective-permute-done | bytes 11552 | tf_op jit(solution)/shard_map/ppermute | solution.py:17
  6.8 1.9 %pad_maximum_fusion.7 = f32[4,57,720]{2,1,0:T(8,128)} fusion(f32[4,1,720]{2,1,0:T(1,128)S(1)} %broadcast_select_fusion.6, f32[4,8,720]{2,1,0:T(8,128)} %param.6, f32[4,8,720]{2,1,0:T(8,128)} %param.5, f32[4,40,720]{2,1,0:T(8,128)S(1)} %bitcast.28), kind=kLoop, calls=%fused_computation.83 | loop fusion | flops 492480 | bytes 1313280 | tf_op jit(solution)/shard_map/concatenate | solution.py:191
  8.7 4.6 %all-to-all-start = ((f32[4,57,720]{2,1,0:T(8,128)}), f32[4,57,720]{2,1,0:T(8,128)}, u32[]{:S(2)}, u32[]{:S(2)}) async-start(f32[4,57,720]{2,1,0:T(8,128)} %pad_maximum_fusion.7), calls=%async_computation | async-start | bytes 1572864 | tf_op jit(solution)/shard_map/all_to_all | solution.py:200
  13.5 13.2 %fusion.5 = (f32[4,720,180]{2,1,0:T(8,128)S(1)}, f32[4,720,180]{2,1,0:T(8,128)}) fusion(s32[4,180]{1,0:T(4,128)S(1)} %iota_add_fusion), kind=kLoop, calls=%fused_computation.9 | loop fusion | flops 4665600 | bytes 4150080 | tf_op jit(solution)/shard_map/cos | solution.py:64
  26.6 6.6 %all-to-all-done = f32[4,57,720]{2,1,0:T(8,128)} async-done(((f32[4,57,720]{2,1,0:T(8,128)}), f32[4,57,720]{2,1,0:T(8,128)}, u32[]{:S(2)}, u32[]{:S(2)}) %all-to-all-start) | async-done | bytes 656672 | tf_op jit(solution)/shard_map/all_to_all | solution.py:200
  33.2 1.1 %slice_bitcast_fusion = f32[4,5,8,720]{3,2,1,0:T(8,128)S(1)} fusion(f32[4,57,720]{2,1,0:T(8,128)} %all-to-all-done), kind=kLoop, calls=%fused_computation.128 | loop fusion | bytes 921600 | tf_op jit(solution)/shard_map/reshape | solution.py:201
  34.5 0.9 slice_bitcast_fusion.1
  35.9 3.4 %collective-permute-start.1 = (f32[4,5,3,720]{3,2,1,0:T(4,128)S(1)}, f32[4,5,3,720]{3,2,1,0:T(4,128)S(1)}, u32[]{:S(2)}, u32[]{:S(2)}) collective-permute-start(f32[4,5,3,720]{3,2,1,0:T(4,128)S(1)} %get-tuple-element.41), channel_id=1, source_target_pairs={{0,4},{4,8},{8,12},{12,16},{16,20},{20,24},{24,28},{1,5},{5,9},{9,... | collective-permute-start | bytes 518408 | tf_op jit(solution)/shard_map/ppermute | solution.py:17
  39.4 2.1 %collective-permute-start.2 = (f32[4,5,3,720]{3,2,1,0:T(4,128)S(1)}, f32[4,5,3,720]{3,2,1,0:T(4,128)S(1)}, u32[]{:S(2)}, u32[]{:S(2)}) collective-permute-start(f32[4,5,3,720]{3,2,1,0:T(4,128)S(1)} %get-tuple-element.42), channel_id=1, source_target_pairs={{4,0},{8,4},{12,8},{16,12},{20,16},{24,20},{28,24},{5,1},{9,5},{13... | collective-permute-start | bytes 518408 | tf_op jit(solution)/shard_map/ppermute | solution.py:17
  41.5 0.2 maximum_maximum_fusion
  41.7 0.5 fusion.90
  42.2 0.5 fusion.83
  42.7 1.0 %fusion.135 = (f32[4,9,720]{2,1,0:T(8,128)S(1)}, f32[4,9,720]{2,1,0:T(8,128)S(1)}, f32[4,9,720]{2,1,0:T(8,128)S(1)}) fusion(f32[4,57,720]{2,1,0:T(8,128)} %all-to-all-done), kind=kLoop, calls=%fused_computation.233 | loop fusion | flops 103680 | bytes 414720 | tf_op jit(solution)/shard_map/slice | solution.py:203
  43.7 1.0 broadcast_compare_fusion
  44.7 3.1 %collective-permute-done.2 = f32[4,5,3,720]{3,2,1,0:T(4,128)S(1)} collective-permute-done((f32[4,5,3,720]{3,2,1,0:T(4,128)S(1)}, f32[4,5,3,720]{3,2,1,0:T(4,128)S(1)}, u32[]{:S(2)}, u32[]{:S(2)}) %collective-permute-start.2) | collective-permute-done | bytes 172832 | tf_op jit(solution)/shard_map/ppermute | solution.py:17
  47.8 0.2 broadcast_select_fusion.4
  48.0 0.2 pad_maximum_fusion.5
  48.2 0.4 fusion.46
  48.7 1.0 fusion.33
  49.7 1.4 %fusion.76 = f32[4,5,8,720]{3,2,1,0:T(8,128)S(1)} fusion(f32[4,5,9,720]{3,2,1,0:T(8,128)S(1)} %fusion.33, f32[4,5,8,721]{3,2,1,0:T(8,128)S(1)} %fusion.83, f32[8]{0:T(128)S(1)} %multiply_cosine_fusion, f32[4,57,720]{2,1,0:T(8,128)} %all-to-all-done), kind=kLoop, calls=%fused_computation.109 | loop fusion | flops 576000 | bytes 2764832 | tf_op jit(solution)/shard_map/sub | solution.py:242
  51.1 0.4 multiply_reduce_fusion.3
  51.5 0.1 copy-done.1
  51.6 3.2 %fusion.49 = f32[4,80,360]{2,1,0:T(8,128)S(1)} fusion(f32[4,40,720]{2,1,0:T(8,128)S(1)} %neg.12, f32[4,40,720]{2,1,0:T(8,128)S(1)} %get-tuple-element.7, f32[4,720,180]{2,1,0:T(8,128)S(1)} %copy-done.1, f32[4,720,180]{2,1,0:T(8,128)S(1)} %get-tuple-element.54), kind=kOutput, calls=%fused_computation.74 | convolution fusion | flops 996595200 | bytes 5529600 | tf_op jit(solution)/shard_map/dot_general | solution.py:74
  54.8 0.2 fusion.132
  55.0 4.7 %fusion.91 = f32[4,80,720]{2,1,0:T(8,128)S(1)} fusion(f32[4,40,180]{2,1,0:T(8,128)S(1)} %get-tuple-element.29, f32[4,40,180]{2,1,0:T(8,128)S(1)} %get-tuple-element.14, f32[4,40,180]{2,1,0:T(8,128)S(1)} %get-tuple-element.15, f32[4,720,180]{2,1,0:T(8,128)S(1)} %copy-done.1, f32[4,720,180]{2,1,0:T(8,128)S(1)} %get-tuple-element.54), kind=kOutput, calls=%fused_computation.132 | convolution fusion | flops 996710400 | bytes 5414400 | tf_op jit(solution)/shard_map/dot_general | solution.py:83
  59.7 0.4 subtract_reduce_fusion.1
  60.5 1.9 %collective-permute-start.3 = (f32[4,5,3,720]{3,2,1,0:T(4,128)S(1)}, f32[4,5,3,720]{3,2,1,0:T(4,128)S(1)}, u32[]{:S(2)}, u32[]{:S(2)}) collective-permute-start(f32[4,5,3,720]{3,2,1,0:T(4,128)S(1)} %get-tuple-element.34), channel_id=1, source_target_pairs={{0,4},{4,8},{8,12},{12,16},{16,20},{20,24},{24,28},{1,5},{5,9},{9,... | collective-permute-start | bytes 518408 | tf_op jit(solution)/shard_map/ppermute | solution.py:17
  62.4 2.6 %collective-permute-start.4 = (f32[4,5,3,720]{3,2,1,0:T(4,128)S(1)}, f32[4,5,3,720]{3,2,1,0:T(4,128)S(1)}, u32[]{:S(2)}, u32[]{:S(2)}) collective-permute-start(f32[4,5,3,720]{3,2,1,0:T(4,128)S(1)} %get-tuple-element.35), channel_id=1, source_target_pairs={{4,0},{8,4},{12,8},{16,12},{20,16},{24,20},{28,24},{5,1},{9,5},{13... | collective-permute-start | bytes 518408 | tf_op jit(solution)/shard_map/ppermute | solution.py:17
  65.1 0.2 maximum_maximum_fusion.2
  65.3 0.5 fusion.73
  65.8 0.5 fusion.66
  66.3 4.5 %collective-permute-done.4 = f32[4,5,3,720]{3,2,1,0:T(4,128)S(1)} collective-permute-done((f32[4,5,3,720]{3,2,1,0:T(4,128)S(1)}, f32[4,5,3,720]{3,2,1,0:T(4,128)S(1)}, u32[]{:S(2)}, u32[]{:S(2)}) %collective-permute-start.4) | collective-permute-done | bytes 172832 | tf_op jit(solution)/shard_map/ppermute | solution.py:17
  70.8 0.2 broadcast_select_fusion.2
  71.1 0.2 pad_maximum_fusion.6
  71.3 0.4 fusion.43
  71.7 1.0 fusion.16
  72.6 0.3 fusion.59
  72.9 0.4 multiply_reduce_fusion.1
  73.3 3.2 %fusion.53 = f32[4,80,360]{2,1,0:T(8,128)S(1)} fusion(f32[4,40,720]{2,1,0:T(8,128)S(1)} %neg.14, f32[4,40,720]{2,1,0:T(8,128)S(1)} %get-tuple-element.5, f32[4,720,180]{2,1,0:T(8,128)S(1)} %copy-done.1, f32[4,720,180]{2,1,0:T(8,128)S(1)} %get-tuple-element.54), kind=kOutput, calls=%fused_computation.79 | convolution fusion | flops 996595200 | bytes 5529600 | tf_op jit(solution)/shard_map/dot_general | solution.py:74
  76.5 0.2 fusion.131
  76.7 4.7 %fusion.99 = f32[4,80,720]{2,1,0:T(8,128)S(1)} fusion(f32[4,40,180]{2,1,0:T(8,128)S(1)} %get-tuple-element.28, f32[4,40,180]{2,1,0:T(8,128)S(1)} %get-tuple-element.9, f32[4,40,180]{2,1,0:T(8,128)S(1)} %get-tuple-element.10, f32[4,720,180]{2,1,0:T(8,128)S(1)} %copy-done.1, f32[4,720,180]{2,1,0:T(8,128)S(1)} %get-tuple-element.54), kind=kOutput, calls=%fused_computation.143 | convolution fusion | flops 996710400 | bytes 5414400 | tf_op jit(solution)/shard_map/dot_general | solution.py:83
  81.4 0.4 subtract_reduce_fusion
  81.9 14.8 %all_to_all.10 = f32[4,5,8,720]{3,2,1,0:T(8,128)S(1)} all-to-all(f32[4,5,8,720]{3,2,1,0:T(8,128)S(1)} %bitcast_select_fusion), channel_id=1, replica_groups=mesh['lat'=8,'lon'=4] {'lon'}, dimensions={0} | all-to-all | bytes 921600 | tf_op jit(solution)/shard_map/all_to_all | solution.py:247
  96.7 0.8 copy.46
  (36 shorter events, 1.7 us)
Async XLA Ops:
  0.0 3.6 %copy-start = (s32[64]{0:T(128)S(1)}, s32[64]{0:T(128)}, u32[]{:S(2)}) copy-start(s32[64]{0:T(128)} %param.7) | copy-start | bytes 772
  0.9 5.9 %collective-permute-start = (f32[4,1,720]{2,1,0:T(1,128)S(1)}, f32[4,1,720]{2,1,0:T(1,128)S(1)}, u32[]{:S(2)}, u32[]{:S(2)}) collective-permute-start(f32[4,1,720]{2,1,0:T(1,128)S(1)} %slice.279), channel_id=1, source_target_pairs={{4,0},{8,4},{12,8},{16,12},{20,16},{24,20},{28,24},{5,1},{9,5},{13... | collective-permute-start | bytes 34568 | tf_op jit(solution)/shard_map/ppermute | solution.py:17
  8.7 24.5 %all-to-all-start = ((f32[4,57,720]{2,1,0:T(8,128)}), f32[4,57,720]{2,1,0:T(8,128)}, u32[]{:S(2)}, u32[]{:S(2)}) async-start(f32[4,57,720]{2,1,0:T(8,128)} %pad_maximum_fusion.7), calls=%async_computation | async-start | bytes 1572864 | tf_op jit(solution)/shard_map/all_to_all | solution.py:200
  35.9 8.7 %collective-permute-start.1 = (f32[4,5,3,720]{3,2,1,0:T(4,128)S(1)}, f32[4,5,3,720]{3,2,1,0:T(4,128)S(1)}, u32[]{:S(2)}, u32[]{:S(2)}) collective-permute-start(f32[4,5,3,720]{3,2,1,0:T(4,128)S(1)} %get-tuple-element.41), channel_id=1, source_target_pairs={{0,4},{4,8},{8,12},{12,16},{16,20},{20,24},{24,28},{1,5},{5,9},{9,... | collective-permute-start | bytes 518408 | tf_op jit(solution)/shard_map/ppermute | solution.py:17
  39.4 8.4 %collective-permute-start.2 = (f32[4,5,3,720]{3,2,1,0:T(4,128)S(1)}, f32[4,5,3,720]{3,2,1,0:T(4,128)S(1)}, u32[]{:S(2)}, u32[]{:S(2)}) collective-permute-start(f32[4,5,3,720]{3,2,1,0:T(4,128)S(1)} %get-tuple-element.42), channel_id=1, source_target_pairs={{4,0},{8,4},{12,8},{16,12},{20,16},{24,20},{28,24},{5,1},{9,5},{13... | collective-permute-start | bytes 518408 | tf_op jit(solution)/shard_map/ppermute | solution.py:17
  49.6 2.0 %copy-start.1 = (f32[4,720,180]{2,1,0:T(8,128)S(1)}, f32[4,720,180]{2,1,0:T(8,128)}, u32[]{:S(2)}) copy-start(f32[4,720,180]{2,1,0:T(8,128)} %get-tuple-element.55) | copy-start | bytes 6220804
  60.5 5.8 %collective-permute-start.3 = (f32[4,5,3,720]{3,2,1,0:T(4,128)S(1)}, f32[4,5,3,720]{3,2,1,0:T(4,128)S(1)}, u32[]{:S(2)}, u32[]{:S(2)}) collective-permute-start(f32[4,5,3,720]{3,2,1,0:T(4,128)S(1)} %get-tuple-element.34), channel_id=1, source_target_pairs={{0,4},{4,8},{8,12},{12,16},{16,20},{20,24},{24,28},{1,5},{5,9},{9,... | collective-permute-start | bytes 518408 | tf_op jit(solution)/shard_map/ppermute | solution.py:17
  62.4 8.4 %collective-permute-start.4 = (f32[4,5,3,720]{3,2,1,0:T(4,128)S(1)}, f32[4,5,3,720]{3,2,1,0:T(4,128)S(1)}, u32[]{:S(2)}, u32[]{:S(2)}) collective-permute-start(f32[4,5,3,720]{3,2,1,0:T(4,128)S(1)} %get-tuple-element.35), channel_id=1, source_target_pairs={{4,0},{8,4},{12,8},{16,12},{20,16},{24,20},{28,24},{5,1},{9,5},{13... | collective-permute-start | bytes 518408 | tf_op jit(solution)/shard_map/ppermute | solution.py:17

commit v4 on v3

--- a/solution.py
+++ b/solution.py
@@ -8,7 +8,7 @@
 KMAX = 720
 SUBSTEPS = 2
 HALO = 3
-HIGHEST = lax.Precision.HIGHEST
+MATMUL_PRECISION = lax.Precision.HIGH
 
 
 def shift(x, axis, by, wrap):
@@ -71,7 +71,7 @@
     z_im = -jnp.sum(sin_dr[:, :, None, None] * rows[None], axis=1)
     z = jnp.concatenate([z_re, z_im], axis=1)
     z = jnp.pad(z, ((0, 0), (0, 0), (halo, halo)))
-    prod = lax.dot_general(z, basis, (((2,), (1,)), ((0,), (0,))), precision=HIGHEST)
+    prod = lax.dot_general(z, basis, (((2,), (1,)), ((0,), (0,))), precision=MATMUL_PRECISION)
     per_class = basis.shape[2] // 2
     zc, zs = prod[:, :count, :per_class], prod[:, :count, per_class:]
     wc, ws = prod[:, count:, :per_class], prod[:, count:, per_class:]
@@ -80,7 +80,7 @@
     spec = jnp.concatenate(
         [jnp.concatenate([real, imag], axis=2), jnp.concatenate([-imag, real], axis=2)], axis=1
     )
-    back = lax.dot_general(spec, basis, (((2,), (2,)), ((0,), (0,))), precision=HIGHEST)
+    back = lax.dot_general(spec, basis, (((2,), (2,)), ((0,), (0,))), precision=MATMUL_PRECISION)
     w_re, w_im = back[:, :count], back[:, count:]
     smooth = jnp.sum(
         cos_dr[:, :, None, None] * w_re[None] - sin_dr[:, :, None, None] * w_im[None], axis=1

time: 98.1 us -> 91.3 us (0.931)
  matrix products: 15.7 us -> 8.98 us
    dot_general x4, matrix products: 15.7 us -> 8.98 us  [the longest x2 5.18 us: filter_rows(): lax.dot_general(spec, basis, (((2,), (2,)), ((0,), (0,))), precision=MATM...]
  transfers between devices with their start and end apart: 6 -> 6, of which waited for: 4 -> 4; matrix products, arithmetic and copies ran while one was open for 20% -> 22% of each run, Pallas kernels for 0% -> 0%
where the time goes in v4:
time: 91.3 us; the launch traced here: 90.8 us
  other arithmetic  27.4 us (30%)
  starting transfers between devices  17 us (19%)
  waiting for transfers between devices  15.8 us (17%)
  blocking collectives  14.8 us (16%)
  matrix products  8.98 us (10%)
  local copies, waits for them, and re-layouts  6.38 us (7%)
    all_to_all x1, blocking collectives, transposed_path(): tiles = lax.all_to_all(state, 'lon', 0, 0)  14.8 us
    cos x1, other arithmetic, class_basis(): return jnp.concatenate([jnp.cos(angle), jnp.sin(angle)], axis=2)  13.2 us
    ppermute x5, starting transfers between devices, shift(): return lax.ppermute(x, axis, pairs)  12.4 us
    ppermute x5, waiting for transfers between devices, shift(): return lax.ppermute(x, axis, pairs)  9.25 us
    all_to_all x1, waiting for transfers between devices, transposed_path(): payload = lax.all_to_all(payload, 'lon', 0, 0)  6.59 us
    dot_general x2, matrix products, filter_rows(): lax.dot_general(spec, basis, (((2,), (2,)), ((0,), (0,))), precision=MATM...  5.18 us
    all_to_all x1, starting transfers between devices, transposed_path(): payload = lax.all_to_all(payload, 'lon', 0, 0)  4.59 us
    dot_general x2, matrix products, filter_rows(): lax.dot_general(z, basis, (((2,), (1,)), ((0,), (0,))), precision=MATMUL_...  3.8 us
  transfers between devices with their start and end apart: 6, of which 4 were waited for; matrix products, arithmetic and copies ran while one was open for 22% of the time, Pallas kernels for 0%

profile of v4, /device:TPU:3, one launch (start us, length us, event | category | flops | bytes accessed | tf_op | source)
XLA Modules:
  0.0 90.8 jit_solution(17188345639513334095)
XLA Ops:
  0.0 0.9 %slice.279 = f32[4,1,720]{2,1,0:T(1,128)S(1)} slice(f32[4,8,720]{2,1,0:T(8,128)} %param.6), slice={[0:4], [0:1], [0:720]} | slice | bytes 23040 | tf_op jit(solution)/shard_map/slice | solution.py:188
  0.9 2.6 %collective-permute-start = (f32[4,1,720]{2,1,0:T(1,128)S(1)}, f32[4,1,720]{2,1,0:T(1,128)S(1)}, u32[]{:S(2)}, u32[]{:S(2)}) collective-permute-start(f32[4,1,720]{2,1,0:T(1,128)S(1)} %slice.279), channel_id=1, source_target_pairs={{4,0},{8,4},{12,8},{16,12},{20,16},{24,20},{28,24},{5,1},{9,5},{13... | collective-permute-start | bytes 34568 | tf_op jit(solution)/shard_map/ppermute | solution.py:17
  3.6 0.8 gather_fusion
  4.4 1.1 %copy.48 = f32[5,4,8,720]{3,2,0,1:T(8,128)S(1)} copy(f32[5,4,8,720]{3,2,1,0:T(8,128)} %param.4) | data formatting | bytes 921600 | tf_op args[0]
  5.5 1.3 %collective-permute-done = f32[4,1,720]{2,1,0:T(1,128)S(1)} collective-permute-done((f32[4,1,720]{2,1,0:T(1,128)S(1)}, f32[4,1,720]{2,1,0:T(1,128)S(1)}, u32[]{:S(2)}, u32[]{:S(2)}) %collective-permute-start) | collective-permute-done | bytes 11552 | tf_op jit(solution)/shard_map/ppermute | solution.py:17
  6.8 1.9 %pad_maximum_fusion.7 = f32[4,57,720]{2,1,0:T(8,128)} fusion(f32[4,1,720]{2,1,0:T(1,128)S(1)} %broadcast_select_fusion.6, f32[4,8,720]{2,1,0:T(8,128)} %param.6, f32[4,8,720]{2,1,0:T(8,128)} %param.5, f32[4,40,720]{2,1,0:T(8,128)S(1)} %bitcast.28), kind=kLoop, calls=%fused_computation.83 | loop fusion | flops 492480 | bytes 1313280 | tf_op jit(solution)/shard_map/concatenate | solution.py:191
  8.7 4.6 %all-to-all-start = ((f32[4,57,720]{2,1,0:T(8,128)}), f32[4,57,720]{2,1,0:T(8,128)}, u32[]{:S(2)}, u32[]{:S(2)}) async-start(f32[4,57,720]{2,1,0:T(8,128)} %pad_maximum_fusion.7), calls=%async_computation | async-start | bytes 1572864 | tf_op jit(solution)/shard_map/all_to_all | solution.py:200
  13.5 13.2 %fusion.5 = (f32[4,720,180]{2,1,0:T(8,128)S(1)}, f32[4,720,180]{2,1,0:T(8,128)}) fusion(s32[4,180]{1,0:T(4,128)S(1)} %iota_add_fusion), kind=kLoop, calls=%fused_computation.9 | loop fusion | flops 4665600 | bytes 4150080 | tf_op jit(solution)/shard_map/cos | solution.py:64
  26.6 6.6 %all-to-all-done = f32[4,57,720]{2,1,0:T(8,128)} async-done(((f32[4,57,720]{2,1,0:T(8,128)}), f32[4,57,720]{2,1,0:T(8,128)}, u32[]{:S(2)}, u32[]{:S(2)}) %all-to-all-start) | async-done | bytes 656672 | tf_op jit(solution)/shard_map/all_to_all | solution.py:200
  33.2 1.1 %slice_bitcast_fusion = f32[4,5,8,720]{3,2,1,0:T(8,128)S(1)} fusion(f32[4,57,720]{2,1,0:T(8,128)} %all-to-all-done), kind=kLoop, calls=%fused_computation.128 | loop fusion | bytes 921600 | tf_op jit(solution)/shard_map/reshape | solution.py:201
  34.5 0.9 %slice_bitcast_fusion.1 = (f32[4,1,8,720]{3,2,0,1:T(8,128)S(1)}, f32[4,8,720]{2,1,0:T(8,128)S(1)}) fusion(f32[4,57,720]{2,1,0:T(8,128)} %all-to-all-done), kind=kLoop, calls=%fused_computation.228 | loop fusion | bytes 276480 | tf_op jit(solution)/shard_map/broadcast_in_dim | solution.py:202
  35.9 3.4 %collective-permute-start.1 = (f32[4,5,3,720]{3,2,1,0:T(4,128)S(1)}, f32[4,5,3,720]{3,2,1,0:T(4,128)S(1)}, u32[]{:S(2)}, u32[]{:S(2)}) collective-permute-start(f32[4,5,3,720]{3,2,1,0:T(4,128)S(1)} %get-tuple-element.41), channel_id=1, source_target_pairs={{0,4},{4,8},{8,12},{12,16},{16,20},{20,24},{24,28},{1,5},{5,9},{9,... | collective-permute-start | bytes 518408 | tf_op jit(solution)/shard_map/ppermute | solution.py:17
  39.4 1.9 %collective-permute-start.2 = (f32[4,5,3,720]{3,2,1,0:T(4,128)S(1)}, f32[4,5,3,720]{3,2,1,0:T(4,128)S(1)}, u32[]{:S(2)}, u32[]{:S(2)}) collective-permute-start(f32[4,5,3,720]{3,2,1,0:T(4,128)S(1)} %get-tuple-element.42), channel_id=1, source_target_pairs={{4,0},{8,4},{12,8},{16,12},{20,16},{24,20},{28,24},{5,1},{9,5},{13... | collective-permute-start | bytes 518408 | tf_op jit(solution)/shard_map/ppermute | solution.py:17
  41.3 0.2 maximum_maximum_fusion
  41.6 0.5 fusion.90
  42.0 0.5 fusion.83
  42.5 1.0 %fusion.135 = (f32[4,9,720]{2,1,0:T(8,128)S(1)}, f32[4,9,720]{2,1,0:T(8,128)S(1)}, f32[4,9,720]{2,1,0:T(8,128)S(1)}) fusion(f32[4,57,720]{2,1,0:T(8,128)} %all-to-all-done), kind=kLoop, calls=%fused_computation.233 | loop fusion | flops 103680 | bytes 414720 | tf_op jit(solution)/shard_map/slice | solution.py:203
  43.5 1.0 %broadcast_compare_fusion = pred[4,9,720]{2,1,0:T(8,128)(4,1)S(1)} fusion(f32[4,57,720]{2,1,0:T(8,128)} %all-to-all-done), kind=kLoop, calls=%fused_computation.185 | loop fusion | flops 25920 | bytes 129600 | tf_op jit(solution)/shard_map/ge | solution.py:44
  44.5 3.3 %collective-permute-done.2 = f32[4,5,3,720]{3,2,1,0:T(4,128)S(1)} collective-permute-done((f32[4,5,3,720]{3,2,1,0:T(4,128)S(1)}, f32[4,5,3,720]{3,2,1,0:T(4,128)S(1)}, u32[]{:S(2)}, u32[]{:S(2)}) %collective-permute-start.2) | collective-permute-done | bytes 172832 | tf_op jit(solution)/shard_map/ppermute | solution.py:17
  47.8 0.2 broadcast_select_fusion.4
  48.0 0.2 pad_maximum_fusion.5
  48.2 0.4 fusion.46
  48.7 1.0 %fusion.33 = f32[4,5,9,720]{3,2,1,0:T(8,128)S(1)} fusion(f32[4,5,8,720]{3,2,1,0:T(8,128)S(1)} %slice_bitcast_fusion, f32[4,5,3,720]{3,2,1,0:T(4,128)S(1)} %get-tuple-element.49, f32[4,5,3,720]{3,2,1,0:T(4,128)S(1)} %get-tuple-element.48, f32[4,5,11,720]{3,2,1,0:T(8,128)S(1)} %fusion.46, f32[9]{0:T(128)S(1)} %or_select_fusion, ...), kind=kLoop, calls=%fused_computation.55 | loop fusion | flops 2980800 | bytes 3216996 | tf_op jit(solution)/shard_map/mul | solution.py:236
  49.7 1.4 %fusion.76 = f32[4,5,8,720]{3,2,1,0:T(8,128)S(1)} fusion(f32[4,5,9,720]{3,2,1,0:T(8,128)S(1)} %fusion.33, f32[4,5,8,721]{3,2,1,0:T(8,128)S(1)} %fusion.83, f32[8]{0:T(128)S(1)} %multiply_cosine_fusion, f32[4,57,720]{2,1,0:T(8,128)} %all-to-all-done), kind=kLoop, calls=%fused_computation.109 | loop fusion | flops 576000 | bytes 2764832 | tf_op jit(solution)/shard_map/sub | solution.py:242
  51.1 0.4 multiply_reduce_fusion.3
  51.5 0.1 copy-done.1
  51.6 1.9 %fusion.49 = f32[4,80,360]{2,1,0:T(8,128)S(1)} fusion(f32[4,40,720]{2,1,0:T(8,128)S(1)} %neg.12, f32[4,40,720]{2,1,0:T(8,128)S(1)} %get-tuple-element.7, f32[4,720,180]{2,1,0:T(8,128)S(1)} %copy-done.1, f32[4,720,180]{2,1,0:T(8,128)S(1)} %get-tuple-element.54), kind=kOutput, calls=%fused_computation.74 | convolution fusion | flops 498931200 | bytes 5529600 | tf_op jit(solution)/shard_map/dot_general | solution.py:74
  53.5 0.2 fusion.132
  53.7 2.6 %fusion.91 = f32[4,80,720]{2,1,0:T(8,128)S(1)} fusion(f32[4,40,180]{2,1,0:T(8,128)S(1)} %get-tuple-element.29, f32[4,40,180]{2,1,0:T(8,128)S(1)} %get-tuple-element.14, f32[4,40,180]{2,1,0:T(8,128)S(1)} %get-tuple-element.15, f32[4,720,180]{2,1,0:T(8,128)S(1)} %copy-done.1, f32[4,720,180]{2,1,0:T(8,128)S(1)} %get-tuple-element.54), kind=kOutput, calls=%fused_computation.132 | convolution fusion | flops 499046400 | bytes 5414400 | tf_op jit(solution)/shard_map/dot_general | solution.py:83
  56.4 0.4 subtract_reduce_fusion.1
  57.1 1.9 %collective-permute-start.3 = (f32[4,5,3,720]{3,2,1,0:T(4,128)S(1)}, f32[4,5,3,720]{3,2,1,0:T(4,128)S(1)}, u32[]{:S(2)}, u32[]{:S(2)}) collective-permute-start(f32[4,5,3,720]{3,2,1,0:T(4,128)S(1)} %get-tuple-element.34), channel_id=1, source_target_pairs={{0,4},{4,8},{8,12},{12,16},{16,20},{20,24},{24,28},{1,5},{5,9},{9,... | collective-permute-start | bytes 518408 | tf_op jit(solution)/shard_map/ppermute | solution.py:17
  59.1 2.6 %collective-permute-start.4 = (f32[4,5,3,720]{3,2,1,0:T(4,128)S(1)}, f32[4,5,3,720]{3,2,1,0:T(4,128)S(1)}, u32[]{:S(2)}, u32[]{:S(2)}) collective-permute-start(f32[4,5,3,720]{3,2,1,0:T(4,128)S(1)} %get-tuple-element.35), channel_id=1, source_target_pairs={{4,0},{8,4},{12,8},{16,12},{20,16},{24,20},{28,24},{5,1},{9,5},{13... | collective-permute-start | bytes 518408 | tf_op jit(solution)/shard_map/ppermute | solution.py:17
  61.6 0.2 maximum_maximum_fusion.2
  61.9 0.5 fusion.73
  62.3 0.5 fusion.66
  62.9 4.6 %collective-permute-done.4 = f32[4,5,3,720]{3,2,1,0:T(4,128)S(1)} collective-permute-done((f32[4,5,3,720]{3,2,1,0:T(4,128)S(1)}, f32[4,5,3,720]{3,2,1,0:T(4,128)S(1)}, u32[]{:S(2)}, u32[]{:S(2)}) %collective-permute-start.4) | collective-permute-done | bytes 172832 | tf_op jit(solution)/shard_map/ppermute | solution.py:17
  67.5 0.2 broadcast_select_fusion.2
  67.7 0.2 pad_maximum_fusion.6
  67.9 0.4 fusion.43
  68.3 1.0 %fusion.16 = f32[4,5,9,720]{3,2,1,0:T(8,128)S(1)} fusion(f32[4,5,8,720]{3,2,1,0:T(8,128)S(1)} %bitcast_select_fusion.1, f32[4,5,3,720]{3,2,1,0:T(4,128)S(1)} %get-tuple-element.45, f32[4,5,3,720]{3,2,1,0:T(4,128)S(1)} %get-tuple-element.44, f32[4,5,11,720]{3,2,1,0:T(8,128)S(1)} %fusion.43, f32[9]{0:T(128)S(1)} %or_select_fusion, ...), kind=kLoop, calls=%fused_computation.38 | loop fusion | flops 2980800 | bytes 3216996 | tf_op jit(solution)/shard_map/mul | solution.py:236
  69.3 0.3 fusion.59
  69.5 0.4 multiply_reduce_fusion.1
  70.0 1.9 %fusion.53 = f32[4,80,360]{2,1,0:T(8,128)S(1)} fusion(f32[4,40,720]{2,1,0:T(8,128)S(1)} %neg.14, f32[4,40,720]{2,1,0:T(8,128)S(1)} %get-tuple-element.5, f32[4,720,180]{2,1,0:T(8,128)S(1)} %copy-done.1, f32[4,720,180]{2,1,0:T(8,128)S(1)} %get-tuple-element.54), kind=kOutput, calls=%fused_computation.79 | convolution fusion | flops 498931200 | bytes 5529600 | tf_op jit(solution)/shard_map/dot_general | solution.py:74
  71.9 0.2 fusion.131
  72.1 2.6 %fusion.99 = f32[4,80,720]{2,1,0:T(8,128)S(1)} fusion(f32[4,40,180]{2,1,0:T(8,128)S(1)} %get-tuple-element.28, f32[4,40,180]{2,1,0:T(8,128)S(1)} %get-tuple-element.9, f32[4,40,180]{2,1,0:T(8,128)S(1)} %get-tuple-element.10, f32[4,720,180]{2,1,0:T(8,128)S(1)} %copy-done.1, f32[4,720,180]{2,1,0:T(8,128)S(1)} %get-tuple-element.54), kind=kOutput, calls=%fused_computation.143 | convolution fusion | flops 499046400 | bytes 5414400 | tf_op jit(solution)/shard_map/dot_general | solution.py:83
  74.7 0.4 subtract_reduce_fusion
  75.2 14.8 %all_to_all.10 = f32[4,5,8,720]{3,2,1,0:T(8,128)S(1)} all-to-all(f32[4,5,8,720]{3,2,1,0:T(8,128)S(1)} %bitcast_select_fusion), channel_id=1, replica_groups=mesh['lat'=8,'lon'=4] {'lon'}, dimensions={0} | all-to-all | bytes 921600 | tf_op jit(solution)/shard_map/all_to_all | solution.py:247
  90.0 0.8 copy.46
  (36 shorter events, 1.7 us)
Async XLA Ops:
  0.0 3.6 %copy-start = (s32[64]{0:T(128)S(1)}, s32[64]{0:T(128)}, u32[]{:S(2)}) copy-start(s32[64]{0:T(128)} %param.7) | copy-start | bytes 772
  0.9 5.9 %collective-permute-start = (f32[4,1,720]{2,1,0:T(1,128)S(1)}, f32[4,1,720]{2,1,0:T(1,128)S(1)}, u32[]{:S(2)}, u32[]{:S(2)}) collective-permute-start(f32[4,1,720]{2,1,0:T(1,128)S(1)} %slice.279), channel_id=1, source_target_pairs={{4,0},{8,4},{12,8},{16,12},{20,16},{24,20},{28,24},{5,1},{9,5},{13... | collective-permute-start | bytes 34568 | tf_op jit(solution)/shard_map/ppermute | solution.py:17
  8.7 24.5 %all-to-all-start = ((f32[4,57,720]{2,1,0:T(8,128)}), f32[4,57,720]{2,1,0:T(8,128)}, u32[]{:S(2)}, u32[]{:S(2)}) async-start(f32[4,57,720]{2,1,0:T(8,128)} %pad_maximum_fusion.7), calls=%async_computation | async-start | bytes 1572864 | tf_op jit(solution)/shard_map/all_to_all | solution.py:200
  35.9 8.5 %collective-permute-start.1 = (f32[4,5,3,720]{3,2,1,0:T(4,128)S(1)}, f32[4,5,3,720]{3,2,1,0:T(4,128)S(1)}, u32[]{:S(2)}, u32[]{:S(2)}) collective-permute-start(f32[4,5,3,720]{3,2,1,0:T(4,128)S(1)} %get-tuple-element.41), channel_id=1, source_target_pairs={{0,4},{4,8},{8,12},{12,16},{16,20},{20,24},{24,28},{1,5},{5,9},{9,... | collective-permute-start | bytes 518408 | tf_op jit(solution)/shard_map/ppermute | solution.py:17
  39.4 8.4 %collective-permute-start.2 = (f32[4,5,3,720]{3,2,1,0:T(4,128)S(1)}, f32[4,5,3,720]{3,2,1,0:T(4,128)S(1)}, u32[]{:S(2)}, u32[]{:S(2)}) collective-permute-start(f32[4,5,3,720]{3,2,1,0:T(4,128)S(1)} %get-tuple-element.42), channel_id=1, source_target_pairs={{4,0},{8,4},{12,8},{16,12},{20,16},{24,20},{28,24},{5,1},{9,5},{13... | collective-permute-start | bytes 518408 | tf_op jit(solution)/shard_map/ppermute | solution.py:17
  49.6 2.0 %copy-start.1 = (f32[4,720,180]{2,1,0:T(8,128)S(1)}, f32[4,720,180]{2,1,0:T(8,128)}, u32[]{:S(2)}) copy-start(f32[4,720,180]{2,1,0:T(8,128)} %get-tuple-element.55) | copy-start | bytes 6220804
  57.1 5.8 %collective-permute-start.3 = (f32[4,5,3,720]{3,2,1,0:T(4,128)S(1)}, f32[4,5,3,720]{3,2,1,0:T(4,128)S(1)}, u32[]{:S(2)}, u32[]{:S(2)}) collective-permute-start(f32[4,5,3,720]{3,2,1,0:T(4,128)S(1)} %get-tuple-element.34), channel_id=1, source_target_pairs={{0,4},{4,8},{8,12},{12,16},{16,20},{20,24},{24,28},{1,5},{5,9},{9,... | collective-permute-start | bytes 518408 | tf_op jit(solution)/shard_map/ppermute | solution.py:17
  59.1 8.4 %collective-permute-start.4 = (f32[4,5,3,720]{3,2,1,0:T(4,128)S(1)}, f32[4,5,3,720]{3,2,1,0:T(4,128)S(1)}, u32[]{:S(2)}, u32[]{:S(2)}) collective-permute-start(f32[4,5,3,720]{3,2,1,0:T(4,128)S(1)} %get-tuple-element.35), channel_id=1, source_target_pairs={{4,0},{8,4},{12,8},{16,12},{20,16},{24,20},{28,24},{5,1},{9,5},{13... | collective-permute-start | bytes 518408 | tf_op jit(solution)/shard_map/ppermute | solution.py:17

commit v5 on v4

--- a/solution.py
+++ b/solution.py
@@ -15,6 +15,17 @@
     size = lax.axis_size(axis)
     pairs = [(i, (i + by) % size) for i in range(size) if wrap or 0 <= i + by < size]
     return lax.ppermute(x, axis, pairs)
+
+
+def exchange(x, axis):
+    size = lax.axis_size(axis)
+    me = lax.axis_index(axis)
+    pieces = [lax.dynamic_index_in_dim(x, me, 0, keepdims=False)]
+    for by in range(1, size):
+        part = lax.dynamic_index_in_dim(x, (me + by) % size, 0, keepdims=False)
+        pieces.append(shift(part, axis, by, True))
+    order = (me - jnp.arange(size, dtype=jnp.int32)) % size
+    return jnp.take(jnp.stack(pieces), order, axis=0)
 
 
 def window(values, first_cell, last_cell, dim_at):
@@ -185,22 +196,21 @@
     is_south = lat_index == 0
     is_north = lat_index == lat_devices - 1
 
-    north_cy = shift(courant_y[:, :1], "lat", -1, False)
-    north_cy = jnp.where(is_north, 0.0, north_cy)
     count = tracer_count * lat_rows
     payload = jnp.concatenate(
         [
             jnp.transpose(tracers, (1, 0, 2, 3)).reshape(level_count, count, lon_cols),
             courant_x,
             courant_y,
-            north_cy,
         ],
         axis=1,
     )
-    payload = lax.all_to_all(payload, "lon", 0, 0)
+    payload = exchange(payload, "lon")
     state = payload[:, :count].reshape(lon_devices, tracer_count, lat_rows, lon_cols)
     cx = payload[:, None, count : count + lat_rows]
-    north_courant = payload[:, None, count + lat_rows :]
+    cy = payload[:, None, count + lat_rows :]
+    north_cy = jnp.where(is_north, 0.0, shift(cy[:, :, :1], "lat", -1, False))
+    north_courant = jnp.concatenate([cy, north_cy], axis=2)
     east_courant = jnp.concatenate([jnp.roll(cx[..., lon_cols - 1 :], 1, axis=0), cx], axis=3)
 
     held_global = lat_index * lat_rows + jnp.arange(count, dtype=jnp.int32) % lat_rows
@@ -244,7 +254,7 @@
         rows = filter_rows(rows, basis, roots, weights, polar, 0)
         state = rows.reshape(lon_devices, tracer_count, lat_rows, lon_cols)
 
-    tiles = lax.all_to_all(state, "lon", 0, 0)
+    tiles = exchange(state, "lon")
     return jnp.transpose(tiles, (1, 0, 2, 3))
 
 

time: 91.3 us -> 83 us (0.909)
  blocking collectives: 14.8 us -> 0 us
  starting transfers between devices: 17 us -> 20.7 us
  local copies, waits for them, and re-layouts: 6.38 us -> 8.56 us
  waiting for transfers between devices: 15.8 us -> 17.1 us
    all_to_all x1 -> x0, blocking collectives: 14.8 us -> none  [transposed_path(): tiles = lax.all_to_all(state, 'lon', 0, 0)]
    ppermute x5 -> x11, starting transfers between devices: 12.4 us -> 20.7 us  [shift(): return lax.ppermute(x, axis, pairs)]
    ppermute x5 -> x11, waiting for transfers between devices: 9.25 us -> 17.1 us  [shift(): return lax.ppermute(x, axis, pairs)]
    all_to_all x1 -> x0, waiting for transfers between devices: 6.59 us -> none  [transposed_path(): payload = lax.all_to_all(payload, 'lon', 0, 0)]
    all_to_all x1 -> x0, starting transfers between devices: 4.59 us -> none  [transposed_path(): payload = lax.all_to_all(payload, 'lon', 0, 0)]
    gather x0 -> x2, local copies, waits for them, and re-layouts: none -> 3.1 us  [exchange(): return jnp.take(jnp.stack(pieces), order, axis=0)]
    another operation x0 -> x2, other arithmetic: none -> 1.96 us  [exchange(): return jnp.take(jnp.stack(pieces), order, axis=0)]
    select_n x1 -> x4, other arithmetic: 0.01 us -> 1.34 us  [the longest x3 1.33 us: exchange(): return jnp.take(jnp.stack(pieces), order, axis=0)]
  transfers between devices with their start and end apart: 6 -> 11, of which waited for: 4 -> 5; matrix products, arithmetic and copies ran while one was open for 22% -> 20% of each run, Pallas kernels for 0% -> 0%
where the time goes in v5:
time: 83 us; the launch traced here: 82.6 us
  other arithmetic  26.8 us (32%)
  starting transfers between devices  20.7 us (25%)
  waiting for transfers between devices  17.1 us (21%)
  matrix products  8.93 us (11%)
  local copies, waits for them, and re-layouts  8.56 us (10%)
    ppermute x11, starting transfers between devices, shift(): return lax.ppermute(x, axis, pairs)  20.7 us
    ppermute x11, waiting for transfers between devices, shift(): return lax.ppermute(x, axis, pairs)  17.1 us
    cos x1, other arithmetic, class_basis(): return jnp.concatenate([jnp.cos(angle), jnp.sin(angle)], axis=2)  13.2 us
    dot_general x2, matrix products, filter_rows(): lax.dot_general(spec, basis, (((2,), (2,)), ((0,), (0,))), precision=MATM...  5.11 us
    dot_general x2, matrix products, filter_rows(): lax.dot_general(z, basis, (((2,), (1,)), ((0,), (0,))), precision=MATMUL_...  3.82 us
    gather x2, local copies, waits for them, and re-layouts, exchange(): return jnp.take(jnp.stack(pieces), order, axis=0)  3.1 us
    unnamed x5, local copies, waits for them, and re-layouts  2.27 us
    another operation x2, other arithmetic, exchange(): return jnp.take(jnp.stack(pieces), order, axis=0)  1.96 us
  transfers between devices with their start and end apart: 11, of which 5 were waited for; matrix products, arithmetic and copies ran while one was open for 20% of the time, Pallas kernels for 0%

profile of v5, /device:TPU:3, one launch (start us, length us, event | category | flops | bytes accessed | tf_op | source)
XLA Modules:
  0.0 82.6 jit_solution(15916902709346845713)
XLA Ops:
  0.0 1.1 %copy.44 = f32[5,4,8,720]{3,2,0,1:T(8,128)S(1)} copy(f32[5,4,8,720]{3,2,1,0:T(8,128)} %param.4) | data formatting | bytes 921600 | tf_op args[0]
  1.1 1.0 %pad_maximum_fusion.7 = f32[4,56,720]{2,1,0:T(8,128)S(1)} fusion(f32[4,8,720]{2,1,0:T(8,128)} %param.6, f32[4,8,720]{2,1,0:T(8,128)} %param.5, f32[4,40,720]{2,1,0:T(8,128)S(1)} %bitcast.55), kind=kLoop, calls=%fused_computation.85 | loop fusion | flops 322560 | bytes 1290240 | tf_op jit(solution)/shard_map/concatenate | solution.py:200
  2.1 0.8 constant_dynamic-slice_fusion.1
  2.9 3.3 %collective-permute-start.2 = (f32[56,720]{1,0:T(8,128)}, f32[56,720]{1,0:T(8,128)S(1)}, u32[]{:S(2)}, u32[]{:S(2)}) collective-permute-start(f32[56,720]{1,0:T(8,128)} %get-tuple-element.28), channel_id=1, source_target_pairs={{0,3},{1,0},{2,1},{3,2},{4,7},{5,4},{6,5},{7,6},{8,11},{9,8},{10,9... | collective-permute-start | bytes 483848 | tf_op jit(solution)/shard_map/ppermute | solution.py:17
  6.2 0.5 collective-permute-start
  6.9 0.8 gather_fusion.1
  7.7 13.2 %fusion.5 = (f32[4,720,180]{2,1,0:T(8,128)S(1)}, f32[4,720,180]{2,1,0:T(8,128)}) fusion(s32[4,180]{1,0:T(4,128)S(1)} %iota_add_fusion), kind=kLoop, calls=%fused_computation.11 | loop fusion | flops 4665600 | bytes 4150080 | tf_op jit(solution)/shard_map/cos | solution.py:75
  20.9 0.3 collective-permute-done.1
  21.2 1.9 %pad_maximum_fusion.8 = f32[4,56,720]{2,1,0:T(8,128)} fusion(f32[1,56,720]{2,1,0:T(8,128)S(1)} %bitcast.56, f32[1,56,720]{2,1,0:T(8,128)} %bitcast.5, f32[1,56,720]{2,1,0:T(8,128)} %bitcast.3, f32[1,56,720]{2,1,0:T(8,128)S(1)} %get-tuple-element.27), kind=kLoop, calls=%fused_computation.86 | loop fusion | flops 483840 | bytes 1290240 | tf_op jit(solution)/shard_map/stack | solution.py:28
  23.1 2.5 %gather_fusion = f32[4,56,720]{2,1,0:T(8,128)} fusion(f32[4,56,720]{2,1,0:T(8,128)} %pad_maximum_fusion.8, s32[1024]{0:T(1024)S(1)} %pad_clamp_fusion.1), kind=kCustom, calls=%fused_computation | custom fusion | bytes 1290256 | tf_op jit(solution)/shard_map/jit(_take)/gather | solution.py:28
  25.6 1.2 %broadcast_select_fusion = f32[4,56,720]{2,1,0:T(8,128)S(1)} fusion(f32[4,56,720]{2,1,0:T(8,128)} %gather_fusion, pred[4]{0:T(512)(128)(4,1)S(1)} %compare_and_fusion), kind=kLoop, calls=%fused_computation.161 | loop fusion | flops 161280 | bytes 1290244 | tf_op jit(solution)/shard_map/jit(_take)/select_n | solution.py:28
  27.7 4.3 %collective-permute-start.4 = (f32[4,5,3,720]{3,2,1,0:T(4,128)S(1)}, f32[4,5,3,720]{3,2,1,0:T(4,128)S(1)}, u32[]{:S(2)}, u32[]{:S(2)}) collective-permute-start(f32[4,5,3,720]{3,2,1,0:T(4,128)S(1)} %get-tuple-element.48), channel_id=1, source_target_pairs={{0,4},{4,8},{8,12},{12,16},{16,20},{20,24},{24,28},{1,5},{5,9},{9,... | collective-permute-start | bytes 518408 | tf_op jit(solution)/shard_map/ppermute | solution.py:17
  31.9 1.9 %collective-permute-start.5 = (f32[4,5,3,720]{3,2,1,0:T(4,128)S(1)}, f32[4,5,3,720]{3,2,1,0:T(4,128)S(1)}, u32[]{:S(2)}, u32[]{:S(2)}) collective-permute-start(f32[4,5,3,720]{3,2,1,0:T(4,128)S(1)} %get-tuple-element.49), channel_id=1, source_target_pairs={{4,0},{8,4},{12,8},{16,12},{20,16},{24,20},{28,24},{5,1},{9,5},{13... | collective-permute-start | bytes 518408 | tf_op jit(solution)/shard_map/ppermute | solution.py:17
  33.9 2.5 %collective-permute-start.3 = (f32[4,1,1,720]{3,2,0,1:T(1,128)S(1)}, f32[4,1,1,720]{3,2,0,1:T(1,128)S(1)}, u32[]{:S(2)}, u32[]{:S(2)}) collective-permute-start(f32[4,1,1,720]{3,2,0,1:T(1,128)S(1)} %slice.379), channel_id=1, source_target_pairs={{4,0},{8,4},{12,8},{16,12},{20,16},{24,20},{28,24},{5,1},{9,5},{13... | collective-permute-start | bytes 34568 | tf_op jit(solution)/shard_map/ppermute | solution.py:17
  36.4 0.2 maximum_maximum_fusion
  36.7 0.5 fusion.90
  37.2 0.5 fusion.83
  37.7 2.8 %collective-permute-done.3 = f32[4,1,1,720]{3,2,0,1:T(1,128)S(1)} collective-permute-done((f32[4,1,1,720]{3,2,0,1:T(1,128)S(1)}, f32[4,1,1,720]{3,2,0,1:T(1,128)S(1)}, u32[]{:S(2)}, u32[]{:S(2)}) %collective-permute-start.3) | collective-permute-done | bytes 11552 | tf_op jit(solution)/shard_map/ppermute | solution.py:17
  40.7 0.2 broadcast_select_fusion.5
  41.1 0.4 fusion.46
  41.5 1.0 %fusion.33 = f32[4,5,9,720]{3,2,1,0:T(8,128)S(1)} fusion(f32[4,5,8,720]{3,2,1,0:T(8,128)S(1)} %slice_bitcast_fusion, f32[4,5,3,720]{3,2,1,0:T(4,128)S(1)} %get-tuple-element.56, f32[4,5,3,720]{3,2,1,0:T(4,128)S(1)} %get-tuple-element.55, f32[4,5,11,720]{3,2,1,0:T(8,128)S(1)} %fusion.46, f32[9]{0:T(128)S(1)} %or_select_fusion, ...), kind=kLoop, calls=%fused_computation.57 | loop fusion | flops 2980800 | bytes 3216996 | tf_op jit(solution)/shard_map/mul | solution.py:246
  42.5 0.2 fusion.76
  42.7 0.4 multiply_reduce_fusion.3
  43.2 1.2 %copy-done.1 = f32[4,720,180]{2,1,0:T(8,128)S(1)} copy-done((f32[4,720,180]{2,1,0:T(8,128)S(1)}, f32[4,720,180]{2,1,0:T(8,128)}, u32[]{:S(2)}) %copy-start.1) | copy-done | bytes 2073624
  44.3 1.9 %fusion.49 = f32[4,80,360]{2,1,0:T(8,128)S(1)} fusion(f32[4,40,720]{2,1,0:T(8,128)S(1)} %neg.12, f32[4,40,720]{2,1,0:T(8,128)S(1)} %get-tuple-element.7, f32[4,720,180]{2,1,0:T(8,128)S(1)} %copy-done.1, f32[4,720,180]{2,1,0:T(8,128)S(1)} %get-tuple-element.63), kind=kOutput, calls=%fused_computation.76 | convolution fusion | flops 498931200 | bytes 5529600 | tf_op jit(solution)/shard_map/dot_general | solution.py:85
  46.4 2.6 %fusion.91 = f32[4,80,720]{2,1,0:T(8,128)S(1)} fusion(f32[4,40,180]{2,1,0:T(8,128)S(1)} %get-tuple-element.32, f32[4,40,180]{2,1,0:T(8,128)S(1)} %get-tuple-element.14, f32[4,40,180]{2,1,0:T(8,128)S(1)} %get-tuple-element.15, f32[4,720,180]{2,1,0:T(8,128)S(1)} %copy-done.1, f32[4,720,180]{2,1,0:T(8,128)S(1)} %get-tuple-element.63), kind=kOutput, calls=%fused_computation.135 | convolution fusion | flops 499046400 | bytes 5414400 | tf_op jit(solution)/shard_map/dot_general | solution.py:94
  49.1 0.4 subtract_reduce_fusion.1
  49.8 1.9 %collective-permute-start.6 = (f32[4,5,3,720]{3,2,1,0:T(4,128)S(1)}, f32[4,5,3,720]{3,2,1,0:T(4,128)S(1)}, u32[]{:S(2)}, u32[]{:S(2)}) collective-permute-start(f32[4,5,3,720]{3,2,1,0:T(4,128)S(1)} %get-tuple-element.41), channel_id=1, source_target_pairs={{0,4},{4,8},{8,12},{12,16},{16,20},{20,24},{24,28},{1,5},{5,9},{9,... | collective-permute-start | bytes 518408 | tf_op jit(solution)/shard_map/ppermute | solution.py:17
  51.7 2.6 %collective-permute-start.7 = (f32[4,5,3,720]{3,2,1,0:T(4,128)S(1)}, f32[4,5,3,720]{3,2,1,0:T(4,128)S(1)}, u32[]{:S(2)}, u32[]{:S(2)}) collective-permute-start(f32[4,5,3,720]{3,2,1,0:T(4,128)S(1)} %get-tuple-element.42), channel_id=1, source_target_pairs={{4,0},{8,4},{12,8},{16,12},{20,16},{24,20},{28,24},{5,1},{9,5},{13... | collective-permute-start | bytes 518408 | tf_op jit(solution)/shard_map/ppermute | solution.py:17
  54.3 0.2 maximum_maximum_fusion.2
  54.6 0.5 fusion.73
  55.0 0.5 fusion.66
  55.6 4.6 %collective-permute-done.7 = f32[4,5,3,720]{3,2,1,0:T(4,128)S(1)} collective-permute-done((f32[4,5,3,720]{3,2,1,0:T(4,128)S(1)}, f32[4,5,3,720]{3,2,1,0:T(4,128)S(1)}, u32[]{:S(2)}, u32[]{:S(2)}) %collective-permute-start.7) | collective-permute-done | bytes 172832 | tf_op jit(solution)/shard_map/ppermute | solution.py:17
  60.2 0.2 broadcast_select_fusion.3
  60.6 0.4 fusion.43
  61.0 1.0 %fusion.16 = f32[4,5,9,720]{3,2,1,0:T(8,128)S(1)} fusion(f32[4,5,8,720]{3,2,1,0:T(8,128)S(1)} %bitcast_select_fusion.1, f32[4,5,3,720]{3,2,1,0:T(4,128)S(1)} %get-tuple-element.52, f32[4,5,3,720]{3,2,1,0:T(4,128)S(1)} %get-tuple-element.51, f32[4,5,11,720]{3,2,1,0:T(8,128)S(1)} %fusion.43, f32[9]{0:T(128)S(1)} %or_select_fusion, ...), kind=kLoop, calls=%fused_computation.40 | loop fusion | flops 2980800 | bytes 3216996 | tf_op jit(solution)/shard_map/mul | solution.py:246
  62.0 0.3 fusion.59
  62.2 0.4 multiply_reduce_fusion.1
  62.7 1.9 %fusion.53 = f32[4,80,360]{2,1,0:T(8,128)S(1)} fusion(f32[4,40,720]{2,1,0:T(8,128)S(1)} %neg.14, f32[4,40,720]{2,1,0:T(8,128)S(1)} %get-tuple-element.5, f32[4,720,180]{2,1,0:T(8,128)S(1)} %copy-done.1, f32[4,720,180]{2,1,0:T(8,128)S(1)} %get-tuple-element.63), kind=kOutput, calls=%fused_computation.81 | convolution fusion | flops 498931200 | bytes 5529600 | tf_op jit(solution)/shard_map/dot_general | solution.py:85
  64.8 2.6 %fusion.99 = f32[4,80,720]{2,1,0:T(8,128)S(1)} fusion(f32[4,40,180]{2,1,0:T(8,128)S(1)} %get-tuple-element.31, f32[4,40,180]{2,1,0:T(8,128)S(1)} %get-tuple-element.9, f32[4,40,180]{2,1,0:T(8,128)S(1)} %get-tuple-element.10, f32[4,720,180]{2,1,0:T(8,128)S(1)} %copy-done.1, f32[4,720,180]{2,1,0:T(8,128)S(1)} %get-tuple-element.63), kind=kOutput, calls=%fused_computation.146 | convolution fusion | flops 499046400 | bytes 5414400 | tf_op jit(solution)/shard_map/dot_general | solution.py:94
  67.4 0.4 subtract_reduce_fusion
  67.9 2.6 %collective-permute-start.10 = (f32[5,8,720]{2,1,0:T(8,128)S(1)}, f32[5,8,720]{2,1,0:T(8,128)S(1)}, u32[]{:S(2)}, u32[]{:S(2)}) collective-permute-start(f32[5,8,720]{2,1,0:T(8,128)S(1)} %get-tuple-element.34), channel_id=1, source_target_pairs={{0,3},{1,0},{2,1},{3,2},{4,7},{5,4},{6,5},{7,6},{8,11},{9,8},{10,9... | collective-permute-start | bytes 345608 | tf_op jit(solution)/shard_map/ppermute | solution.py:17
  70.5 0.8 %collective-permute-start.9 = (f32[5,8,720]{2,1,0:T(8,128)S(1)}, f32[5,8,720]{2,1,0:T(8,128)S(1)}, u32[]{:S(2)}, u32[]{:S(2)}) collective-permute-start(f32[5,8,720]{2,1,0:T(8,128)S(1)} %get-tuple-element.35), channel_id=1, source_target_pairs={{0,2},{1,3},{2,0},{3,1},{4,6},{5,7},{6,4},{7,5},{8,10},{9,11},{10,... | collective-permute-start | bytes 345608 | tf_op jit(solution)/shard_map/ppermute | solution.py:17
  71.4 0.2 collective-permute-start.8
  71.6 2.1 %collective-permute-done.10 = f32[5,8,720]{2,1,0:T(8,128)S(1)} collective-permute-done((f32[5,8,720]{2,1,0:T(8,128)S(1)}, f32[5,8,720]{2,1,0:T(8,128)S(1)}, u32[]{:S(2)}, u32[]{:S(2)}) %collective-permute-start.10) | collective-permute-done | bytes 115232 | tf_op jit(solution)/shard_map/ppermute | solution.py:17
  73.7 7.4 %collective-permute-done.9 = f32[5,8,720]{2,1,0:T(8,128)S(1)} collective-permute-done((f32[5,8,720]{2,1,0:T(8,128)S(1)}, f32[5,8,720]{2,1,0:T(8,128)S(1)}, u32[]{:S(2)}, u32[]{:S(2)}) %collective-permute-start.9) | collective-permute-done | bytes 115232 | tf_op jit(solution)/shard_map/ppermute | solution.py:17
  81.1 0.6 gather_fusion.2
  81.8 0.8 copy.42
  (58 shorter events, 2.8 us)
Async XLA Ops:
  0.0 6.9 %copy-start = (s32[64]{0:T(128)S(1)}, s32[64]{0:T(128)}, u32[]{:S(2)}) copy-start(s32[64]{0:T(128)} %param.7) | copy-start | bytes 772
  2.9 18.0 %collective-permute-start.2 = (f32[56,720]{1,0:T(8,128)}, f32[56,720]{1,0:T(8,128)S(1)}, u32[]{:S(2)}, u32[]{:S(2)}) collective-permute-start(f32[56,720]{1,0:T(8,128)} %get-tuple-element.28), channel_id=1, source_target_pairs={{0,3},{1,0},{2,1},{3,2},{4,7},{5,4},{6,5},{7,6},{8,11},{9,8},{10,9... | collective-permute-start | bytes 483848 | tf_op jit(solution)/shard_map/ppermute | solution.py:17
  6.2 15.0 %collective-permute-start.1 = (f32[56,720]{1,0:T(8,128)}, f32[56,720]{1,0:T(8,128)}, u32[]{:S(2)}, u32[]{:S(2)}) collective-permute-start(f32[56,720]{1,0:T(8,128)} %get-tuple-element.29), channel_id=1, source_target_pairs={{0,2},{1,3},{2,0},{3,1},{4,6},{5,7},{6,4},{7,5},{8,10},{9,11},{10,... | collective-permute-start | bytes 483848 | tf_op jit(solution)/shard_map/ppermute | solution.py:17
  6.2 15.0 %collective-permute-start = (f32[56,720]{1,0:T(8,128)S(1)}, f32[56,720]{1,0:T(8,128)}, u32[]{:S(2)}, u32[]{:S(2)}) collective-permute-start(f32[56,720]{1,0:T(8,128)S(1)} %get-tuple-element.30), channel_id=1, source_target_pairs={{0,1},{1,2},{2,3},{3,0},{4,5},{5,6},{6,7},{7,4},{8,9},{9,10},{10,1... | collective-permute-start | bytes 483848 | tf_op jit(solution)/shard_map/ppermute | solution.py:17
  27.7 13.0 %collective-permute-start.4 = (f32[4,5,3,720]{3,2,1,0:T(4,128)S(1)}, f32[4,5,3,720]{3,2,1,0:T(4,128)S(1)}, u32[]{:S(2)}, u32[]{:S(2)}) collective-permute-start(f32[4,5,3,720]{3,2,1,0:T(4,128)S(1)} %get-tuple-element.48), channel_id=1, source_target_pairs={{0,4},{4,8},{8,12},{12,16},{16,20},{20,24},{24,28},{1,5},{5,9},{9,... | collective-permute-start | bytes 518408 | tf_op jit(solution)/shard_map/ppermute | solution.py:17
  31.9 8.7 %collective-permute-start.5 = (f32[4,5,3,720]{3,2,1,0:T(4,128)S(1)}, f32[4,5,3,720]{3,2,1,0:T(4,128)S(1)}, u32[]{:S(2)}, u32[]{:S(2)}) collective-permute-start(f32[4,5,3,720]{3,2,1,0:T(4,128)S(1)} %get-tuple-element.49), channel_id=1, source_target_pairs={{4,0},{8,4},{12,8},{16,12},{20,16},{24,20},{28,24},{5,1},{9,5},{13... | collective-permute-start | bytes 518408 | tf_op jit(solution)/shard_map/ppermute | solution.py:17
  33.9 6.6 %collective-permute-start.3 = (f32[4,1,1,720]{3,2,0,1:T(1,128)S(1)}, f32[4,1,1,720]{3,2,0,1:T(1,128)S(1)}, u32[]{:S(2)}, u32[]{:S(2)}) collective-permute-start(f32[4,1,1,720]{3,2,0,1:T(1,128)S(1)} %slice.379), channel_id=1, source_target_pairs={{4,0},{8,4},{12,8},{16,12},{20,16},{24,20},{28,24},{5,1},{9,5},{13... | collective-permute-start | bytes 34568 | tf_op jit(solution)/shard_map/ppermute | solution.py:17
  42.5 1.8 %copy-start.1 = (f32[4,720,180]{2,1,0:T(8,128)S(1)}, f32[4,720,180]{2,1,0:T(8,128)}, u32[]{:S(2)}) copy-start(f32[4,720,180]{2,1,0:T(8,128)} %get-tuple-element.64) | copy-start | bytes 6220804
  49.8 5.8 %collective-permute-start.6 = (f32[4,5,3,720]{3,2,1,0:T(4,128)S(1)}, f32[4,5,3,720]{3,2,1,0:T(4,128)S(1)}, u32[]{:S(2)}, u32[]{:S(2)}) collective-permute-start(f32[4,5,3,720]{3,2,1,0:T(4,128)S(1)} %get-tuple-element.41), channel_id=1, source_target_pairs={{0,4},{4,8},{8,12},{12,16},{16,20},{20,24},{24,28},{1,5},{5,9},{9,... | collective-permute-start | bytes 518408 | tf_op jit(solution)/shard_map/ppermute | solution.py:17
  51.7 8.4 %collective-permute-start.7 = (f32[4,5,3,720]{3,2,1,0:T(4,128)S(1)}, f32[4,5,3,720]{3,2,1,0:T(4,128)S(1)}, u32[]{:S(2)}, u32[]{:S(2)}) collective-permute-start(f32[4,5,3,720]{3,2,1,0:T(4,128)S(1)} %get-tuple-element.42), channel_id=1, source_target_pairs={{4,0},{8,4},{12,8},{16,12},{20,16},{24,20},{28,24},{5,1},{9,5},{13... | collective-permute-start | bytes 518408 | tf_op jit(solution)/shard_map/ppermute | solution.py:17
  67.9 5.8 %collective-permute-start.10 = (f32[5,8,720]{2,1,0:T(8,128)S(1)}, f32[5,8,720]{2,1,0:T(8,128)S(1)}, u32[]{:S(2)}, u32[]{:S(2)}) collective-permute-start(f32[5,8,720]{2,1,0:T(8,128)S(1)} %get-tuple-element.34), channel_id=1, source_target_pairs={{0,3},{1,0},{2,1},{3,2},{4,7},{5,4},{6,5},{7,6},{8,11},{9,8},{10,9... | collective-permute-start | bytes 345608 | tf_op jit(solution)/shard_map/ppermute | solution.py:17
  70.5 10.5 %collective-permute-start.9 = (f32[5,8,720]{2,1,0:T(8,128)S(1)}, f32[5,8,720]{2,1,0:T(8,128)S(1)}, u32[]{:S(2)}, u32[]{:S(2)}) collective-permute-start(f32[5,8,720]{2,1,0:T(8,128)S(1)} %get-tuple-element.35), channel_id=1, source_target_pairs={{0,2},{1,3},{2,0},{3,1},{4,6},{5,7},{6,4},{7,5},{8,10},{9,11},{10,... | collective-permute-start | bytes 345608 | tf_op jit(solution)/shard_map/ppermute | solution.py:17
  71.4 9.7 %collective-permute-start.8 = (f32[5,8,720]{2,1,0:T(8,128)S(1)}, f32[5,8,720]{2,1,0:T(8,128)S(1)}, u32[]{:S(2)}, u32[]{:S(2)}) collective-permute-start(f32[5,8,720]{2,1,0:T(8,128)S(1)} %get-tuple-element.36), channel_id=1, source_target_pairs={{0,1},{1,2},{2,3},{3,0},{4,5},{5,6},{6,7},{7,4},{8,9},{9,10},{10,1... | collective-permute-start | bytes 345608 | tf_op jit(solution)/shard_map/ppermute | solution.py:17

commit v6 on v5

--- a/solution.py
+++ b/solution.py
@@ -17,15 +17,40 @@
     return lax.ppermute(x, axis, pairs)
 
 
-def exchange(x, axis):
+def gather_arrival(x, axis):
     size = lax.axis_size(axis)
     me = lax.axis_index(axis)
     pieces = [lax.dynamic_index_in_dim(x, me, 0, keepdims=False)]
     for by in range(1, size):
         part = lax.dynamic_index_in_dim(x, (me + by) % size, 0, keepdims=False)
         pieces.append(shift(part, axis, by, True))
+    return jnp.stack(pieces)
+
+
+def scatter_arrival(x, axis):
+    size = lax.axis_size(axis)
+    me = lax.axis_index(axis)
+    pieces = [x[0]] + [shift(x[(size - by) % size], axis, by, True) for by in range(1, size)]
     order = (me - jnp.arange(size, dtype=jnp.int32)) % size
     return jnp.take(jnp.stack(pieces), order, axis=0)
+
+
+def product_basis(tiles, cols, circle):
+    split = max(b for b in range(1, cols + 1) if cols % b == 0 and b * b <= cols)
+    per_class = KMAX // tiles
+    k = tiles * jnp.arange(per_class, dtype=jnp.int32)[None, :] + jnp.arange(
+        tiles, dtype=jnp.int32
+    )[:, None]
+    a = jnp.arange(cols // split, dtype=jnp.int32)
+    b = jnp.arange(split, dtype=jnp.int32)
+    step = 2.0 * math.pi / circle
+    coarse = ((split * a[None, :, None] * k[:, None, :]) % circle).astype(jnp.float32) * step
+    fine = ((b[None, :, None] * k[:, None, :]) % circle).astype(jnp.float32) * step
+    ca, sa = jnp.cos(coarse)[:, :, None], jnp.sin(coarse)[:, :, None]
+    cb, sb = jnp.cos(fine)[:, None], jnp.sin(fine)[:, None]
+    cos_qk = (ca * cb - sa * sb).reshape(tiles, cols, per_class)
+    sin_qk = (sa * cb + ca * sb).reshape(tiles, cols, per_class)
+    return jnp.concatenate([cos_qk, sin_qk], axis=2)
 
 
 def window(values, first_cell, last_cell, dim_at):
@@ -55,9 +80,10 @@
     return courant * jnp.where(courant >= 0.0, from_left, from_right)
 
 
-def root_table(count):
+def root_table(count, tile_of=None):
     d = jnp.arange(count, dtype=jnp.int32)
-    angle = (d[:, None] * d[None, :] % count).astype(jnp.float32) * (2.0 * math.pi / count)
+    tile = d if tile_of is None else tile_of
+    angle = (d[:, None] * tile[None, :] % count).astype(jnp.float32) * (2.0 * math.pi / count)
     cos_dr, sin_dr = jnp.cos(angle), jnp.sin(angle)
     cos_dr = jnp.where(jnp.abs(cos_dr) < 1e-6, 0.0, cos_dr)
     sin_dr = jnp.where(jnp.abs(sin_dr) < 1e-6, 0.0, sin_dr)
@@ -94,7 +120,7 @@
     back = lax.dot_general(spec, basis, (((2,), (2,)), ((0,), (0,))), precision=MATMUL_PRECISION)
     w_re, w_im = back[:, :count], back[:, count:]
     smooth = jnp.sum(
-        cos_dr[:, :, None, None] * w_re[None] - sin_dr[:, :, None, None] * w_im[None], axis=1
+        cos_dr[:, :, None, None] * w_re[:, None] - sin_dr[:, :, None, None] * w_im[:, None], axis=0
     )
     wide = rows
     if halo:
@@ -205,13 +231,13 @@
         ],
         axis=1,
     )
-    payload = exchange(payload, "lon")
+    payload = gather_arrival(payload, "lon")
     state = payload[:, :count].reshape(lon_devices, tracer_count, lat_rows, lon_cols)
     cx = payload[:, None, count : count + lat_rows]
     cy = payload[:, None, count + lat_rows :]
     north_cy = jnp.where(is_north, 0.0, shift(cy[:, :, :1], "lat", -1, False))
     north_courant = jnp.concatenate([cy, north_cy], axis=2)
-    east_courant = jnp.concatenate([jnp.roll(cx[..., lon_cols - 1 :], 1, axis=0), cx], axis=3)
+    east_courant = jnp.concatenate([jnp.roll(cx[..., lon_cols - 1 :], -1, axis=0), cx], axis=3)
 
     held_global = lat_index * lat_rows + jnp.arange(count, dtype=jnp.int32) % lat_rows
     polar = (held_global < total_rows // 4) | (held_global >= total_rows - total_rows // 4)
@@ -222,8 +248,10 @@
     )[:, None]
     scale = jnp.where(k == 0, 1.0 / circle, 2.0 / circle).astype(jnp.float32)
     weights = jnp.where(k[:, None, :] < cut[None, :, None], scale[:, None, :], 0.0)
-    basis = class_basis(lon_devices, lon_cols, circle, 0)
-    roots = root_table(lon_devices)
+    basis = product_basis(lon_devices, lon_cols, circle)
+    roots = root_table(
+        lon_devices, (lax.axis_index("lon") - jnp.arange(lon_devices, dtype=jnp.int32)) % lon_devices
+    )
 
     for substep in range(SUBSTEPS):
         south_in = shift(state[:, :, lat_rows - HALO :], "lat", 1, False)
@@ -236,9 +264,9 @@
         extended = jnp.concatenate([south_rows, state, north_rows], axis=2)
         wrapped = jnp.concatenate(
             [
-                jnp.roll(state[..., lon_cols - HALO :], 1, axis=0),
+                jnp.roll(state[..., lon_cols - HALO :], -1, axis=0),
                 state,
-                jnp.roll(state[..., :HALO], -1, axis=0),
+                jnp.roll(state[..., :HALO], 1, axis=0),
             ],
             axis=3,
         )
@@ -254,7 +282,7 @@
         rows = filter_rows(rows, basis, roots, weights, polar, 0)
         state = rows.reshape(lon_devices, tracer_count, lat_rows, lon_cols)
 
-    tiles = exchange(state, "lon")
+    tiles = scatter_arrival(state, "lon")
     return jnp.transpose(tiles, (1, 0, 2, 3))
 
 

time: 83 us -> 77.8 us (0.937)
  other arithmetic: 26.8 us -> 15.5 us
  waiting for transfers between devices: 17.1 us -> 25.4 us
  local copies, waits for them, and re-layouts: 8.56 us -> 6 us
    cos x1 -> x2, other arithmetic: 13.2 us -> 1.05 us  [the longest x1 0.62 us: product_basis(): ca, sa = (jnp.cos(coarse)[:, :, None], jnp.sin(coarse)[:, :, None])]
    ppermute x11, waiting for transfers between devices: 17.1 us -> 25.4 us  [shift(): return lax.ppermute(x, axis, pairs)]
    gather x2 -> x1, local copies, waits for them, and re-layouts: 3.1 us -> 0.58 us  [scatter_arrival(): return jnp.take(jnp.stack(pieces), order, axis=0)]
    sub x0 -> x1, other arithmetic: none -> 2.18 us  [product_basis(): cos_qk = (ca * cb - sa * sb).reshape(tiles, cols, per_class)]
    select_n x3, other arithmetic: 1.33 us -> 0.13 us  [the longest x2 0.12 us: scatter_arrival(): return jnp.take(jnp.stack(pieces), order, axis=0)]
    another operation x2, other arithmetic: 1.96 us -> 1.03 us  [the longest x1 0.98 us: gather_arrival(): return jnp.stack(pieces)]
  transfers between devices with their start and end apart: 11 -> 11, of which waited for: 5 -> 5; matrix products, arithmetic and copies ran while one was open for 20% -> 9% of each run, Pallas kernels for 0% -> 0%
where the time goes in v6:
time: 77.8 us; the launch traced here: 77.1 us
  waiting for transfers between devices  25.4 us (33%)
  starting transfers between devices  20.8 us (27%)
  other arithmetic  15.5 us (20%)
  matrix products  8.97 us (12%)
  local copies, waits for them, and re-layouts  6 us (8%)
    ppermute x11, waiting for transfers between devices, shift(): return lax.ppermute(x, axis, pairs)  25.4 us
    ppermute x11, starting transfers between devices, shift(): return lax.ppermute(x, axis, pairs)  20.8 us
    dot_general x2, matrix products, filter_rows(): lax.dot_general(spec, basis, (((2,), (2,)), ((0,), (0,))), precision=MATM...  5.18 us
    dot_general x2, matrix products, filter_rows(): lax.dot_general(z, basis, (((2,), (1,)), ((0,), (0,))), precision=MATMUL_...  3.8 us
    unnamed x5, local copies, waits for them, and re-layouts  2.27 us
    sub x1, other arithmetic, product_basis(): cos_qk = (ca * cb - sa * sb).reshape(tiles, cols, per_class)  2.18 us
    mul x2, other arithmetic, transposed_path(): ppm_flux(extended, north_courant, 2, lat_rows) * face_weight[:, None]  1.95 us
    sub x4, other arithmetic, ppm_flux(): 7.0 / 12.0  1.8 us
  transfers between devices with their start and end apart: 11, of which 5 were waited for; matrix products, arithmetic and copies ran while one was open for 9% of the time, Pallas kernels for 0%

profile of v6, /device:TPU:3, one launch (start us, length us, event | category | flops | bytes accessed | tf_op | source)
XLA Modules:
  0.0 77.1 jit_solution(4044840781385927880)
XLA Ops:
  0.0 1.1 %copy.46 = f32[5,4,8,720]{3,2,0,1:T(8,128)S(1)} copy(f32[5,4,8,720]{3,2,1,0:T(8,128)} %param.4) | data formatting | bytes 921600 | tf_op args[0]
  1.1 1.0 %pad_maximum_fusion.7 = f32[4,56,720]{2,1,0:T(8,128)S(1)} fusion(f32[4,8,720]{2,1,0:T(8,128)} %param.6, f32[4,8,720]{2,1,0:T(8,128)} %param.5, f32[4,40,720]{2,1,0:T(8,128)S(1)} %bitcast.63), kind=kLoop, calls=%fused_computation.77 | loop fusion | flops 322560 | bytes 1290240 | tf_op jit(solution)/shard_map/concatenate | solution.py:226
  2.1 0.8 %constant_dynamic-slice_fusion = (f32[1,56,720]{2,1,0:T(8,128)S(1)}, f32[56,720]{1,0:T(8,128)}, f32[56,720]{1,0:T(8,128)}, f32[56,720]{1,0:T(8,128)}) fusion(f32[4,56,720]{2,1,0:T(8,128)S(1)} %pad_maximum_fusion.7, s32[]{:T(128)S(6)} %select_n.274, s32[]{:T(128)S(6)} %select_n.280, s32[]{:T(128)S(6)} %select_n.278, s32[]{:T(128)S(6)} %select_n.276), kind=kLoop, calls=%fused_computation.259 | loop fusion | bytes 1290256 | tf_op jit(solution)/shard_map/jit(dynamic_index_in_dim)/dynamic_slice | solution.py:23
  2.9 3.3 %collective-permute-start.2 = (f32[56,720]{1,0:T(8,128)}, f32[56,720]{1,0:T(8,128)S(1)}, u32[]{:S(2)}, u32[]{:S(2)}) collective-permute-start(f32[56,720]{1,0:T(8,128)} %get-tuple-element.26), channel_id=1, source_target_pairs={{0,3},{1,0},{2,1},{3,2},{4,7},{5,4},{6,5},{7,6},{8,11},{9,8},{10,9... | collective-permute-start | bytes 483848 | tf_op jit(solution)/shard_map/ppermute | solution.py:17
  6.2 0.5 collective-permute-start
  6.9 0.8 %gather_fusion = s32[40]{0:T(128)S(1)} fusion(s32[64]{0:T(128)S(1)} %copy-done, s32[1024]{0:T(1024)S(1)} %pad_clamp_fusion.1), kind=kCustom, calls=%fused_computation | custom fusion | bytes 480 | tf_op jit(solution)/shard_map/jit(_take)/gather | solution.py:244
  7.7 0.4 fusion.121
  8.1 0.6 fusion.114
  8.8 2.2 %multiply_subtract_fusion = (f32[4,30,24,180]{3,2,1,0:T(8,128)S(1)}, f32[4,30,24,180]{3,2,1,0:T(8,128)}) fusion(f32[4,24,180]{2,1,0:T(8,128)S(1)} %get-tuple-element.66, f32[4,30,180]{2,1,0:T(8,128)S(1)} %get-tuple-element.64, f32[4,24,180]{2,1,0:T(8,128)S(1)} %get-tuple-element.65, f32[4,30,180]{2,1,0:T(8,128)S(1)} %get-tuple-element.63), kind=kLoop, calls=%fused_computation.4 | loop fusion | flops 3110400 | bytes 4458240 | tf_op jit(solution)/shard_map/sub | solution.py:51
  11.0 10.1 %collective-permute-done.1 = f32[56,720]{1,0:T(8,128)S(1)} collective-permute-done((f32[56,720]{1,0:T(8,128)}, f32[56,720]{1,0:T(8,128)S(1)}, u32[]{:S(2)}, u32[]{:S(2)}) %collective-permute-start.1) | collective-permute-done | bytes 161312 | tf_op jit(solution)/shard_map/ppermute | solution.py:17
  21.1 1.0 %pad_maximum_fusion.8 = f32[4,56,720]{2,1,0:T(8,128)S(1)} fusion(f32[1,56,720]{2,1,0:T(8,128)S(1)} %bitcast.69, f32[1,56,720]{2,1,0:T(8,128)S(1)} %bitcast.71, f32[1,56,720]{2,1,0:T(8,128)} %bitcast.3, f32[1,56,720]{2,1,0:T(8,128)S(1)} %get-tuple-element.25), kind=kLoop, calls=%fused_computation.78 | loop fusion | flops 483840 | bytes 1290240 | tf_op jit(solution)/shard_map/stack | solution.py:27
  22.1 0.8 %pad_maximum_fusion.18 = (f32[4,8,720]{2,1,0:T(8,128)S(1)}, f32[4,8,720]{2,1,0:T(8,128)S(1)}) fusion(f32[1,56,720]{2,1,0:T(8,128)S(1)} %bitcast.70, f32[1,56,720]{2,1,0:T(8,128)S(1)} %bitcast.72, f32[1,56,720]{2,1,0:T(8,128)} %bitcast.3, f32[1,56,720]{2,1,0:T(8,128)S(1)} %get-tuple-element.25), kind=kLoop, calls=%fused_computation.205 | loop fusion | flops 138240 | bytes 829440 | tf_op jit(solution)/shard_map/slice | solution.py:236
  23.6 3.9 %collective-permute-start.4 = (f32[4,5,3,720]{3,2,1,0:T(4,128)S(1)}, f32[4,5,3,720]{3,2,1,0:T(4,128)S(1)}, u32[]{:S(2)}, u32[]{:S(2)}) collective-permute-start(f32[4,5,3,720]{3,2,1,0:T(4,128)S(1)} %get-tuple-element.46), channel_id=1, source_target_pairs={{0,4},{4,8},{8,12},{12,16},{16,20},{20,24},{24,28},{1,5},{5,9},{9,... | collective-permute-start | bytes 518408 | tf_op jit(solution)/shard_map/ppermute | solution.py:17
  27.5 1.9 %collective-permute-start.5 = (f32[4,5,3,720]{3,2,1,0:T(4,128)S(1)}, f32[4,5,3,720]{3,2,1,0:T(4,128)S(1)}, u32[]{:S(2)}, u32[]{:S(2)}) collective-permute-start(f32[4,5,3,720]{3,2,1,0:T(4,128)S(1)} %get-tuple-element.47), channel_id=1, source_target_pairs={{4,0},{8,4},{12,8},{16,12},{20,16},{24,20},{28,24},{5,1},{9,5},{13... | collective-permute-start | bytes 518408 | tf_op jit(solution)/shard_map/ppermute | solution.py:17
  29.5 2.5 %collective-permute-start.3 = (f32[4,1,1,720]{3,2,0,1:T(1,128)S(1)}, f32[4,1,1,720]{3,2,0,1:T(1,128)S(1)}, u32[]{:S(2)}, u32[]{:S(2)}) collective-permute-start(f32[4,1,1,720]{3,2,0,1:T(1,128)S(1)} %slice.398), channel_id=1, source_target_pairs={{4,0},{8,4},{12,8},{16,12},{20,16},{24,20},{28,24},{5,1},{9,5},{13... | collective-permute-start | bytes 34568 | tf_op jit(solution)/shard_map/ppermute | solution.py:17
  32.0 0.2 maximum_maximum_fusion
  32.2 0.5 fusion.84
  32.7 0.5 fusion.77
  33.3 2.8 %collective-permute-done.3 = f32[4,1,1,720]{3,2,0,1:T(1,128)S(1)} collective-permute-done((f32[4,1,1,720]{3,2,0,1:T(1,128)S(1)}, f32[4,1,1,720]{3,2,0,1:T(1,128)S(1)}, u32[]{:S(2)}, u32[]{:S(2)}) %collective-permute-start.3) | collective-permute-done | bytes 11552 | tf_op jit(solution)/shard_map/ppermute | solution.py:17
  36.2 0.2 broadcast_select_fusion.5
  36.7 0.4 fusion.39
  37.1 1.0 %fusion.26 = f32[4,5,9,720]{3,2,1,0:T(8,128)S(1)} fusion(f32[4,5,8,720]{3,2,1,0:T(8,128)S(1)} %slice_bitcast_fusion, f32[4,5,3,720]{3,2,1,0:T(4,128)S(1)} %get-tuple-element.56, f32[4,5,3,720]{3,2,1,0:T(4,128)S(1)} %get-tuple-element.55, f32[4,5,11,720]{3,2,1,0:T(8,128)S(1)} %fusion.39, f32[9]{0:T(128)S(1)} %or_select_fusion, ...), kind=kLoop, calls=%fused_computation.49 | loop fusion | flops 2980800 | bytes 3216996 | tf_op jit(solution)/shard_map/mul | solution.py:274
  38.3 0.4 multiply_reduce_fusion.3
  38.7 1.2 %copy-done.1 = f32[4,30,24,180]{3,2,1,0:T(8,128)S(1)} copy-done((f32[4,30,24,180]{3,2,1,0:T(8,128)S(1)}, f32[4,30,24,180]{3,2,1,0:T(8,128)}, u32[]{:S(2)}) %copy-start.1) | copy-done | bytes 2073624
  39.9 1.9 %fusion.42 = f32[4,80,360]{2,1,0:T(8,128)S(1)} fusion(f32[4,40,720]{2,1,0:T(8,128)S(1)} %neg.12, f32[4,40,720]{2,1,0:T(8,128)S(1)} %get-tuple-element.7, f32[4,720,180]{2,1,0:T(8,128)S(1)} %bitcast.58, f32[4,720,180]{2,1,0:T(8,128)S(1)} %bitcast.54), kind=kOutput, calls=%fused_computation.68 | convolution fusion | flops 498931200 | bytes 5529600 | tf_op jit(solution)/shard_map/dot_general | solution.py:111
  42.0 2.6 %fusion.85 = f32[4,80,720]{2,1,0:T(8,128)S(1)} fusion(f32[4,40,180]{2,1,0:T(8,128)S(1)} %get-tuple-element.30, f32[4,40,180]{2,1,0:T(8,128)S(1)} %get-tuple-element.14, f32[4,40,180]{2,1,0:T(8,128)S(1)} %get-tuple-element.15, f32[4,720,180]{2,1,0:T(8,128)S(1)} %bitcast.59, f32[4,720,180]{2,1,0:T(8,128)S(1)} %bitcast.55), kind=kOutput, calls=%fused_computation.128 | convolution fusion | flops 499046400 | bytes 5414400 | tf_op jit(solution)/shard_map/dot_general | solution.py:120
  44.6 0.3 subtract_reduce_fusion.1
  45.4 1.9 %collective-permute-start.6 = (f32[4,5,3,720]{3,2,1,0:T(4,128)S(1)}, f32[4,5,3,720]{3,2,1,0:T(4,128)S(1)}, u32[]{:S(2)}, u32[]{:S(2)}) collective-permute-start(f32[4,5,3,720]{3,2,1,0:T(4,128)S(1)} %get-tuple-element.39), channel_id=1, source_target_pairs={{0,4},{4,8},{8,12},{12,16},{16,20},{20,24},{24,28},{1,5},{5,9},{9,... | collective-permute-start | bytes 518408 | tf_op jit(solution)/shard_map/ppermute | solution.py:17
  47.3 2.6 %collective-permute-start.7 = (f32[4,5,3,720]{3,2,1,0:T(4,128)S(1)}, f32[4,5,3,720]{3,2,1,0:T(4,128)S(1)}, u32[]{:S(2)}, u32[]{:S(2)}) collective-permute-start(f32[4,5,3,720]{3,2,1,0:T(4,128)S(1)} %get-tuple-element.40), channel_id=1, source_target_pairs={{4,0},{8,4},{12,8},{16,12},{20,16},{24,20},{28,24},{5,1},{9,5},{13... | collective-permute-start | bytes 518408 | tf_op jit(solution)/shard_map/ppermute | solution.py:17
  49.9 0.2 maximum_maximum_fusion.2
  50.1 0.5 fusion.67
  50.6 0.5 fusion.60
  51.1 4.6 %collective-permute-done.7 = f32[4,5,3,720]{3,2,1,0:T(4,128)S(1)} collective-permute-done((f32[4,5,3,720]{3,2,1,0:T(4,128)S(1)}, f32[4,5,3,720]{3,2,1,0:T(4,128)S(1)}, u32[]{:S(2)}, u32[]{:S(2)}) %collective-permute-start.7) | collective-permute-done | bytes 172832 | tf_op jit(solution)/shard_map/ppermute | solution.py:17
  55.7 0.2 broadcast_select_fusion.3
  56.1 0.4 fusion.36
  56.6 1.0 %fusion.9 = f32[4,5,9,720]{3,2,1,0:T(8,128)S(1)} fusion(f32[4,5,8,720]{3,2,1,0:T(8,128)S(1)} %bitcast_select_fusion, f32[4,5,3,720]{3,2,1,0:T(4,128)S(1)} %get-tuple-element.52, f32[4,5,3,720]{3,2,1,0:T(4,128)S(1)} %get-tuple-element.51, f32[4,5,11,720]{3,2,1,0:T(8,128)S(1)} %fusion.36, f32[9]{0:T(128)S(1)} %or_select_fusion, ...), kind=kLoop, calls=%fused_computation.32 | loop fusion | flops 2980800 | bytes 3216996 | tf_op jit(solution)/shard_map/mul | solution.py:274
  57.5 0.3 fusion.53
  57.8 0.4 multiply_reduce_fusion.1
  58.2 1.9 %fusion.46 = f32[4,80,360]{2,1,0:T(8,128)S(1)} fusion(f32[4,40,720]{2,1,0:T(8,128)S(1)} %neg.14, f32[4,40,720]{2,1,0:T(8,128)S(1)} %get-tuple-element.5, f32[4,720,180]{2,1,0:T(8,128)S(1)} %bitcast.60, f32[4,720,180]{2,1,0:T(8,128)S(1)} %bitcast.56), kind=kOutput, calls=%fused_computation.73 | convolution fusion | flops 498931200 | bytes 5529600 | tf_op jit(solution)/shard_map/dot_general | solution.py:111
  60.3 2.6 %fusion.93 = f32[4,80,720]{2,1,0:T(8,128)S(1)} fusion(f32[4,40,180]{2,1,0:T(8,128)S(1)} %get-tuple-element.29, f32[4,40,180]{2,1,0:T(8,128)S(1)} %get-tuple-element.9, f32[4,40,180]{2,1,0:T(8,128)S(1)} %get-tuple-element.10, f32[4,720,180]{2,1,0:T(8,128)S(1)} %bitcast.61, f32[4,720,180]{2,1,0:T(8,128)S(1)} %bitcast.57), kind=kOutput, calls=%fused_computation.139 | convolution fusion | flops 499046400 | bytes 5414400 | tf_op jit(solution)/shard_map/dot_general | solution.py:120
  63.0 0.3 subtract_reduce_fusion
  63.5 0.6 collective-permute-start.10
  64.1 2.1 %collective-permute-start.9 = (f32[5,8,720]{2,1,0:T(8,128)S(1)}, f32[5,8,720]{2,1,0:T(8,128)S(1)}, u32[]{:S(2)}, u32[]{:S(2)}) collective-permute-start(f32[5,8,720]{2,1,0:T(8,128)S(1)} %get-tuple-element.33), channel_id=1, source_target_pairs={{0,2},{1,3},{2,0},{3,1},{4,6},{5,7},{6,4},{7,5},{8,10},{9,11},{10,... | collective-permute-start | bytes 345608 | tf_op jit(solution)/shard_map/ppermute | solution.py:17
  66.3 1.4 %collective-permute-start.8 = (f32[5,8,720]{2,1,0:T(8,128)S(1)}, f32[5,8,720]{2,1,0:T(8,128)S(1)}, u32[]{:S(2)}, u32[]{:S(2)}) collective-permute-start(f32[5,8,720]{2,1,0:T(8,128)S(1)} %get-tuple-element.34), channel_id=1, source_target_pairs={{0,1},{1,2},{2,3},{3,0},{4,5},{5,6},{6,7},{7,4},{8,9},{9,10},{10,1... | collective-permute-start | bytes 345608 | tf_op jit(solution)/shard_map/ppermute | solution.py:17
  67.7 1.1 %collective-permute-done.10 = f32[5,8,720]{2,1,0:T(8,128)S(1)} collective-permute-done((f32[5,8,720]{2,1,0:T(8,128)S(1)}, f32[5,8,720]{2,1,0:T(8,128)S(1)}, u32[]{:S(2)}, u32[]{:S(2)}) %collective-permute-start.10) | collective-permute-done | bytes 115232 | tf_op jit(solution)/shard_map/ppermute | solution.py:17
  68.7 6.8 %collective-permute-done.9 = f32[5,8,720]{2,1,0:T(8,128)S(1)} collective-permute-done((f32[5,8,720]{2,1,0:T(8,128)S(1)}, f32[5,8,720]{2,1,0:T(8,128)S(1)}, u32[]{:S(2)}, u32[]{:S(2)}) %collective-permute-start.9) | collective-permute-done | bytes 115232 | tf_op jit(solution)/shard_map/ppermute | solution.py:17
  75.6 0.6 gather_fusion.1
  76.3 0.8 %copy.44 = f32[5,4,8,720]{3,2,1,0:T(8,128)} copy(f32[5,4,8,720]{3,2,0,1:T(8,128)S(1)} %select_bitcast_fusion) | data formatting | bytes 921600 | tf_op jit(solution)/shard_map/jit(_take)/select_n | solution.py:35
  (61 shorter events, 3.0 us)
Async XLA Ops:
  0.0 6.9 %copy-start = (s32[64]{0:T(128)S(1)}, s32[64]{0:T(128)}, u32[]{:S(2)}) copy-start(s32[64]{0:T(128)} %param.7) | copy-start | bytes 772
  2.9 8.1 %collective-permute-start.2 = (f32[56,720]{1,0:T(8,128)}, f32[56,720]{1,0:T(8,128)S(1)}, u32[]{:S(2)}, u32[]{:S(2)}) collective-permute-start(f32[56,720]{1,0:T(8,128)} %get-tuple-element.26), channel_id=1, source_target_pairs={{0,3},{1,0},{2,1},{3,2},{4,7},{5,4},{6,5},{7,6},{8,11},{9,8},{10,9... | collective-permute-start | bytes 483848 | tf_op jit(solution)/shard_map/ppermute | solution.py:17
  6.2 14.9 %collective-permute-start.1 = (f32[56,720]{1,0:T(8,128)}, f32[56,720]{1,0:T(8,128)S(1)}, u32[]{:S(2)}, u32[]{:S(2)}) collective-permute-start(f32[56,720]{1,0:T(8,128)} %get-tuple-element.27), channel_id=1, source_target_pairs={{0,2},{1,3},{2,0},{3,1},{4,6},{5,7},{6,4},{7,5},{8,10},{9,11},{10,... | collective-permute-start | bytes 483848 | tf_op jit(solution)/shard_map/ppermute | solution.py:17
  6.2 14.9 %collective-permute-start = (f32[56,720]{1,0:T(8,128)}, f32[56,720]{1,0:T(8,128)}, u32[]{:S(2)}, u32[]{:S(2)}) collective-permute-start(f32[56,720]{1,0:T(8,128)} %get-tuple-element.28), channel_id=1, source_target_pairs={{0,1},{1,2},{2,3},{3,0},{4,5},{5,6},{6,7},{7,4},{8,9},{9,10},{10,1... | collective-permute-start | bytes 483848 | tf_op jit(solution)/shard_map/ppermute | solution.py:17
  23.6 12.6 %collective-permute-start.4 = (f32[4,5,3,720]{3,2,1,0:T(4,128)S(1)}, f32[4,5,3,720]{3,2,1,0:T(4,128)S(1)}, u32[]{:S(2)}, u32[]{:S(2)}) collective-permute-start(f32[4,5,3,720]{3,2,1,0:T(4,128)S(1)} %get-tuple-element.46), channel_id=1, source_target_pairs={{0,4},{4,8},{8,12},{12,16},{16,20},{20,24},{24,28},{1,5},{5,9},{9,... | collective-permute-start | bytes 518408 | tf_op jit(solution)/shard_map/ppermute | solution.py:17
  27.5 8.7 %collective-permute-start.5 = (f32[4,5,3,720]{3,2,1,0:T(4,128)S(1)}, f32[4,5,3,720]{3,2,1,0:T(4,128)S(1)}, u32[]{:S(2)}, u32[]{:S(2)}) collective-permute-start(f32[4,5,3,720]{3,2,1,0:T(4,128)S(1)} %get-tuple-element.47), channel_id=1, source_target_pairs={{4,0},{8,4},{12,8},{16,12},{20,16},{24,20},{28,24},{5,1},{9,5},{13... | collective-permute-start | bytes 518408 | tf_op jit(solution)/shard_map/ppermute | solution.py:17
  29.5 6.6 %collective-permute-start.3 = (f32[4,1,1,720]{3,2,0,1:T(1,128)S(1)}, f32[4,1,1,720]{3,2,0,1:T(1,128)S(1)}, u32[]{:S(2)}, u32[]{:S(2)}) collective-permute-start(f32[4,1,1,720]{3,2,0,1:T(1,128)S(1)} %slice.398), channel_id=1, source_target_pairs={{4,0},{8,4},{12,8},{16,12},{20,16},{24,20},{28,24},{5,1},{9,5},{13... | collective-permute-start | bytes 34568 | tf_op jit(solution)/shard_map/ppermute | solution.py:17
  38.1 1.8 %copy-start.1 = (f32[4,30,24,180]{3,2,1,0:T(8,128)S(1)}, f32[4,30,24,180]{3,2,1,0:T(8,128)}, u32[]{:S(2)}) copy-start(f32[4,30,24,180]{3,2,1,0:T(8,128)} %get-tuple-element.50) | copy-start | bytes 6220804
  45.4 5.8 %collective-permute-start.6 = (f32[4,5,3,720]{3,2,1,0:T(4,128)S(1)}, f32[4,5,3,720]{3,2,1,0:T(4,128)S(1)}, u32[]{:S(2)}, u32[]{:S(2)}) collective-permute-start(f32[4,5,3,720]{3,2,1,0:T(4,128)S(1)} %get-tuple-element.39), channel_id=1, source_target_pairs={{0,4},{4,8},{8,12},{12,16},{16,20},{20,24},{24,28},{1,5},{5,9},{9,... | collective-permute-start | bytes 518408 | tf_op jit(solution)/shard_map/ppermute | solution.py:17
  47.3 8.4 %collective-permute-start.7 = (f32[4,5,3,720]{3,2,1,0:T(4,128)S(1)}, f32[4,5,3,720]{3,2,1,0:T(4,128)S(1)}, u32[]{:S(2)}, u32[]{:S(2)}) collective-permute-start(f32[4,5,3,720]{3,2,1,0:T(4,128)S(1)} %get-tuple-element.40), channel_id=1, source_target_pairs={{4,0},{8,4},{12,8},{16,12},{20,16},{24,20},{28,24},{5,1},{9,5},{13... | collective-permute-start | bytes 518408 | tf_op jit(solution)/shard_map/ppermute | solution.py:17
  63.5 5.2 %collective-permute-start.10 = (f32[5,8,720]{2,1,0:T(8,128)S(1)}, f32[5,8,720]{2,1,0:T(8,128)S(1)}, u32[]{:S(2)}, u32[]{:S(2)}) collective-permute-start(f32[5,8,720]{2,1,0:T(8,128)S(1)} %get-tuple-element.32), channel_id=1, source_target_pairs={{0,3},{1,0},{2,1},{3,2},{4,7},{5,4},{6,5},{7,6},{8,11},{9,8},{10,9... | collective-permute-start | bytes 345608 | tf_op jit(solution)/shard_map/ppermute | solution.py:17
  64.1 11.5 %collective-permute-start.9 = (f32[5,8,720]{2,1,0:T(8,128)S(1)}, f32[5,8,720]{2,1,0:T(8,128)S(1)}, u32[]{:S(2)}, u32[]{:S(2)}) collective-permute-start(f32[5,8,720]{2,1,0:T(8,128)S(1)} %get-tuple-element.33), channel_id=1, source_target_pairs={{0,2},{1,3},{2,0},{3,1},{4,6},{5,7},{6,4},{7,5},{8,10},{9,11},{10,... | collective-permute-start | bytes 345608 | tf_op jit(solution)/shard_map/ppermute | solution.py:17
  66.3 9.3 %collective-permute-start.8 = (f32[5,8,720]{2,1,0:T(8,128)S(1)}, f32[5,8,720]{2,1,0:T(8,128)S(1)}, u32[]{:S(2)}, u32[]{:S(2)}) collective-permute-start(f32[5,8,720]{2,1,0:T(8,128)S(1)} %get-tuple-element.34), channel_id=1, source_target_pairs={{0,1},{1,2},{2,3},{3,0},{4,5},{5,6},{6,7},{7,4},{8,9},{9,10},{10,1... | collective-permute-start | bytes 345608 | tf_op jit(solution)/shard_map/ppermute | solution.py:17

commit v7 on v6

--- a/solution.py
+++ b/solution.py
@@ -15,24 +15,6 @@
     size = lax.axis_size(axis)
     pairs = [(i, (i + by) % size) for i in range(size) if wrap or 0 <= i + by < size]
     return lax.ppermute(x, axis, pairs)
-
-
-def gather_arrival(x, axis):
-    size = lax.axis_size(axis)
-    me = lax.axis_index(axis)
-    pieces = [lax.dynamic_index_in_dim(x, me, 0, keepdims=False)]
-    for by in range(1, size):
-        part = lax.dynamic_index_in_dim(x, (me + by) % size, 0, keepdims=False)
-        pieces.append(shift(part, axis, by, True))
-    return jnp.stack(pieces)
-
-
-def scatter_arrival(x, axis):
-    size = lax.axis_size(axis)
-    me = lax.axis_index(axis)
-    pieces = [x[0]] + [shift(x[(size - by) % size], axis, by, True) for by in range(1, size)]
-    order = (me - jnp.arange(size, dtype=jnp.int32)) % size
-    return jnp.take(jnp.stack(pieces), order, axis=0)
 
 
 def product_basis(tiles, cols, circle):
@@ -223,20 +205,25 @@
     is_north = lat_index == lat_devices - 1
 
     count = tracer_count * lat_rows
-    payload = jnp.concatenate(
-        [
-            jnp.transpose(tracers, (1, 0, 2, 3)).reshape(level_count, count, lon_cols),
-            courant_x,
-            courant_y,
-        ],
-        axis=1,
-    )
-    payload = gather_arrival(payload, "lon")
+    lon_index = lax.axis_index("lon")
+
+    def payload_for(level):
+        return jnp.concatenate(
+            [
+                lax.dynamic_index_in_dim(tracers, level, 1, keepdims=False).reshape(count, lon_cols),
+                lax.dynamic_index_in_dim(courant_x, level, 0, keepdims=False),
+                lax.dynamic_index_in_dim(courant_y, level, 0, keepdims=False),
+            ],
+            axis=0,
+        )
+
+    pieces = [payload_for(lon_index)]
+    for by in range(1, lon_devices):
+        pieces.append(shift(payload_for((lon_index + by) % lon_devices), "lon", by, True))
+    payload = jnp.stack(pieces)
     state = payload[:, :count].reshape(lon_devices, tracer_count, lat_rows, lon_cols)
     cx = payload[:, None, count : count + lat_rows]
     cy = payload[:, None, count + lat_rows :]
-    north_cy = jnp.where(is_north, 0.0, shift(cy[:, :, :1], "lat", -1, False))
-    north_courant = jnp.concatenate([cy, north_cy], axis=2)
     east_courant = jnp.concatenate([jnp.roll(cx[..., lon_cols - 1 :], -1, axis=0), cx], axis=3)
 
     held_global = lat_index * lat_rows + jnp.arange(count, dtype=jnp.int32) % lat_rows
@@ -255,7 +242,19 @@
 
     for substep in range(SUBSTEPS):
         south_in = shift(state[:, :, lat_rows - HALO :], "lat", 1, False)
-        north_in = shift(state[:, :, :HALO], "lat", -1, False)
+        if substep == 0:
+            going = jnp.concatenate(
+                [state[:, :, :HALO].reshape(lon_devices, tracer_count * HALO, lon_cols), cy[:, 0, :1]],
+                axis=1,
+            )
+            coming = shift(going, "lat", -1, False)
+            north_in = coming[:, : tracer_count * HALO].reshape(
+                lon_devices, tracer_count, HALO, lon_cols
+            )
+            north_cy = jnp.where(is_north, 0.0, coming[:, None, tracer_count * HALO :])
+            north_courant = jnp.concatenate([cy, north_cy], axis=2)
+        else:
+            north_in = shift(state[:, :, :HALO], "lat", -1, False)
         edge = jnp.where(is_south, state[:, :, :HALO], state[:, :, lat_rows - HALO :])
         far = jnp.roll(edge, lon_devices // 2, axis=0)
         far_rev = jnp.concatenate([far[:, :, 2:3], far[:, :, 1:2], far[:, :, 0:1]], axis=2)
@@ -282,8 +281,16 @@
         rows = filter_rows(rows, basis, roots, weights, polar, 0)
         state = rows.reshape(lon_devices, tracer_count, lat_rows, lon_cols)
 
-    tiles = scatter_arrival(state, "lon")
-    return jnp.transpose(tiles, (1, 0, 2, 3))
+    back = [state[0]] + [
+        shift(state[(lon_devices - by) % lon_devices], "lon", by, True) for by in range(1, lon_devices)
+    ]
+    levels = []
+    for level in range(level_count):
+        pick = back[0]
+        for by in range(1, lon_devices):
+            pick = jnp.where((lon_index - by) % lon_devices == level, back[by], pick)
+        levels.append(pick)
+    return jnp.stack(levels, axis=1)
 
 
 def on_device(tracers, courant_x, courant_y, cutoffs):

time: 77.8 us -> 76 us (0.977)
  starting transfers between devices: 20.8 us -> 18.9 us
  other arithmetic: 15.5 us -> 16.6 us
    ppermute x11 -> x10, starting transfers between devices: 20.8 us -> 18.9 us  [shift(): return lax.ppermute(x, axis, pairs)]
    reshape x0 -> x2, local copies, waits for them, and re-layouts: none -> 1.81 us  [the longest x1 1.77 us: payload_for(): lax.dynamic_index_in_dim(tracers, level, 1, keepdims=False)]
    unnamed x5 -> x4, local copies, waits for them, and re-layouts: 2.27 us -> 1.19 us
    concatenate x2 -> x4, other arithmetic: 1 us -> 2.07 us  [the longest x3 2.04 us: payload_for(): jnp.concatenate([lax.dynamic_index_in_dim(tracers, level, 1, keepdims=Fal...]
    squeeze x0 -> x3, local copies, waits for them, and re-layouts: none -> 0.91 us  [the longest x1 0.88 us: payload_for(): lax.dynamic_index_in_dim(courant_y, level, 0, keepdims=False)]
    another operation x2 -> x4, other arithmetic: 1.03 us -> 1.87 us  [the longest x2 0.99 us: transposed_path(): payload = jnp.stack(pieces)]
    select_n x1 -> x0, local copies, waits for them, and re-layouts: 0.82 us -> none  [scatter_arrival(): return jnp.take(jnp.stack(pieces), order, axis=0)]
    dynamic_slice x1 -> x0, local copies, waits for them, and re-layouts: 0.8 us -> none  [gather_arrival(): pieces = [lax.dynamic_index_in_dim(x, me, 0, keepdims=False)]]
  transfers between devices with their start and end apart: 11 -> 10, of which waited for: 5 -> 5; matrix products, arithmetic and copies ran while one was open for 9% -> 12% of each run, Pallas kernels for 0% -> 0%
where the time goes in v7:
time: 76 us; the launch traced here: 75.3 us
  waiting for transfers between devices  24.9 us (33%)
  starting transfers between devices  18.9 us (25%)
  other arithmetic  16.6 us (22%)
  matrix products  8.93 us (12%)
  local copies, waits for them, and re-layouts  5.57 us (7%)
    ppermute x10, waiting for transfers between devices, shift(): return lax.ppermute(x, axis, pairs)  24.9 us
    ppermute x10, starting transfers between devices, shift(): return lax.ppermute(x, axis, pairs)  18.9 us
    dot_general x2, matrix products, filter_rows(): lax.dot_general(spec, basis, (((2,), (2,)), ((0,), (0,))), precision=MATM...  5.11 us
    dot_general x2, matrix products, filter_rows(): lax.dot_general(z, basis, (((2,), (1,)), ((0,), (0,))), precision=MATMUL_...  3.82 us
    sub x1, other arithmetic, product_basis(): cos_qk = (ca * cb - sa * sb).reshape(tiles, cols, per_class)  2.22 us
    concatenate x3, other arithmetic, payload_for(): jnp.concatenate([lax.dynamic_index_in_dim(tracers, level, 1, keepdims=Fal...  2.04 us
    mul x2, other arithmetic, transposed_path(): ppm_flux(extended, north_courant, 2, lat_rows) * face_weight[:, None]  1.95 us
    sub x4, other arithmetic, ppm_flux(): 7.0 / 12.0  1.78 us
  transfers between devices with their start and end apart: 10, of which 5 were waited for; matrix products, arithmetic and copies ran while one was open for 12% of the time, Pallas kernels for 0%

profile of v7, /device:TPU:3, one launch (start us, length us, event | category | flops | bytes accessed | tf_op | source)
XLA Modules:
  0.0 75.3 jit_solution(16640759122493650898)
XLA Ops:
  0.0 1.8 %dynamic-slice_bitcast_fusion.3 = (f32[40,720]{1,0:T(8,128)}, f32[40,720]{1,0:T(8,128)S(1)}, f32[40,720]{1,0:T(8,128)S(1)}, f32[40,720]{1,0:T(8,128)S(1)}) fusion(f32[5,4,8,720]{3,2,1,0:T(8,128)} %param.4, s32[]{:T(128)S(6)} %select_n.364, s32[]{:T(128)S(6)} %select_n.368, s32[]{:T(128)S(6)} %select_n.366, s32[]{:T(128)S(6)} %select_n.370), kind=kLoop, calls=%fused_computation.202 | loop fusion | bytes 921616 | tf_op jit(solution)/shard_map/reshape | solution.py:213
  1.8 0.9 %dynamic-slice_bitcast_fusion.10 = (f32[8,720]{1,0:T(8,128)S(1)}, f32[8,720]{1,0:T(8,128)S(1)}, f32[8,720]{1,0:T(8,128)S(1)}, f32[8,720]{1,0:T(8,128)S(1)}, f32[...) fusion(f32[4,8,720]{2,1,0:T(8,128)} %param.6, s32[]{:T(128)S(6)} %select_n.364, ...), kind=kLoop, calls=%fused_computation.229 | loop fusion | bytes 368656 | tf_op jit(solution)/shard_map/jit(dynamic_index_in_dim)/squeeze | solution.py:215
  2.6 0.7 pad_maximum_fusion.19
  3.3 3.3 %collective-permute-start.2 = (f32[56,720]{1,0:T(8,128)}, f32[56,720]{1,0:T(8,128)S(1)}, u32[]{:S(2)}, u32[]{:S(2)}) collective-permute-start(f32[56,720]{1,0:T(8,128)} %pad_maximum_fusion.19), channel_id=1, source_target_pairs={{0,3},{1,0},{2,1},{3,2},{4,7},{5,4},{6,5},{7,6},{8,11},{9,8},{10,9... | collective-permute-start | bytes 483848 | tf_op jit(solution)/shard_map/ppermute | solution.py:17
  6.7 0.7 pad_maximum_fusion.18
  7.3 0.7 pad_maximum_fusion.17
  8.0 0.5 collective-permute-start
  8.7 0.8 %gather_fusion = s32[40]{0:T(128)S(1)} fusion(s32[64]{0:T(128)S(1)} %copy-done, s32[1024]{0:T(1024)S(1)} %pad_clamp_fusion), kind=kCustom, calls=%fused_computation | custom fusion | bytes 480 | tf_op jit(solution)/shard_map/jit(_take)/gather | solution.py:231
  9.5 0.4 fusion.121
  9.9 0.6 fusion.114
  10.6 2.2 %multiply_subtract_fusion = (f32[4,30,24,180]{3,2,1,0:T(8,128)S(1)}, f32[4,30,24,180]{3,2,1,0:T(8,128)}) fusion(f32[4,24,180]{2,1,0:T(8,128)S(1)} %get-tuple-element.77, f32[4,30,180]{2,1,0:T(8,128)S(1)} %get-tuple-element.75, f32[4,24,180]{2,1,0:T(8,128)S(1)} %get-tuple-element.76, f32[4,30,180]{2,1,0:T(8,128)S(1)} %get-tuple-element.74), kind=kLoop, calls=%fused_computation.3 | loop fusion | flops 3110400 | bytes 4458240 | tf_op jit(solution)/shard_map/sub | solution.py:33
  12.8 0.9 %maximum_bitcast_fusion.1 = f32[1,56,720]{2,1,0:T(8,128)S(1)} fusion(f32[8,720]{1,0:T(8,128)S(1)} %get-tuple-element.70, f32[8,720]{1,0:T(8,128)S(1)} %get-tuple-element.83, f32[40,720]{1,0:T(8,128)} %get-tuple-element.48), kind=kLoop, calls=%fused_computation.174 | loop fusion | flops 80640 | bytes 322560 | tf_op jit(solution)/shard_map/stack | solution.py:223
  13.7 7.6 %collective-permute-done.1 = f32[56,720]{1,0:T(8,128)S(1)} collective-permute-done((f32[56,720]{1,0:T(8,128)}, f32[56,720]{1,0:T(8,128)S(1)}, u32[]{:S(2)}, u32[]{:S(2)}) %collective-permute-start.1) | collective-permute-done | bytes 161312 | tf_op jit(solution)/shard_map/ppermute | solution.py:17
  22.2 4.1 %collective-permute-start.4 = (f32[4,5,3,720]{3,2,1,0:T(4,128)S(1)}, f32[4,5,3,720]{3,2,1,0:T(4,128)S(1)}, u32[]{:S(2)}, u32[]{:S(2)}) collective-permute-start(f32[4,5,3,720]{3,2,1,0:T(4,128)S(1)} %get-tuple-element.45), channel_id=1, source_target_pairs={{0,4},{4,8},{8,12},{12,16},{16,20},{20,24},{24,28},{1,5},{5,9},{9,... | collective-permute-start | bytes 518408 | tf_op jit(solution)/shard_map/ppermute | solution.py:17
  26.5 1.9 %collective-permute-start.3 = (f32[4,16,720]{2,1,0:T(8,128)S(1)}, f32[4,16,720]{2,1,0:T(8,128)S(1)}, u32[]{:S(2)}, u32[]{:S(2)}) collective-permute-start(f32[4,16,720]{2,1,0:T(8,128)S(1)} %pad_maximum_fusion.15), channel_id=1, source_target_pairs={{4,0},{8,4},{12,8},{16,12},{20,16},{24,20},{28,24},{5,1},{9,5},{13... | collective-permute-start | bytes 552968 | tf_op jit(solution)/shard_map/ppermute | solution.py:17
  28.4 0.2 maximum_maximum_fusion
  28.6 0.5 fusion.84
  29.1 0.5 fusion.77
  29.6 4.7 %collective-permute-done.3 = f32[4,16,720]{2,1,0:T(8,128)S(1)} collective-permute-done((f32[4,16,720]{2,1,0:T(8,128)S(1)}, f32[4,16,720]{2,1,0:T(8,128)S(1)}, u32[]{:S(2)}, u32[]{:S(2)}) %collective-permute-start.3) | collective-permute-done | bytes 184352 | tf_op jit(solution)/shard_map/ppermute | solution.py:17
  34.6 0.2 broadcast_select_fusion.4
  35.1 0.4 fusion.39
  35.5 1.0 %fusion.26 = f32[4,5,9,720]{3,2,1,0:T(8,128)S(1)} fusion(f32[4,5,8,720]{3,2,1,0:T(8,128)S(1)} %slice_bitcast_fusion, f32[4,5,3,720]{3,2,1,0:T(4,128)S(1)} %get-tuple-element.59, f32[4,5,3,720]{3,2,1,0:T(4,128)S(1)} %get-tuple-element.58, f32[4,5,11,720]{3,2,1,0:T(8,128)S(1)} %fusion.39, f32[9]{0:T(128)S(1)} %or_select_fusion, ...), kind=kLoop, calls=%fused_computation.48 | loop fusion | flops 2980800 | bytes 3216996 | tf_op jit(solution)/shard_map/mul | solution.py:273
  36.5 0.2 fusion.70
  36.7 0.4 multiply_reduce_fusion.3
  37.2 1.2 %copy-done.1 = f32[4,30,24,180]{3,2,1,0:T(8,128)S(1)} copy-done((f32[4,30,24,180]{3,2,1,0:T(8,128)S(1)}, f32[4,30,24,180]{3,2,1,0:T(8,128)}, u32[]{:S(2)}) %copy-start.1) | copy-done | bytes 2073624
  38.4 1.9 %fusion.42 = f32[4,80,360]{2,1,0:T(8,128)S(1)} fusion(f32[4,40,720]{2,1,0:T(8,128)S(1)} %neg.12, f32[4,40,720]{2,1,0:T(8,128)S(1)} %get-tuple-element.7, f32[4,720,180]{2,1,0:T(8,128)S(1)} %bitcast.101, f32[4,720,180]{2,1,0:T(8,128)S(1)} %bitcast.97), kind=kOutput, calls=%fused_computation.67 | convolution fusion | flops 498931200 | bytes 5529600 | tf_op jit(solution)/shard_map/dot_general | solution.py:93
  40.4 2.6 %fusion.85 = f32[4,80,720]{2,1,0:T(8,128)S(1)} fusion(f32[4,40,180]{2,1,0:T(8,128)S(1)} %get-tuple-element.30, f32[4,40,180]{2,1,0:T(8,128)S(1)} %get-tuple-element.14, f32[4,40,180]{2,1,0:T(8,128)S(1)} %get-tuple-element.15, f32[4,720,180]{2,1,0:T(8,128)S(1)} %bitcast.102, f32[4,720,180]{2,1,0:T(8,128)S(1)} %bitcast.98), kind=kOutput, calls=%fused_computation.126 | convolution fusion | flops 499046400 | bytes 5414400 | tf_op jit(solution)/shard_map/dot_general | solution.py:102
  43.1 0.3 subtract_reduce_fusion.1
  43.8 1.9 %collective-permute-start.5 = (f32[4,5,3,720]{3,2,1,0:T(4,128)S(1)}, f32[4,5,3,720]{3,2,1,0:T(4,128)S(1)}, u32[]{:S(2)}, u32[]{:S(2)}) collective-permute-start(f32[4,5,3,720]{3,2,1,0:T(4,128)S(1)} %get-tuple-element.38), channel_id=1, source_target_pairs={{0,4},{4,8},{8,12},{12,16},{16,20},{20,24},{24,28},{1,5},{5,9},{9,... | collective-permute-start | bytes 518408 | tf_op jit(solution)/shard_map/ppermute | solution.py:17
  45.7 2.6 %collective-permute-start.6 = (f32[4,5,3,720]{3,2,1,0:T(4,128)S(1)}, f32[4,5,3,720]{3,2,1,0:T(4,128)S(1)}, u32[]{:S(2)}, u32[]{:S(2)}) collective-permute-start(f32[4,5,3,720]{3,2,1,0:T(4,128)S(1)} %get-tuple-element.39), channel_id=1, source_target_pairs={{4,0},{8,4},{12,8},{16,12},{20,16},{24,20},{28,24},{5,1},{9,5},{13... | collective-permute-start | bytes 518408 | tf_op jit(solution)/shard_map/ppermute | solution.py:17
  48.3 0.2 maximum_maximum_fusion.2
  48.6 0.5 fusion.67
  49.0 0.5 fusion.60
  49.6 4.6 %collective-permute-done.6 = f32[4,5,3,720]{3,2,1,0:T(4,128)S(1)} collective-permute-done((f32[4,5,3,720]{3,2,1,0:T(4,128)S(1)}, f32[4,5,3,720]{3,2,1,0:T(4,128)S(1)}, u32[]{:S(2)}, u32[]{:S(2)}) %collective-permute-start.6) | collective-permute-done | bytes 172832 | tf_op jit(solution)/shard_map/ppermute | solution.py:17
  54.2 0.2 broadcast_select_fusion.2
  54.6 0.4 fusion.36
  55.0 1.0 %fusion.9 = f32[4,5,9,720]{3,2,1,0:T(8,128)S(1)} fusion(f32[4,5,8,720]{3,2,1,0:T(8,128)S(1)} %bitcast_select_fusion, f32[4,5,3,720]{3,2,1,0:T(4,128)S(1)} %get-tuple-element.55, f32[4,5,3,720]{3,2,1,0:T(4,128)S(1)} %get-tuple-element.54, f32[4,5,11,720]{3,2,1,0:T(8,128)S(1)} %fusion.36, f32[9]{0:T(128)S(1)} %or_select_fusion, ...), kind=kLoop, calls=%fused_computation.31 | loop fusion | flops 2980800 | bytes 3216996 | tf_op jit(solution)/shard_map/mul | solution.py:273
  56.0 0.3 fusion.53
  56.2 0.4 multiply_reduce_fusion.1
  56.7 1.9 %fusion.46 = f32[4,80,360]{2,1,0:T(8,128)S(1)} fusion(f32[4,40,720]{2,1,0:T(8,128)S(1)} %neg.14, f32[4,40,720]{2,1,0:T(8,128)S(1)} %get-tuple-element.5, f32[4,720,180]{2,1,0:T(8,128)S(1)} %bitcast.103, f32[4,720,180]{2,1,0:T(8,128)S(1)} %bitcast.99), kind=kOutput, calls=%fused_computation.72 | convolution fusion | flops 498931200 | bytes 5529600 | tf_op jit(solution)/shard_map/dot_general | solution.py:93
  58.8 2.6 %fusion.93 = f32[4,80,720]{2,1,0:T(8,128)S(1)} fusion(f32[4,40,180]{2,1,0:T(8,128)S(1)} %get-tuple-element.29, f32[4,40,180]{2,1,0:T(8,128)S(1)} %get-tuple-element.9, f32[4,40,180]{2,1,0:T(8,128)S(1)} %get-tuple-element.10, f32[4,720,180]{2,1,0:T(8,128)S(1)} %bitcast.104, f32[4,720,180]{2,1,0:T(8,128)S(1)} %bitcast.100), kind=kOutput, calls=%fused_computation.137 | convolution fusion | flops 499046400 | bytes 5414400 | tf_op jit(solution)/shard_map/dot_general | solution.py:102
  61.4 0.3 subtract_reduce_fusion
  61.9 0.5 collective-permute-start.7
  62.4 2.7 %collective-permute-start.8 = (f32[5,8,720]{2,1,0:T(8,128)S(1)}, f32[5,8,720]{2,1,0:T(8,128)S(1)}, u32[]{:S(2)}, u32[]{:S(2)}) collective-permute-start(f32[5,8,720]{2,1,0:T(8,128)S(1)} %get-tuple-element.32), channel_id=1, source_target_pairs={{0,2},{1,3},{2,0},{3,1},{4,6},{5,7},{6,4},{7,5},{8,10},{9,11},{10,... | collective-permute-start | bytes 345608 | tf_op jit(solution)/shard_map/ppermute | solution.py:17
  65.1 1.4 %collective-permute-start.9 = (f32[5,8,720]{2,1,0:T(8,128)S(1)}, f32[5,8,720]{2,1,0:T(8,128)S(1)}, u32[]{:S(2)}, u32[]{:S(2)}) collective-permute-start(f32[5,8,720]{2,1,0:T(8,128)S(1)} %get-tuple-element.31), channel_id=1, source_target_pairs={{0,1},{1,2},{2,3},{3,0},{4,5},{5,6},{6,7},{7,4},{8,9},{9,10},{10,1... | collective-permute-start | bytes 345608 | tf_op jit(solution)/shard_map/ppermute | solution.py:17
  66.5 0.6 collective-permute-done.7
  67.1 7.3 %collective-permute-done.8 = f32[5,8,720]{2,1,0:T(8,128)S(1)} collective-permute-done((f32[5,8,720]{2,1,0:T(8,128)S(1)}, f32[5,8,720]{2,1,0:T(8,128)S(1)}, u32[]{:S(2)}, u32[]{:S(2)}) %collective-permute-start.8) | collective-permute-done | bytes 115232 | tf_op jit(solution)/shard_map/ppermute | solution.py:17
  74.5 0.8 %pad_maximum_fusion.10 = f32[5,4,8,720]{3,2,1,0:T(8,128)} fusion(f32[5,1,8,720]{3,2,1,0:T(8,128)S(1)} %get-tuple-element.24, f32[5,1,8,720]{3,2,1,0:T(8,128)S(1)} %get-tuple-element.25, f32[5,1,8,720]{3,2,1,0:T(8,128)S(1)} %get-tuple-element.26, f32[5,1,8,720]{3,2,1,0:T(8,128)S(1)} %get-tuple-element.23), kind=kLoop, calls=%fused_computation.145 | loop fusion | flops 345600 | bytes 921600 | tf_op jit(solution)/shard_map/stack | solution.py:293
  (61 shorter events, 3.0 us)
Async XLA Ops:
  0.0 8.7 %copy-start = (s32[64]{0:T(128)S(1)}, s32[64]{0:T(128)}, u32[]{:S(2)}) copy-start(s32[64]{0:T(128)} %param.7) | copy-start | bytes 772
  3.3 10.4 %collective-permute-start.2 = (f32[56,720]{1,0:T(8,128)}, f32[56,720]{1,0:T(8,128)S(1)}, u32[]{:S(2)}, u32[]{:S(2)}) collective-permute-start(f32[56,720]{1,0:T(8,128)} %pad_maximum_fusion.19), channel_id=1, source_target_pairs={{0,3},{1,0},{2,1},{3,2},{4,7},{5,4},{6,5},{7,6},{8,11},{9,8},{10,9... | collective-permute-start | bytes 483848 | tf_op jit(solution)/shard_map/ppermute | solution.py:17
  7.3 14.0 %collective-permute-start.1 = (f32[56,720]{1,0:T(8,128)}, f32[56,720]{1,0:T(8,128)S(1)}, u32[]{:S(2)}, u32[]{:S(2)}) collective-permute-start(f32[56,720]{1,0:T(8,128)} %pad_maximum_fusion.18), channel_id=1, source_target_pairs={{0,2},{1,3},{2,0},{3,1},{4,6},{5,7},{6,4},{7,5},{8,10},{9,11},{10,... | collective-permute-start | bytes 483848 | tf_op jit(solution)/shard_map/ppermute | solution.py:17
  8.0 13.3 %collective-permute-start = (f32[56,720]{1,0:T(8,128)}, f32[56,720]{1,0:T(8,128)S(1)}, u32[]{:S(2)}, u32[]{:S(2)}) collective-permute-start(f32[56,720]{1,0:T(8,128)} %pad_maximum_fusion.17), channel_id=1, source_target_pairs={{0,1},{1,2},{2,3},{3,0},{4,5},{5,6},{6,7},{7,4},{8,9},{9,10},{10,1... | collective-permute-start | bytes 483848 | tf_op jit(solution)/shard_map/ppermute | solution.py:17
  22.2 12.4 %collective-permute-start.4 = (f32[4,5,3,720]{3,2,1,0:T(4,128)S(1)}, f32[4,5,3,720]{3,2,1,0:T(4,128)S(1)}, u32[]{:S(2)}, u32[]{:S(2)}) collective-permute-start(f32[4,5,3,720]{3,2,1,0:T(4,128)S(1)} %get-tuple-element.45), channel_id=1, source_target_pairs={{0,4},{4,8},{8,12},{12,16},{16,20},{20,24},{24,28},{1,5},{5,9},{9,... | collective-permute-start | bytes 518408 | tf_op jit(solution)/shard_map/ppermute | solution.py:17
  26.5 7.9 %collective-permute-start.3 = (f32[4,16,720]{2,1,0:T(8,128)S(1)}, f32[4,16,720]{2,1,0:T(8,128)S(1)}, u32[]{:S(2)}, u32[]{:S(2)}) collective-permute-start(f32[4,16,720]{2,1,0:T(8,128)S(1)} %pad_maximum_fusion.15), channel_id=1, source_target_pairs={{4,0},{8,4},{12,8},{16,12},{20,16},{24,20},{28,24},{5,1},{9,5},{13... | collective-permute-start | bytes 552968 | tf_op jit(solution)/shard_map/ppermute | solution.py:17
  36.5 1.8 %copy-start.1 = (f32[4,30,24,180]{3,2,1,0:T(8,128)S(1)}, f32[4,30,24,180]{3,2,1,0:T(8,128)}, u32[]{:S(2)}) copy-start(f32[4,30,24,180]{3,2,1,0:T(8,128)} %get-tuple-element.53) | copy-start | bytes 6220804
  43.8 5.8 %collective-permute-start.5 = (f32[4,5,3,720]{3,2,1,0:T(4,128)S(1)}, f32[4,5,3,720]{3,2,1,0:T(4,128)S(1)}, u32[]{:S(2)}, u32[]{:S(2)}) collective-permute-start(f32[4,5,3,720]{3,2,1,0:T(4,128)S(1)} %get-tuple-element.38), channel_id=1, source_target_pairs={{0,4},{4,8},{8,12},{12,16},{16,20},{20,24},{24,28},{1,5},{5,9},{9,... | collective-permute-start | bytes 518408 | tf_op jit(solution)/shard_map/ppermute | solution.py:17
  45.7 8.4 %collective-permute-start.6 = (f32[4,5,3,720]{3,2,1,0:T(4,128)S(1)}, f32[4,5,3,720]{3,2,1,0:T(4,128)S(1)}, u32[]{:S(2)}, u32[]{:S(2)}) collective-permute-start(f32[4,5,3,720]{3,2,1,0:T(4,128)S(1)} %get-tuple-element.39), channel_id=1, source_target_pairs={{4,0},{8,4},{12,8},{16,12},{20,16},{24,20},{28,24},{5,1},{9,5},{13... | collective-permute-start | bytes 518408 | tf_op jit(solution)/shard_map/ppermute | solution.py:17
  61.9 5.2 %collective-permute-start.7 = (f32[5,8,720]{2,1,0:T(8,128)S(1)}, f32[5,8,720]{2,1,0:T(8,128)S(1)}, u32[]{:S(2)}, u32[]{:S(2)}) collective-permute-start(f32[5,8,720]{2,1,0:T(8,128)S(1)} %get-tuple-element.33), channel_id=1, source_target_pairs={{0,3},{1,0},{2,1},{3,2},{4,7},{5,4},{6,5},{7,6},{8,11},{9,8},{10,9... | collective-permute-start | bytes 345608 | tf_op jit(solution)/shard_map/ppermute | solution.py:17
  62.4 12.0 %collective-permute-start.8 = (f32[5,8,720]{2,1,0:T(8,128)S(1)}, f32[5,8,720]{2,1,0:T(8,128)S(1)}, u32[]{:S(2)}, u32[]{:S(2)}) collective-permute-start(f32[5,8,720]{2,1,0:T(8,128)S(1)} %get-tuple-element.32), channel_id=1, source_target_pairs={{0,2},{1,3},{2,0},{3,1},{4,6},{5,7},{6,4},{7,5},{8,10},{9,11},{10,... | collective-permute-start | bytes 345608 | tf_op jit(solution)/shard_map/ppermute | solution.py:17
  65.1 9.3 %collective-permute-start.9 = (f32[5,8,720]{2,1,0:T(8,128)S(1)}, f32[5,8,720]{2,1,0:T(8,128)S(1)}, u32[]{:S(2)}, u32[]{:S(2)}) collective-permute-start(f32[5,8,720]{2,1,0:T(8,128)S(1)} %get-tuple-element.31), channel_id=1, source_target_pairs={{0,1},{1,2},{2,3},{3,0},{4,5},{5,6},{6,7},{7,4},{8,9},{9,10},{10,1... | collective-permute-start | bytes 345608 | tf_op jit(solution)/shard_map/ppermute | solution.py:17

commit v8 on v7

--- a/solution.py
+++ b/solution.py
@@ -8,7 +8,6 @@
 KMAX = 720
 SUBSTEPS = 2
 HALO = 3
-MATMUL_PRECISION = lax.Precision.HIGH
 
 
 def shift(x, axis, by, wrap):
@@ -83,15 +82,34 @@
     return jnp.concatenate([jnp.cos(angle), jnp.sin(angle)], axis=2)
 
 
-def filter_rows(rows, basis, roots, weights, polar, halo=HALO):
+def split_bf16(x):
+    high = lax.reduce_precision(x, exponent_bits=8, mantissa_bits=7)
+    return high.astype(jnp.bfloat16), (x - high).astype(jnp.bfloat16)
+
+
+def split_basis(basis):
+    high, low = split_bf16(basis)
+    return jnp.concatenate([high, low, high], axis=1), jnp.concatenate([high, low, high], axis=2)
+
+
+def three_products(lhs, rhs, lhs_axis, rhs_axis):
+    high, low = split_bf16(lhs)
+    wide = jnp.concatenate([high, high, low], axis=2)
+    return lax.dot_general(
+        wide, rhs, (((2,), (rhs_axis,)), ((0,), (0,))), preferred_element_type=jnp.float32
+    )
+
+
+def filter_rows(rows, bases, roots, weights, polar, halo=HALO):
     tiles, count, cols = rows.shape
+    along_q, along_m = bases
     cos_dr, sin_dr = roots
     z_re = jnp.sum(cos_dr[:, :, None, None] * rows[None], axis=1)
     z_im = -jnp.sum(sin_dr[:, :, None, None] * rows[None], axis=1)
     z = jnp.concatenate([z_re, z_im], axis=1)
     z = jnp.pad(z, ((0, 0), (0, 0), (halo, halo)))
-    prod = lax.dot_general(z, basis, (((2,), (1,)), ((0,), (0,))), precision=MATMUL_PRECISION)
-    per_class = basis.shape[2] // 2
+    prod = three_products(z, along_q, 2, 1)
+    per_class = along_m.shape[2] // 6
     zc, zs = prod[:, :count, :per_class], prod[:, :count, per_class:]
     wc, ws = prod[:, count:, :per_class], prod[:, count:, per_class:]
     real = (zc + ws) * weights
@@ -99,7 +117,7 @@
     spec = jnp.concatenate(
         [jnp.concatenate([real, imag], axis=2), jnp.concatenate([-imag, real], axis=2)], axis=1
     )
-    back = lax.dot_general(spec, basis, (((2,), (2,)), ((0,), (0,))), precision=MATMUL_PRECISION)
+    back = three_products(spec, along_m, 2, 2)
     w_re, w_im = back[:, :count], back[:, count:]
     smooth = jnp.sum(
         cos_dr[:, :, None, None] * w_re[:, None] - sin_dr[:, :, None, None] * w_im[:, None], axis=0
@@ -142,7 +160,7 @@
     )[:, None]
     scale = jnp.where(k == 0, 1.0 / circle, 2.0 / circle).astype(jnp.float32)
     weights = jnp.where(k[:, None, :] < cut[None, :, None], scale[:, None, :], 0.0)
-    basis = class_basis(lon_devices, lon_cols, circle)
+    basis = split_basis(class_basis(lon_devices, lon_cols, circle))
     roots = root_table(lon_devices)
 
     west_cx = shift(courant_x[:, :, lon_cols - 1 :], "lon", 1, True)
@@ -235,7 +253,7 @@
     )[:, None]
     scale = jnp.where(k == 0, 1.0 / circle, 2.0 / circle).astype(jnp.float32)
     weights = jnp.where(k[:, None, :] < cut[None, :, None], scale[:, None, :], 0.0)
-    basis = product_basis(lon_devices, lon_cols, circle)
+    basis = split_basis(product_basis(lon_devices, lon_cols, circle))
     roots = root_table(
         lon_devices, (lax.axis_index("lon") - jnp.arange(lon_devices, dtype=jnp.int32)) % lon_devices
     )

time: 76 us -> 113 us (1.49)
  local copies, waits for them, and re-layouts: 5.57 us -> 30.7 us
  other arithmetic: 16.6 us -> 25.7 us
  matrix products: 8.93 us -> 17.7 us
  waiting for transfers between devices: 24.9 us -> 18.7 us
    concatenate x0 -> x5, local copies, waits for them, and re-layouts: none -> 19.6 us  [the longest x1 10.4 us: split_basis(): jnp.concatenate([high, low, high], axis=1)]
    dot_general x4, matrix products: 8.93 us -> 17.7 us  [three_products(): lax.dot_general(wide, rhs, (((2,), (rhs_axis,)), ((0,), (0,))), preferred...]
    convert_element_type x0 -> x5, other arithmetic: none -> 6.57 us  [split_bf16(): return (high.astype(jnp.bfloat16), (x - high).astype(jnp.bfloat16))]
    ppermute x10, waiting for transfers between devices: 24.9 us -> 18.7 us  [shift(): return lax.ppermute(x, axis, pairs)]
    add x0 -> x1, local copies, waits for them, and re-layouts: none -> 3.34 us  [product_basis(): sin_qk = (sa * cb + ca * sb).reshape(tiles, cols, per_class)]
    sub x0 -> x1, local copies, waits for them, and re-layouts: none -> 2.12 us  [product_basis(): cos_qk = (ca * cb - sa * sb).reshape(tiles, cols, per_class)]
  transfers between devices with their start and end apart: 10 -> 10, of which waited for: 5 -> 4; matrix products, arithmetic and copies ran while one was open for 12% -> 29% of each run, Pallas kernels for 0% -> 0%
where the time goes in v8:
time: 113 us; the launch traced here: 112 us
  local copies, waits for them, and re-layouts  30.7 us (27%)
  other arithmetic  25.7 us (23%)
  waiting for transfers between devices  18.7 us (17%)
  starting transfers between devices  18.4 us (16%)
  matrix products  17.7 us (16%)
    ppermute x10, waiting for transfers between devices, shift(): return lax.ppermute(x, axis, pairs)  18.7 us
    ppermute x10, starting transfers between devices, shift(): return lax.ppermute(x, axis, pairs)  18.4 us
    dot_general x4, matrix products, three_products(): lax.dot_general(wide, rhs, (((2,), (rhs_axis,)), ((0,), (0,))), preferred...  17.7 us
    concatenate x1, local copies, waits for them, and re-layouts, split_basis(): jnp.concatenate([high, low, high], axis=1)  10.4 us
    concatenate x4, local copies, waits for them, and re-layouts, three_products(): wide = jnp.concatenate([high, high, low], axis=2)  9.26 us
    convert_element_type x5, other arithmetic, split_bf16(): return (high.astype(jnp.bfloat16), (x - high).astype(jnp.bfloat16))  6.57 us
    add x1, local copies, waits for them, and re-layouts, product_basis(): sin_qk = (sa * cb + ca * sb).reshape(tiles, cols, per_class)  3.34 us
  transfers between devices with their start and end apart: 10, of which 4 were waited for; matrix products, arithmetic and copies ran while one was open for 29% of the time, Pallas kernels for 0%

profile of v8, /device:TPU:3, one launch (start us, length us, event | category | flops | bytes accessed | tf_op | source)
XLA Modules:
  0.0 111.8 jit_solution(13585387215972781617)
XLA Ops:
  0.0 1.8 %dynamic-slice_bitcast_fusion.3 = (f32[40,720]{1,0:T(8,128)}, f32[40,720]{1,0:T(8,128)S(1)}, f32[40,720]{1,0:T(8,128)S(1)}, f32[40,720]{1,0:T(8,128)S(1)}) fusion(f32[5,4,8,720]{3,2,1,0:T(8,128)} %param.4, s32[]{:T(128)S(6)} %select_n.364, s32[]{:T(128)S(6)} %select_n.368, s32[]{:T(128)S(6)} %select_n.366, s32[]{:T(128)S(6)} %select_n.370), kind=kLoop, calls=%fused_computation.200 | loop fusion | bytes 921616 | tf_op jit(solution)/shard_map/reshape | solution.py:231
  1.8 0.9 dynamic-slice_bitcast_fusion.10
  2.7 0.7 pad_maximum_fusion.24
  3.3 3.3 %collective-permute-start.2 = (f32[56,720]{1,0:T(8,128)}, f32[56,720]{1,0:T(8,128)S(1)}, u32[]{:S(2)}, u32[]{:S(2)}) collective-permute-start(f32[56,720]{1,0:T(8,128)} %pad_maximum_fusion.24), channel_id=1, source_target_pairs={{0,3},{1,0},{2,1},{3,2},{4,7},{5,4},{6,5},{7,6},{8,11},{9,8},{10,9... | collective-permute-start | bytes 483848 | tf_op jit(solution)/shard_map/ppermute | solution.py:16
  6.7 0.7 pad_maximum_fusion.23
  7.4 0.7 pad_maximum_fusion.22
  8.1 0.5 collective-permute-start
  8.5 0.6 compare_select_fusion
  9.1 0.6 or_select_fusion
  9.8 0.6 multiply_cosine_fusion
  10.4 0.5 fusion.111
  10.9 0.8 gather_fusion
  11.7 0.6 and_select_fusion.1
  12.8 0.6 fusion.97
  13.4 2.2 %multiply_subtract_fusion = (f32[4,30,24,180]{3,2,1,0:T(8,128)S(1)}, f32[4,30,24,180]{3,2,1,0:T(8,128)}) fusion(f32[4,24,180]{2,1,0:T(8,128)S(1)} %get-tuple-element.87, f32[4,30,180]{2,1,0:T(8,128)S(1)} %get-tuple-element.85, f32[4,24,180]{2,1,0:T(8,128)S(1)} %get-tuple-element.86, f32[4,30,180]{2,1,0:T(8,128)S(1)} %get-tuple-element.84), kind=kLoop, calls=%fused_computation.9 | loop fusion | flops 3110400 | bytes 4458240 | tf_op jit(solution)/shard_map/sub | solution.py:32
  15.6 3.3 %copy.98 = f32[4,720,180]{1,2,0:T(8,128)} copy(f32[4,720,180]{2,1,0:T(8,128)} %bitcast.104) | data formatting | bytes 4147200 | tf_op jit(solution)/shard_map/add | solution.py:33
  19.0 2.1 %copy.97 = f32[4,720,180]{1,2,0:T(8,128)} copy(f32[4,720,180]{2,1,0:T(8,128)S(1)} %bitcast.103) | data formatting | bytes 4147200 | tf_op jit(solution)/shard_map/sub | solution.py:32
  21.1 4.4 %fusion = (bf16[4,720,360]{1,2,0:T(8,128)(2,1)}, bf16[4,720,360]{1,2,0:T(8,128)(2,1)S(1)}) fusion(f32[4,720,180]{1,2,0:T(8,128)} %copy.98, f32[4,720,180]{1,2,0:T(8,128)} %copy.97), kind=kLoop, calls=%fused_computation.4 | loop fusion | flops 5184000 | bytes 8294400 | tf_op jit(solution)/shard_map/convert_element_type | solution.py:87
  25.5 0.6 compare_or_fusion
  26.1 10.4 %concatenate.197 = bf16[4,2160,360]{1,2,0:T(8,128)(2,1)} concatenate(bf16[4,720,360]{1,2,0:T(8,128)(2,1)S(1)} %get-tuple-element.20, bf16[4,720,360]{1,2,0:T(8,128)(2,1)} %get-tuple-element.19, bf16[4,720,360]{1,2,0:T(8,128)(2,1)S(1)} %get-tuple-element.20), dimensions={1} | concatenate | bytes 12441600 | tf_op jit(solution)/shard_map/concatenate | solution.py:92
  37.4 4.5 %collective-permute-start.4 = (f32[4,5,3,720]{3,2,1,0:T(4,128)S(1)}, f32[4,5,3,720]{3,2,1,0:T(4,128)S(1)}, u32[]{:S(2)}, u32[]{:S(2)}) collective-permute-start(f32[4,5,3,720]{3,2,1,0:T(4,128)S(1)} %get-tuple-element.55), channel_id=1, source_target_pairs={{0,4},{4,8},{8,12},{12,16},{16,20},{20,24},{24,28},{1,5},{5,9},{9,... | collective-permute-start | bytes 518408 | tf_op jit(solution)/shard_map/ppermute | solution.py:16
  42.1 2.1 %collective-permute-start.3 = (f32[4,16,720]{2,1,0:T(8,128)S(1)}, f32[4,16,720]{2,1,0:T(8,128)S(1)}, u32[]{:S(2)}, u32[]{:S(2)}) collective-permute-start(f32[4,16,720]{2,1,0:T(8,128)S(1)} %pad_maximum_fusion.20), channel_id=1, source_target_pairs={{4,0},{8,4},{12,8},{16,12},{20,16},{24,20},{28,24},{5,1},{9,5},{13... | collective-permute-start | bytes 552968 | tf_op jit(solution)/shard_map/ppermute | solution.py:16
  44.4 0.5 fusion.83
  44.9 0.5 fusion.76
  45.5 4.5 %collective-permute-done.3 = f32[4,16,720]{2,1,0:T(8,128)S(1)} collective-permute-done((f32[4,16,720]{2,1,0:T(8,128)S(1)}, f32[4,16,720]{2,1,0:T(8,128)S(1)}, u32[]{:S(2)}, u32[]{:S(2)}) %collective-permute-start.3) | collective-permute-done | bytes 184352 | tf_op jit(solution)/shard_map/ppermute | solution.py:16
  51.4 1.0 fusion.29
  53.0 0.9 fusion.43
  53.9 3.4 %concatenate.195 = bf16[4,80,2160]{2,1,0:T(8,128)(2,1)} concatenate(bf16[4,80,720]{2,1,0:T(8,128)(2,1)S(1)} %get-tuple-element.28, bf16[4,80,720]{2,1,0:T(8,128)(2,1)S(1)} %get-tuple-element.28, bf16[4,80,720]{2,1,0:T(8,128)(2,1)} %get-tuple-element.27), dimensions={2} | concatenate | bytes 2764800 | tf_op jit(solution)/shard_map/concatenate | solution.py:97
  57.3 5.1 %fusion.136 = f32[4,80,360]{2,1,0:T(8,128)S(1)} fusion(bf16[4,80,2160]{2,1,0:T(8,128)(2,1)} %concatenate.195, bf16[4,2160,360]{1,2,0:T(8,128)(2,1)} %concatenate.197), kind=kOutput, calls=%fused_computation.285 | convolution fusion | flops 497664000 | bytes 8064000 | tf_op jit(solution)/shard_map/dot_general | solution.py:98
  62.7 1.3 %concatenate.201 = bf16[4,80,1080]{2,1,0:T(8,128)(2,1)} concatenate(bf16[4,80,360]{2,1,0:T(8,128)(2,1)S(1)} %get-tuple-element.50, bf16[4,80,360]{2,1,0:T(8,128)(2,1)S(1)} %get-tuple-element.50, bf16[4,80,360]{2,1,0:T(8,128)(2,1)S(1)} %get-tuple-element.49), dimensions={2} | concatenate | bytes 1382400 | tf_op jit(solution)/shard_map/concatenate | solution.py:97
  63.9 3.8 %fusion.2 = f32[4,80,720]{2,1,0:T(8,128)S(1)} fusion(bf16[4,80,1080]{2,1,0:T(8,128)(2,1)} %concatenate.201, bf16[4,720,360]{1,2,0:T(8,128)(2,1)S(1)} %get-tuple-element.20, bf16[4,720,360]{1,2,0:T(8,128)(2,1)} %get-tuple-element.19), kind=kOutput, calls=%fused_computation.7 | convolution fusion | flops 516326400 | bytes 5760000 | tf_op jit(solution)/shard_map/dot_general | solution.py:98
  68.8 1.9 %collective-permute-start.5 = (f32[4,5,3,720]{3,2,1,0:T(4,128)S(1)}, f32[4,5,3,720]{3,2,1,0:T(4,128)S(1)}, u32[]{:S(2)}, u32[]{:S(2)}) collective-permute-start(f32[4,5,3,720]{3,2,1,0:T(4,128)S(1)} %get-tuple-element.46), channel_id=1, source_target_pairs={{0,4},{4,8},{8,12},{12,16},{16,20},{20,24},{24,28},{1,5},{5,9},{9,... | collective-permute-start | bytes 518408 | tf_op jit(solution)/shard_map/ppermute | solution.py:16
  70.7 2.6 %collective-permute-start.6 = (f32[4,5,3,720]{3,2,1,0:T(4,128)S(1)}, f32[4,5,3,720]{3,2,1,0:T(4,128)S(1)}, u32[]{:S(2)}, u32[]{:S(2)}) collective-permute-start(f32[4,5,3,720]{3,2,1,0:T(4,128)S(1)} %get-tuple-element.47), channel_id=1, source_target_pairs={{4,0},{8,4},{12,8},{16,12},{20,16},{24,20},{28,24},{5,1},{9,5},{13... | collective-permute-start | bytes 518408 | tf_op jit(solution)/shard_map/ppermute | solution.py:16
  73.5 0.5 fusion.66
  74.1 0.5 fusion.59
  74.6 4.5 %collective-permute-done.6 = f32[4,5,3,720]{3,2,1,0:T(4,128)S(1)} collective-permute-done((f32[4,5,3,720]{3,2,1,0:T(4,128)S(1)}, f32[4,5,3,720]{3,2,1,0:T(4,128)S(1)}, u32[]{:S(2)}, u32[]{:S(2)}) %collective-permute-start.6) | collective-permute-done | bytes 172832 | tf_op jit(solution)/shard_map/ppermute | solution.py:16
  80.0 0.5 copy-done.2
  80.5 1.0 fusion.12
  82.2 0.9 fusion.44
  83.1 3.4 %concatenate.214 = bf16[4,80,2160]{2,1,0:T(8,128)(2,1)} concatenate(bf16[4,80,720]{2,1,0:T(8,128)(2,1)S(1)} %get-tuple-element.24, bf16[4,80,720]{2,1,0:T(8,128)(2,1)S(1)} %get-tuple-element.24, bf16[4,80,720]{2,1,0:T(8,128)(2,1)} %get-tuple-element.23), dimensions={2} | concatenate | bytes 2764800 | tf_op jit(solution)/shard_map/concatenate | solution.py:97
  86.5 5.1 %fusion.137 = f32[4,80,360]{2,1,0:T(8,128)S(1)} fusion(bf16[4,80,2160]{2,1,0:T(8,128)(2,1)} %concatenate.214, bf16[4,2160,360]{1,2,0:T(8,128)(2,1)} %concatenate.197), kind=kOutput, calls=%fused_computation.286 | convolution fusion | flops 497664000 | bytes 8064000 | tf_op jit(solution)/shard_map/dot_general | solution.py:98
  91.9 1.3 %concatenate.218 = bf16[4,80,1080]{2,1,0:T(8,128)(2,1)} concatenate(bf16[4,80,360]{2,1,0:T(8,128)(2,1)S(1)} %get-tuple-element.41, bf16[4,80,360]{2,1,0:T(8,128)(2,1)S(1)} %get-tuple-element.41, bf16[4,80,360]{2,1,0:T(8,128)(2,1)S(1)} %get-tuple-element.40), dimensions={2} | concatenate | bytes 1382400 | tf_op jit(solution)/shard_map/concatenate | solution.py:97
  93.2 3.8 %fusion.1 = f32[4,80,720]{2,1,0:T(8,128)S(1)} fusion(bf16[4,80,1080]{2,1,0:T(8,128)(2,1)} %concatenate.218, bf16[4,720,360]{1,2,0:T(8,128)(2,1)S(1)} %get-tuple-element.20, bf16[4,720,360]{1,2,0:T(8,128)(2,1)} %get-tuple-element.19), kind=kOutput, calls=%fused_computation.6 | convolution fusion | flops 516326400 | bytes 5760000 | tf_op jit(solution)/shard_map/dot_general | solution.py:98
  97.8 2.6 %collective-permute-start.7 = (f32[5,8,720]{2,1,0:T(8,128)S(1)}, f32[5,8,720]{2,1,0:T(8,128)S(1)}, u32[]{:S(2)}, u32[]{:S(2)}) collective-permute-start(f32[5,8,720]{2,1,0:T(8,128)S(1)} %get-tuple-element.39), channel_id=1, source_target_pairs={{0,3},{1,0},{2,1},{3,2},{4,7},{5,4},{6,5},{7,6},{8,11},{9,8},{10,9... | collective-permute-start | bytes 345608 | tf_op jit(solution)/shard_map/ppermute | solution.py:16
  100.4 0.8 collective-permute-start.8
  101.2 2.3 %collective-permute-done.7 = f32[5,8,720]{2,1,0:T(8,128)S(1)} collective-permute-done((f32[5,8,720]{2,1,0:T(8,128)S(1)}, f32[5,8,720]{2,1,0:T(8,128)S(1)}, u32[]{:S(2)}, u32[]{:S(2)}) %collective-permute-start.7) | collective-permute-done | bytes 115232 | tf_op jit(solution)/shard_map/ppermute | solution.py:16
  103.5 7.4 %collective-permute-done.8 = f32[5,8,720]{2,1,0:T(8,128)S(1)} collective-permute-done((f32[5,8,720]{2,1,0:T(8,128)S(1)}, f32[5,8,720]{2,1,0:T(8,128)S(1)}, u32[]{:S(2)}, u32[]{:S(2)}) %collective-permute-start.8) | collective-permute-done | bytes 115232 | tf_op jit(solution)/shard_map/ppermute | solution.py:16
  111.0 0.8 pad_maximum_fusion.15
  (113 shorter events, 8.0 us)
Async XLA Ops:
  0.0 10.9 %copy-start = (s32[64]{0:T(128)S(1)}, s32[64]{0:T(128)}, u32[]{:S(2)}) copy-start(s32[64]{0:T(128)} %param.7) | copy-start | bytes 772
  3.3 33.1 %collective-permute-start.2 = (f32[56,720]{1,0:T(8,128)}, f32[56,720]{1,0:T(8,128)S(1)}, u32[]{:S(2)}, u32[]{:S(2)}) collective-permute-start(f32[56,720]{1,0:T(8,128)} %pad_maximum_fusion.24), channel_id=1, source_target_pairs={{0,3},{1,0},{2,1},{3,2},{4,7},{5,4},{6,5},{7,6},{8,11},{9,8},{10,9... | collective-permute-start | bytes 483848 | tf_op jit(solution)/shard_map/ppermute | solution.py:16
  7.4 29.1 %collective-permute-start.1 = (f32[56,720]{1,0:T(8,128)}, f32[56,720]{1,0:T(8,128)S(1)}, u32[]{:S(2)}, u32[]{:S(2)}) collective-permute-start(f32[56,720]{1,0:T(8,128)} %pad_maximum_fusion.23), channel_id=1, source_target_pairs={{0,2},{1,3},{2,0},{3,1},{4,6},{5,7},{6,4},{7,5},{8,10},{9,11},{10,... | collective-permute-start | bytes 483848 | tf_op jit(solution)/shard_map/ppermute | solution.py:16
  8.1 28.5 %collective-permute-start = (f32[56,720]{1,0:T(8,128)}, f32[56,720]{1,0:T(8,128)S(1)}, u32[]{:S(2)}, u32[]{:S(2)}) collective-permute-start(f32[56,720]{1,0:T(8,128)} %pad_maximum_fusion.22), channel_id=1, source_target_pairs={{0,1},{1,2},{2,3},{3,0},{4,5},{5,6},{6,7},{7,4},{8,9},{9,10},{10,1... | collective-permute-start | bytes 483848 | tf_op jit(solution)/shard_map/ppermute | solution.py:16
  26.1 10.4 %copy-start.9 = (f32[40,720]{1,0:T(8,128)S(1)}, f32[40,720]{1,0:T(8,128)}, u32[]{:S(2)}) copy-start(f32[40,720]{1,0:T(8,128)} %get-tuple-element.58) | copy-start | bytes 345604
  37.1 7.9 %copy-start.7 = (f32[4,8,721]{2,1,0:T(8,128)}, f32[4,8,721]{2,1,0:T(8,128)S(1)}, u32[]{:S(2)}) copy-start(f32[4,8,721]{2,1,0:T(8,128)S(1)} %maximum_bitcast_fusion.2) | copy-start | bytes 276868
  37.2 7.7 %copy-start.5 = (f32[4,8,721]{2,1,0:T(8,128)}, f32[4,8,721]{2,1,0:T(8,128)S(1)}, u32[]{:S(2)}) copy-start(f32[4,8,721]{2,1,0:T(8,128)S(1)} %get-tuple-element.73) | copy-start | bytes 276868
  37.3 7.6 %copy-start.10 = (pred[4,8,721]{2,1,0:T(8,128)(4,1)}, pred[4,8,721]{2,1,0:T(8,128)(4,1)S(1)}, u32[]{:S(2)}) copy-start(pred[4,8,721]{2,1,0:T(8,128)(4,1)S(1)} %broadcast_compare_fusion) | copy-start | bytes 69220
  37.4 12.8 %collective-permute-start.4 = (f32[4,5,3,720]{3,2,1,0:T(4,128)S(1)}, f32[4,5,3,720]{3,2,1,0:T(4,128)S(1)}, u32[]{:S(2)}, u32[]{:S(2)}) collective-permute-start(f32[4,5,3,720]{3,2,1,0:T(4,128)S(1)} %get-tuple-element.55), channel_id=1, source_target_pairs={{0,4},{4,8},{8,12},{12,16},{16,20},{20,24},{24,28},{1,5},{5,9},{9,... | collective-permute-start | bytes 518408 | tf_op jit(solution)/shard_map/ppermute | solution.py:16
  42.1 7.9 %collective-permute-start.3 = (f32[4,16,720]{2,1,0:T(8,128)S(1)}, f32[4,16,720]{2,1,0:T(8,128)S(1)}, u32[]{:S(2)}, u32[]{:S(2)}) collective-permute-start(f32[4,16,720]{2,1,0:T(8,128)S(1)} %pad_maximum_fusion.20), channel_id=1, source_target_pairs={{4,0},{8,4},{12,8},{16,12},{20,16},{24,20},{28,24},{5,1},{9,5},{13... | collective-permute-start | bytes 552968 | tf_op jit(solution)/shard_map/ppermute | solution.py:16
  50.2 1.0 copy-start.1
  50.2 1.0 copy-start.3
  50.7 0.7 copy-start.17
  51.4 1.0 copy-start.19
  57.3 5.1 %copy-start.12 = (f32[4,180]{1,0:T(4,128)S(1)}, f32[4,180]{1,0:T(4,128)}, u32[]{:S(2)}) copy-start(f32[4,180]{1,0:T(4,128)} %compare_select_fusion) | copy-start | bytes 8644
  57.3 5.1 %copy-start.15 = (s32[40]{0:T(128)S(1)}, s32[40]{0:T(128)}, u32[]{:S(2)}) copy-start(s32[40]{0:T(128)} %and_select_fusion.1) | copy-start | bytes 484
  67.7 0.6 copy-start.14
  68.6 5.5 %copy-start.6 = (f32[4,8,721]{2,1,0:T(8,128)S(1)}, f32[4,8,721]{2,1,0:T(8,128)}, u32[]{:S(2)}) copy-start(f32[4,8,721]{2,1,0:T(8,128)} %copy-done.5) | copy-start | bytes 276868
  68.6 5.5 %copy-start.8 = (f32[4,8,721]{2,1,0:T(8,128)S(1)}, f32[4,8,721]{2,1,0:T(8,128)}, u32[]{:S(2)}) copy-start(f32[4,8,721]{2,1,0:T(8,128)} %copy-done.7) | copy-start | bytes 276868
  68.6 5.5 %copy-start.11 = (pred[4,8,721]{2,1,0:T(8,128)(4,1)S(1)}, pred[4,8,721]{2,1,0:T(8,128)(4,1)}, u32[]{:S(2)}) copy-start(pred[4,8,721]{2,1,0:T(8,128)(4,1)} %copy-done.10) | copy-start | bytes 69220
  68.8 5.8 %collective-permute-start.5 = (f32[4,5,3,720]{3,2,1,0:T(4,128)S(1)}, f32[4,5,3,720]{3,2,1,0:T(4,128)S(1)}, u32[]{:S(2)}, u32[]{:S(2)}) collective-permute-start(f32[4,5,3,720]{3,2,1,0:T(4,128)S(1)} %get-tuple-element.46), channel_id=1, source_target_pairs={{0,4},{4,8},{8,12},{12,16},{16,20},{20,24},{24,28},{1,5},{5,9},{9,... | collective-permute-start | bytes 518408 | tf_op jit(solution)/shard_map/ppermute | solution.py:16
  70.7 8.4 %collective-permute-start.6 = (f32[4,5,3,720]{3,2,1,0:T(4,128)S(1)}, f32[4,5,3,720]{3,2,1,0:T(4,128)S(1)}, u32[]{:S(2)}, u32[]{:S(2)}) collective-permute-start(f32[4,5,3,720]{3,2,1,0:T(4,128)S(1)} %get-tuple-element.47), channel_id=1, source_target_pairs={{4,0},{8,4},{12,8},{16,12},{20,16},{24,20},{28,24},{5,1},{9,5},{13... | collective-permute-start | bytes 518408 | tf_op jit(solution)/shard_map/ppermute | solution.py:16
  79.5 0.9 copy-start.2
  79.5 1.0 copy-start.4
  79.5 1.0 copy-start.18
  80.5 1.0 copy-start.20
  86.5 5.1 %copy-start.13 = (f32[4,180]{1,0:T(4,128)S(1)}, f32[4,180]{1,0:T(4,128)}, u32[]{:S(2)}) copy-start(f32[4,180]{1,0:T(4,128)} %compare_select_fusion) | copy-start | bytes 8644
  86.5 5.1 %copy-start.16 = (s32[40]{0:T(128)S(1)}, s32[40]{0:T(128)}, u32[]{:S(2)}) copy-start(s32[40]{0:T(128)} %and_select_fusion.1) | copy-start | bytes 484
  97.0 0.7 copy-start.21
  97.8 5.7 %collective-permute-start.7 = (f32[5,8,720]{2,1,0:T(8,128)S(1)}, f32[5,8,720]{2,1,0:T(8,128)S(1)}, u32[]{:S(2)}, u32[]{:S(2)}) collective-permute-start(f32[5,8,720]{2,1,0:T(8,128)S(1)} %get-tuple-element.39), channel_id=1, source_target_pairs={{0,3},{1,0},{2,1},{3,2},{4,7},{5,4},{6,5},{7,6},{8,11},{9,8},{10,9... | collective-permute-start | bytes 345608 | tf_op jit(solution)/shard_map/ppermute | solution.py:16
  100.4 10.5 %collective-permute-start.8 = (f32[5,8,720]{2,1,0:T(8,128)S(1)}, f32[5,8,720]{2,1,0:T(8,128)S(1)}, u32[]{:S(2)}, u32[]{:S(2)}) collective-permute-start(f32[5,8,720]{2,1,0:T(8,128)S(1)} %get-tuple-element.38), channel_id=1, source_target_pairs={{0,2},{1,3},{2,0},{3,1},{4,6},{5,7},{6,4},{7,5},{8,10},{9,11},{10,... | collective-permute-start | bytes 345608 | tf_op jit(solution)/shard_map/ppermute | solution.py:16
  101.2 9.7 %collective-permute-start.9 = (f32[5,8,720]{2,1,0:T(8,128)S(1)}, f32[5,8,720]{2,1,0:T(8,128)S(1)}, u32[]{:S(2)}, u32[]{:S(2)}) collective-permute-start(f32[5,8,720]{2,1,0:T(8,128)S(1)} %get-tuple-element.37), channel_id=1, source_target_pairs={{0,1},{1,2},{2,3},{3,0},{4,5},{5,6},{6,7},{7,4},{8,9},{9,10},{10,1... | collective-permute-start | bytes 345608 | tf_op jit(solution)/shard_map/ppermute | solution.py:16

commit v9 on v7

--- a/solution.py
+++ b/solution.py
@@ -194,13 +194,6 @@
     lat_index = lax.axis_index("lat")
     circle = lon_cols * lon_devices
     total_rows = lat_rows * lat_devices
-    row_global = lat_index * lat_rows + jnp.arange(lat_rows, dtype=jnp.int32)
-    face_global = lat_index * lat_rows + jnp.arange(lat_rows + 1, dtype=jnp.int32)
-    face_angle = (face_global.astype(jnp.float32) / total_rows - 0.5) * math.pi
-    face_weight = jnp.where(
-        (face_global == 0) | (face_global == total_rows), 0.0, jnp.cos(face_angle)
-    )
-    center_weight = jnp.cos(((row_global.astype(jnp.float32) + 0.5) / total_rows - 0.5) * math.pi)
     is_south = lat_index == 0
     is_north = lat_index == lat_devices - 1
 
@@ -224,43 +217,43 @@
     state = payload[:, :count].reshape(lon_devices, tracer_count, lat_rows, lon_cols)
     cx = payload[:, None, count : count + lat_rows]
     cy = payload[:, None, count + lat_rows :]
-    east_courant = jnp.concatenate([jnp.roll(cx[..., lon_cols - 1 :], -1, axis=0), cx], axis=3)
-
-    held_global = lat_index * lat_rows + jnp.arange(count, dtype=jnp.int32) % lat_rows
-    polar = (held_global < total_rows // 4) | (held_global >= total_rows - total_rows // 4)
-    cut = jnp.take(cutoffs, held_global)
+
+    wide_rows = lat_rows + 2 * HALO
+    deep = 2 * HALO
     per_class = KMAX // lon_devices
     k = lon_devices * jnp.arange(per_class, dtype=jnp.int32)[None, :] + jnp.arange(
         lon_devices, dtype=jnp.int32
     )[:, None]
     scale = jnp.where(k == 0, 1.0 / circle, 2.0 / circle).astype(jnp.float32)
-    weights = jnp.where(k[:, None, :] < cut[None, :, None], scale[:, None, :], 0.0)
+
+    def row_tables(first_row, rows_out):
+        held = lat_index * lat_rows + first_row + jnp.arange(tracer_count * rows_out) % rows_out
+        polar = (held < total_rows // 4) | (held >= total_rows - total_rows // 4)
+        cut = jnp.take(cutoffs, jnp.clip(held, 0, total_rows - 1))
+        weights = jnp.where(k[:, None, :] < cut[None, :, None], scale[:, None, :], 0.0)
+        return polar, weights
+
+    tables = [row_tables(-HALO, wide_rows), row_tables(0, lat_rows)]
     basis = product_basis(lon_devices, lon_cols, circle)
     roots = root_table(
         lon_devices, (lax.axis_index("lon") - jnp.arange(lon_devices, dtype=jnp.int32)) % lon_devices
     )
 
-    for substep in range(SUBSTEPS):
-        south_in = shift(state[:, :, lat_rows - HALO :], "lat", 1, False)
-        if substep == 0:
-            going = jnp.concatenate(
-                [state[:, :, :HALO].reshape(lon_devices, tracer_count * HALO, lon_cols), cy[:, 0, :1]],
-                axis=1,
-            )
-            coming = shift(going, "lat", -1, False)
-            north_in = coming[:, : tracer_count * HALO].reshape(
-                lon_devices, tracer_count, HALO, lon_cols
-            )
-            north_cy = jnp.where(is_north, 0.0, coming[:, None, tracer_count * HALO :])
-            north_courant = jnp.concatenate([cy, north_cy], axis=2)
-        else:
-            north_in = shift(state[:, :, :HALO], "lat", -1, False)
-        edge = jnp.where(is_south, state[:, :, :HALO], state[:, :, lat_rows - HALO :])
-        far = jnp.roll(edge, lon_devices // 2, axis=0)
-        far_rev = jnp.concatenate([far[:, :, 2:3], far[:, :, 1:2], far[:, :, 0:1]], axis=2)
-        south_rows = jnp.where(is_south, far_rev, south_in)
-        north_rows = jnp.where(is_north, far_rev, north_in)
-        extended = jnp.concatenate([south_rows, state, north_rows], axis=2)
+    def flip(rows):
+        return jnp.concatenate([rows[:, :, i : i + 1] for i in range(rows.shape[2] - 1, -1, -1)], axis=2)
+
+    def poles(south, band, north, depth):
+        edge = jnp.where(is_south, band[:, :, :depth], band[:, :, band.shape[2] - depth :])
+        far = flip(jnp.roll(edge, lon_devices // 2, axis=0))
+        return jnp.where(is_south, far, south), jnp.where(is_north, far, north)
+
+    def advance(extended, first_row, rows_out, cx_rows, cy_faces, polar, weights):
+        faces = lat_index * lat_rows + first_row + jnp.arange(rows_out + 1, dtype=jnp.int32)
+        face_angle = (faces.astype(jnp.float32) / total_rows - 0.5) * math.pi
+        face_weight = jnp.where((faces == 0) | (faces == total_rows), 0.0, jnp.cos(face_angle))
+        cells = lat_index * lat_rows + first_row + jnp.arange(rows_out, dtype=jnp.int32)
+        center_weight = jnp.cos(((cells.astype(jnp.float32) + 0.5) / total_rows - 0.5) * math.pi)
+        state = extended[:, :, HALO : HALO + rows_out]
         wrapped = jnp.concatenate(
             [
                 jnp.roll(state[..., lon_cols - HALO :], -1, axis=0),
@@ -269,17 +262,67 @@
             ],
             axis=3,
         )
+        east_courant = jnp.concatenate(
+            [jnp.roll(cx_rows[..., lon_cols - 1 :], -1, axis=0), cx_rows], axis=3
+        )
         zonal = ppm_flux(wrapped, east_courant, 3, lon_cols)
-        meridional = ppm_flux(extended, north_courant, 2, lat_rows) * face_weight[:, None]
+        meridional = ppm_flux(extended, cy_faces, 2, rows_out) * face_weight[:, None]
         change = (
             zonal[..., 1:]
             - zonal[..., :-1]
             + (meridional[:, :, 1:] - meridional[:, :, :-1]) / center_weight[:, None]
         )
         state = state - change
-        rows = state.reshape(lon_devices, count, lon_cols)
+        rows = state.reshape(lon_devices, tracer_count * rows_out, lon_cols)
         rows = filter_rows(rows, basis, roots, weights, polar, 0)
-        state = rows.reshape(lon_devices, tracer_count, lat_rows, lon_cols)
+        return rows.reshape(lon_devices, tracer_count, rows_out, lon_cols)
+
+    up = jnp.concatenate(
+        [
+            state[:, :, lat_rows - deep :].reshape(lon_devices, tracer_count * deep, lon_cols),
+            cx[:, 0, lat_rows - HALO :],
+            cy[:, 0, lat_rows - HALO :],
+        ],
+        axis=1,
+    )
+    down = jnp.concatenate(
+        [
+            state[:, :, :deep].reshape(lon_devices, tracer_count * deep, lon_cols),
+            cx[:, 0, :HALO],
+            cy[:, 0, : HALO + 1],
+        ],
+        axis=1,
+    )
+    from_south = shift(up, "lat", 1, False)
+    from_north = shift(down, "lat", -1, False)
+    rows6 = tracer_count * deep
+    south = from_south[:, :rows6].reshape(lon_devices, tracer_count, deep, lon_cols)
+    north = from_north[:, :rows6].reshape(lon_devices, tracer_count, deep, lon_cols)
+    south, north = poles(south, state, north, deep)
+    extended = jnp.concatenate([south, state, north], axis=2)
+    cx_wide = jnp.concatenate(
+        [from_south[:, rows6 : rows6 + HALO], cx[:, 0], from_north[:, rows6 : rows6 + HALO]], axis=1
+    )[:, None]
+    cy_wide = jnp.concatenate(
+        [from_south[:, rows6 + HALO :], cy[:, 0], from_north[:, rows6 + HALO :]], axis=1
+    )[:, None]
+
+    wide = advance(extended, -HALO, wide_rows, cx_wide, cy_wide, *tables[0])
+    south, north = poles(
+        wide[:, :, :HALO], wide[:, :, HALO : HALO + lat_rows], wide[:, :, HALO + lat_rows :], HALO
+    )
+    extended = jnp.concatenate([south, wide[:, :, HALO : HALO + lat_rows], north], axis=2)
+    state = advance(
+        extended, 0, lat_rows, cx, cy_wide[:, :, HALO : HALO + lat_rows + 1], *tables[1]
+    )
+    for substep in range(2, SUBSTEPS):
+        south_in = shift(state[:, :, lat_rows - HALO :], "lat", 1, False)
+        north_in = shift(state[:, :, :HALO], "lat", -1, False)
+        south, north = poles(south_in, state, north_in, HALO)
+        extended = jnp.concatenate([south, state, north], axis=2)
+        state = advance(
+            extended, 0, lat_rows, cx, cy_wide[:, :, HALO : HALO + lat_rows + 1], *tables[1]
+        )
 
     back = [state[0]] + [
         shift(state[(lon_devices - by) % lon_devices], "lon", by, True) for by in range(1, lon_devices)
@@ -295,7 +338,7 @@
 
 def on_device(tracers, courant_x, courant_y, cutoffs):
     field_count = tracers.shape[0] * tracers.shape[1]
-    if tracers.shape[1] == lax.axis_size("lon") and tracers.shape[2] >= HALO:
+    if tracers.shape[1] == lax.axis_size("lon") and tracers.shape[2] >= 2 * HALO and SUBSTEPS >= 2:
         return transposed_path(tracers, courant_x, courant_y, cutoffs)
     return tiled_path(tracers, courant_x, courant_y, cutoffs)
 

time: 76 us -> 90.3 us (1.19)
  other arithmetic: 16.6 us -> 36.7 us
  waiting for transfers between devices: 24.9 us -> 12.6 us
  local copies, waits for them, and re-layouts: 5.57 us -> 15.1 us
  starting transfers between devices: 18.9 us -> 14.5 us
    ppermute x10 -> x8, waiting for transfers between devices: 24.9 us -> 12.6 us  [shift(): return lax.ppermute(x, axis, pairs)]
    slice x10 -> x19, local copies, waits for them, and re-layouts: 0.71 us -> 6.97 us  [the longest x2 1.27 us: transposed_path(): from_south[:, :rows6].reshape(lon_devices, tracer_count, deep, lon_cols)]
    ppermute x10 -> x8, starting transfers between devices: 18.9 us -> 14.5 us  [shift(): return lax.ppermute(x, axis, pairs)]
    reduce_sum x2, other arithmetic: 0.76 us -> 4.84 us  [filter_rows(): z_re = jnp.sum(cos_dr[:, :, None, None] * rows[None], axis=1)]
    concatenate x6 -> x9, other arithmetic: 0.84 us -> 4.45 us  [the longest x1 1.05 us: poles(): far = flip(jnp.roll(edge, lon_devices // 2, axis=0))]
    select_n x7 -> x9, other arithmetic: 0.55 us -> 2.85 us  [the longest x2 1.25 us: advance(): jnp.where((faces == 0) | (faces == total_rows), 0.0, jnp.cos(face_angle))]
    concatenate x0 -> x1, local copies, waits for them, and re-layouts: none -> 2.06 us  [flip(): jnp.concatenate([rows[:, :, i:i + 1] for i in range(rows.shape[2] - 1, -1...]
    reduce_sum x2, other arithmetic: 0.69 us -> 2.12 us  [filter_rows(): jnp.sum(cos_dr[:, :, None, None] * w_re[:, None] - sin_dr[:, :, None, Non...]
  transfers between devices with their start and end apart: 10 -> 8, of which waited for: 5 -> 4; matrix products, arithmetic and copies ran while one was open for 12% -> 24% of each run, Pallas kernels for 0% -> 0%
where the time goes in v9:
time: 90.3 us; the launch traced here: 89.5 us
  other arithmetic  36.7 us (41%)
  local copies, waits for them, and re-layouts  15.1 us (17%)
  starting transfers between devices  14.5 us (16%)
  waiting for transfers between devices  12.6 us (14%)
  matrix products  9.77 us (11%)
    ppermute x8, starting transfers between devices, shift(): return lax.ppermute(x, axis, pairs)  14.5 us
    ppermute x8, waiting for transfers between devices, shift(): return lax.ppermute(x, axis, pairs)  12.6 us
    dot_general x2, matrix products, filter_rows(): lax.dot_general(spec, basis, (((2,), (2,)), ((0,), (0,))), precision=MATM...  5.35 us
    reduce_sum x2, other arithmetic, filter_rows(): z_re = jnp.sum(cos_dr[:, :, None, None] * rows[None], axis=1)  4.84 us
    dot_general x2, matrix products, filter_rows(): lax.dot_general(z, basis, (((2,), (1,)), ((0,), (0,))), precision=MATMUL_...  4.42 us
    sub x4, other arithmetic, ppm_flux(): 7.0 / 12.0  2.35 us
    mul x5, other arithmetic, ppm_flux(): return courant * jnp.where(courant >= 0.0, from_left, from_right)  2.23 us
    sub x1, other arithmetic, product_basis(): cos_qk = (ca * cb - sa * sb).reshape(tiles, cols, per_class)  2.23 us
  transfers between devices with their start and end apart: 8, of which 4 were waited for; matrix products, arithmetic and copies ran while one was open for 24% of the time, Pallas kernels for 0%

profile of v9, /device:TPU:3, one launch (start us, length us, event | category | flops | bytes accessed | tf_op | source)
XLA Modules:
  0.0 89.5 jit_solution(4654731368738996351)
XLA Ops:
  0.0 1.1 %dynamic-slice_bitcast_fusion.3 = (f32[40,720]{1,0:T(8,128)S(1)}, f32[40,720]{1,0:T(8,128)S(1)}, f32[40,720]{1,0:T(8,128)S(1)}, f32[40,720]{1,0:T(8,128)S(1)}) fusion(f32[5,4,8,720]{3,2,1,0:T(8,128)} %param.4, s32[]{:T(128)S(6)} %select_n.418, s32[]{:T(128)S(6)} %select_n.422, s32[]{:T(128)S(6)} %select_n.420, s32[]{:T(128)S(6)} %select_n.424), kind=kLoop, calls=%fused_computation.204 | loop fusion | bytes 921616 | tf_op jit(solution)/shard_map/reshape | solution.py:206
  1.1 1.5 %dynamic-slice_bitcast_fusion.10 = (f32[8,720]{1,0:T(8,128)S(1)}, f32[8,720]{1,0:T(8,128)S(1)}, f32[8,720]{1,0:T(8,128)S(1)}, f32[8,720]{1,0:T(8,128)S(1)}, f32[...) fusion(f32[4,8,720]{2,1,0:T(8,128)} %param.6, s32[]{:T(128)S(6)} %select_n.418, ...), kind=kLoop, calls=%fused_computation.241 | loop fusion | bytes 368656 | tf_op jit(solution)/shard_map/jit(dynamic_index_in_dim)/squeeze | solution.py:208
  2.6 0.7 pad_maximum_fusion.16
  3.3 3.3 %collective-permute-start.2 = (f32[56,720]{1,0:T(8,128)}, f32[56,720]{1,0:T(8,128)S(1)}, u32[]{:S(2)}, u32[]{:S(2)}) collective-permute-start(f32[56,720]{1,0:T(8,128)} %pad_maximum_fusion.16), channel_id=1, source_target_pairs={{0,3},{1,0},{2,1},{3,2},{4,7},{5,4},{6,5},{7,6},{8,11},{9,8},{10,9... | collective-permute-start | bytes 483848 | tf_op jit(solution)/shard_map/ppermute | solution.py:17
  6.6 0.7 pad_maximum_fusion.15
  7.3 0.7 pad_maximum_fusion.14
  9.1 0.6 or_select_fusion.1
  10.9 0.6 or_select_fusion
  12.1 0.8 gather_fusion.1
  13.4 1.2 %gather_fusion = s32[70]{0:T(128)S(1)} fusion(s32[64]{0:T(128)S(1)} %copy-done, s32[1024]{0:T(1024)S(1)} %pad_clamp_fusion.1), kind=kCustom, calls=%fused_computation | custom fusion | bytes 840 | tf_op jit(solution)/shard_map/jit(_take)/gather | solution.py:232
  15.2 0.7 fusion.123
  16.3 0.6 fusion.104
  16.9 2.2 %multiply_subtract_fusion = (f32[4,30,24,180]{3,2,1,0:T(8,128)S(1)}, f32[4,30,24,180]{3,2,1,0:T(8,128)}) fusion(f32[4,24,180]{2,1,0:T(8,128)S(1)} %get-tuple-element.91, f32[4,30,180]{2,1,0:T(8,128)S(1)} %get-tuple-element.89, f32[4,24,180]{2,1,0:T(8,128)S(1)} %get-tuple-element.90, f32[4,30,180]{2,1,0:T(8,128)S(1)} %get-tuple-element.88), kind=kLoop, calls=%fused_computation.7 | loop fusion | flops 3110400 | bytes 4458240 | tf_op jit(solution)/shard_map/sub | solution.py:33
  19.7 0.7 maximum_bitcast_fusion.2
  20.5 0.8 collective-permute-done.1
  21.3 1.0 %pad_maximum_fusion.6 = f32[4,56,720]{2,1,0:T(8,128)S(1)} fusion(f32[1,56,720]{2,1,0:T(8,128)S(1)} %bitcast.133, f32[1,56,720]{2,1,0:T(8,128)S(1)} %bitcast.135, f32[1,56,720]{2,1,0:T(8,128)} %bitcast.7, f32[1,56,720]{2,1,0:T(8,128)S(1)} %maximum_bitcast_fusion.2), kind=kLoop, calls=%fused_computation.103 | loop fusion | flops 483840 | bytes 1290240 | tf_op jit(solution)/shard_map/stack | solution.py:216
  22.3 0.8 pad_maximum_fusion.20
  23.2 0.7 slice.519
  24.3 0.8 pad_maximum_fusion.7
  25.2 4.1 %collective-permute-start.3 = (f32[4,36,720]{2,1,0:T(8,128)}, f32[4,36,720]{2,1,0:T(8,128)}, u32[]{:S(2)}, u32[]{:S(2)}) collective-permute-start(f32[4,36,720]{2,1,0:T(8,128)} %pad_maximum_fusion.7), channel_id=1, source_target_pairs={{0,4},{4,8},{8,12},{12,16},{16,20},{20,24},{24,28},{1,5},{5,9},{9,... | collective-permute-start | bytes 1244168 | tf_op jit(solution)/shard_map/ppermute | solution.py:17
  29.5 0.8 pad_maximum_fusion.8
  30.3 1.9 %collective-permute-start.4 = (f32[4,37,720]{2,1,0:T(8,128)}, f32[4,37,720]{2,1,0:T(8,128)}, u32[]{:S(2)}, u32[]{:S(2)}) collective-permute-start(f32[4,37,720]{2,1,0:T(8,128)} %pad_maximum_fusion.8), channel_id=1, source_target_pairs={{4,0},{8,4},{12,8},{16,12},{20,16},{24,20},{28,24},{5,1},{9,5},{13... | collective-permute-start | bytes 1278728 | tf_op jit(solution)/shard_map/ppermute | solution.py:17
  32.2 1.1 %pad_maximum_fusion.22 = (f32[4,5,1,720]{3,2,1,0:T(1,128)}, f32[4,5,1,720]{3,2,1,0:T(1,128)}, f32[4,5,1,720]{3,2,1,0:T(1,128)}, f32[4,5,1,720]{3,2,1,0:T(1,128)}...) fusion(f32[2,5,6,720]{3,2,1,0:T(8,128)S(1)} %get-tuple-element.58, f32[2,5,6,720]{3,2,1,0:T(8,128)S(1)} %get-tuple-element.57), kind=kLoop, calls=%fused_computation.221 | loop fusion | flops 86400 | bytes 691200 | tf_op jit(solution)/shard_map/jit(_roll_static)/concatenate | solution.py:247
  33.3 2.1 %concatenate.181 = f32[4,5,6,720]{3,2,1,0:T(8,128)} concatenate(f32[4,5,1,720]{3,2,1,0:T(1,128)} %get-tuple-element.56, f32[4,5,1,720]{3,2,1,0:T(1,128)} %get-tuple-element.55, f32[4,5,1,720]{3,2,1,0:T(1,128)} %get-tuple-element.54, f32[4,5,1,720]{3,2,1,0:T(1,128)} %get-tuple-element.53, f32[4,5,1,720]{3,2,1,0:T(1,128)} %get-tuple-element.52, f32[4,5,1,720]{3,2,1,0:T(1,128)} %get-tuple-element.51), dimensions={2} | concatenate | bytes 691200 | tf_op jit(solution)/shard_map/concatenate | solution.py:243
  35.4 0.8 maximum_bitcast_fusion.5
  36.1 0.8 maximum_bitcast_fusion.3
  37.1 1.0 %slice.480 = f32[4,30,720]{2,1,0:T(8,128)S(1)} slice(f32[4,36,720]{2,1,0:T(8,128)} %collective-permute-done.3), slice={[0:4], [0:30], [0:720]} | slice | bytes 691200 | tf_op jit(solution)/shard_map/slice | solution.py:299
  38.4 1.0 %fusion.146 = (f32[4,3,720]{2,1,0:T(4,128)S(1)}, f32[4,3,720]{2,1,0:T(4,128)S(1)}) fusion(f32[4,36,720]{2,1,0:T(8,128)} %collective-permute-done.3), kind=kLoop, calls=%fused_computation.308 | loop fusion | bytes 138240 | tf_op jit(solution)/shard_map/slice | solution.py:304
  39.4 2.8 %collective-permute-done.4 = f32[4,37,720]{2,1,0:T(8,128)} collective-permute-done((f32[4,37,720]{2,1,0:T(8,128)}, f32[4,37,720]{2,1,0:T(8,128)}, u32[]{:S(2)}, u32[]{:S(2)}) %collective-permute-start.4) | collective-permute-done | bytes 426272 | tf_op jit(solution)/shard_map/ppermute | solution.py:17
  42.2 0.9 %slice.499 = f32[4,4,720]{2,1,0:T(4,128)S(1)} slice(f32[4,37,720]{2,1,0:T(8,128)} %collective-permute-done.4), slice={[0:4], [33:37], [0:720]} | slice | bytes 92160 | tf_op jit(solution)/shard_map/slice | solution.py:307
  43.2 1.0 %fusion.139 = (f32[4,1,15,720]{3,2,0,1:T(8,128)S(1)}, f32[4,15,720]{2,1,0:T(8,128)S(1)}, f32[4,15,720]{2,1,0:T(8,128)S(1)}, f32[4,15,720]{2,1,0:T(8,128)S(1)}) fusion(f32[4,4,720]{2,1,0:T(4,128)S(1)} %slice.499, f32[4,8,720]{2,1,0:T(8,128)} %copy-done.3, f32[4,3,720]{2,1,0:T(4,128)S(1)} %get-tuple-element.45), kind=kLoop, calls=%fused_computation.301 | loop fusion | flops 259200 | bytes 864000 | tf_op jit(solution)/shard_map/broadcast_in_dim | solution.py:306
  44.2 1.0 %slice.483 = f32[4,30,720]{2,1,0:T(8,128)S(1)} slice(f32[4,37,720]{2,1,0:T(8,128)} %collective-permute-done.4), slice={[0:4], [0:30], [0:720]} | slice | bytes 691200 | tf_op jit(solution)/shard_map/slice | solution.py:300
  46.8 0.9 %slice.486 = f32[4,3,720]{2,1,0:T(4,128)S(1)} slice(f32[4,37,720]{2,1,0:T(8,128)} %collective-permute-done.4), slice={[0:4], [30:33], [0:720]} | slice | bytes 69120 | tf_op jit(solution)/shard_map/slice | solution.py:304
  48.8 0.9 %fusion.57 = (f32[4,5,14,723]{3,2,1,0:T(8,128)S(1)}, f32[4,5,14,723]{3,2,1,0:T(8,128)S(1)}, f32[4,5,14,723]{3,2,1,0:T(8,128)S(1)}) fusion(f32[4,5,14,726]{3,2,1,0:T(8,128)S(1)} %maximum_maximum_fusion, f32[4,5,14,720]{3,2,1,0:T(8,128)S(1)} %slice.484, f32[1,5,14,3]{3,2,1,0:T(8,128)S(1)} %get-tuple-element.23, f32[3,5,14,3]{3,2,1,0:T(8,128)S(1)} %get-tuple-element.21, ...), kind=kLoop, calls=%fused_computation.85 | loop fusion | flops 1821960 | bytes 4861920 | tf_op jit(solution)/shard_map/sub | solution.py:43
  49.8 0.9 %fusion.38 = f32[4,5,15,720]{3,2,1,0:T(8,128)S(1)} fusion(f32[4,5,20,720]{3,2,1,0:T(8,128)S(1)} %pad_maximum_fusion.1, f32[4,5,17,720]{3,2,1,0:T(8,128)S(1)} %fusion.5, f32[15]{0:T(128)S(1)} %copy-done.17, f32[4,15,720]{2,1,0:T(8,128)S(1)} %get-tuple-element.74, f32[4,15,720]{2,1,0:T(8,128)S(1)} %get-tuple-element.73, ...), kind=kLoop, calls=%fused_computation.61 | loop fusion | flops 4536000 | bytes 5745660 | tf_op jit(solution)/shard_map/mul | solution.py:269
  50.7 0.8 fusion.50
  52.7 4.5 %multiply_reduce_fusion.1 = (f32[4,70,720]{2,1,0:T(8,128)S(1)}, f32[4,70,720]{2,1,0:T(8,128)S(1)}) fusion(f32[4,70,720]{2,0,1:T(4,128)S(1)} %bitcast.125, f32[4,4]{1,0:T(4,128)S(1)} %copy-done.8, f32[4,4]{1,0:T(4,128)S(1)} %copy-done.7), kind=kLoop, calls=%fused_computation.5 | loop fusion | flops 2822400 | bytes 2419328 | tf_op jit(solution)/shard_map/reduce_sum | solution.py:89
  57.3 2.5 %fusion = f32[4,140,360]{2,1,0:T(8,128)S(1)} fusion(f32[4,70,720]{2,1,0:T(8,128)S(1)} %neg.12, f32[4,70,720]{2,1,0:T(8,128)S(1)} %get-tuple-element.5, f32[4,720,180]{2,1,0:T(8,128)S(1)} %bitcast.117, f32[4,720,180]{2,1,0:T(8,128)S(1)} %bitcast.113), kind=kOutput, calls=%fused_computation.11 | convolution fusion | flops 872352000 | bytes 6566400 | tf_op jit(solution)/shard_map/dot_general | solution.py:93
  60.0 2.7 %fusion.62 = f32[4,140,720]{2,1,0:T(8,128)S(1)} fusion(f32[4,70,180]{2,1,0:T(8,128)S(1)} %get-tuple-element.33, f32[4,70,180]{2,1,0:T(8,128)S(1)} %get-tuple-element.14, f32[4,70,180]{2,1,0:T(8,128)S(1)} %get-tuple-element.15, f32[4,720,180]{2,1,0:T(8,128)S(1)} %bitcast.118, f32[4,720,180]{2,1,0:T(8,128)S(1)} %bitcast.114), kind=kOutput, calls=%fused_computation.95 | convolution fusion | flops 872553600 | bytes 6364800 | tf_op jit(solution)/shard_map/dot_general | solution.py:102
  62.9 1.8 %subtract_reduce_fusion = f32[4,70,720]{2,0,1:T(4,128)S(1)} fusion(f32[4,70,720]{2,1,0:T(8,128)S(1)} %get-tuple-element.20, f32[4,70,720]{2,1,0:T(8,128)S(1)} %get-tuple-element.19, f32[4,4]{1,0:T(4,128)S(1)} %copy-done.7, f32[4,4]{1,0:T(4,128)S(1)} %copy-done.8), kind=kLoop, calls=%fused_computation.3 | loop fusion | flops 3024000 | bytes 2419328 | tf_op jit(solution)/shard_map/reduce_sum | solution.py:104
  67.1 1.0 %fusion.16 = f32[4,5,9,720]{3,2,1,0:T(8,128)S(1)} fusion(f32[4,5,8,720]{3,2,1,0:T(8,128)S(1)} %slice.517, f32[4,5,3,720]{3,2,1,0:T(4,128)S(1)} %get-tuple-element.26, f32[4,5,3,720]{3,2,1,0:T(4,128)S(1)} %get-tuple-element.25, f32[4,5,11,720]{3,2,1,0:T(8,128)S(1)} %fusion.26, f32[9]{0:T(128)S(1)} %copy-done.14, f32[4,9,720]{2,1,0:T(8,128)S(1)} %get-tuple-element.71, ...), kind=kLoop, calls=%fused_computation.36 | loop fusion | flops 2980800 | bytes 3216996 | tf_op jit(solution)/shard_map/mul | solution.py:269
  69.4 1.9 %fusion.58 = f32[4,80,360]{2,1,0:T(8,128)S(1)} fusion(f32[4,40,720]{2,1,0:T(8,128)S(1)} %neg.14, f32[4,40,720]{2,1,0:T(8,128)S(1)} %get-tuple-element.7, f32[4,720,180]{2,1,0:T(8,128)S(1)} %bitcast.119, f32[4,720,180]{2,1,0:T(8,128)S(1)} %bitcast.115), kind=kOutput, calls=%fused_computation.90 | convolution fusion | flops 498931200 | bytes 5529600 | tf_op jit(solution)/shard_map/dot_general | solution.py:93
  71.5 2.6 %fusion.88 = f32[4,80,720]{2,1,0:T(8,128)S(1)} fusion(f32[4,40,180]{2,1,0:T(8,128)S(1)} %get-tuple-element.40, f32[4,40,180]{2,1,0:T(8,128)S(1)} %get-tuple-element.9, f32[4,40,180]{2,1,0:T(8,128)S(1)} %get-tuple-element.10, f32[4,720,180]{2,1,0:T(8,128)S(1)} %bitcast.120, f32[4,720,180]{2,1,0:T(8,128)S(1)} %bitcast.116), kind=kOutput, calls=%fused_computation.133 | convolution fusion | flops 499046400 | bytes 5414400 | tf_op jit(solution)/shard_map/dot_general | solution.py:102
  75.0 2.2 %collective-permute-start.5 = (f32[5,8,720]{2,1,0:T(8,128)S(1)}, f32[5,8,720]{2,1,0:T(8,128)S(1)}, u32[]{:S(2)}, u32[]{:S(2)}) collective-permute-start(f32[5,8,720]{2,1,0:T(8,128)S(1)} %get-tuple-element.43), channel_id=1, source_target_pairs={{0,3},{1,0},{2,1},{3,2},{4,7},{5,4},{6,5},{7,6},{8,11},{9,8},{10,9... | collective-permute-start | bytes 345608 | tf_op jit(solution)/shard_map/ppermute | solution.py:17
  77.1 1.2 %collective-permute-start.6 = (f32[5,8,720]{2,1,0:T(8,128)S(1)}, f32[5,8,720]{2,1,0:T(8,128)S(1)}, u32[]{:S(2)}, u32[]{:S(2)}) collective-permute-start(f32[5,8,720]{2,1,0:T(8,128)S(1)} %get-tuple-element.42), channel_id=1, source_target_pairs={{0,2},{1,3},{2,0},{3,1},{4,6},{5,7},{6,4},{7,5},{8,10},{9,11},{10,... | collective-permute-start | bytes 345608 | tf_op jit(solution)/shard_map/ppermute | solution.py:17
  78.3 1.4 %collective-permute-start.7 = (f32[5,8,720]{2,1,0:T(8,128)S(1)}, f32[5,8,720]{2,1,0:T(8,128)S(1)}, u32[]{:S(2)}, u32[]{:S(2)}) collective-permute-start(f32[5,8,720]{2,1,0:T(8,128)S(1)} %get-tuple-element.41), channel_id=1, source_target_pairs={{0,1},{1,2},{2,3},{3,0},{4,5},{5,6},{6,7},{7,4},{8,9},{9,10},{10,1... | collective-permute-start | bytes 345608 | tf_op jit(solution)/shard_map/ppermute | solution.py:17
  80.3 8.4 %collective-permute-done.6 = f32[5,8,720]{2,1,0:T(8,128)S(1)} collective-permute-done((f32[5,8,720]{2,1,0:T(8,128)S(1)}, f32[5,8,720]{2,1,0:T(8,128)S(1)}, u32[]{:S(2)}, u32[]{:S(2)}) %collective-permute-start.6) | collective-permute-done | bytes 115232 | tf_op jit(solution)/shard_map/ppermute | solution.py:17
  88.7 0.8 pad_maximum_fusion.10
  (117 shorter events, 15.5 us)
Async XLA Ops:
  0.0 12.1 %copy-start = (s32[64]{0:T(128)S(1)}, s32[64]{0:T(128)}, u32[]{:S(2)}) copy-start(s32[64]{0:T(128)} %param.7) | copy-start | bytes 772
  3.3 17.2 %collective-permute-start.2 = (f32[56,720]{1,0:T(8,128)}, f32[56,720]{1,0:T(8,128)S(1)}, u32[]{:S(2)}, u32[]{:S(2)}) collective-permute-start(f32[56,720]{1,0:T(8,128)} %pad_maximum_fusion.16), channel_id=1, source_target_pairs={{0,3},{1,0},{2,1},{3,2},{4,7},{5,4},{6,5},{7,6},{8,11},{9,8},{10,9... | collective-permute-start | bytes 483848 | tf_op jit(solution)/shard_map/ppermute | solution.py:17
  7.3 14.0 %collective-permute-start.1 = (f32[56,720]{1,0:T(8,128)}, f32[56,720]{1,0:T(8,128)S(1)}, u32[]{:S(2)}, u32[]{:S(2)}) collective-permute-start(f32[56,720]{1,0:T(8,128)} %pad_maximum_fusion.15), channel_id=1, source_target_pairs={{0,2},{1,3},{2,0},{3,1},{4,6},{5,7},{6,4},{7,5},{8,10},{9,11},{10,... | collective-permute-start | bytes 483848 | tf_op jit(solution)/shard_map/ppermute | solution.py:17
  8.0 13.3 %collective-permute-start = (f32[56,720]{1,0:T(8,128)}, f32[56,720]{1,0:T(8,128)}, u32[]{:S(2)}, u32[]{:S(2)}) collective-permute-start(f32[56,720]{1,0:T(8,128)} %pad_maximum_fusion.14), channel_id=1, source_target_pairs={{0,1},{1,2},{2,3},{3,0},{4,5},{5,6},{6,7},{7,4},{8,9},{9,10},{10,1... | collective-permute-start | bytes 483848 | tf_op jit(solution)/shard_map/ppermute | solution.py:17
  9.0 7.9 %copy-start.5 = (s32[4,180]{1,0:T(4,128)}, s32[4,180]{1,0:T(4,128)S(1)}, u32[]{:S(2)}) copy-start(s32[4,180]{1,0:T(4,128)S(1)} %iota_add_fusion) | copy-start | bytes 8644
  23.1 0.7 copy-start.3
  25.2 12.0 %collective-permute-start.3 = (f32[4,36,720]{2,1,0:T(8,128)}, f32[4,36,720]{2,1,0:T(8,128)}, u32[]{:S(2)}, u32[]{:S(2)}) collective-permute-start(f32[4,36,720]{2,1,0:T(8,128)} %pad_maximum_fusion.7), channel_id=1, source_target_pairs={{0,4},{4,8},{8,12},{12,16},{16,20},{20,24},{24,28},{1,5},{5,9},{9,... | collective-permute-start | bytes 1244168 | tf_op jit(solution)/shard_map/ppermute | solution.py:17
  30.3 11.9 %collective-permute-start.4 = (f32[4,37,720]{2,1,0:T(8,128)}, f32[4,37,720]{2,1,0:T(8,128)}, u32[]{:S(2)}, u32[]{:S(2)}) collective-permute-start(f32[4,37,720]{2,1,0:T(8,128)} %pad_maximum_fusion.8), channel_id=1, source_target_pairs={{4,0},{8,4},{12,8},{16,12},{20,16},{24,20},{28,24},{5,1},{9,5},{13... | collective-permute-start | bytes 1278728 | tf_op jit(solution)/shard_map/ppermute | solution.py:17
  35.4 8.8 %copy-start.4 = (f32[4,8,720]{2,1,0:T(8,128)S(1)}, f32[4,8,720]{2,1,0:T(8,128)}, u32[]{:S(2)}) copy-start(f32[4,8,720]{2,1,0:T(8,128)} %copy-done.3) | copy-start | bytes 276484
  35.4 10.1 %copy-start.2 = (f32[4,5,6,720]{3,2,1,0:T(8,128)S(1)}, f32[4,5,6,720]{3,2,1,0:T(8,128)}, u32[]{:S(2)}) copy-start(f32[4,5,6,720]{3,2,1,0:T(8,128)} %concatenate.181) | copy-start | bytes 1036804
  48.8 0.9 %copy-start.17 = (f32[15]{0:T(128)S(1)}, f32[15]{0:T(128)}, u32[]{:S(2)}) copy-start(f32[15]{0:T(128)} %or_select_fusion.1) | copy-start | bytes 184
  50.7 0.9 copy-start.16
  51.6 1.1 %copy-start.7 = (f32[4,4]{1,0:T(4,128)S(1)}, f32[4,4]{1,0:T(4,128)}, u32[]{:S(2)}) copy-start(f32[4,4]{1,0:T(4,128)} %get-tuple-element.92) | copy-start | bytes 196
  51.6 1.1 %copy-start.8 = (f32[4,4]{1,0:T(4,128)S(1)}, f32[4,4]{1,0:T(4,128)}, u32[]{:S(2)}) copy-start(f32[4,4]{1,0:T(4,128)} %get-tuple-element.93) | copy-start | bytes 196
  52.1 5.1 %copy-start.1 = (f32[4,30,24,180]{3,2,1,0:T(8,128)S(1)}, f32[4,30,24,180]{3,2,1,0:T(8,128)}, u32[]{:S(2)}) copy-start(f32[4,30,24,180]{3,2,1,0:T(8,128)} %get-tuple-element.64) | copy-start | bytes 6220804
  57.2 2.5 %copy-start.6 = (s32[4,180]{1,0:T(4,128)S(1)}, s32[4,180]{1,0:T(4,128)}, u32[]{:S(2)}) copy-start(s32[4,180]{1,0:T(4,128)} %copy-done.5) | copy-start | bytes 8644
  57.2 2.5 %copy-start.9 = (f32[4,180]{1,0:T(4,128)S(1)}, f32[4,180]{1,0:T(4,128)}, u32[]{:S(2)}) copy-start(f32[4,180]{1,0:T(4,128)} %compare_select_fusion) | copy-start | bytes 8644
  57.3 2.5 %copy-start.15 = (s32[70]{0:T(128)S(1)}, s32[70]{0:T(128)}, u32[]{:S(2)}) copy-start(s32[70]{0:T(128)} %and_select_fusion.3) | copy-start | bytes 844
  62.8 1.9 %copy-start.10 = (pred[5,14]{1,0:T(8,128)(4,1)S(1)}, pred[5,14]{1,0:T(8,128)(4,1)}, u32[]{:S(2)}) copy-start(pred[5,14]{1,0:T(8,128)(4,1)} %fusion.118) | copy-start | bytes 214
  66.4 0.7 copy-start.14
  68.1 0.6 copy-start.13
  69.4 2.0 %copy-start.11 = (s32[40]{0:T(128)S(1)}, s32[40]{0:T(128)}, u32[]{:S(2)}) copy-start(s32[40]{0:T(128)} %and_select_fusion.1) | copy-start | bytes 484
  74.1 0.7 copy-start.12
  75.0 5.4 %collective-permute-start.5 = (f32[5,8,720]{2,1,0:T(8,128)S(1)}, f32[5,8,720]{2,1,0:T(8,128)S(1)}, u32[]{:S(2)}, u32[]{:S(2)}) collective-permute-start(f32[5,8,720]{2,1,0:T(8,128)S(1)} %get-tuple-element.43), channel_id=1, source_target_pairs={{0,3},{1,0},{2,1},{3,2},{4,7},{5,4},{6,5},{7,6},{8,11},{9,8},{10,9... | collective-permute-start | bytes 345608 | tf_op jit(solution)/shard_map/ppermute | solution.py:17
  77.1 11.5 %collective-permute-start.6 = (f32[5,8,720]{2,1,0:T(8,128)S(1)}, f32[5,8,720]{2,1,0:T(8,128)S(1)}, u32[]{:S(2)}, u32[]{:S(2)}) collective-permute-start(f32[5,8,720]{2,1,0:T(8,128)S(1)} %get-tuple-element.42), channel_id=1, source_target_pairs={{0,2},{1,3},{2,0},{3,1},{4,6},{5,7},{6,4},{7,5},{8,10},{9,11},{10,... | collective-permute-start | bytes 345608 | tf_op jit(solution)/shard_map/ppermute | solution.py:17
  78.3 10.4 %collective-permute-start.7 = (f32[5,8,720]{2,1,0:T(8,128)S(1)}, f32[5,8,720]{2,1,0:T(8,128)S(1)}, u32[]{:S(2)}, u32[]{:S(2)}) collective-permute-start(f32[5,8,720]{2,1,0:T(8,128)S(1)} %get-tuple-element.41), channel_id=1, source_target_pairs={{0,1},{1,2},{2,3},{3,0},{4,5},{5,6},{6,7},{7,4},{8,9},{9,10},{10,1... | collective-permute-start | bytes 345608 | tf_op jit(solution)/shard_map/ppermute | solution.py:17

commit v10 on v7

--- a/solution.py
+++ b/solution.py
@@ -26,13 +26,13 @@
     a = jnp.arange(cols // split, dtype=jnp.int32)
     b = jnp.arange(split, dtype=jnp.int32)
     step = 2.0 * math.pi / circle
-    coarse = ((split * a[None, :, None] * k[:, None, :]) % circle).astype(jnp.float32) * step
-    fine = ((b[None, :, None] * k[:, None, :]) % circle).astype(jnp.float32) * step
-    ca, sa = jnp.cos(coarse)[:, :, None], jnp.sin(coarse)[:, :, None]
-    cb, sb = jnp.cos(fine)[:, None], jnp.sin(fine)[:, None]
-    cos_qk = (ca * cb - sa * sb).reshape(tiles, cols, per_class)
-    sin_qk = (sa * cb + ca * sb).reshape(tiles, cols, per_class)
-    return jnp.concatenate([cos_qk, sin_qk], axis=2)
+    coarse = ((split * a[None, None, :] * k[:, :, None]) % circle).astype(jnp.float32) * step
+    fine = ((b[None, None, :] * k[:, :, None]) % circle).astype(jnp.float32) * step
+    ca, sa = jnp.cos(coarse)[:, :, :, None], jnp.sin(coarse)[:, :, :, None]
+    cb, sb = jnp.cos(fine)[:, :, None], jnp.sin(fine)[:, :, None]
+    cos_qk = (ca * cb - sa * sb).reshape(tiles, per_class, cols)
+    sin_qk = (sa * cb + ca * sb).reshape(tiles, per_class, cols)
+    return jnp.concatenate([cos_qk, sin_qk], axis=1)
 
 
 def window(values, first_cell, last_cell, dim_at):
@@ -83,15 +83,16 @@
     return jnp.concatenate([jnp.cos(angle), jnp.sin(angle)], axis=2)
 
 
-def filter_rows(rows, basis, roots, weights, polar, halo=HALO):
+def filter_rows(rows, basis, roots, weights, polar, halo=HALO, m_major=False):
     tiles, count, cols = rows.shape
     cos_dr, sin_dr = roots
     z_re = jnp.sum(cos_dr[:, :, None, None] * rows[None], axis=1)
     z_im = -jnp.sum(sin_dr[:, :, None, None] * rows[None], axis=1)
     z = jnp.concatenate([z_re, z_im], axis=1)
     z = jnp.pad(z, ((0, 0), (0, 0), (halo, halo)))
-    prod = lax.dot_general(z, basis, (((2,), (1,)), ((0,), (0,))), precision=MATMUL_PRECISION)
-    per_class = basis.shape[2] // 2
+    q_axis, m_axis = (2, 1) if m_major else (1, 2)
+    prod = lax.dot_general(z, basis, (((2,), (q_axis,)), ((0,), (0,))), precision=MATMUL_PRECISION)
+    per_class = basis.shape[m_axis] // 2
     zc, zs = prod[:, :count, :per_class], prod[:, :count, per_class:]
     wc, ws = prod[:, count:, :per_class], prod[:, count:, per_class:]
     real = (zc + ws) * weights
@@ -99,7 +100,7 @@
     spec = jnp.concatenate(
         [jnp.concatenate([real, imag], axis=2), jnp.concatenate([-imag, real], axis=2)], axis=1
     )
-    back = lax.dot_general(spec, basis, (((2,), (2,)), ((0,), (0,))), precision=MATMUL_PRECISION)
+    back = lax.dot_general(spec, basis, (((2,), (m_axis,)), ((0,), (0,))), precision=MATMUL_PRECISION)
     w_re, w_im = back[:, :count], back[:, count:]
     smooth = jnp.sum(
         cos_dr[:, :, None, None] * w_re[:, None] - sin_dr[:, :, None, None] * w_im[:, None], axis=0
@@ -278,7 +279,7 @@
         )
         state = state - change
         rows = state.reshape(lon_devices, count, lon_cols)
-        rows = filter_rows(rows, basis, roots, weights, polar, 0)
+        rows = filter_rows(rows, basis, roots, weights, polar, 0, True)
         state = rows.reshape(lon_devices, tracer_count, lat_rows, lon_cols)
 
     back = [state[0]] + [

time: 76 us -> 72.6 us (0.955)
  waiting for transfers between devices: 24.9 us -> 20.1 us
  local copies, waits for them, and re-layouts: 5.57 us -> 10.3 us
  other arithmetic: 16.6 us -> 14.7 us
  matrix products: 8.93 us -> 7.77 us
    ppermute x10, waiting for transfers between devices: 24.9 us -> 20.1 us  [shift(): return lax.ppermute(x, axis, pairs)]
    sub x0 -> x1, local copies, waits for them, and re-layouts: none -> 3.3 us  [product_basis(): cos_qk = (ca * cb - sa * sb).reshape(tiles, per_class, cols)]
    add x0 -> x1, local copies, waits for them, and re-layouts: none -> 2.3 us  [product_basis(): sin_qk = (sa * cb + ca * sb).reshape(tiles, per_class, cols)]
    concatenate x3, other arithmetic: 2.04 us -> 0.04 us  [payload_for(): jnp.concatenate([lax.dynamic_index_in_dim(tracers, level, 1, keepdims=Fal...]
    dot_general x4, matrix products: 8.93 us -> 7.77 us  [the longest x2 4.14 us: filter_rows(): lax.dot_general(z, basis, (((2,), (q_axis,)), ((0,), (0,))), precision=MA...]
    sub x1, other arithmetic: 2.22 us -> 3.26 us  [product_basis(): cos_qk = (ca * cb - sa * sb).reshape(tiles, per_class, cols)]
    another operation x2, other arithmetic: 0.99 us -> 0.08 us  [transposed_path(): payload = jnp.stack(pieces)]
  transfers between devices with their start and end apart: 10 -> 10, of which waited for: 5 -> 5; matrix products, arithmetic and copies ran while one was open for 12% -> 19% of each run, Pallas kernels for 0% -> 0%
where the time goes in v10:
time: 72.6 us; the launch traced here: 72 us
  waiting for transfers between devices  20.1 us (28%)
  starting transfers between devices  18.5 us (25%)
  other arithmetic  14.7 us (20%)
  local copies, waits for them, and re-layouts  10.3 us (14%)
  matrix products  7.77 us (11%)
    ppermute x10, waiting for transfers between devices, shift(): return lax.ppermute(x, axis, pairs)  20.1 us
    ppermute x10, starting transfers between devices, shift(): return lax.ppermute(x, axis, pairs)  18.5 us
    dot_general x2, matrix products, filter_rows(): lax.dot_general(z, basis, (((2,), (q_axis,)), ((0,), (0,))), precision=MA...  4.14 us
    dot_general x2, matrix products, filter_rows(): lax.dot_general(spec, basis, (((2,), (m_axis,)), ((0,), (0,))), precision...  3.62 us
    sub x1, local copies, waits for them, and re-layouts, product_basis(): cos_qk = (ca * cb - sa * sb).reshape(tiles, per_class, cols)  3.3 us
    sub x1, other arithmetic, product_basis(): cos_qk = (ca * cb - sa * sb).reshape(tiles, per_class, cols)  3.26 us
    add x1, local copies, waits for them, and re-layouts, product_basis(): sin_qk = (sa * cb + ca * sb).reshape(tiles, per_class, cols)  2.3 us
    mul x2, other arithmetic, transposed_path(): ppm_flux(extended, north_courant, 2, lat_rows) * face_weight[:, None]  1.93 us
  transfers between devices with their start and end apart: 10, of which 5 were waited for; matrix products, arithmetic and copies ran while one was open for 19% of the time, Pallas kernels for 0%

profile of v10, /device:TPU:3, one launch (start us, length us, event | category | flops | bytes accessed | tf_op | source)
XLA Modules:
  0.0 72.0 jit_solution(18442535089811781590)
XLA Ops:
  0.0 1.1 %dynamic-slice_bitcast_fusion.3 = (f32[40,720]{1,0:T(8,128)S(1)}, f32[40,720]{1,0:T(8,128)S(1)}, f32[40,720]{1,0:T(8,128)S(1)}, f32[40,720]{1,0:T(8,128)S(1)}) fusion(f32[5,4,8,720]{3,2,1,0:T(8,128)} %param.4, s32[]{:T(128)S(6)} %select_n.364, s32[]{:T(128)S(6)} %select_n.368, s32[]{:T(128)S(6)} %select_n.366, s32[]{:T(128)S(6)} %select_n.370), kind=kLoop, calls=%fused_computation.202 | loop fusion | bytes 921616 | tf_op jit(solution)/shard_map/reshape | solution.py:214
  1.1 0.9 %dynamic-slice_bitcast_fusion.10 = (f32[8,720]{1,0:T(8,128)S(1)}, f32[8,720]{1,0:T(8,128)S(1)}, f32[8,720]{1,0:T(8,128)S(1)}, f32[8,720]{1,0:T(8,128)S(1)}, f32[...) fusion(f32[4,8,720]{2,1,0:T(8,128)} %param.6, s32[]{:T(128)S(6)} %select_n.364, ...), kind=kLoop, calls=%fused_computation.229 | loop fusion | bytes 368656 | tf_op jit(solution)/shard_map/jit(dynamic_index_in_dim)/squeeze | solution.py:216
  2.0 3.4 %collective-permute-start.2 = (f32[56,720]{1,0:T(8,128)S(1)}, f32[56,720]{1,0:T(8,128)S(1)}, u32[]{:S(2)}, u32[]{:S(2)}) collective-permute-start(f32[56,720]{1,0:T(8,128)S(1)} %pad_maximum_fusion.23), channel_id=1, source_target_pairs={{0,3},{1,0},{2,1},{3,2},{4,7},{5,4},{6,5},{7,6},{8,11},{9,8},{10,9... | collective-permute-start | bytes 483848 | tf_op jit(solution)/shard_map/ppermute | solution.py:17
  5.5 0.5 collective-permute-start
  6.2 0.4 fusion.121
  6.6 0.6 fusion.114
  7.3 0.8 %gather_fusion = s32[40]{0:T(128)S(1)} fusion(s32[64]{0:T(128)S(1)} %copy-done, s32[1024]{0:T(1024)S(1)} %pad_clamp_fusion), kind=kCustom, calls=%fused_computation | custom fusion | bytes 480 | tf_op jit(solution)/shard_map/jit(_take)/gather | solution.py:232
  8.1 3.3 %multiply_subtract_fusion = (f32[4,180,30,24]{1,3,2,0:T(8,128)}, f32[4,180,30,24]{1,3,2,0:T(8,128)}) fusion(f32[4,180,24]{1,2,0:T(8,128)S(1)} %get-tuple-element.77, f32[4,180,30]{1,2,0:T(8,128)S(1)} %get-tuple-element.75, f32[4,180,24]{1,2,0:T(8,128)S(1)} %get-tuple-element.76, f32[4,180,30]{1,2,0:T(8,128)S(1)} %get-tuple-element.74), kind=kLoop, calls=%fused_computation.3 | loop fusion | flops 3110400 | bytes 4458240 | tf_op jit(solution)/shard_map/sub | solution.py:33
  11.4 2.3 %copy.90 = f32[4,180,720]{2,1,0:T(8,128)S(1)} copy(f32[4,180,720]{1,2,0:T(8,128)} %bitcast.98) | data formatting | bytes 4147200 | tf_op jit(solution)/shard_map/add | solution.py:34
  13.7 3.3 %copy.89 = f32[4,180,720]{2,1,0:T(8,128)} copy(f32[4,180,720]{1,2,0:T(8,128)} %bitcast.97) | data formatting | bytes 4147200 | tf_op jit(solution)/shard_map/sub | solution.py:33
  17.0 3.1 %collective-permute-done.1 = f32[56,720]{1,0:T(8,128)S(1)} collective-permute-done((f32[56,720]{1,0:T(8,128)S(1)}, f32[56,720]{1,0:T(8,128)S(1)}, u32[]{:S(2)}, u32[]{:S(2)}) %collective-permute-start.1) | collective-permute-done | bytes 161312 | tf_op jit(solution)/shard_map/ppermute | solution.py:17
  21.0 3.8 %collective-permute-start.4 = (f32[4,5,3,720]{3,2,1,0:T(4,128)S(1)}, f32[4,5,3,720]{3,2,1,0:T(4,128)S(1)}, u32[]{:S(2)}, u32[]{:S(2)}) collective-permute-start(f32[4,5,3,720]{3,2,1,0:T(4,128)S(1)} %get-tuple-element.45), channel_id=1, source_target_pairs={{0,4},{4,8},{8,12},{12,16},{16,20},{20,24},{24,28},{1,5},{5,9},{9,... | collective-permute-start | bytes 518408 | tf_op jit(solution)/shard_map/ppermute | solution.py:17
  25.0 2.1 %collective-permute-start.3 = (f32[4,16,720]{2,1,0:T(8,128)S(1)}, f32[4,16,720]{2,1,0:T(8,128)S(1)}, u32[]{:S(2)}, u32[]{:S(2)}) collective-permute-start(f32[4,16,720]{2,1,0:T(8,128)S(1)} %pad_maximum_fusion.19), channel_id=1, source_target_pairs={{4,0},{8,4},{12,8},{16,12},{20,16},{24,20},{28,24},{5,1},{9,5},{13... | collective-permute-start | bytes 552968 | tf_op jit(solution)/shard_map/ppermute | solution.py:17
  27.1 0.2 maximum_maximum_fusion
  27.3 0.5 fusion.86
  27.8 0.5 fusion.79
  28.3 4.5 %collective-permute-done.3 = f32[4,16,720]{2,1,0:T(8,128)S(1)} collective-permute-done((f32[4,16,720]{2,1,0:T(8,128)S(1)}, f32[4,16,720]{2,1,0:T(8,128)S(1)}, u32[]{:S(2)}, u32[]{:S(2)}) %collective-permute-start.3) | collective-permute-done | bytes 184352 | tf_op jit(solution)/shard_map/ppermute | solution.py:17
  33.1 0.2 broadcast_select_fusion.4
  33.4 0.2 pad_maximum_fusion.9
  33.6 0.4 fusion.43
  34.0 1.0 %fusion.30 = f32[4,5,9,720]{3,2,1,0:T(8,128)S(1)} fusion(f32[4,5,8,720]{3,2,1,0:T(8,128)S(1)} %slice_bitcast_fusion, f32[4,5,3,720]{3,2,1,0:T(4,128)S(1)} %get-tuple-element.59, f32[4,5,3,720]{3,2,1,0:T(4,128)S(1)} %get-tuple-element.58, f32[4,5,11,720]{3,2,1,0:T(8,128)S(1)} %fusion.43, f32[9]{0:T(128)S(1)} %or_select_fusion, ...), kind=kLoop, calls=%fused_computation.52 | loop fusion | flops 2980800 | bytes 3216996 | tf_op jit(solution)/shard_map/mul | solution.py:274
  35.0 0.2 fusion.72
  35.2 0.4 multiply_reduce_fusion.3
  35.7 1.0 %copy-done.1 = f32[4,180,720]{2,1,0:T(8,128)S(1)} copy-done((f32[4,180,720]{2,1,0:T(8,128)S(1)}, f32[4,180,720]{2,1,0:T(8,128)}, u32[]{:S(2)}) %copy-start.1) | copy-done | bytes 2073624
  36.7 2.1 %fusion.3 = f32[4,80,360]{2,1,0:T(8,128)S(1)} fusion(f32[4,180,720]{2,1,0:T(8,128)S(1)} %copy.90, f32[4,180,720]{2,1,0:T(8,128)S(1)} %copy-done.1, f32[4,40,720]{2,1,0:T(8,128)S(1)} %neg.12, f32[4,40,720]{2,1,0:T(8,128)S(1)} %get-tuple-element.7), kind=kOutput, calls=%fused_computation.13 | convolution fusion | flops 498931200 | bytes 5529600 | tf_op jit(solution)/shard_map/dot_general | solution.py:94
  38.9 1.8 %fusion.2 = f32[4,80,720]{2,1,0:T(8,128)S(1)} fusion(f32[4,180,720]{2,1,0:T(8,128)S(1)} %copy.90, f32[4,180,720]{2,1,0:T(8,128)S(1)} %copy-done.1, f32[4,40,180]{2,1,0:T(8,128)S(1)} %get-tuple-element.30, f32[4,40,180]{2,1,0:T(8,128)S(1)} %get-tuple-element.14, f32[4,40,180]{2,1,0:T(8,128)S(1)} %get-tuple-element.15), kind=kOutput, calls=%fused_computation.12 | convolution fusion | flops 499046400 | bytes 5414400 | tf_op jit(solution)/shard_map/dot_general | solution.py:103
  40.8 0.3 subtract_reduce_fusion.1
  41.5 1.9 %collective-permute-start.5 = (f32[4,5,3,720]{3,2,1,0:T(4,128)S(1)}, f32[4,5,3,720]{3,2,1,0:T(4,128)S(1)}, u32[]{:S(2)}, u32[]{:S(2)}) collective-permute-start(f32[4,5,3,720]{3,2,1,0:T(4,128)S(1)} %get-tuple-element.38), channel_id=1, source_target_pairs={{0,4},{4,8},{8,12},{12,16},{16,20},{20,24},{24,28},{1,5},{5,9},{9,... | collective-permute-start | bytes 518408 | tf_op jit(solution)/shard_map/ppermute | solution.py:17
  43.5 2.6 %collective-permute-start.6 = (f32[4,5,3,720]{3,2,1,0:T(4,128)S(1)}, f32[4,5,3,720]{3,2,1,0:T(4,128)S(1)}, u32[]{:S(2)}, u32[]{:S(2)}) collective-permute-start(f32[4,5,3,720]{3,2,1,0:T(4,128)S(1)} %get-tuple-element.39), channel_id=1, source_target_pairs={{4,0},{8,4},{12,8},{16,12},{20,16},{24,20},{28,24},{5,1},{9,5},{13... | collective-permute-start | bytes 518408 | tf_op jit(solution)/shard_map/ppermute | solution.py:17
  46.1 0.2 maximum_maximum_fusion.2
  46.3 0.5 fusion.69
  46.8 0.5 fusion.62
  47.3 4.5 %collective-permute-done.6 = f32[4,5,3,720]{3,2,1,0:T(4,128)S(1)} collective-permute-done((f32[4,5,3,720]{3,2,1,0:T(4,128)S(1)}, f32[4,5,3,720]{3,2,1,0:T(4,128)S(1)}, u32[]{:S(2)}, u32[]{:S(2)}) %collective-permute-start.6) | collective-permute-done | bytes 172832 | tf_op jit(solution)/shard_map/ppermute | solution.py:17
  51.9 0.2 broadcast_select_fusion.2
  52.1 0.2 pad_maximum_fusion.10
  52.3 0.4 fusion.40
  52.7 1.0 %fusion.13 = f32[4,5,9,720]{3,2,1,0:T(8,128)S(1)} fusion(f32[4,5,8,720]{3,2,1,0:T(8,128)S(1)} %bitcast_select_fusion, f32[4,5,3,720]{3,2,1,0:T(4,128)S(1)} %get-tuple-element.55, f32[4,5,3,720]{3,2,1,0:T(4,128)S(1)} %get-tuple-element.54, f32[4,5,11,720]{3,2,1,0:T(8,128)S(1)} %fusion.40, f32[9]{0:T(128)S(1)} %or_select_fusion, ...), kind=kLoop, calls=%fused_computation.35 | loop fusion | flops 2980800 | bytes 3216996 | tf_op jit(solution)/shard_map/mul | solution.py:274
  53.7 0.3 fusion.55
  53.9 0.4 multiply_reduce_fusion.1
  54.4 2.1 %fusion.1 = f32[4,80,360]{2,1,0:T(8,128)S(1)} fusion(f32[4,180,720]{2,1,0:T(8,128)S(1)} %copy.90, f32[4,180,720]{2,1,0:T(8,128)S(1)} %copy-done.1, f32[4,40,720]{2,1,0:T(8,128)S(1)} %neg.14, f32[4,40,720]{2,1,0:T(8,128)S(1)} %get-tuple-element.5), kind=kOutput, calls=%fused_computation.11 | convolution fusion | flops 498931200 | bytes 5529600 | tf_op jit(solution)/shard_map/dot_general | solution.py:94
  56.6 1.8 %fusion = f32[4,80,720]{2,1,0:T(8,128)S(1)} fusion(f32[4,180,720]{2,1,0:T(8,128)S(1)} %copy.90, f32[4,180,720]{2,1,0:T(8,128)S(1)} %copy-done.1, f32[4,40,180]{2,1,0:T(8,128)S(1)} %get-tuple-element.29, f32[4,40,180]{2,1,0:T(8,128)S(1)} %get-tuple-element.9, f32[4,40,180]{2,1,0:T(8,128)S(1)} %get-tuple-element.10), kind=kOutput, calls=%fused_computation.10 | convolution fusion | flops 499046400 | bytes 5414400 | tf_op jit(solution)/shard_map/dot_general | solution.py:103
  58.5 0.3 subtract_reduce_fusion
  59.0 0.6 collective-permute-start.7
  59.7 2.1 %collective-permute-start.8 = (f32[5,8,720]{2,1,0:T(8,128)S(1)}, f32[5,8,720]{2,1,0:T(8,128)S(1)}, u32[]{:S(2)}, u32[]{:S(2)}) collective-permute-start(f32[5,8,720]{2,1,0:T(8,128)S(1)} %get-tuple-element.32), channel_id=1, source_target_pairs={{0,2},{1,3},{2,0},{3,1},{4,6},{5,7},{6,4},{7,5},{8,10},{9,11},{10,... | collective-permute-start | bytes 345608 | tf_op jit(solution)/shard_map/ppermute | solution.py:17
  61.8 1.4 %collective-permute-start.9 = (f32[5,8,720]{2,1,0:T(8,128)S(1)}, f32[5,8,720]{2,1,0:T(8,128)S(1)}, u32[]{:S(2)}, u32[]{:S(2)}) collective-permute-start(f32[5,8,720]{2,1,0:T(8,128)S(1)} %get-tuple-element.31), channel_id=1, source_target_pairs={{0,1},{1,2},{2,3},{3,0},{4,5},{5,6},{6,7},{7,4},{8,9},{9,10},{10,1... | collective-permute-start | bytes 345608 | tf_op jit(solution)/shard_map/ppermute | solution.py:17
  63.2 1.1 %collective-permute-done.7 = f32[5,8,720]{2,1,0:T(8,128)S(1)} collective-permute-done((f32[5,8,720]{2,1,0:T(8,128)S(1)}, f32[5,8,720]{2,1,0:T(8,128)S(1)}, u32[]{:S(2)}, u32[]{:S(2)}) %collective-permute-start.7) | collective-permute-done | bytes 115232 | tf_op jit(solution)/shard_map/ppermute | solution.py:17
  64.3 6.8 %collective-permute-done.8 = f32[5,8,720]{2,1,0:T(8,128)S(1)} collective-permute-done((f32[5,8,720]{2,1,0:T(8,128)S(1)}, f32[5,8,720]{2,1,0:T(8,128)S(1)}, u32[]{:S(2)}, u32[]{:S(2)}) %collective-permute-start.8) | collective-permute-done | bytes 115232 | tf_op jit(solution)/shard_map/ppermute | solution.py:17
  71.2 0.8 %pad_maximum_fusion.14 = f32[5,4,8,720]{3,2,1,0:T(8,128)} fusion(f32[5,1,8,720]{3,2,1,0:T(8,128)S(1)} %get-tuple-element.24, f32[5,1,8,720]{3,2,1,0:T(8,128)S(1)} %get-tuple-element.25, f32[5,1,8,720]{3,2,1,0:T(8,128)S(1)} %get-tuple-element.26, f32[5,1,8,720]{3,2,1,0:T(8,128)S(1)} %get-tuple-element.23), kind=kLoop, calls=%fused_computation.145 | loop fusion | flops 345600 | bytes 921600 | tf_op jit(solution)/shard_map/stack | solution.py:294
  (63 shorter events, 2.8 us)
Async XLA Ops:
  0.0 7.3 %copy-start = (s32[64]{0:T(128)S(1)}, s32[64]{0:T(128)}, u32[]{:S(2)}) copy-start(s32[64]{0:T(128)} %param.7) | copy-start | bytes 772
  2.0 15.0 %collective-permute-start.2 = (f32[56,720]{1,0:T(8,128)S(1)}, f32[56,720]{1,0:T(8,128)S(1)}, u32[]{:S(2)}, u32[]{:S(2)}) collective-permute-start(f32[56,720]{1,0:T(8,128)S(1)} %pad_maximum_fusion.23), channel_id=1, source_target_pairs={{0,3},{1,0},{2,1},{3,2},{4,7},{5,4},{6,5},{7,6},{8,11},{9,8},{10,9... | collective-permute-start | bytes 483848 | tf_op jit(solution)/shard_map/ppermute | solution.py:17
  5.4 14.7 %collective-permute-start.1 = (f32[56,720]{1,0:T(8,128)S(1)}, f32[56,720]{1,0:T(8,128)S(1)}, u32[]{:S(2)}, u32[]{:S(2)}) collective-permute-start(f32[56,720]{1,0:T(8,128)S(1)} %pad_maximum_fusion.22), channel_id=1, source_target_pairs={{0,2},{1,3},{2,0},{3,1},{4,6},{5,7},{6,4},{7,5},{8,10},{9,11},{10,... | collective-permute-start | bytes 483848 | tf_op jit(solution)/shard_map/ppermute | solution.py:17
  5.5 14.6 %collective-permute-start = (f32[56,720]{1,0:T(8,128)S(1)}, f32[56,720]{1,0:T(8,128)S(1)}, u32[]{:S(2)}, u32[]{:S(2)}) collective-permute-start(f32[56,720]{1,0:T(8,128)S(1)} %pad_maximum_fusion.21), channel_id=1, source_target_pairs={{0,1},{1,2},{2,3},{3,0},{4,5},{5,6},{6,7},{7,4},{8,9},{9,10},{10,1... | collective-permute-start | bytes 483848 | tf_op jit(solution)/shard_map/ppermute | solution.py:17
  21.0 12.2 %collective-permute-start.4 = (f32[4,5,3,720]{3,2,1,0:T(4,128)S(1)}, f32[4,5,3,720]{3,2,1,0:T(4,128)S(1)}, u32[]{:S(2)}, u32[]{:S(2)}) collective-permute-start(f32[4,5,3,720]{3,2,1,0:T(4,128)S(1)} %get-tuple-element.45), channel_id=1, source_target_pairs={{0,4},{4,8},{8,12},{12,16},{16,20},{20,24},{24,28},{1,5},{5,9},{9,... | collective-permute-start | bytes 518408 | tf_op jit(solution)/shard_map/ppermute | solution.py:17
  25.0 7.9 %collective-permute-start.3 = (f32[4,16,720]{2,1,0:T(8,128)S(1)}, f32[4,16,720]{2,1,0:T(8,128)S(1)}, u32[]{:S(2)}, u32[]{:S(2)}) collective-permute-start(f32[4,16,720]{2,1,0:T(8,128)S(1)} %pad_maximum_fusion.19), channel_id=1, source_target_pairs={{4,0},{8,4},{12,8},{16,12},{20,16},{24,20},{28,24},{5,1},{9,5},{13... | collective-permute-start | bytes 552968 | tf_op jit(solution)/shard_map/ppermute | solution.py:17
  35.0 1.6 %copy-start.1 = (f32[4,180,720]{2,1,0:T(8,128)S(1)}, f32[4,180,720]{2,1,0:T(8,128)}, u32[]{:S(2)}) copy-start(f32[4,180,720]{2,1,0:T(8,128)} %copy.89) | copy-start | bytes 6220804
  41.5 5.8 %collective-permute-start.5 = (f32[4,5,3,720]{3,2,1,0:T(4,128)S(1)}, f32[4,5,3,720]{3,2,1,0:T(4,128)S(1)}, u32[]{:S(2)}, u32[]{:S(2)}) collective-permute-start(f32[4,5,3,720]{3,2,1,0:T(4,128)S(1)} %get-tuple-element.38), channel_id=1, source_target_pairs={{0,4},{4,8},{8,12},{12,16},{16,20},{20,24},{24,28},{1,5},{5,9},{9,... | collective-permute-start | bytes 518408 | tf_op jit(solution)/shard_map/ppermute | solution.py:17
  43.5 8.4 %collective-permute-start.6 = (f32[4,5,3,720]{3,2,1,0:T(4,128)S(1)}, f32[4,5,3,720]{3,2,1,0:T(4,128)S(1)}, u32[]{:S(2)}, u32[]{:S(2)}) collective-permute-start(f32[4,5,3,720]{3,2,1,0:T(4,128)S(1)} %get-tuple-element.39), channel_id=1, source_target_pairs={{4,0},{8,4},{12,8},{16,12},{20,16},{24,20},{28,24},{5,1},{9,5},{13... | collective-permute-start | bytes 518408 | tf_op jit(solution)/shard_map/ppermute | solution.py:17
  59.0 5.2 %collective-permute-start.7 = (f32[5,8,720]{2,1,0:T(8,128)S(1)}, f32[5,8,720]{2,1,0:T(8,128)S(1)}, u32[]{:S(2)}, u32[]{:S(2)}) collective-permute-start(f32[5,8,720]{2,1,0:T(8,128)S(1)} %get-tuple-element.33), channel_id=1, source_target_pairs={{0,3},{1,0},{2,1},{3,2},{4,7},{5,4},{6,5},{7,6},{8,11},{9,8},{10,9... | collective-permute-start | bytes 345608 | tf_op jit(solution)/shard_map/ppermute | solution.py:17
  59.7 11.4 %collective-permute-start.8 = (f32[5,8,720]{2,1,0:T(8,128)S(1)}, f32[5,8,720]{2,1,0:T(8,128)S(1)}, u32[]{:S(2)}, u32[]{:S(2)}) collective-permute-start(f32[5,8,720]{2,1,0:T(8,128)S(1)} %get-tuple-element.32), channel_id=1, source_target_pairs={{0,2},{1,3},{2,0},{3,1},{4,6},{5,7},{6,4},{7,5},{8,10},{9,11},{10,... | collective-permute-start | bytes 345608 | tf_op jit(solution)/shard_map/ppermute | solution.py:17
  61.8 9.3 %collective-permute-start.9 = (f32[5,8,720]{2,1,0:T(8,128)S(1)}, f32[5,8,720]{2,1,0:T(8,128)S(1)}, u32[]{:S(2)}, u32[]{:S(2)}) collective-permute-start(f32[5,8,720]{2,1,0:T(8,128)S(1)} %get-tuple-element.31), channel_id=1, source_target_pairs={{0,1},{1,2},{2,3},{3,0},{4,5},{5,6},{6,7},{7,4},{8,9},{9,10},{10,1... | collective-permute-start | bytes 345608 | tf_op jit(solution)/shard_map/ppermute | solution.py:17

commit v11 on v10

--- a/solution.py
+++ b/solution.py
@@ -4,6 +4,7 @@
 import jax.numpy as jnp
 from jax import lax
 from jax.sharding import PartitionSpec as P
+
 
 KMAX = 720
 SUBSTEPS = 2
@@ -84,7 +85,7 @@
 
 
 def filter_rows(rows, basis, roots, weights, polar, halo=HALO, m_major=False):
-    tiles, count, cols = rows.shape
+    _, count, cols = rows.shape
     cos_dr, sin_dr = roots
     z_re = jnp.sum(cos_dr[:, :, None, None] * rows[None], axis=1)
     z_im = -jnp.sum(sin_dr[:, :, None, None] * rows[None], axis=1)
@@ -271,12 +272,9 @@
             axis=3,
         )
         zonal = ppm_flux(wrapped, east_courant, 3, lon_cols)
+        zonal_change = lax.optimization_barrier(zonal[..., 1:] - zonal[..., :-1])
         meridional = ppm_flux(extended, north_courant, 2, lat_rows) * face_weight[:, None]
-        change = (
-            zonal[..., 1:]
-            - zonal[..., :-1]
-            + (meridional[:, :, 1:] - meridional[:, :, :-1]) / center_weight[:, None]
-        )
+        change = zonal_change + (meridional[:, :, 1:] - meridional[:, :, :-1]) / center_weight[:, None]
         state = state - change
         rows = state.reshape(lon_devices, count, lon_cols)
         rows = filter_rows(rows, basis, roots, weights, polar, 0, True)
@@ -295,7 +293,6 @@
 
 
 def on_device(tracers, courant_x, courant_y, cutoffs):
-    field_count = tracers.shape[0] * tracers.shape[1]
     if tracers.shape[1] == lax.axis_size("lon") and tracers.shape[2] >= HALO:
         return transposed_path(tracers, courant_x, courant_y, cutoffs)
     return tiled_path(tracers, courant_x, courant_y, cutoffs)

time: 72.6 us -> 75.4 us (1.039)
  waiting for transfers between devices: 20.1 us -> 22.5 us
    ppermute x10, waiting for transfers between devices: 20.1 us -> 22.5 us  [shift(): return lax.ppermute(x, axis, pairs)]
  transfers between devices with their start and end apart: 10 -> 10, of which waited for: 5 -> 6; matrix products, arithmetic and copies ran while one was open for 19% -> 15% of each run, Pallas kernels for 0% -> 0%
where the time goes in v11:
time: 75.4 us; the launch traced here: 74.7 us
  waiting for transfers between devices  22.5 us (30%)
  starting transfers between devices  18.5 us (25%)
  other arithmetic  15 us (20%)
  local copies, waits for them, and re-layouts  10.4 us (14%)
  matrix products  7.76 us (10%)
    ppermute x10, waiting for transfers between devices, shift(): return lax.ppermute(x, axis, pairs)  22.5 us
    ppermute x10, starting transfers between devices, shift(): return lax.ppermute(x, axis, pairs)  18.5 us
    dot_general x2, matrix products, filter_rows(): lax.dot_general(z, basis, (((2,), (q_axis,)), ((0,), (0,))), precision=MA...  4.14 us
    dot_general x2, matrix products, filter_rows(): lax.dot_general(spec, basis, (((2,), (m_axis,)), ((0,), (0,))), precision...  3.62 us
    sub x1, local copies, waits for them, and re-layouts, product_basis(): cos_qk = (ca * cb - sa * sb).reshape(tiles, per_class, cols)  3.3 us
    sub x1, other arithmetic, product_basis(): cos_qk = (ca * cb - sa * sb).reshape(tiles, per_class, cols)  3.26 us
    add x1, local copies, waits for them, and re-layouts, product_basis(): sin_qk = (sa * cb + ca * sb).reshape(tiles, per_class, cols)  2.3 us
    mul x2, other arithmetic, transposed_path(): ppm_flux(extended, north_courant, 2, lat_rows) * face_weight[:, None]  1.93 us
  transfers between devices with their start and end apart: 10, of which 6 were waited for; matrix products, arithmetic and copies ran while one was open for 15% of the time, Pallas kernels for 0%

profile of v11, /device:TPU:3, one launch (start us, length us, event | category | flops | bytes accessed | tf_op | source)
XLA Modules:
  0.0 74.7 jit_solution(11890044798978883792)
XLA Ops:
  0.0 1.1 %dynamic-slice_bitcast_fusion.3 = (f32[40,720]{1,0:T(8,128)S(1)}, f32[40,720]{1,0:T(8,128)S(1)}, f32[40,720]{1,0:T(8,128)S(1)}, f32[40,720]{1,0:T(8,128)S(1)}) fusion(f32[5,4,8,720]{3,2,1,0:T(8,128)} %param.4, s32[]{:T(128)S(6)} %select_n.364, s32[]{:T(128)S(6)} %select_n.368, s32[]{:T(128)S(6)} %select_n.366, s32[]{:T(128)S(6)} %select_n.370), kind=kLoop, calls=%fused_computation.202 | loop fusion | bytes 921616 | tf_op jit(solution)/shard_map/reshape | solution.py:215
  1.1 0.9 %dynamic-slice_bitcast_fusion.10 = (f32[8,720]{1,0:T(8,128)S(1)}, f32[8,720]{1,0:T(8,128)S(1)}, f32[8,720]{1,0:T(8,128)S(1)}, f32[8,720]{1,0:T(8,128)S(1)}, f32[...) fusion(f32[4,8,720]{2,1,0:T(8,128)} %param.6, s32[]{:T(128)S(6)} %select_n.364, ...), kind=kLoop, calls=%fused_computation.229 | loop fusion | bytes 368656 | tf_op jit(solution)/shard_map/jit(dynamic_index_in_dim)/squeeze | solution.py:217
  2.0 3.4 %collective-permute-start.2 = (f32[56,720]{1,0:T(8,128)S(1)}, f32[56,720]{1,0:T(8,128)S(1)}, u32[]{:S(2)}, u32[]{:S(2)}) collective-permute-start(f32[56,720]{1,0:T(8,128)S(1)} %pad_maximum_fusion.23), channel_id=1, source_target_pairs={{0,3},{1,0},{2,1},{3,2},{4,7},{5,4},{6,5},{7,6},{8,11},{9,8},{10,9... | collective-permute-start | bytes 483848 | tf_op jit(solution)/shard_map/ppermute | solution.py:18
  5.5 0.5 collective-permute-start
  6.2 0.4 fusion.121
  6.6 0.6 fusion.114
  7.3 0.8 %gather_fusion = s32[40]{0:T(128)S(1)} fusion(s32[64]{0:T(128)S(1)} %copy-done, s32[1024]{0:T(1024)S(1)} %pad_clamp_fusion), kind=kCustom, calls=%fused_computation | custom fusion | bytes 480 | tf_op jit(solution)/shard_map/jit(_take)/gather | solution.py:233
  8.1 3.3 %multiply_subtract_fusion = (f32[4,180,30,24]{1,3,2,0:T(8,128)}, f32[4,180,30,24]{1,3,2,0:T(8,128)}) fusion(f32[4,180,24]{1,2,0:T(8,128)S(1)} %get-tuple-element.77, f32[4,180,30]{1,2,0:T(8,128)S(1)} %get-tuple-element.75, f32[4,180,24]{1,2,0:T(8,128)S(1)} %get-tuple-element.76, f32[4,180,30]{1,2,0:T(8,128)S(1)} %get-tuple-element.74), kind=kLoop, calls=%fused_computation.3 | loop fusion | flops 3110400 | bytes 4458240 | tf_op jit(solution)/shard_map/sub | solution.py:34
  11.4 2.3 %copy.90 = f32[4,180,720]{2,1,0:T(8,128)S(1)} copy(f32[4,180,720]{1,2,0:T(8,128)} %bitcast.98) | data formatting | bytes 4147200 | tf_op jit(solution)/shard_map/add | solution.py:35
  13.7 3.3 %copy.89 = f32[4,180,720]{2,1,0:T(8,128)} copy(f32[4,180,720]{1,2,0:T(8,128)} %bitcast.97) | data formatting | bytes 4147200 | tf_op jit(solution)/shard_map/sub | solution.py:34
  17.0 3.1 %collective-permute-done.1 = f32[56,720]{1,0:T(8,128)S(1)} collective-permute-done((f32[56,720]{1,0:T(8,128)S(1)}, f32[56,720]{1,0:T(8,128)S(1)}, u32[]{:S(2)}, u32[]{:S(2)}) %collective-permute-start.1) | collective-permute-done | bytes 161312 | tf_op jit(solution)/shard_map/ppermute | solution.py:18
  20.9 0.2 maximum_maximum_fusion
  21.1 0.5 fusion.86
  21.6 0.5 fusion.79
  22.1 0.2 slice_subtract_fusion.3
  22.4 3.8 %collective-permute-start.4 = (f32[4,5,3,720]{3,2,1,0:T(4,128)S(1)}, f32[4,5,3,720]{3,2,1,0:T(4,128)S(1)}, u32[]{:S(2)}, u32[]{:S(2)}) collective-permute-start(f32[4,5,3,720]{3,2,1,0:T(4,128)S(1)} %get-tuple-element.41), channel_id=1, source_target_pairs={{0,4},{4,8},{8,12},{12,16},{16,20},{20,24},{24,28},{1,5},{5,9},{9,... | collective-permute-start | bytes 518408 | tf_op jit(solution)/shard_map/ppermute | solution.py:18
  26.4 2.1 %collective-permute-start.3 = (f32[4,16,720]{2,1,0:T(8,128)S(1)}, f32[4,16,720]{2,1,0:T(8,128)S(1)}, u32[]{:S(2)}, u32[]{:S(2)}) collective-permute-start(f32[4,16,720]{2,1,0:T(8,128)S(1)} %pad_maximum_fusion.19), channel_id=1, source_target_pairs={{4,0},{8,4},{12,8},{16,12},{20,16},{24,20},{28,24},{5,1},{9,5},{13... | collective-permute-start | bytes 552968 | tf_op jit(solution)/shard_map/ppermute | solution.py:18
  28.5 5.7 %collective-permute-done.3 = f32[4,16,720]{2,1,0:T(8,128)S(1)} collective-permute-done((f32[4,16,720]{2,1,0:T(8,128)S(1)}, f32[4,16,720]{2,1,0:T(8,128)S(1)}, u32[]{:S(2)}, u32[]{:S(2)}) %collective-permute-start.3) | collective-permute-done | bytes 184352 | tf_op jit(solution)/shard_map/ppermute | solution.py:18
  34.5 0.2 broadcast_select_fusion.4
  34.9 0.4 fusion.43
  35.4 1.0 %fusion.30 = f32[4,5,9,720]{3,2,1,0:T(8,128)S(1)} fusion(f32[4,5,8,720]{3,2,1,0:T(8,128)S(1)} %slice_bitcast_fusion, f32[4,5,3,720]{3,2,1,0:T(4,128)S(1)} %get-tuple-element.59, f32[4,5,3,720]{3,2,1,0:T(4,128)S(1)} %get-tuple-element.58, f32[4,5,11,720]{3,2,1,0:T(8,128)S(1)} %fusion.43, f32[9]{0:T(128)S(1)} %or_select_fusion, ...), kind=kLoop, calls=%fused_computation.52 | loop fusion | flops 2980800 | bytes 3216996 | tf_op jit(solution)/shard_map/mul | solution.py:276
  36.6 0.4 multiply_reduce_fusion.3
  37.0 1.0 %copy-done.1 = f32[4,180,720]{2,1,0:T(8,128)S(1)} copy-done((f32[4,180,720]{2,1,0:T(8,128)S(1)}, f32[4,180,720]{2,1,0:T(8,128)}, u32[]{:S(2)}) %copy-start.1) | copy-done | bytes 2073624
  38.0 2.1 %fusion.3 = f32[4,80,360]{2,1,0:T(8,128)S(1)} fusion(f32[4,180,720]{2,1,0:T(8,128)S(1)} %copy.90, f32[4,180,720]{2,1,0:T(8,128)S(1)} %copy-done.1, f32[4,40,720]{2,1,0:T(8,128)S(1)} %neg.12, f32[4,40,720]{2,1,0:T(8,128)S(1)} %get-tuple-element.7), kind=kOutput, calls=%fused_computation.13 | convolution fusion | flops 498931200 | bytes 5529600 | tf_op jit(solution)/shard_map/dot_general | solution.py:95
  40.3 1.8 %fusion.2 = f32[4,80,720]{2,1,0:T(8,128)S(1)} fusion(f32[4,180,720]{2,1,0:T(8,128)S(1)} %copy.90, f32[4,180,720]{2,1,0:T(8,128)S(1)} %copy-done.1, f32[4,40,180]{2,1,0:T(8,128)S(1)} %get-tuple-element.30, f32[4,40,180]{2,1,0:T(8,128)S(1)} %get-tuple-element.14, f32[4,40,180]{2,1,0:T(8,128)S(1)} %get-tuple-element.15), kind=kOutput, calls=%fused_computation.12 | convolution fusion | flops 499046400 | bytes 5414400 | tf_op jit(solution)/shard_map/dot_general | solution.py:104
  42.2 0.3 subtract_reduce_fusion.1
  42.9 0.2 maximum_maximum_fusion.2
  43.1 0.5 fusion.69
  43.6 0.5 fusion.62
  44.1 0.2 slice_subtract_fusion.1
  44.3 1.9 %collective-permute-start.5 = (f32[4,5,3,720]{3,2,1,0:T(4,128)S(1)}, f32[4,5,3,720]{3,2,1,0:T(4,128)S(1)}, u32[]{:S(2)}, u32[]{:S(2)}) collective-permute-start(f32[4,5,3,720]{3,2,1,0:T(4,128)S(1)} %get-tuple-element.34), channel_id=1, source_target_pairs={{0,4},{4,8},{8,12},{12,16},{16,20},{20,24},{24,28},{1,5},{5,9},{9,... | collective-permute-start | bytes 518408 | tf_op jit(solution)/shard_map/ppermute | solution.py:18
  46.2 2.6 %collective-permute-start.6 = (f32[4,5,3,720]{3,2,1,0:T(4,128)S(1)}, f32[4,5,3,720]{3,2,1,0:T(4,128)S(1)}, u32[]{:S(2)}, u32[]{:S(2)}) collective-permute-start(f32[4,5,3,720]{3,2,1,0:T(4,128)S(1)} %get-tuple-element.35), channel_id=1, source_target_pairs={{4,0},{8,4},{12,8},{16,12},{20,16},{24,20},{28,24},{5,1},{9,5},{13... | collective-permute-start | bytes 518408 | tf_op jit(solution)/shard_map/ppermute | solution.py:18
  48.9 0.4 collective-permute-done.5
  49.4 5.3 %collective-permute-done.6 = f32[4,5,3,720]{3,2,1,0:T(4,128)S(1)} collective-permute-done((f32[4,5,3,720]{3,2,1,0:T(4,128)S(1)}, f32[4,5,3,720]{3,2,1,0:T(4,128)S(1)}, u32[]{:S(2)}, u32[]{:S(2)}) %collective-permute-start.6) | collective-permute-done | bytes 172832 | tf_op jit(solution)/shard_map/ppermute | solution.py:18
  54.6 0.2 broadcast_select_fusion.2
  55.1 0.4 fusion.40
  55.5 1.0 %fusion.13 = f32[4,5,9,720]{3,2,1,0:T(8,128)S(1)} fusion(f32[4,5,8,720]{3,2,1,0:T(8,128)S(1)} %bitcast_select_fusion, f32[4,5,3,720]{3,2,1,0:T(4,128)S(1)} %get-tuple-element.55, f32[4,5,3,720]{3,2,1,0:T(4,128)S(1)} %get-tuple-element.54, f32[4,5,11,720]{3,2,1,0:T(8,128)S(1)} %fusion.40, f32[9]{0:T(128)S(1)} %or_select_fusion, ...), kind=kLoop, calls=%fused_computation.35 | loop fusion | flops 2980800 | bytes 3216996 | tf_op jit(solution)/shard_map/mul | solution.py:276
  56.5 0.2 fusion.55
  56.7 0.4 multiply_reduce_fusion.1
  57.1 2.1 %fusion.1 = f32[4,80,360]{2,1,0:T(8,128)S(1)} fusion(f32[4,180,720]{2,1,0:T(8,128)S(1)} %copy.90, f32[4,180,720]{2,1,0:T(8,128)S(1)} %copy-done.1, f32[4,40,720]{2,1,0:T(8,128)S(1)} %neg.14, f32[4,40,720]{2,1,0:T(8,128)S(1)} %get-tuple-element.5), kind=kOutput, calls=%fused_computation.11 | convolution fusion | flops 498931200 | bytes 5529600 | tf_op jit(solution)/shard_map/dot_general | solution.py:95
  59.3 1.8 %fusion = f32[4,80,720]{2,1,0:T(8,128)S(1)} fusion(f32[4,180,720]{2,1,0:T(8,128)S(1)} %copy.90, f32[4,180,720]{2,1,0:T(8,128)S(1)} %copy-done.1, f32[4,40,180]{2,1,0:T(8,128)S(1)} %get-tuple-element.29, f32[4,40,180]{2,1,0:T(8,128)S(1)} %get-tuple-element.9, f32[4,40,180]{2,1,0:T(8,128)S(1)} %get-tuple-element.10), kind=kOutput, calls=%fused_computation.10 | convolution fusion | flops 499046400 | bytes 5414400 | tf_op jit(solution)/shard_map/dot_general | solution.py:104
  61.2 0.3 subtract_reduce_fusion
  61.8 0.6 collective-permute-start.7
  62.4 2.1 %collective-permute-start.8 = (f32[5,8,720]{2,1,0:T(8,128)S(1)}, f32[5,8,720]{2,1,0:T(8,128)S(1)}, u32[]{:S(2)}, u32[]{:S(2)}) collective-permute-start(f32[5,8,720]{2,1,0:T(8,128)S(1)} %get-tuple-element.32), channel_id=1, source_target_pairs={{0,2},{1,3},{2,0},{3,1},{4,6},{5,7},{6,4},{7,5},{8,10},{9,11},{10,... | collective-permute-start | bytes 345608 | tf_op jit(solution)/shard_map/ppermute | solution.py:18
  64.5 1.4 %collective-permute-start.9 = (f32[5,8,720]{2,1,0:T(8,128)S(1)}, f32[5,8,720]{2,1,0:T(8,128)S(1)}, u32[]{:S(2)}, u32[]{:S(2)}) collective-permute-start(f32[5,8,720]{2,1,0:T(8,128)S(1)} %get-tuple-element.31), channel_id=1, source_target_pairs={{0,1},{1,2},{2,3},{3,0},{4,5},{5,6},{6,7},{7,4},{8,9},{9,10},{10,1... | collective-permute-start | bytes 345608 | tf_op jit(solution)/shard_map/ppermute | solution.py:18
  65.9 1.1 %collective-permute-done.7 = f32[5,8,720]{2,1,0:T(8,128)S(1)} collective-permute-done((f32[5,8,720]{2,1,0:T(8,128)S(1)}, f32[5,8,720]{2,1,0:T(8,128)S(1)}, u32[]{:S(2)}, u32[]{:S(2)}) %collective-permute-start.7) | collective-permute-done | bytes 115232 | tf_op jit(solution)/shard_map/ppermute | solution.py:18
  67.0 6.8 %collective-permute-done.8 = f32[5,8,720]{2,1,0:T(8,128)S(1)} collective-permute-done((f32[5,8,720]{2,1,0:T(8,128)S(1)}, f32[5,8,720]{2,1,0:T(8,128)S(1)}, u32[]{:S(2)}, u32[]{:S(2)}) %collective-permute-start.8) | collective-permute-done | bytes 115232 | tf_op jit(solution)/shard_map/ppermute | solution.py:18
  73.9 0.8 %pad_maximum_fusion.14 = f32[5,4,8,720]{3,2,1,0:T(8,128)} fusion(f32[5,1,8,720]{3,2,1,0:T(8,128)S(1)} %get-tuple-element.24, f32[5,1,8,720]{3,2,1,0:T(8,128)S(1)} %get-tuple-element.25, f32[5,1,8,720]{3,2,1,0:T(8,128)S(1)} %get-tuple-element.26, f32[5,1,8,720]{3,2,1,0:T(8,128)S(1)} %get-tuple-element.23), kind=kLoop, calls=%fused_computation.145 | loop fusion | flops 345600 | bytes 921600 | tf_op jit(solution)/shard_map/stack | solution.py:292
  (65 shorter events, 3.3 us)
Async XLA Ops:
  0.0 7.3 %copy-start = (s32[64]{0:T(128)S(1)}, s32[64]{0:T(128)}, u32[]{:S(2)}) copy-start(s32[64]{0:T(128)} %param.7) | copy-start | bytes 772
  2.0 15.0 %collective-permute-start.2 = (f32[56,720]{1,0:T(8,128)S(1)}, f32[56,720]{1,0:T(8,128)S(1)}, u32[]{:S(2)}, u32[]{:S(2)}) collective-permute-start(f32[56,720]{1,0:T(8,128)S(1)} %pad_maximum_fusion.23), channel_id=1, source_target_pairs={{0,3},{1,0},{2,1},{3,2},{4,7},{5,4},{6,5},{7,6},{8,11},{9,8},{10,9... | collective-permute-start | bytes 483848 | tf_op jit(solution)/shard_map/ppermute | solution.py:18
  5.4 14.7 %collective-permute-start.1 = (f32[56,720]{1,0:T(8,128)S(1)}, f32[56,720]{1,0:T(8,128)S(1)}, u32[]{:S(2)}, u32[]{:S(2)}) collective-permute-start(f32[56,720]{1,0:T(8,128)S(1)} %pad_maximum_fusion.22), channel_id=1, source_target_pairs={{0,2},{1,3},{2,0},{3,1},{4,6},{5,7},{6,4},{7,5},{8,10},{9,11},{10,... | collective-permute-start | bytes 483848 | tf_op jit(solution)/shard_map/ppermute | solution.py:18
  5.5 14.6 %collective-permute-start = (f32[56,720]{1,0:T(8,128)S(1)}, f32[56,720]{1,0:T(8,128)S(1)}, u32[]{:S(2)}, u32[]{:S(2)}) collective-permute-start(f32[56,720]{1,0:T(8,128)S(1)} %pad_maximum_fusion.21), channel_id=1, source_target_pairs={{0,1},{1,2},{2,3},{3,0},{4,5},{5,6},{6,7},{7,4},{8,9},{9,10},{10,1... | collective-permute-start | bytes 483848 | tf_op jit(solution)/shard_map/ppermute | solution.py:18
  22.4 12.2 %collective-permute-start.4 = (f32[4,5,3,720]{3,2,1,0:T(4,128)S(1)}, f32[4,5,3,720]{3,2,1,0:T(4,128)S(1)}, u32[]{:S(2)}, u32[]{:S(2)}) collective-permute-start(f32[4,5,3,720]{3,2,1,0:T(4,128)S(1)} %get-tuple-element.41), channel_id=1, source_target_pairs={{0,4},{4,8},{8,12},{12,16},{16,20},{20,24},{24,28},{1,5},{5,9},{9,... | collective-permute-start | bytes 518408 | tf_op jit(solution)/shard_map/ppermute | solution.py:18
  26.4 7.9 %collective-permute-start.3 = (f32[4,16,720]{2,1,0:T(8,128)S(1)}, f32[4,16,720]{2,1,0:T(8,128)S(1)}, u32[]{:S(2)}, u32[]{:S(2)}) collective-permute-start(f32[4,16,720]{2,1,0:T(8,128)S(1)} %pad_maximum_fusion.19), channel_id=1, source_target_pairs={{4,0},{8,4},{12,8},{16,12},{20,16},{24,20},{28,24},{5,1},{9,5},{13... | collective-permute-start | bytes 552968 | tf_op jit(solution)/shard_map/ppermute | solution.py:18
  36.4 1.6 %copy-start.1 = (f32[4,180,720]{2,1,0:T(8,128)S(1)}, f32[4,180,720]{2,1,0:T(8,128)}, u32[]{:S(2)}) copy-start(f32[4,180,720]{2,1,0:T(8,128)} %copy.89) | copy-start | bytes 6220804
  44.3 5.0 %collective-permute-start.5 = (f32[4,5,3,720]{3,2,1,0:T(4,128)S(1)}, f32[4,5,3,720]{3,2,1,0:T(4,128)S(1)}, u32[]{:S(2)}, u32[]{:S(2)}) collective-permute-start(f32[4,5,3,720]{3,2,1,0:T(4,128)S(1)} %get-tuple-element.34), channel_id=1, source_target_pairs={{0,4},{4,8},{8,12},{12,16},{16,20},{20,24},{24,28},{1,5},{5,9},{9,... | collective-permute-start | bytes 518408 | tf_op jit(solution)/shard_map/ppermute | solution.py:18
  46.2 8.4 %collective-permute-start.6 = (f32[4,5,3,720]{3,2,1,0:T(4,128)S(1)}, f32[4,5,3,720]{3,2,1,0:T(4,128)S(1)}, u32[]{:S(2)}, u32[]{:S(2)}) collective-permute-start(f32[4,5,3,720]{3,2,1,0:T(4,128)S(1)} %get-tuple-element.35), channel_id=1, source_target_pairs={{4,0},{8,4},{12,8},{16,12},{20,16},{24,20},{28,24},{5,1},{9,5},{13... | collective-permute-start | bytes 518408 | tf_op jit(solution)/shard_map/ppermute | solution.py:18
  61.8 5.2 %collective-permute-start.7 = (f32[5,8,720]{2,1,0:T(8,128)S(1)}, f32[5,8,720]{2,1,0:T(8,128)S(1)}, u32[]{:S(2)}, u32[]{:S(2)}) collective-permute-start(f32[5,8,720]{2,1,0:T(8,128)S(1)} %get-tuple-element.33), channel_id=1, source_target_pairs={{0,3},{1,0},{2,1},{3,2},{4,7},{5,4},{6,5},{7,6},{8,11},{9,8},{10,9... | collective-permute-start | bytes 345608 | tf_op jit(solution)/shard_map/ppermute | solution.py:18
  62.4 11.4 %collective-permute-start.8 = (f32[5,8,720]{2,1,0:T(8,128)S(1)}, f32[5,8,720]{2,1,0:T(8,128)S(1)}, u32[]{:S(2)}, u32[]{:S(2)}) collective-permute-start(f32[5,8,720]{2,1,0:T(8,128)S(1)} %get-tuple-element.32), channel_id=1, source_target_pairs={{0,2},{1,3},{2,0},{3,1},{4,6},{5,7},{6,4},{7,5},{8,10},{9,11},{10,... | collective-permute-start | bytes 345608 | tf_op jit(solution)/shard_map/ppermute | solution.py:18
  64.5 9.3 %collective-permute-start.9 = (f32[5,8,720]{2,1,0:T(8,128)S(1)}, f32[5,8,720]{2,1,0:T(8,128)S(1)}, u32[]{:S(2)}, u32[]{:S(2)}) collective-permute-start(f32[5,8,720]{2,1,0:T(8,128)S(1)} %get-tuple-element.31), channel_id=1, source_target_pairs={{0,1},{1,2},{2,3},{3,0},{4,5},{5,6},{6,7},{7,4},{8,9},{9,10},{10,1... | collective-permute-start | bytes 345608 | tf_op jit(solution)/shard_map/ppermute | solution.py:18

commit v12 on v11

--- a/solution.py
+++ b/solution.py
@@ -221,12 +221,18 @@
 
     pieces = [payload_for(lon_index)]
     for by in range(1, lon_devices):
-        pieces.append(shift(payload_for((lon_index + by) % lon_devices), "lon", by, True))
+        pieces.append(
+            lax.ppermute(payload_for(lon_index ^ by), "lon", [(i, i ^ by) for i in range(lon_devices)])
+        )
+    positions = jnp.arange(lon_devices, dtype=jnp.int32)
+    tile_at = lon_index ^ positions
+    west_at = lon_index ^ ((tile_at - 1) % lon_devices)
+    east_at = lon_index ^ ((tile_at + 1) % lon_devices)
     payload = jnp.stack(pieces)
     state = payload[:, :count].reshape(lon_devices, tracer_count, lat_rows, lon_cols)
     cx = payload[:, None, count : count + lat_rows]
     cy = payload[:, None, count + lat_rows :]
-    east_courant = jnp.concatenate([jnp.roll(cx[..., lon_cols - 1 :], -1, axis=0), cx], axis=3)
+    east_courant = jnp.concatenate([jnp.take(cx[..., lon_cols - 1 :], west_at, axis=0), cx], axis=3)
 
     held_global = lat_index * lat_rows + jnp.arange(count, dtype=jnp.int32) % lat_rows
     polar = (held_global < total_rows // 4) | (held_global >= total_rows - total_rows // 4)
@@ -238,25 +244,34 @@
     scale = jnp.where(k == 0, 1.0 / circle, 2.0 / circle).astype(jnp.float32)
     weights = jnp.where(k[:, None, :] < cut[None, :, None], scale[:, None, :], 0.0)
     basis = product_basis(lon_devices, lon_cols, circle)
-    roots = root_table(
-        lon_devices, (lax.axis_index("lon") - jnp.arange(lon_devices, dtype=jnp.int32)) % lon_devices
-    )
+    roots = root_table(lon_devices, tile_at)
 
     for substep in range(SUBSTEPS):
-        south_in = shift(state[:, :, lat_rows - HALO :], "lat", 1, False)
+        top = state[:, :, lat_rows - HALO :].reshape(lon_devices, tracer_count * HALO, lon_cols)
+        bottom = state[:, :, :HALO].reshape(lon_devices, tracer_count * HALO, lon_cols)
         if substep == 0:
-            going = jnp.concatenate(
-                [state[:, :, :HALO].reshape(lon_devices, tracer_count * HALO, lon_cols), cy[:, 0, :1]],
-                axis=1,
-            )
-            coming = shift(going, "lat", -1, False)
-            north_in = coming[:, : tracer_count * HALO].reshape(
-                lon_devices, tracer_count, HALO, lon_cols
-            )
-            north_cy = jnp.where(is_north, 0.0, coming[:, None, tracer_count * HALO :])
+            bottom = jnp.concatenate([bottom, cy[:, 0, :1]], axis=1)
+            top = jnp.concatenate([top, jnp.zeros_like(cy[:, 0, :1])], axis=1)
+        is_even = lat_index % 2 == 0
+        recv_a = lax.ppermute(
+            jnp.where(is_even, top, bottom), "lat", [(i, i ^ 1) for i in range(lat_devices) if i ^ 1 < lat_devices]
+        )
+        recv_b = lax.ppermute(
+            jnp.where(is_even, bottom, top),
+            "lat",
+            [(i, i + (1 if i % 2 else -1)) for i in range(lat_devices) if 0 <= i + (1 if i % 2 else -1) < lat_devices],
+        )
+        from_south = jnp.where(is_even, recv_b, recv_a)
+        from_north = jnp.where(is_even, recv_a, recv_b)
+        south_in = from_south[:, : tracer_count * HALO].reshape(
+            lon_devices, tracer_count, HALO, lon_cols
+        )
+        north_in = from_north[:, : tracer_count * HALO].reshape(
+            lon_devices, tracer_count, HALO, lon_cols
+        )
+        if substep == 0:
+            north_cy = jnp.where(is_north, 0.0, from_north[:, None, tracer_count * HALO :])
             north_courant = jnp.concatenate([cy, north_cy], axis=2)
-        else:
-            north_in = shift(state[:, :, :HALO], "lat", -1, False)
         edge = jnp.where(is_south, state[:, :, :HALO], state[:, :, lat_rows - HALO :])
         far = jnp.roll(edge, lon_devices // 2, axis=0)
         far_rev = jnp.concatenate([far[:, :, 2:3], far[:, :, 1:2], far[:, :, 0:1]], axis=2)
@@ -265,9 +280,9 @@
         extended = jnp.concatenate([south_rows, state, north_rows], axis=2)
         wrapped = jnp.concatenate(
             [
-                jnp.roll(state[..., lon_cols - HALO :], -1, axis=0),
+                jnp.take(state[..., lon_cols - HALO :], west_at, axis=0),
                 state,
-                jnp.roll(state[..., :HALO], 1, axis=0),
+                jnp.take(state[..., :HALO], east_at, axis=0),
             ],
             axis=3,
         )
@@ -281,19 +296,22 @@
         state = rows.reshape(lon_devices, tracer_count, lat_rows, lon_cols)
 
     back = [state[0]] + [
-        shift(state[(lon_devices - by) % lon_devices], "lon", by, True) for by in range(1, lon_devices)
+        lax.ppermute(state[by], "lon", [(i, i ^ by) for i in range(lon_devices)])
+        for by in range(1, lon_devices)
     ]
     levels = []
     for level in range(level_count):
         pick = back[0]
         for by in range(1, lon_devices):
-            pick = jnp.where((lon_index - by) % lon_devices == level, back[by], pick)
+            pick = jnp.where((lon_index ^ by) == level, back[by], pick)
         levels.append(pick)
     return jnp.stack(levels, axis=1)
 
 
 def on_device(tracers, courant_x, courant_y, cutoffs):
-    if tracers.shape[1] == lax.axis_size("lon") and tracers.shape[2] >= HALO:
+    lon_devices = lax.axis_size("lon")
+    power_of_two = lon_devices & (lon_devices - 1) == 0
+    if tracers.shape[1] == lon_devices and power_of_two and tracers.shape[2] >= HALO:
         return transposed_path(tracers, courant_x, courant_y, cutoffs)
     return tiled_path(tracers, courant_x, courant_y, cutoffs)
 

time: 75.4 us -> 113 us (1.50)
  local copies, waits for them, and re-layouts: 10.4 us -> 37 us
  other arithmetic: 15 us -> 31.5 us
  waiting for transfers between devices: 22.5 us -> 18.6 us
  starting transfers between devices: 18.5 us -> 15.7 us
    gather x0 -> x11, local copies, waits for them, and re-layouts: none -> 14.7 us  [the longest x4 7.35 us: transposed_path(): jnp.take(state[..., lon_cols - HALO:], west_at, axis=0)]
    unnamed x4 -> x88, local copies, waits for them, and re-layouts: 1.04 us -> 8.5 us
    select_n x3 -> x15, other arithmetic: 0.04 us -> 6.55 us  [the longest x3 1.97 us: transposed_path(): jnp.take(state[..., :HALO], east_at, axis=0)]
    slice x7 -> x8, local copies, waits for them, and re-layouts: 0.57 us -> 4.66 us  [the longest x3 3.13 us: transposed_path(): state[..., lon_cols - HALO:]]
    ppermute x10, waiting for transfers between devices: 22.5 us -> 18.6 us  [the longest x2 10.6 us: transposed_path(): lax.ppermute(jnp.where(is_even, bottom, top), 'lat', [(i, i + (1 if i % 2...]
    ppermute x10, starting transfers between devices: 18.5 us -> 15.7 us  [the longest x2 6.56 us: transposed_path(): lax.ppermute(jnp.where(is_even, bottom, top), 'lat', [(i, i + (1 if i % 2...]
    gather x0 -> x3, other arithmetic: none -> 1.79 us
    slice x1, other arithmetic: 0.02 us -> 1.49 us  [transposed_path(): cy = payload[:, None, count + lat_rows:]]
  transfers between devices with their start and end apart: 10 -> 10, of which waited for: 6 -> 4; matrix products, arithmetic and copies ran while one was open for 15% -> 16% of each run, Pallas kernels for 0% -> 0%
where the time goes in v12:
time: 113 us; the launch traced here: 112 us
  local copies, waits for them, and re-layouts  37 us (33%)
  other arithmetic  31.5 us (28%)
  waiting for transfers between devices  18.6 us (16%)
  starting transfers between devices  15.7 us (14%)
  matrix products  7.76 us (7%)
    ppermute x2, waiting for transfers between devices, transposed_path(): lax.ppermute(jnp.where(is_even, bottom, top), 'lat', [(i, i + (1 if i % 2...  10.6 us
    unnamed x88, local copies, waits for them, and re-layouts  8.5 us
    ppermute x3, waiting for transfers between devices, transposed_path(): lax.ppermute(state[by], 'lon', [(i, i ^ by) for i in range(lon_devices)])  7.98 us
    gather x4, local copies, waits for them, and re-layouts, transposed_path(): jnp.take(state[..., lon_cols - HALO:], west_at, axis=0)  7.35 us
    ppermute x2, starting transfers between devices, transposed_path(): lax.ppermute(jnp.where(is_even, bottom, top), 'lat', [(i, i + (1 if i % 2...  6.56 us
    gather x4, local copies, waits for them, and re-layouts, transposed_path(): jnp.take(state[..., :HALO], east_at, axis=0)  5.21 us
    dot_general x2, matrix products, filter_rows(): lax.dot_general(z, basis, (((2,), (q_axis,)), ((0,), (0,))), precision=MA...  4.13 us
    ppermute x3, starting transfers between devices, transposed_path(): lax.ppermute(payload_for(lon_index ^ by), 'lon', [(i, i ^ by) for i in ra...  3.81 us
  transfers between devices with their start and end apart: 10, of which 4 were waited for; matrix products, arithmetic and copies ran while one was open for 16% of the time, Pallas kernels for 0%

profile of v12, /device:TPU:3, one launch (start us, length us, event | category | flops | bytes accessed | tf_op | source)
XLA Modules:
  0.0 111.5 jit_solution(10148735228910517030)
XLA Ops:
  0.0 1.1 %dynamic-slice_bitcast_fusion.3 = (f32[40,720]{1,0:T(8,128)S(1)}, f32[40,720]{1,0:T(8,128)S(1)}, f32[40,720]{1,0:T(8,128)S(1)}, f32[40,720]{1,0:T(8,128)S(1)}) fusion(f32[5,4,8,720]{3,2,1,0:T(8,128)} %param.6, s32[]{:T(128)S(6)} %select_n.432, s32[]{:T(128)S(6)} %select_n.434, s32[]{:T(128)S(6)} %select_n.433, s32[]{:T(128)S(6)} %select_n.435), kind=kLoop, calls=%fused_computation.227 | loop fusion | bytes 921616 | tf_op jit(solution)/shard_map/reshape | solution.py:215
  1.1 0.9 dynamic-slice_bitcast_fusion.10
  2.0 3.4 %collective-permute-start.2 = (f32[56,720]{1,0:T(8,128)S(1)}, f32[56,720]{1,0:T(8,128)S(1)}, u32[]{:S(2)}, u32[]{:S(2)}) collective-permute-start(f32[56,720]{1,0:T(8,128)S(1)} %pad_maximum_fusion.25), channel_id=1, source_target_pairs={{0,3},{1,2},{2,1},{3,0},{4,7},{5,6},{6,5},{7,4},{8,11},{9,10},{10,... | collective-permute-start | bytes 483848 | tf_op jit(solution)/shard_map/ppermute | solution.py:225
  10.5 0.8 gather_fusion.1
  13.8 3.2 %multiply_subtract_fusion = (f32[4,180,30,24]{1,3,2,0:T(8,128)}, f32[4,180,30,24]{1,3,2,0:T(8,128)}) fusion(f32[4,180,24]{1,2,0:T(8,128)S(1)} %get-tuple-element.76, f32[4,180,30]{1,2,0:T(8,128)S(1)} %get-tuple-element.74, f32[4,180,24]{1,2,0:T(8,128)S(1)} %get-tuple-element.75, f32[4,180,30]{1,2,0:T(8,128)S(1)} %get-tuple-element.73), kind=kLoop, calls=%fused_computation.8 | loop fusion | flops 3110400 | bytes 4458240 | tf_op jit(solution)/shard_map/sub | solution.py:34
  17.5 2.3 %copy.314 = f32[4,180,720]{2,1,0:T(8,128)S(1)} copy(f32[4,180,720]{1,2,0:T(8,128)} %bitcast.106) | data formatting | bytes 4147200 | tf_op jit(solution)/shard_map/add | solution.py:35
  19.8 3.3 %copy.313 = f32[4,180,720]{2,1,0:T(8,128)} copy(f32[4,180,720]{1,2,0:T(8,128)} %bitcast.105) | data formatting | bytes 4147200 | tf_op jit(solution)/shard_map/sub | solution.py:34
  24.0 1.5 %pad_maximum_fusion.26 = (f32[4,8,720]{2,1,0:T(8,128)}, f32[4,8,720]{2,1,0:T(8,128)S(1)}) fusion(f32[1,56,720]{2,1,0:T(8,128)S(1)} %bitcast.120, f32[1,56,720]{2,1,0:T(8,128)S(1)} %bitcast.122, f32[1,56,720]{2,1,0:T(8,128)} %bitcast.124, f32[1,56,720]{2,1,0:T(8,128)S(1)} %maximum_bitcast_fusion.1), kind=kLoop, calls=%fused_computation.231 | loop fusion | flops 138240 | bytes 829440 | tf_op jit(solution)/shard_map/slice | solution.py:234
  27.1 0.8 abs_multiply_fusion
  28.6 0.7 fusion.168
  29.3 1.7 %copy.335 = f32[4,5,8,3]{2,3,1,0:T(4,128)} copy(f32[4,5,8,3]{3,2,1,0:T(8,128)} %get-tuple-element.38) | data formatting | bytes 3840
  31.0 2.1 %gather_fusion.3 = f32[4,5,8,3]{2,3,1,0:T(4,128)} fusion(f32[4,5,8,3]{2,3,1,0:T(4,128)} %copy.335, s32[1024]{0:T(1024)} %pad_clamp_fusion.1), kind=kCustom, calls=%fused_computation.1.clone | custom fusion | bytes 3856 | tf_op jit(solution)/shard_map/jit(_take)/gather | solution.py:285
  33.1 1.6 %copy.298 = f32[4,5,8,3]{3,2,1,0:T(8,128)} copy(f32[4,5,8,3]{2,3,1,0:T(4,128)} %gather_fusion.3) | data formatting | bytes 3840 | tf_op jit(solution)/shard_map/jit(_take)/gather | solution.py:285
  34.7 1.7 %copy.334 = f32[4,5,8,3]{2,3,1,0:T(4,128)} copy(f32[4,5,8,3]{3,2,1,0:T(8,128)} %get-tuple-element.37) | data formatting | bytes 3840
  36.4 2.1 %gather_fusion.2 = f32[4,5,8,3]{2,3,1,0:T(4,128)} fusion(f32[4,5,8,3]{2,3,1,0:T(4,128)} %copy.334, s32[1024]{0:T(1024)} %pad_clamp_fusion.2), kind=kCustom, calls=%fused_computation.clone | custom fusion | bytes 3856 | tf_op jit(solution)/shard_map/jit(_take)/gather | solution.py:283
  38.5 1.6 %copy.296 = f32[4,5,8,3]{3,2,1,0:T(8,128)} copy(f32[4,5,8,3]{2,3,1,0:T(4,128)} %gather_fusion.2) | data formatting | bytes 3840 | tf_op jit(solution)/shard_map/jit(_take)/gather | solution.py:283
  40.1 1.0 broadcast_select_fusion.8
  41.0 1.0 broadcast_select_fusion.7
  42.8 1.4 %copy.293 = f32[4,1,8,1]{3,2,0,1:T(8,128)} copy(f32[4,1,8,1]{2,0,3,1:T(4,128)} %bitcast.128) | data formatting | bytes 256 | tf_op jit(solution)/shard_map/jit(_take)/gather | solution.py:235
  44.1 0.8 broadcast_select_fusion.11
  45.1 1.5 %fusion.82 = f32[4,5,8,721]{3,2,1,0:T(8,128)S(1)} fusion(f32[4,5,8,3]{3,2,1,0:T(8,128)} %copy-done.13, f32[4,5,8,3]{3,2,1,0:T(8,128)} %copy-done.12, f32[4,5,8,723]{3,2,1,0:T(8,128)S(1)} %fusion.73, f32[4,5,8,720]{3,2,1,0:T(8,128)S(1)} %slice_bitcast_fusion, f32[4,8,721]{2,1,0:T(8,128)S(1)} %copy-done.19, f32[4,8,721]{2,1,0:T(8,128)S(1)} %copy-done.17, ...), kind=kLoop, calls=%fused_computation.122 | loop fusion | flops 2537920 | bytes 2610336 | tf_op jit(solution)/shard_map/mul | solution.py:63
  47.6 1.5 %collective-permute-start.3 = (f32[4,16,720]{2,1,0:T(8,128)S(1)}, f32[4,16,720]{2,1,0:T(8,128)S(1)}, u32[]{:S(2)}, u32[]{:S(2)}) collective-permute-start(f32[4,16,720]{2,1,0:T(8,128)S(1)} %get-tuple-element.46), channel_id=1, source_target_pairs={{0,4},{4,0},{8,12},{12,8},{16,20},{20,16},{24,28},{28,24},{1,5},{5... | collective-permute-start | bytes 552968 | tf_op jit(solution)/shard_map/ppermute | solution.py:256
  49.1 3.2 %collective-permute-start.4 = (f32[4,16,720]{2,1,0:T(8,128)S(1)}, f32[4,16,720]{2,1,0:T(8,128)S(1)}, u32[]{:S(2)}, u32[]{:S(2)}) collective-permute-start(f32[4,16,720]{2,1,0:T(8,128)S(1)} %get-tuple-element.45), channel_id=1, source_target_pairs={{4,8},{8,4},{12,16},{16,12},{20,24},{24,20},{5,9},{9,5},{13,17},{1... | collective-permute-start | bytes 552968 | tf_op jit(solution)/shard_map/ppermute | solution.py:259
  52.5 6.0 %collective-permute-done.4 = f32[4,16,720]{2,1,0:T(8,128)S(1)} collective-permute-done((f32[4,16,720]{2,1,0:T(8,128)S(1)}, f32[4,16,720]{2,1,0:T(8,128)S(1)}, u32[]{:S(2)}, u32[]{:S(2)}) %collective-permute-start.4) | collective-permute-done | bytes 184352 | tf_op jit(solution)/shard_map/ppermute | solution.py:259
  60.0 1.0 fusion.30
  61.6 1.0 copy-done.1
  62.7 2.1 %fusion.3 = f32[4,80,360]{2,1,0:T(8,128)S(1)} fusion(f32[4,180,720]{2,1,0:T(8,128)S(1)} %copy.314, f32[4,180,720]{2,1,0:T(8,128)S(1)} %copy-done.1, f32[4,40,720]{2,1,0:T(8,128)S(1)} %neg.12, f32[4,40,720]{2,1,0:T(8,128)S(1)} %get-tuple-element.8), kind=kOutput, calls=%fused_computation.18 | convolution fusion | flops 498931200 | bytes 5529600 | tf_op jit(solution)/shard_map/dot_general | solution.py:95
  65.0 1.8 %fusion.2 = f32[4,80,720]{2,1,0:T(8,128)S(1)} fusion(f32[4,180,720]{2,1,0:T(8,128)S(1)} %copy.314, f32[4,180,720]{2,1,0:T(8,128)S(1)} %copy-done.1, f32[4,40,180]{2,1,0:T(8,128)S(1)} %get-tuple-element.25, f32[4,40,180]{2,1,0:T(8,128)S(1)} %get-tuple-element.12, f32[4,40,180]{2,1,0:T(8,128)S(1)} %get-tuple-element.13), kind=kOutput, calls=%fused_computation.17 | convolution fusion | flops 499046400 | bytes 5414400 | tf_op jit(solution)/shard_map/dot_general | solution.py:104
  67.3 0.8 copy-done.3
  68.1 0.7 fusion.166
  68.9 0.9 slice_select_fusion.2
  69.8 1.1 copy.317
  70.9 0.7 gather_fusion.5
  71.6 0.8 copy.318
  72.4 1.0 broadcast_select_fusion.5
  73.4 1.7 %copy.315 = f32[4,5,8,3]{2,3,1,0:T(4,128)} copy(f32[4,5,8,3]{3,2,1,0:T(8,128)} %get-tuple-element.32) | data formatting | bytes 3840 | tf_op jit(solution)/shard_map/slice | solution.py:283
  75.1 2.1 %gather_fusion.4 = f32[4,5,8,3]{2,3,1,0:T(4,128)} fusion(f32[4,5,8,3]{2,3,1,0:T(4,128)} %copy.315, s32[1024]{0:T(1024)} %pad_clamp_fusion.2), kind=kCustom, calls=%fused_computation.2.clone | custom fusion | bytes 3856 | tf_op jit(solution)/shard_map/jit(_take)/gather | solution.py:283
  77.1 1.6 %copy.316 = f32[4,5,8,3]{3,2,1,0:T(8,128)} copy(f32[4,5,8,3]{2,3,1,0:T(4,128)} %gather_fusion.4) | data formatting | bytes 3840 | tf_op jit(solution)/shard_map/jit(_take)/gather | solution.py:283
  78.7 1.0 broadcast_select_fusion.6
  81.7 3.4 %collective-permute-start.5 = (f32[4,15,720]{2,0,1:T(4,128)S(1)}, f32[4,15,720]{2,0,1:T(4,128)S(1)}, u32[]{:S(2)}, u32[]{:S(2)}) collective-permute-start(f32[4,15,720]{2,0,1:T(4,128)S(1)} %bitcast.125), channel_id=1, source_target_pairs={{4,8},{8,4},{12,16},{16,12},{20,24},{24,20},{5,9},{9,5},{13,17},{1... | collective-permute-start | bytes 518408 | tf_op jit(solution)/shard_map/ppermute | solution.py:259
  85.3 4.6 %collective-permute-done.5 = f32[4,15,720]{2,0,1:T(4,128)S(1)} collective-permute-done((f32[4,15,720]{2,0,1:T(4,128)S(1)}, f32[4,15,720]{2,0,1:T(4,128)S(1)}, u32[]{:S(2)}, u32[]{:S(2)}) %collective-permute-start.5) | collective-permute-done | bytes 172832 | tf_op jit(solution)/shard_map/ppermute | solution.py:259
  91.4 1.0 fusion.13
  94.0 2.1 %fusion.1 = f32[4,80,360]{2,1,0:T(8,128)S(1)} fusion(f32[4,180,720]{2,1,0:T(8,128)S(1)} %copy.314, f32[4,180,720]{2,1,0:T(8,128)S(1)} %copy-done.2, f32[4,40,720]{2,1,0:T(8,128)S(1)} %neg.14, f32[4,40,720]{2,1,0:T(8,128)S(1)} %get-tuple-element.6), kind=kOutput, calls=%fused_computation.16 | convolution fusion | flops 498931200 | bytes 5529600 | tf_op jit(solution)/shard_map/dot_general | solution.py:95
  96.3 1.8 %fusion = f32[4,80,720]{2,1,0:T(8,128)S(1)} fusion(f32[4,180,720]{2,1,0:T(8,128)S(1)} %copy.314, f32[4,180,720]{2,1,0:T(8,128)S(1)} %copy-done.2, f32[4,40,180]{2,1,0:T(8,128)S(1)} %get-tuple-element.24, f32[4,40,180]{2,1,0:T(8,128)S(1)} %get-tuple-element.10, f32[4,40,180]{2,1,0:T(8,128)S(1)} %get-tuple-element.11), kind=kOutput, calls=%fused_computation.15 | convolution fusion | flops 499046400 | bytes 5414400 | tf_op jit(solution)/shard_map/dot_general | solution.py:104
  98.9 3.4 %collective-permute-start.7 = (f32[5,8,720]{2,1,0:T(8,128)S(1)}, f32[5,8,720]{2,1,0:T(8,128)S(1)}, u32[]{:S(2)}, u32[]{:S(2)}) collective-permute-start(f32[5,8,720]{2,1,0:T(8,128)S(1)} %get-tuple-element.28), channel_id=1, source_target_pairs={{0,3},{1,2},{2,1},{3,0},{4,7},{5,6},{6,5},{7,4},{8,11},{9,10},{10,... | collective-permute-start | bytes 345608 | tf_op jit(solution)/shard_map/ppermute | solution.py:299
  102.7 2.8 %collective-permute-done.7 = f32[5,8,720]{2,1,0:T(8,128)S(1)} collective-permute-done((f32[5,8,720]{2,1,0:T(8,128)S(1)}, f32[5,8,720]{2,1,0:T(8,128)S(1)}, u32[]{:S(2)}, u32[]{:S(2)}) %collective-permute-start.7) | collective-permute-done | bytes 115232 | tf_op jit(solution)/shard_map/ppermute | solution.py:299
  105.4 5.2 %collective-permute-done.8 = f32[5,8,720]{2,1,0:T(8,128)S(1)} collective-permute-done((f32[5,8,720]{2,1,0:T(8,128)S(1)}, f32[5,8,720]{2,1,0:T(8,128)S(1)}, u32[]{:S(2)}, u32[]{:S(2)}) %collective-permute-start.8) | collective-permute-done | bytes 115232 | tf_op jit(solution)/shard_map/ppermute | solution.py:299
  110.7 0.8 pad_maximum_fusion.18
  (187 shorter events, 22.2 us)
Async XLA Ops:
  0.0 10.5 %copy-start = (s32[64]{0:T(128)S(1)}, s32[64]{0:T(128)}, u32[]{:S(2)}) copy-start(s32[64]{0:T(128)} %param.9) | copy-start | bytes 772
  2.0 21.1 %collective-permute-start.2 = (f32[56,720]{1,0:T(8,128)S(1)}, f32[56,720]{1,0:T(8,128)S(1)}, u32[]{:S(2)}, u32[]{:S(2)}) collective-permute-start(f32[56,720]{1,0:T(8,128)S(1)} %pad_maximum_fusion.25), channel_id=1, source_target_pairs={{0,3},{1,2},{2,1},{3,0},{4,7},{5,6},{6,5},{7,4},{8,11},{9,10},{10,... | collective-permute-start | bytes 483848 | tf_op jit(solution)/shard_map/ppermute | solution.py:225
  5.5 17.8 %collective-permute-start.1 = (f32[56,720]{1,0:T(8,128)S(1)}, f32[56,720]{1,0:T(8,128)S(1)}, u32[]{:S(2)}, u32[]{:S(2)}) collective-permute-start(f32[56,720]{1,0:T(8,128)S(1)} %pad_maximum_fusion.24), channel_id=1, source_target_pairs={{0,2},{1,3},{2,0},{3,1},{4,6},{5,7},{6,4},{7,5},{8,10},{9,11},{10,... | collective-permute-start | bytes 483848 | tf_op jit(solution)/shard_map/ppermute | solution.py:225
  5.6 17.7 %collective-permute-start = (f32[56,720]{1,0:T(8,128)S(1)}, f32[56,720]{1,0:T(8,128)S(1)}, u32[]{:S(2)}, u32[]{:S(2)}) collective-permute-start(f32[56,720]{1,0:T(8,128)S(1)} %pad_maximum_fusion.23), channel_id=1, source_target_pairs={{0,1},{1,0},{2,3},{3,2},{4,5},{5,4},{6,7},{7,6},{8,9},{9,8},{10,11... | collective-permute-start | bytes 483848 | tf_op jit(solution)/shard_map/ppermute | solution.py:225
  13.7 53.1 %copy-start.27 = (f32[4,4]{1,0:T(4,128)}, f32[4,4]{1,0:T(4,128)S(1)}, u32[]{:S(2)}) copy-start(f32[4,4]{1,0:T(4,128)S(1)} %get-tuple-element.77) | copy-start | bytes 196
  13.8 53.1 %copy-start.29 = (f32[4,4]{1,0:T(4,128)}, f32[4,4]{1,0:T(4,128)S(1)}, u32[]{:S(2)}) copy-start(f32[4,4]{1,0:T(4,128)S(1)} %get-tuple-element.78) | copy-start | bytes 196
  24.0 18.1 %copy-start.5 = (f32[4,56,720]{2,1,0:T(8,128)}, f32[4,56,720]{2,1,0:T(8,128)S(1)}, u32[]{:S(2)}) copy-start(f32[4,56,720]{2,1,0:T(8,128)S(1)} %pad_maximum_fusion.11) | copy-start | bytes 1935364
  26.3 1.6 %copy-start.33 = (f32[4,8]{1,0:T(4,128)}, f32[4,8]{1,0:T(4,128)S(1)}, u32[]{:S(2)}) copy-start(f32[4,8]{1,0:T(4,128)S(1)} %gather_fusion) | copy-start | bytes 388
  41.0 1.7 %copy-start.12 = (f32[4,5,8,3]{3,2,1,0:T(8,128)}, f32[4,5,8,3]{3,2,1,0:T(8,128)S(1)}, u32[]{:S(2)}) copy-start(f32[4,5,8,3]{3,2,1,0:T(8,128)S(1)} %broadcast_select_fusion.8) | copy-start | bytes 5764
  42.0 0.7 copy-start.13
  42.3 2.8 %copy-start.17 = (f32[4,8,721]{2,1,0:T(8,128)S(1)}, f32[4,8,721]{2,1,0:T(8,128)}, u32[]{:S(2)}) copy-start(f32[4,8,721]{2,1,0:T(8,128)} %get-tuple-element.61) | copy-start | bytes 276868
  42.3 2.8 %copy-start.19 = (f32[4,8,721]{2,1,0:T(8,128)S(1)}, f32[4,8,721]{2,1,0:T(8,128)}, u32[]{:S(2)}) copy-start(f32[4,8,721]{2,1,0:T(8,128)} %get-tuple-element.62) | copy-start | bytes 276868
  45.0 1.8 %copy-start.21 = (f32[4,8,721]{2,1,0:T(8,128)}, f32[4,8,721]{2,1,0:T(8,128)S(1)}, u32[]{:S(2)}) copy-start(f32[4,8,721]{2,1,0:T(8,128)S(1)} %maximum_bitcast_fusion.2) | copy-start | bytes 276868
  46.5 0.9 copy-start.11
  47.6 4.9 %collective-permute-start.3 = (f32[4,16,720]{2,1,0:T(8,128)S(1)}, f32[4,16,720]{2,1,0:T(8,128)S(1)}, u32[]{:S(2)}, u32[]{:S(2)}) collective-permute-start(f32[4,16,720]{2,1,0:T(8,128)S(1)} %get-tuple-element.46), channel_id=1, source_target_pairs={{0,4},{4,0},{8,12},{12,8},{16,20},{20,16},{24,28},{28,24},{1,5},{5... | collective-permute-start | bytes 552968 | tf_op jit(solution)/shard_map/ppermute | solution.py:256
  49.1 9.4 %collective-permute-start.4 = (f32[4,16,720]{2,1,0:T(8,128)S(1)}, f32[4,16,720]{2,1,0:T(8,128)S(1)}, u32[]{:S(2)}, u32[]{:S(2)}) collective-permute-start(f32[4,16,720]{2,1,0:T(8,128)S(1)} %get-tuple-element.45), channel_id=1, source_target_pairs={{4,8},{8,4},{12,16},{16,12},{20,24},{24,20},{5,9},{9,5},{13,17},{1... | collective-permute-start | bytes 552968 | tf_op jit(solution)/shard_map/ppermute | solution.py:259
  58.6 1.2 %copy-start.7 = (f32[4,9,720]{2,1,0:T(8,128)}, f32[4,9,720]{2,1,0:T(8,128)S(1)}, u32[]{:S(2)}) copy-start(f32[4,9,720]{2,1,0:T(8,128)S(1)} %get-tuple-element.63) | copy-start | bytes 311044
  58.6 1.2 %copy-start.9 = (f32[4,9,720]{2,1,0:T(8,128)}, f32[4,9,720]{2,1,0:T(8,128)S(1)}, u32[]{:S(2)}) copy-start(f32[4,9,720]{2,1,0:T(8,128)S(1)} %get-tuple-element.64) | copy-start | bytes 311044
  58.7 1.1 %copy-start.24 = (pred[4,9,720]{2,1,0:T(8,128)(4,1)}, pred[4,9,720]{2,1,0:T(8,128)(4,1)S(1)}, u32[]{:S(2)}) copy-start(pred[4,9,720]{2,1,0:T(8,128)(4,1)S(1)} %fusion.114) | copy-start | bytes 77764
  60.0 1.1 copy-start.6
  60.0 1.1 copy-start.40
  61.1 1.6 %copy-start.1 = (f32[4,180,720]{2,1,0:T(8,128)S(1)}, f32[4,180,720]{2,1,0:T(8,128)}, u32[]{:S(2)}) copy-start(f32[4,180,720]{2,1,0:T(8,128)} %copy.313) | copy-start | bytes 6220804
  62.7 2.1 %copy-start.31 = (f32[4,180]{1,0:T(4,128)S(1)}, f32[4,180]{1,0:T(4,128)}, u32[]{:S(2)}) copy-start(f32[4,180]{1,0:T(4,128)} %compare_select_fusion) | copy-start | bytes 8644
  62.7 2.1 %copy-start.36 = (s32[40]{0:T(128)S(1)}, s32[40]{0:T(128)}, u32[]{:S(2)}) copy-start(s32[40]{0:T(128)} %and_select_fusion.1) | copy-start | bytes 484
  66.8 1.2 %copy-start.34 = (pred[5,8]{1,0:T(8,128)(4,1)S(1)}, pred[5,8]{1,0:T(8,128)(4,1)}, u32[]{:S(2)}) copy-start(pred[5,8]{1,0:T(8,128)(4,1)} %fusion.141) | copy-start | bytes 124
  67.2 0.8 copy-start.3
  69.8 10.7 %copy-start.26 = (pred[4,8,721]{2,1,0:T(8,128)(4,1)S(1)}, pred[4,8,721]{2,1,0:T(8,128)(4,1)}, u32[]{:S(2)}) copy-start(pred[4,8,721]{2,1,0:T(8,128)(4,1)} %broadcast_compare_fusion) | copy-start | bytes 69220
  78.7 1.7 %copy-start.18 = (f32[4,8,721]{2,1,0:T(8,128)S(1)}, f32[4,8,721]{2,1,0:T(8,128)}, u32[]{:S(2)}) copy-start(f32[4,8,721]{2,1,0:T(8,128)} %get-tuple-element.61) | copy-start | bytes 276868
  78.7 1.7 %copy-start.20 = (f32[4,8,721]{2,1,0:T(8,128)S(1)}, f32[4,8,721]{2,1,0:T(8,128)}, u32[]{:S(2)}) copy-start(f32[4,8,721]{2,1,0:T(8,128)} %get-tuple-element.62) | copy-start | bytes 276868
  78.7 1.7 %copy-start.22 = (f32[4,8,721]{2,1,0:T(8,128)S(1)}, f32[4,8,721]{2,1,0:T(8,128)}, u32[]{:S(2)}) copy-start(f32[4,8,721]{2,1,0:T(8,128)} %copy-done.21) | copy-start | bytes 276868
  80.5 0.9 copy-start.16
  80.5 1.1 copy-start.15
  80.5 4.5 %copy-start.14 = (f32[4,5,3,720]{3,2,1,0:T(4,128)S(1)}, f32[4,5,3,720]{3,2,1,0:T(4,128)}, u32[]{:S(2)}) copy-start(f32[4,5,3,720]{3,2,1,0:T(4,128)} %get-tuple-element.30) | copy-start | bytes 518404
  81.7 8.2 %collective-permute-start.5 = (f32[4,15,720]{2,0,1:T(4,128)S(1)}, f32[4,15,720]{2,0,1:T(4,128)S(1)}, u32[]{:S(2)}, u32[]{:S(2)}) collective-permute-start(f32[4,15,720]{2,0,1:T(4,128)S(1)} %bitcast.125), channel_id=1, source_target_pairs={{4,8},{8,4},{12,16},{16,12},{20,24},{24,20},{5,9},{9,5},{13,17},{1... | collective-permute-start | bytes 518408 | tf_op jit(solution)/shard_map/ppermute | solution.py:259
  85.1 4.8 %collective-permute-start.6 = (f32[4,15,720]{2,0,1:T(4,128)S(1)}, f32[4,15,720]{2,0,1:T(4,128)S(1)}, u32[]{:S(2)}, u32[]{:S(2)}) collective-permute-start(f32[4,15,720]{2,0,1:T(4,128)S(1)} %bitcast.126), channel_id=1, source_target_pairs={{0,4},{4,0},{8,12},{12,8},{16,20},{20,16},{24,28},{28,24},{1,5},{5... | collective-permute-start | bytes 518408 | tf_op jit(solution)/shard_map/ppermute | solution.py:256
  90.3 0.9 copy-start.8
  90.3 1.0 copy-start.10
  90.3 1.0 copy-start.25
  90.3 1.0 copy-start.39
  91.3 1.0 copy-start.4
  91.3 1.0 copy-start.35
  91.4 1.0 copy-start.41
  92.4 1.6 %copy-start.2 = (f32[4,180,720]{2,1,0:T(8,128)S(1)}, f32[4,180,720]{2,1,0:T(8,128)}, u32[]{:S(2)}) copy-start(f32[4,180,720]{2,1,0:T(8,128)} %copy.313) | copy-start | bytes 6220804
  94.0 2.1 %copy-start.32 = (f32[4,180]{1,0:T(4,128)S(1)}, f32[4,180]{1,0:T(4,128)}, u32[]{:S(2)}) copy-start(f32[4,180]{1,0:T(4,128)} %compare_select_fusion) | copy-start | bytes 8644
  94.0 2.1 %copy-start.37 = (s32[40]{0:T(128)S(1)}, s32[40]{0:T(128)}, u32[]{:S(2)}) copy-start(s32[40]{0:T(128)} %and_select_fusion.1) | copy-start | bytes 484
  98.9 6.5 %collective-permute-start.7 = (f32[5,8,720]{2,1,0:T(8,128)S(1)}, f32[5,8,720]{2,1,0:T(8,128)S(1)}, u32[]{:S(2)}, u32[]{:S(2)}) collective-permute-start(f32[5,8,720]{2,1,0:T(8,128)S(1)} %get-tuple-element.28), channel_id=1, source_target_pairs={{0,3},{1,2},{2,1},{3,0},{4,7},{5,6},{6,5},{7,4},{8,11},{9,10},{10,... | collective-permute-start | bytes 345608 | tf_op jit(solution)/shard_map/ppermute | solution.py:299
  102.3 8.3 %collective-permute-start.8 = (f32[5,8,720]{2,1,0:T(8,128)S(1)}, f32[5,8,720]{2,1,0:T(8,128)S(1)}, u32[]{:S(2)}, u32[]{:S(2)}) collective-permute-start(f32[5,8,720]{2,1,0:T(8,128)S(1)} %get-tuple-element.27), channel_id=1, source_target_pairs={{0,2},{1,3},{2,0},{3,1},{4,6},{5,7},{6,4},{7,5},{8,10},{9,11},{10,... | collective-permute-start | bytes 345608 | tf_op jit(solution)/shard_map/ppermute | solution.py:299
  102.3 8.3 %collective-permute-start.9 = (f32[5,8,720]{2,1,0:T(8,128)S(1)}, f32[5,8,720]{2,1,0:T(8,128)S(1)}, u32[]{:S(2)}, u32[]{:S(2)}) collective-permute-start(f32[5,8,720]{2,1,0:T(8,128)S(1)} %get-tuple-element.26), channel_id=1, source_target_pairs={{0,1},{1,0},{2,3},{3,2},{4,5},{5,4},{6,7},{7,6},{8,9},{9,8},{10,11... | collective-permute-start | bytes 345608 | tf_op jit(solution)/shard_map/ppermute | solution.py:299
  (5 other events, 3.3 us)

commit v13 on v12

--- a/solution.py
+++ b/solution.py
@@ -221,18 +221,12 @@
 
     pieces = [payload_for(lon_index)]
     for by in range(1, lon_devices):
-        pieces.append(
-            lax.ppermute(payload_for(lon_index ^ by), "lon", [(i, i ^ by) for i in range(lon_devices)])
-        )
-    positions = jnp.arange(lon_devices, dtype=jnp.int32)
-    tile_at = lon_index ^ positions
-    west_at = lon_index ^ ((tile_at - 1) % lon_devices)
-    east_at = lon_index ^ ((tile_at + 1) % lon_devices)
+        pieces.append(shift(payload_for((lon_index + by) % lon_devices), "lon", by, True))
     payload = jnp.stack(pieces)
     state = payload[:, :count].reshape(lon_devices, tracer_count, lat_rows, lon_cols)
     cx = payload[:, None, count : count + lat_rows]
     cy = payload[:, None, count + lat_rows :]
-    east_courant = jnp.concatenate([jnp.take(cx[..., lon_cols - 1 :], west_at, axis=0), cx], axis=3)
+    east_courant = jnp.concatenate([jnp.roll(cx[..., lon_cols - 1 :], -1, axis=0), cx], axis=3)
 
     held_global = lat_index * lat_rows + jnp.arange(count, dtype=jnp.int32) % lat_rows
     polar = (held_global < total_rows // 4) | (held_global >= total_rows - total_rows // 4)
@@ -244,7 +238,9 @@
     scale = jnp.where(k == 0, 1.0 / circle, 2.0 / circle).astype(jnp.float32)
     weights = jnp.where(k[:, None, :] < cut[None, :, None], scale[:, None, :], 0.0)
     basis = product_basis(lon_devices, lon_cols, circle)
-    roots = root_table(lon_devices, tile_at)
+    roots = root_table(
+        lon_devices, (lax.axis_index("lon") - jnp.arange(lon_devices, dtype=jnp.int32)) % lon_devices
+    )
 
     for substep in range(SUBSTEPS):
         top = state[:, :, lat_rows - HALO :].reshape(lon_devices, tracer_count * HALO, lon_cols)
@@ -280,9 +276,9 @@
         extended = jnp.concatenate([south_rows, state, north_rows], axis=2)
         wrapped = jnp.concatenate(
             [
-                jnp.take(state[..., lon_cols - HALO :], west_at, axis=0),
+                jnp.roll(state[..., lon_cols - HALO :], -1, axis=0),
                 state,
-                jnp.take(state[..., :HALO], east_at, axis=0),
+                jnp.roll(state[..., :HALO], 1, axis=0),
             ],
             axis=3,
         )
@@ -296,22 +292,19 @@
         state = rows.reshape(lon_devices, tracer_count, lat_rows, lon_cols)
 
     back = [state[0]] + [
-        lax.ppermute(state[by], "lon", [(i, i ^ by) for i in range(lon_devices)])
-        for by in range(1, lon_devices)
+        shift(state[(lon_devices - by) % lon_devices], "lon", by, True) for by in range(1, lon_devices)
     ]
     levels = []
     for level in range(level_count):
         pick = back[0]
         for by in range(1, lon_devices):
-            pick = jnp.where((lon_index ^ by) == level, back[by], pick)
+            pick = jnp.where((lon_index - by) % lon_devices == level, back[by], pick)
         levels.append(pick)
     return jnp.stack(levels, axis=1)
 
 
 def on_device(tracers, courant_x, courant_y, cutoffs):
-    lon_devices = lax.axis_size("lon")
-    power_of_two = lon_devices & (lon_devices - 1) == 0
-    if tracers.shape[1] == lon_devices and power_of_two and tracers.shape[2] >= HALO:
+    if tracers.shape[1] == lax.axis_size("lon") and tracers.shape[2] >= HALO:
         return transposed_path(tracers, courant_x, courant_y, cutoffs)
     return tiled_path(tracers, courant_x, courant_y, cutoffs)
 

time: 113 us -> 71.7 us (0.63); the launches traced: 112 us -> 71.4 us
  local copies, waits for them, and re-layouts: 37 us -> 10.7 us
  other arithmetic: 31.5 us -> 15.1 us
  waiting for transfers between devices: 18.6 us -> 21.5 us
    gather x11 -> x0, local copies, waits for them, and re-layouts: 14.7 us -> none  [the longest x4 7.35 us: transposed_path(): jnp.take(state[..., lon_cols - HALO:], west_at, axis=0)]
    unnamed x88 -> x4, local copies, waits for them, and re-layouts: 8.5 us -> 1.04 us
    select_n x8 -> x3, other arithmetic: 5.43 us -> 0.22 us  [the longest x2 0.21 us: transposed_path(): jnp.where(is_south, state[:, :, :HALO], state[:, :, lat_rows - HALO:])]
    slice x5 -> x6, local copies, waits for them, and re-layouts: 4.37 us -> 0.45 us  [the longest x4 0.31 us: transposed_path(): jnp.roll(state[..., lon_cols - HALO:], -1, axis=0)]
    ppermute x6, waiting for transfers between devices: 7.99 us -> 10.9 us  [shift(): return lax.ppermute(x, axis, pairs)]
    gather x3 -> x0, other arithmetic: 1.79 us -> none
    slice x1, other arithmetic: 1.49 us -> 0.02 us  [transposed_path(): cy = payload[:, None, count + lat_rows:]]
    and x2 -> x0, other arithmetic: 1.14 us -> none  [the longest x1 0.61 us: transposed_path(): jnp.take(state[..., :HALO], east_at, axis=0)]
  transfers between devices with their start and end apart: 10 -> 10, of which waited for: 4 -> 5; matrix products, arithmetic and copies ran while one was open for 16% -> 16% of each run, Pallas kernels for 0% -> 0%
where the time goes in v13:
time: 71.7 us; the launch traced here: 71.4 us
  waiting for transfers between devices  21.5 us (30%)
  starting transfers between devices  15.8 us (22%)
  other arithmetic  15.1 us (21%)
  local copies, waits for them, and re-layouts  10.7 us (15%)
  matrix products  7.76 us (11%)
    ppermute x6, waiting for transfers between devices, shift(): return lax.ppermute(x, axis, pairs)  10.9 us
    ppermute x2, waiting for transfers between devices, transposed_path(): lax.ppermute(jnp.where(is_even, bottom, top), 'lat', [(i, i + (1 if i % 2...  10.6 us
    ppermute x6, starting transfers between devices, shift(): return lax.ppermute(x, axis, pairs)  8.05 us
    ppermute x2, starting transfers between devices, transposed_path(): lax.ppermute(jnp.where(is_even, bottom, top), 'lat', [(i, i + (1 if i % 2...  6.77 us
    dot_general x2, matrix products, filter_rows(): lax.dot_general(z, basis, (((2,), (q_axis,)), ((0,), (0,))), precision=MA...  4.14 us
    dot_general x2, matrix products, filter_rows(): lax.dot_general(spec, basis, (((2,), (m_axis,)), ((0,), (0,))), precision...  3.62 us
    sub x1, local copies, waits for them, and re-layouts, product_basis(): cos_qk = (ca * cb - sa * sb).reshape(tiles, per_class, cols)  3.3 us
    sub x1, other arithmetic, product_basis(): cos_qk = (ca * cb - sa * sb).reshape(tiles, per_class, cols)  3.25 us
  transfers between devices with their start and end apart: 10, of which 5 were waited for; matrix products, arithmetic and copies ran while one was open for 16% of the time, Pallas kernels for 0%

profile of v13, /device:TPU:3, one launch (start us, length us, event | category | flops | bytes accessed | tf_op | source)
XLA Modules:
  0.0 71.4 jit_solution(13987896325762916660)
XLA Ops:
  0.0 1.1 %dynamic-slice_bitcast_fusion.3 = (f32[40,720]{1,0:T(8,128)S(1)}, f32[40,720]{1,0:T(8,128)S(1)}, f32[40,720]{1,0:T(8,128)S(1)}, f32[40,720]{1,0:T(8,128)S(1)}) fusion(f32[5,4,8,720]{3,2,1,0:T(8,128)} %param.4, s32[]{:T(128)S(6)} %select_n.418, s32[]{:T(128)S(6)} %select_n.422, s32[]{:T(128)S(6)} %select_n.420, s32[]{:T(128)S(6)} %select_n.424), kind=kLoop, calls=%fused_computation.211 | loop fusion | bytes 921616 | tf_op jit(solution)/shard_map/reshape | solution.py:215
  1.1 0.9 %dynamic-slice_bitcast_fusion.10 = (f32[8,720]{1,0:T(8,128)S(1)}, f32[8,720]{1,0:T(8,128)S(1)}, f32[8,720]{1,0:T(8,128)S(1)}, f32[8,720]{1,0:T(8,128)S(1)}, f32[...) fusion(f32[4,8,720]{2,1,0:T(8,128)} %param.6, s32[]{:T(128)S(6)} %select_n.418, ...), kind=kLoop, calls=%fused_computation.237 | loop fusion | bytes 368656 | tf_op jit(solution)/shard_map/jit(dynamic_index_in_dim)/squeeze | solution.py:217
  2.0 3.4 %collective-permute-start.2 = (f32[56,720]{1,0:T(8,128)S(1)}, f32[56,720]{1,0:T(8,128)S(1)}, u32[]{:S(2)}, u32[]{:S(2)}) collective-permute-start(f32[56,720]{1,0:T(8,128)S(1)} %pad_maximum_fusion.23), channel_id=1, source_target_pairs={{0,3},{1,0},{2,1},{3,2},{4,7},{5,4},{6,5},{7,6},{8,11},{9,8},{10,9... | collective-permute-start | bytes 483848 | tf_op jit(solution)/shard_map/ppermute | solution.py:18
  5.5 0.5 collective-permute-start
  6.2 0.4 fusion.121
  6.6 0.6 fusion.114
  7.3 0.8 %gather_fusion = s32[40]{0:T(128)S(1)} fusion(s32[64]{0:T(128)S(1)} %copy-done, s32[1024]{0:T(1024)S(1)} %pad_clamp_fusion), kind=kCustom, calls=%fused_computation | custom fusion | bytes 480 | tf_op jit(solution)/shard_map/jit(_take)/gather | solution.py:233
  8.1 3.3 %multiply_subtract_fusion = (f32[4,180,30,24]{1,3,2,0:T(8,128)}, f32[4,180,30,24]{1,3,2,0:T(8,128)}) fusion(f32[4,180,24]{1,2,0:T(8,128)S(1)} %get-tuple-element.81, f32[4,180,30]{1,2,0:T(8,128)S(1)} %get-tuple-element.79, f32[4,180,24]{1,2,0:T(8,128)S(1)} %get-tuple-element.80, f32[4,180,30]{1,2,0:T(8,128)S(1)} %get-tuple-element.78), kind=kLoop, calls=%fused_computation.3 | loop fusion | flops 3110400 | bytes 4458240 | tf_op jit(solution)/shard_map/sub | solution.py:34
  11.4 2.3 %copy.118 = f32[4,180,720]{2,1,0:T(8,128)S(1)} copy(f32[4,180,720]{1,2,0:T(8,128)} %bitcast.104) | data formatting | bytes 4147200 | tf_op jit(solution)/shard_map/add | solution.py:35
  13.7 3.3 %copy.117 = f32[4,180,720]{2,1,0:T(8,128)} copy(f32[4,180,720]{1,2,0:T(8,128)} %bitcast.103) | data formatting | bytes 4147200 | tf_op jit(solution)/shard_map/sub | solution.py:34
  17.0 3.1 %collective-permute-done.1 = f32[56,720]{1,0:T(8,128)S(1)} collective-permute-done((f32[56,720]{1,0:T(8,128)S(1)}, f32[56,720]{1,0:T(8,128)S(1)}, u32[]{:S(2)}, u32[]{:S(2)}) %collective-permute-start.1) | collective-permute-done | bytes 161312 | tf_op jit(solution)/shard_map/ppermute | solution.py:18
  20.9 0.2 maximum_maximum_fusion
  21.1 0.5 fusion.86
  21.6 0.5 fusion.79
  22.1 0.2 slice_subtract_fusion.3
  22.6 0.9 %collective-permute-start.3 = (f32[4,16,720]{2,1,0:T(8,128)S(1)}, f32[4,16,720]{2,1,0:T(8,128)S(1)}, u32[]{:S(2)}, u32[]{:S(2)}) collective-permute-start(f32[4,16,720]{2,1,0:T(8,128)S(1)} %get-tuple-element.55), channel_id=1, source_target_pairs={{0,4},{4,0},{8,12},{12,8},{16,20},{20,16},{24,28},{28,24},{1,5},{5... | collective-permute-start | bytes 552968 | tf_op jit(solution)/shard_map/ppermute | solution.py:252
  23.6 3.2 %collective-permute-start.4 = (f32[4,16,720]{2,1,0:T(8,128)S(1)}, f32[4,16,720]{2,1,0:T(8,128)S(1)}, u32[]{:S(2)}, u32[]{:S(2)}) collective-permute-start(f32[4,16,720]{2,1,0:T(8,128)S(1)} %get-tuple-element.54), channel_id=1, source_target_pairs={{4,8},{8,4},{12,16},{16,12},{20,24},{24,20},{5,9},{9,5},{13,17},{1... | collective-permute-start | bytes 552968 | tf_op jit(solution)/shard_map/ppermute | solution.py:255
  26.8 6.1 %collective-permute-done.4 = f32[4,16,720]{2,1,0:T(8,128)S(1)} collective-permute-done((f32[4,16,720]{2,1,0:T(8,128)S(1)}, f32[4,16,720]{2,1,0:T(8,128)S(1)}, u32[]{:S(2)}, u32[]{:S(2)}) %collective-permute-start.4) | collective-permute-done | bytes 184352 | tf_op jit(solution)/shard_map/ppermute | solution.py:255
  33.4 0.2 copy_select_fusion.3
  33.6 0.2 pad_maximum_fusion.9
  33.8 0.4 fusion.43
  34.3 1.0 %fusion.30 = f32[4,5,9,720]{3,2,1,0:T(8,128)S(1)} fusion(f32[4,5,8,720]{3,2,1,0:T(8,128)S(1)} %slice_bitcast_fusion, f32[4,5,3,720]{3,2,1,0:T(4,128)S(1)} %get-tuple-element.63, f32[4,5,3,720]{3,2,1,0:T(4,128)S(1)} %get-tuple-element.62, f32[4,5,11,720]{3,2,1,0:T(8,128)S(1)} %fusion.43, f32[9]{0:T(128)S(1)} %or_select_fusion, ...), kind=kLoop, calls=%fused_computation.52 | loop fusion | flops 2980800 | bytes 3216996 | tf_op jit(solution)/shard_map/mul | solution.py:287
  35.4 0.4 multiply_reduce_fusion.3
  35.9 1.0 %copy-done.1 = f32[4,180,720]{2,1,0:T(8,128)S(1)} copy-done((f32[4,180,720]{2,1,0:T(8,128)S(1)}, f32[4,180,720]{2,1,0:T(8,128)}, u32[]{:S(2)}) %copy-start.1) | copy-done | bytes 2073624
  36.9 2.1 %fusion.3 = f32[4,80,360]{2,1,0:T(8,128)S(1)} fusion(f32[4,180,720]{2,1,0:T(8,128)S(1)} %copy.118, f32[4,180,720]{2,1,0:T(8,128)S(1)} %copy-done.1, f32[4,40,720]{2,1,0:T(8,128)S(1)} %neg.12, f32[4,40,720]{2,1,0:T(8,128)S(1)} %get-tuple-element.7), kind=kOutput, calls=%fused_computation.13 | convolution fusion | flops 498931200 | bytes 5529600 | tf_op jit(solution)/shard_map/dot_general | solution.py:95
  39.1 1.8 %fusion.2 = f32[4,80,720]{2,1,0:T(8,128)S(1)} fusion(f32[4,180,720]{2,1,0:T(8,128)S(1)} %copy.118, f32[4,180,720]{2,1,0:T(8,128)S(1)} %copy-done.1, f32[4,40,180]{2,1,0:T(8,128)S(1)} %get-tuple-element.30, f32[4,40,180]{2,1,0:T(8,128)S(1)} %get-tuple-element.14, f32[4,40,180]{2,1,0:T(8,128)S(1)} %get-tuple-element.15), kind=kOutput, calls=%fused_computation.12 | convolution fusion | flops 499046400 | bytes 5414400 | tf_op jit(solution)/shard_map/dot_general | solution.py:104
  41.0 0.3 subtract_reduce_fusion.1
  41.8 0.2 maximum_maximum_fusion.2
  42.0 0.5 fusion.69
  42.5 0.5 fusion.62
  42.9 0.2 slice_subtract_fusion.1
  43.2 3.6 %collective-permute-start.5 = (f32[4,15,720]{2,0,1:T(4,128)S(1)}, f32[4,15,720]{2,0,1:T(4,128)S(1)}, u32[]{:S(2)}, u32[]{:S(2)}) collective-permute-start(f32[4,15,720]{2,0,1:T(4,128)S(1)} %bitcast.124), channel_id=1, source_target_pairs={{4,8},{8,4},{12,16},{16,12},{20,24},{24,20},{5,9},{9,5},{13,17},{1... | collective-permute-start | bytes 518408 | tf_op jit(solution)/shard_map/ppermute | solution.py:255
  47.0 4.5 %collective-permute-done.5 = f32[4,15,720]{2,0,1:T(4,128)S(1)} collective-permute-done((f32[4,15,720]{2,0,1:T(4,128)S(1)}, f32[4,15,720]{2,0,1:T(4,128)S(1)}, u32[]{:S(2)}, u32[]{:S(2)}) %collective-permute-start.5) | collective-permute-done | bytes 172832 | tf_op jit(solution)/shard_map/ppermute | solution.py:255
  51.5 0.2 copy_select_fusion.1
  51.7 0.2 pad_maximum_fusion.10
  51.9 0.4 fusion.40
  52.4 1.0 %fusion.13 = f32[4,5,9,720]{3,2,1,0:T(8,128)S(1)} fusion(f32[4,5,8,720]{3,2,1,0:T(8,128)S(1)} %bitcast_select_fusion, f32[4,5,3,720]{3,2,1,0:T(4,128)S(1)} %get-tuple-element.59, f32[4,5,3,720]{3,2,1,0:T(4,128)S(1)} %get-tuple-element.58, f32[4,5,11,720]{3,2,1,0:T(8,128)S(1)} %fusion.40, f32[9]{0:T(128)S(1)} %or_select_fusion, ...), kind=kLoop, calls=%fused_computation.35 | loop fusion | flops 2980800 | bytes 3216996 | tf_op jit(solution)/shard_map/mul | solution.py:287
  53.3 0.2 fusion.55
  53.5 0.4 multiply_reduce_fusion.1
  54.0 2.1 %fusion.1 = f32[4,80,360]{2,1,0:T(8,128)S(1)} fusion(f32[4,180,720]{2,1,0:T(8,128)S(1)} %copy.118, f32[4,180,720]{2,1,0:T(8,128)S(1)} %copy-done.1, f32[4,40,720]{2,1,0:T(8,128)S(1)} %neg.14, f32[4,40,720]{2,1,0:T(8,128)S(1)} %get-tuple-element.5), kind=kOutput, calls=%fused_computation.11 | convolution fusion | flops 498931200 | bytes 5529600 | tf_op jit(solution)/shard_map/dot_general | solution.py:95
  56.2 1.8 %fusion = f32[4,80,720]{2,1,0:T(8,128)S(1)} fusion(f32[4,180,720]{2,1,0:T(8,128)S(1)} %copy.118, f32[4,180,720]{2,1,0:T(8,128)S(1)} %copy-done.1, f32[4,40,180]{2,1,0:T(8,128)S(1)} %get-tuple-element.29, f32[4,40,180]{2,1,0:T(8,128)S(1)} %get-tuple-element.9, f32[4,40,180]{2,1,0:T(8,128)S(1)} %get-tuple-element.10), kind=kOutput, calls=%fused_computation.10 | convolution fusion | flops 499046400 | bytes 5414400 | tf_op jit(solution)/shard_map/dot_general | solution.py:104
  58.1 0.3 subtract_reduce_fusion
  58.6 0.6 collective-permute-start.7
  59.2 2.1 %collective-permute-start.8 = (f32[5,8,720]{2,1,0:T(8,128)S(1)}, f32[5,8,720]{2,1,0:T(8,128)S(1)}, u32[]{:S(2)}, u32[]{:S(2)}) collective-permute-start(f32[5,8,720]{2,1,0:T(8,128)S(1)} %get-tuple-element.32), channel_id=1, source_target_pairs={{0,2},{1,3},{2,0},{3,1},{4,6},{5,7},{6,4},{7,5},{8,10},{9,11},{10,... | collective-permute-start | bytes 345608 | tf_op jit(solution)/shard_map/ppermute | solution.py:18
  61.4 1.4 %collective-permute-start.9 = (f32[5,8,720]{2,1,0:T(8,128)S(1)}, f32[5,8,720]{2,1,0:T(8,128)S(1)}, u32[]{:S(2)}, u32[]{:S(2)}) collective-permute-start(f32[5,8,720]{2,1,0:T(8,128)S(1)} %get-tuple-element.31), channel_id=1, source_target_pairs={{0,1},{1,2},{2,3},{3,0},{4,5},{5,6},{6,7},{7,4},{8,9},{9,10},{10,1... | collective-permute-start | bytes 345608 | tf_op jit(solution)/shard_map/ppermute | solution.py:18
  62.7 1.2 %collective-permute-done.7 = f32[5,8,720]{2,1,0:T(8,128)S(1)} collective-permute-done((f32[5,8,720]{2,1,0:T(8,128)S(1)}, f32[5,8,720]{2,1,0:T(8,128)S(1)}, u32[]{:S(2)}, u32[]{:S(2)}) %collective-permute-start.7) | collective-permute-done | bytes 115232 | tf_op jit(solution)/shard_map/ppermute | solution.py:18
  64.0 6.6 %collective-permute-done.8 = f32[5,8,720]{2,1,0:T(8,128)S(1)} collective-permute-done((f32[5,8,720]{2,1,0:T(8,128)S(1)}, f32[5,8,720]{2,1,0:T(8,128)S(1)}, u32[]{:S(2)}, u32[]{:S(2)}) %collective-permute-start.8) | collective-permute-done | bytes 115232 | tf_op jit(solution)/shard_map/ppermute | solution.py:18
  70.6 0.8 %pad_maximum_fusion.14 = f32[5,4,8,720]{3,2,1,0:T(8,128)} fusion(f32[5,1,8,720]{3,2,1,0:T(8,128)S(1)} %get-tuple-element.24, f32[5,1,8,720]{3,2,1,0:T(8,128)S(1)} %get-tuple-element.25, f32[5,1,8,720]{3,2,1,0:T(8,128)S(1)} %get-tuple-element.26, f32[5,1,8,720]{3,2,1,0:T(8,128)S(1)} %get-tuple-element.23), kind=kLoop, calls=%fused_computation.145 | loop fusion | flops 345600 | bytes 921600 | tf_op jit(solution)/shard_map/stack | solution.py:303
  (73 shorter events, 3.4 us)
Async XLA Ops:
  0.0 7.3 %copy-start = (s32[64]{0:T(128)S(1)}, s32[64]{0:T(128)}, u32[]{:S(2)}) copy-start(s32[64]{0:T(128)} %param.7) | copy-start | bytes 772
  2.0 15.0 %collective-permute-start.2 = (f32[56,720]{1,0:T(8,128)S(1)}, f32[56,720]{1,0:T(8,128)S(1)}, u32[]{:S(2)}, u32[]{:S(2)}) collective-permute-start(f32[56,720]{1,0:T(8,128)S(1)} %pad_maximum_fusion.23), channel_id=1, source_target_pairs={{0,3},{1,0},{2,1},{3,2},{4,7},{5,4},{6,5},{7,6},{8,11},{9,8},{10,9... | collective-permute-start | bytes 483848 | tf_op jit(solution)/shard_map/ppermute | solution.py:18
  5.4 14.7 %collective-permute-start.1 = (f32[56,720]{1,0:T(8,128)S(1)}, f32[56,720]{1,0:T(8,128)S(1)}, u32[]{:S(2)}, u32[]{:S(2)}) collective-permute-start(f32[56,720]{1,0:T(8,128)S(1)} %pad_maximum_fusion.22), channel_id=1, source_target_pairs={{0,2},{1,3},{2,0},{3,1},{4,6},{5,7},{6,4},{7,5},{8,10},{9,11},{10,... | collective-permute-start | bytes 483848 | tf_op jit(solution)/shard_map/ppermute | solution.py:18
  5.5 14.6 %collective-permute-start = (f32[56,720]{1,0:T(8,128)S(1)}, f32[56,720]{1,0:T(8,128)S(1)}, u32[]{:S(2)}, u32[]{:S(2)}) collective-permute-start(f32[56,720]{1,0:T(8,128)S(1)} %pad_maximum_fusion.21), channel_id=1, source_target_pairs={{0,1},{1,2},{2,3},{3,0},{4,5},{5,6},{6,7},{7,4},{8,9},{9,10},{10,1... | collective-permute-start | bytes 483848 | tf_op jit(solution)/shard_map/ppermute | solution.py:18
  22.6 4.2 %collective-permute-start.3 = (f32[4,16,720]{2,1,0:T(8,128)S(1)}, f32[4,16,720]{2,1,0:T(8,128)S(1)}, u32[]{:S(2)}, u32[]{:S(2)}) collective-permute-start(f32[4,16,720]{2,1,0:T(8,128)S(1)} %get-tuple-element.55), channel_id=1, source_target_pairs={{0,4},{4,0},{8,12},{12,8},{16,20},{20,16},{24,28},{28,24},{1,5},{5... | collective-permute-start | bytes 552968 | tf_op jit(solution)/shard_map/ppermute | solution.py:252
  23.6 9.4 %collective-permute-start.4 = (f32[4,16,720]{2,1,0:T(8,128)S(1)}, f32[4,16,720]{2,1,0:T(8,128)S(1)}, u32[]{:S(2)}, u32[]{:S(2)}) collective-permute-start(f32[4,16,720]{2,1,0:T(8,128)S(1)} %get-tuple-element.54), channel_id=1, source_target_pairs={{4,8},{8,4},{12,16},{16,12},{20,24},{24,20},{5,9},{9,5},{13,17},{1... | collective-permute-start | bytes 552968 | tf_op jit(solution)/shard_map/ppermute | solution.py:255
  35.3 1.6 %copy-start.1 = (f32[4,180,720]{2,1,0:T(8,128)S(1)}, f32[4,180,720]{2,1,0:T(8,128)}, u32[]{:S(2)}) copy-start(f32[4,180,720]{2,1,0:T(8,128)} %copy.117) | copy-start | bytes 6220804
  43.2 8.2 %collective-permute-start.5 = (f32[4,15,720]{2,0,1:T(4,128)S(1)}, f32[4,15,720]{2,0,1:T(4,128)S(1)}, u32[]{:S(2)}, u32[]{:S(2)}) collective-permute-start(f32[4,15,720]{2,0,1:T(4,128)S(1)} %bitcast.124), channel_id=1, source_target_pairs={{4,8},{8,4},{12,16},{16,12},{20,24},{24,20},{5,9},{9,5},{13,17},{1... | collective-permute-start | bytes 518408 | tf_op jit(solution)/shard_map/ppermute | solution.py:255
  46.8 4.6 %collective-permute-start.6 = (f32[4,15,720]{2,0,1:T(4,128)S(1)}, f32[4,15,720]{2,0,1:T(4,128)S(1)}, u32[]{:S(2)}, u32[]{:S(2)}) collective-permute-start(f32[4,15,720]{2,0,1:T(4,128)S(1)} %bitcast.125), channel_id=1, source_target_pairs={{0,4},{4,0},{8,12},{12,8},{16,20},{20,16},{24,28},{28,24},{1,5},{5... | collective-permute-start | bytes 518408 | tf_op jit(solution)/shard_map/ppermute | solution.py:252
  58.6 5.3 %collective-permute-start.7 = (f32[5,8,720]{2,1,0:T(8,128)S(1)}, f32[5,8,720]{2,1,0:T(8,128)S(1)}, u32[]{:S(2)}, u32[]{:S(2)}) collective-permute-start(f32[5,8,720]{2,1,0:T(8,128)S(1)} %get-tuple-element.33), channel_id=1, source_target_pairs={{0,3},{1,0},{2,1},{3,2},{4,7},{5,4},{6,5},{7,6},{8,11},{9,8},{10,9... | collective-permute-start | bytes 345608 | tf_op jit(solution)/shard_map/ppermute | solution.py:18
  59.2 11.3 %collective-permute-start.8 = (f32[5,8,720]{2,1,0:T(8,128)S(1)}, f32[5,8,720]{2,1,0:T(8,128)S(1)}, u32[]{:S(2)}, u32[]{:S(2)}) collective-permute-start(f32[5,8,720]{2,1,0:T(8,128)S(1)} %get-tuple-element.32), channel_id=1, source_target_pairs={{0,2},{1,3},{2,0},{3,1},{4,6},{5,7},{6,4},{7,5},{8,10},{9,11},{10,... | collective-permute-start | bytes 345608 | tf_op jit(solution)/shard_map/ppermute | solution.py:18
  61.4 9.2 %collective-permute-start.9 = (f32[5,8,720]{2,1,0:T(8,128)S(1)}, f32[5,8,720]{2,1,0:T(8,128)S(1)}, u32[]{:S(2)}, u32[]{:S(2)}) collective-permute-start(f32[5,8,720]{2,1,0:T(8,128)S(1)} %get-tuple-element.31), channel_id=1, source_target_pairs={{0,1},{1,2},{2,3},{3,0},{4,5},{5,6},{6,7},{7,4},{8,9},{9,10},{10,1... | collective-permute-start | bytes 345608 | tf_op jit(solution)/shard_map/ppermute | solution.py:18

commit v14 on v13

--- a/solution.py
+++ b/solution.py
@@ -291,20 +291,24 @@
         rows = filter_rows(rows, basis, roots, weights, polar, 0, True)
         state = rows.reshape(lon_devices, tracer_count, lat_rows, lon_cols)
 
-    back = [state[0]] + [
-        shift(state[(lon_devices - by) % lon_devices], "lon", by, True) for by in range(1, lon_devices)
-    ]
+    back = [state[0]]
+    for by in range(1, lon_devices):
+        held_at = (lon_index - (lon_index ^ by)) % lon_devices
+        part = lax.dynamic_index_in_dim(state, held_at, 0, keepdims=False)
+        back.append(lax.ppermute(part, "lon", [(i, i ^ by) for i in range(lon_devices)]))
     levels = []
     for level in range(level_count):
         pick = back[0]
         for by in range(1, lon_devices):
-            pick = jnp.where((lon_index - by) % lon_devices == level, back[by], pick)
+            pick = jnp.where((lon_index ^ by) == level, back[by], pick)
         levels.append(pick)
     return jnp.stack(levels, axis=1)
 
 
 def on_device(tracers, courant_x, courant_y, cutoffs):
-    if tracers.shape[1] == lax.axis_size("lon") and tracers.shape[2] >= HALO:
+    lon_devices = lax.axis_size("lon")
+    power_of_two = lon_devices & (lon_devices - 1) == 0
+    if tracers.shape[1] == lon_devices and power_of_two and tracers.shape[2] >= HALO:
         return transposed_path(tracers, courant_x, courant_y, cutoffs)
     return tiled_path(tracers, courant_x, courant_y, cutoffs)
 

time: 71.7 us -> 71.8 us (level)
    ppermute x0 -> x3, waiting for transfers between devices: none -> 8.28 us  [transposed_path(): lax.ppermute(part, 'lon', [(i, i ^ by) for i in range(lon_devices)])]
    ppermute x6 -> x3, waiting for transfers between devices: 10.9 us -> 3.01 us  [shift(): return lax.ppermute(x, axis, pairs)]
    ppermute x6 -> x3, starting transfers between devices: 8.05 us -> 3.93 us  [shift(): return lax.ppermute(x, axis, pairs)]
    ppermute x0 -> x3, starting transfers between devices: none -> 3.61 us  [transposed_path(): lax.ppermute(part, 'lon', [(i, i ^ by) for i in range(lon_devices)])]
where the time goes in v14:
time: 71.8 us; the launch traced here: 71.5 us
  waiting for transfers between devices  21.9 us (31%)
  starting transfers between devices  15.3 us (21%)
  other arithmetic  15.2 us (21%)
  local copies, waits for them, and re-layouts  10.7 us (15%)
  matrix products  7.76 us (11%)
    ppermute x2, waiting for transfers between devices, transposed_path(): lax.ppermute(jnp.where(is_even, bottom, top), 'lat', [(i, i + (1 if i % 2...  10.6 us
    ppermute x3, waiting for transfers between devices, transposed_path(): lax.ppermute(part, 'lon', [(i, i ^ by) for i in range(lon_devices)])  8.28 us
    ppermute x2, starting transfers between devices, transposed_path(): lax.ppermute(jnp.where(is_even, bottom, top), 'lat', [(i, i + (1 if i % 2...  6.77 us
    dot_general x2, matrix products, filter_rows(): lax.dot_general(z, basis, (((2,), (q_axis,)), ((0,), (0,))), precision=MA...  4.14 us
    ppermute x3, starting transfers between devices, shift(): return lax.ppermute(x, axis, pairs)  3.93 us
    dot_general x2, matrix products, filter_rows(): lax.dot_general(spec, basis, (((2,), (m_axis,)), ((0,), (0,))), precision...  3.62 us
    ppermute x3, starting transfers between devices, transposed_path(): lax.ppermute(part, 'lon', [(i, i ^ by) for i in range(lon_devices)])  3.61 us
    sub x1, local copies, waits for them, and re-layouts, product_basis(): cos_qk = (ca * cb - sa * sb).reshape(tiles, per_class, cols)  3.33 us
  transfers between devices with their start and end apart: 10, of which 5 were waited for; matrix products, arithmetic and copies ran while one was open for 16% of the time, Pallas kernels for 0%

profile of v14, /device:TPU:3, one launch (start us, length us, event | category | flops | bytes accessed | tf_op | source)
XLA Modules:
  0.0 71.5 jit_solution(17664907158617264524)
XLA Ops:
  0.0 1.1 %dynamic-slice_bitcast_fusion.6 = (f32[40,720]{1,0:T(8,128)S(1)}, f32[40,720]{1,0:T(8,128)S(1)}, f32[40,720]{1,0:T(8,128)S(1)}, f32[40,720]{1,0:T(8,128)S(1)}) fusion(f32[5,4,8,720]{3,2,1,0:T(8,128)} %param.4, s32[]{:T(128)S(6)} %select_n.411, s32[]{:T(128)S(6)} %select_n.415, s32[]{:T(128)S(6)} %select_n.413, s32[]{:T(128)S(6)} %select_n.417), kind=kLoop, calls=%fused_computation.211 | loop fusion | bytes 921616 | tf_op jit(solution)/shard_map/reshape | solution.py:215
  1.1 0.9 %dynamic-slice_bitcast_fusion.13 = (f32[8,720]{1,0:T(8,128)S(1)}, f32[8,720]{1,0:T(8,128)S(1)}, f32[8,720]{1,0:T(8,128)S(1)}, f32[8,720]{1,0:T(8,128)S(1)}, f32[...) fusion(f32[4,8,720]{2,1,0:T(8,128)} %param.6, s32[]{:T(128)S(6)} %select_n.411, ...), kind=kLoop, calls=%fused_computation.237 | loop fusion | bytes 368656 | tf_op jit(solution)/shard_map/jit(dynamic_index_in_dim)/squeeze | solution.py:217
  2.0 3.4 %collective-permute-start.2 = (f32[56,720]{1,0:T(8,128)S(1)}, f32[56,720]{1,0:T(8,128)S(1)}, u32[]{:S(2)}, u32[]{:S(2)}) collective-permute-start(f32[56,720]{1,0:T(8,128)S(1)} %pad_maximum_fusion.23), channel_id=1, source_target_pairs={{0,3},{1,0},{2,1},{3,2},{4,7},{5,4},{6,5},{7,6},{8,11},{9,8},{10,9... | collective-permute-start | bytes 483848 | tf_op jit(solution)/shard_map/ppermute | solution.py:18
  5.5 0.5 collective-permute-start
  6.1 0.4 fusion.121
  6.6 0.6 fusion.113
  7.2 0.8 %gather_fusion = s32[40]{0:T(128)S(1)} fusion(s32[64]{0:T(128)S(1)} %copy-done, s32[1024]{0:T(1024)S(1)} %pad_clamp_fusion), kind=kCustom, calls=%fused_computation | custom fusion | bytes 480 | tf_op jit(solution)/shard_map/jit(_take)/gather | solution.py:233
  8.1 3.2 %multiply_subtract_fusion = (f32[4,180,30,24]{1,3,2,0:T(8,128)}, f32[4,180,30,24]{1,3,2,0:T(8,128)}) fusion(f32[4,180,24]{1,2,0:T(8,128)S(1)} %get-tuple-element.82, f32[4,180,30]{1,2,0:T(8,128)S(1)} %get-tuple-element.80, f32[4,180,24]{1,2,0:T(8,128)S(1)} %get-tuple-element.81, f32[4,180,30]{1,2,0:T(8,128)S(1)} %get-tuple-element.79), kind=kLoop, calls=%fused_computation.3 | loop fusion | flops 3110400 | bytes 4458240 | tf_op jit(solution)/shard_map/sub | solution.py:34
  11.4 2.3 %copy.140 = f32[4,180,720]{2,1,0:T(8,128)S(1)} copy(f32[4,180,720]{1,2,0:T(8,128)} %bitcast.98) | data formatting | bytes 4147200 | tf_op jit(solution)/shard_map/add | solution.py:35
  13.8 3.3 %copy.139 = f32[4,180,720]{2,1,0:T(8,128)} copy(f32[4,180,720]{1,2,0:T(8,128)} %bitcast.97) | data formatting | bytes 4147200 | tf_op jit(solution)/shard_map/sub | solution.py:34
  17.1 3.0 %collective-permute-done.1 = f32[56,720]{1,0:T(8,128)S(1)} collective-permute-done((f32[56,720]{1,0:T(8,128)S(1)}, f32[56,720]{1,0:T(8,128)S(1)}, u32[]{:S(2)}, u32[]{:S(2)}) %collective-permute-start.1) | collective-permute-done | bytes 161312 | tf_op jit(solution)/shard_map/ppermute | solution.py:18
  20.9 0.2 maximum_maximum_fusion
  21.1 0.5 fusion.85
  21.6 0.5 fusion.78
  22.1 0.2 slice_subtract_fusion.3
  22.6 0.9 %collective-permute-start.3 = (f32[4,16,720]{2,1,0:T(8,128)S(1)}, f32[4,16,720]{2,1,0:T(8,128)S(1)}, u32[]{:S(2)}, u32[]{:S(2)}) collective-permute-start(f32[4,16,720]{2,1,0:T(8,128)S(1)} %get-tuple-element.56), channel_id=1, source_target_pairs={{0,4},{4,0},{8,12},{12,8},{16,20},{20,16},{24,28},{28,24},{1,5},{5... | collective-permute-start | bytes 552968 | tf_op jit(solution)/shard_map/ppermute | solution.py:252
  23.6 3.2 %collective-permute-start.4 = (f32[4,16,720]{2,1,0:T(8,128)S(1)}, f32[4,16,720]{2,1,0:T(8,128)S(1)}, u32[]{:S(2)}, u32[]{:S(2)}) collective-permute-start(f32[4,16,720]{2,1,0:T(8,128)S(1)} %get-tuple-element.55), channel_id=1, source_target_pairs={{4,8},{8,4},{12,16},{16,12},{20,24},{24,20},{5,9},{9,5},{13,17},{1... | collective-permute-start | bytes 552968 | tf_op jit(solution)/shard_map/ppermute | solution.py:255
  26.8 6.1 %collective-permute-done.4 = f32[4,16,720]{2,1,0:T(8,128)S(1)} collective-permute-done((f32[4,16,720]{2,1,0:T(8,128)S(1)}, f32[4,16,720]{2,1,0:T(8,128)S(1)}, u32[]{:S(2)}, u32[]{:S(2)}) %collective-permute-start.4) | collective-permute-done | bytes 184352 | tf_op jit(solution)/shard_map/ppermute | solution.py:255
  33.4 0.2 copy_select_fusion.3
  33.6 0.2 pad_maximum_fusion.9
  33.8 0.4 fusion.43
  34.3 1.0 %fusion.30 = f32[4,5,9,720]{3,2,1,0:T(8,128)S(1)} fusion(f32[4,5,8,720]{3,2,1,0:T(8,128)S(1)} %slice_bitcast_fusion, f32[4,5,3,720]{3,2,1,0:T(4,128)S(1)} %get-tuple-element.64, f32[4,5,3,720]{3,2,1,0:T(4,128)S(1)} %get-tuple-element.63, f32[4,5,11,720]{3,2,1,0:T(8,128)S(1)} %fusion.43, f32[9]{0:T(128)S(1)} %or_select_fusion, ...), kind=kLoop, calls=%fused_computation.52 | loop fusion | flops 2980800 | bytes 3216996 | tf_op jit(solution)/shard_map/mul | solution.py:287
  35.4 0.4 multiply_reduce_fusion.3
  35.9 1.0 %copy-done.1 = f32[4,180,720]{2,1,0:T(8,128)S(1)} copy-done((f32[4,180,720]{2,1,0:T(8,128)S(1)}, f32[4,180,720]{2,1,0:T(8,128)}, u32[]{:S(2)}) %copy-start.1) | copy-done | bytes 2073624
  36.9 2.1 %fusion.3 = f32[4,80,360]{2,1,0:T(8,128)S(1)} fusion(f32[4,180,720]{2,1,0:T(8,128)S(1)} %copy.140, f32[4,180,720]{2,1,0:T(8,128)S(1)} %copy-done.1, f32[4,40,720]{2,1,0:T(8,128)S(1)} %neg.12, f32[4,40,720]{2,1,0:T(8,128)S(1)} %get-tuple-element.7), kind=kOutput, calls=%fused_computation.13 | convolution fusion | flops 498931200 | bytes 5529600 | tf_op jit(solution)/shard_map/dot_general | solution.py:95
  39.1 1.8 %fusion.2 = f32[4,80,720]{2,1,0:T(8,128)S(1)} fusion(f32[4,180,720]{2,1,0:T(8,128)S(1)} %copy.140, f32[4,180,720]{2,1,0:T(8,128)S(1)} %copy-done.1, f32[4,40,180]{2,1,0:T(8,128)S(1)} %get-tuple-element.28, f32[4,40,180]{2,1,0:T(8,128)S(1)} %get-tuple-element.16, f32[4,40,180]{2,1,0:T(8,128)S(1)} %get-tuple-element.17), kind=kOutput, calls=%fused_computation.12 | convolution fusion | flops 499046400 | bytes 5414400 | tf_op jit(solution)/shard_map/dot_general | solution.py:104
  41.0 0.3 subtract_reduce_fusion.1
  41.8 0.2 maximum_maximum_fusion.2
  42.0 0.5 fusion.68
  42.5 0.5 fusion.61
  42.9 0.2 slice_subtract_fusion.1
  43.2 3.6 %collective-permute-start.5 = (f32[4,15,720]{2,0,1:T(4,128)S(1)}, f32[4,15,720]{2,0,1:T(4,128)S(1)}, u32[]{:S(2)}, u32[]{:S(2)}) collective-permute-start(f32[4,15,720]{2,0,1:T(4,128)S(1)} %bitcast.120), channel_id=1, source_target_pairs={{4,8},{8,4},{12,16},{16,12},{20,24},{24,20},{5,9},{9,5},{13,17},{1... | collective-permute-start | bytes 518408 | tf_op jit(solution)/shard_map/ppermute | solution.py:255
  47.0 4.5 %collective-permute-done.5 = f32[4,15,720]{2,0,1:T(4,128)S(1)} collective-permute-done((f32[4,15,720]{2,0,1:T(4,128)S(1)}, f32[4,15,720]{2,0,1:T(4,128)S(1)}, u32[]{:S(2)}, u32[]{:S(2)}) %collective-permute-start.5) | collective-permute-done | bytes 172832 | tf_op jit(solution)/shard_map/ppermute | solution.py:255
  51.5 0.2 copy_select_fusion.1
  51.7 0.2 pad_maximum_fusion.10
  51.9 0.4 fusion.40
  52.4 1.0 %fusion.13 = f32[4,5,9,720]{3,2,1,0:T(8,128)S(1)} fusion(f32[4,5,8,720]{3,2,1,0:T(8,128)S(1)} %bitcast_select_fusion.1, f32[4,5,3,720]{3,2,1,0:T(4,128)S(1)} %get-tuple-element.60, f32[4,5,3,720]{3,2,1,0:T(4,128)S(1)} %get-tuple-element.59, f32[4,5,11,720]{3,2,1,0:T(8,128)S(1)} %fusion.40, f32[9]{0:T(128)S(1)} %or_select_fusion, ...), kind=kLoop, calls=%fused_computation.35 | loop fusion | flops 2980800 | bytes 3216996 | tf_op jit(solution)/shard_map/mul | solution.py:287
  53.3 0.2 fusion.54
  53.5 0.4 multiply_reduce_fusion.1
  54.0 2.1 %fusion.1 = f32[4,80,360]{2,1,0:T(8,128)S(1)} fusion(f32[4,180,720]{2,1,0:T(8,128)S(1)} %copy.140, f32[4,180,720]{2,1,0:T(8,128)S(1)} %copy-done.1, f32[4,40,720]{2,1,0:T(8,128)S(1)} %neg.14, f32[4,40,720]{2,1,0:T(8,128)S(1)} %get-tuple-element.5), kind=kOutput, calls=%fused_computation.11 | convolution fusion | flops 498931200 | bytes 5529600 | tf_op jit(solution)/shard_map/dot_general | solution.py:95
  56.2 1.8 %fusion = f32[4,80,720]{2,1,0:T(8,128)S(1)} fusion(f32[4,180,720]{2,1,0:T(8,128)S(1)} %copy.140, f32[4,180,720]{2,1,0:T(8,128)S(1)} %copy-done.1, f32[4,40,180]{2,1,0:T(8,128)S(1)} %get-tuple-element.27, f32[4,40,180]{2,1,0:T(8,128)S(1)} %get-tuple-element.11, f32[4,40,180]{2,1,0:T(8,128)S(1)} %get-tuple-element.12), kind=kOutput, calls=%fused_computation.10 | convolution fusion | flops 499046400 | bytes 5414400 | tf_op jit(solution)/shard_map/dot_general | solution.py:104
  58.1 0.3 subtract_reduce_fusion
  58.6 0.6 collective-permute-start.7
  59.2 2.1 %collective-permute-start.8 = (f32[5,8,720]{2,1,0:T(8,128)S(1)}, f32[5,8,720]{2,1,0:T(8,128)S(1)}, u32[]{:S(2)}, u32[]{:S(2)}) collective-permute-start(f32[5,8,720]{2,1,0:T(8,128)S(1)} %get-tuple-element.33), channel_id=1, source_target_pairs={{0,2},{1,3},{2,0},{3,1},{4,6},{5,7},{6,4},{7,5},{8,10},{9,11},{10,... | collective-permute-start | bytes 345608 | tf_op jit(solution)/shard_map/ppermute | solution.py:298
  61.4 0.9 %collective-permute-start.9 = (f32[5,8,720]{2,1,0:T(8,128)S(1)}, f32[5,8,720]{2,1,0:T(8,128)S(1)}, u32[]{:S(2)}, u32[]{:S(2)}) collective-permute-start(f32[5,8,720]{2,1,0:T(8,128)S(1)} %get-tuple-element.32), channel_id=1, source_target_pairs={{0,1},{1,0},{2,3},{3,2},{4,5},{5,4},{6,7},{7,6},{8,9},{9,8},{10,11... | collective-permute-start | bytes 345608 | tf_op jit(solution)/shard_map/ppermute | solution.py:298
  62.2 3.4 %collective-permute-done.7 = f32[5,8,720]{2,1,0:T(8,128)S(1)} collective-permute-done((f32[5,8,720]{2,1,0:T(8,128)S(1)}, f32[5,8,720]{2,1,0:T(8,128)S(1)}, u32[]{:S(2)}, u32[]{:S(2)}) %collective-permute-start.7) | collective-permute-done | bytes 115232 | tf_op jit(solution)/shard_map/ppermute | solution.py:298
  65.6 4.9 %collective-permute-done.8 = f32[5,8,720]{2,1,0:T(8,128)S(1)} collective-permute-done((f32[5,8,720]{2,1,0:T(8,128)S(1)}, f32[5,8,720]{2,1,0:T(8,128)S(1)}, u32[]{:S(2)}, u32[]{:S(2)}) %collective-permute-start.8) | collective-permute-done | bytes 115232 | tf_op jit(solution)/shard_map/ppermute | solution.py:298
  70.7 0.8 %pad_maximum_fusion.14 = f32[5,4,8,720]{3,2,1,0:T(8,128)} fusion(f32[5,1,8,720]{3,2,1,0:T(8,128)S(1)} %get-tuple-element.30, f32[5,1,8,720]{3,2,1,0:T(8,128)S(1)} %get-tuple-element.31, f32[5,1,8,720]{3,2,1,0:T(8,128)S(1)} %get-tuple-element.29, f32[5,1,8,720]{3,2,1,0:T(8,128)S(1)} %get-tuple-element.9), kind=kLoop, calls=%fused_computation.144 | loop fusion | flops 345600 | bytes 921600 | tf_op jit(solution)/shard_map/stack | solution.py:305
  (74 shorter events, 3.5 us)
Async XLA Ops:
  0.0 7.2 %copy-start = (s32[64]{0:T(128)S(1)}, s32[64]{0:T(128)}, u32[]{:S(2)}) copy-start(s32[64]{0:T(128)} %param.7) | copy-start | bytes 772
  2.0 15.1 %collective-permute-start.2 = (f32[56,720]{1,0:T(8,128)S(1)}, f32[56,720]{1,0:T(8,128)S(1)}, u32[]{:S(2)}, u32[]{:S(2)}) collective-permute-start(f32[56,720]{1,0:T(8,128)S(1)} %pad_maximum_fusion.23), channel_id=1, source_target_pairs={{0,3},{1,0},{2,1},{3,2},{4,7},{5,4},{6,5},{7,6},{8,11},{9,8},{10,9... | collective-permute-start | bytes 483848 | tf_op jit(solution)/shard_map/ppermute | solution.py:18
  5.4 14.7 %collective-permute-start.1 = (f32[56,720]{1,0:T(8,128)S(1)}, f32[56,720]{1,0:T(8,128)S(1)}, u32[]{:S(2)}, u32[]{:S(2)}) collective-permute-start(f32[56,720]{1,0:T(8,128)S(1)} %pad_maximum_fusion.22), channel_id=1, source_target_pairs={{0,2},{1,3},{2,0},{3,1},{4,6},{5,7},{6,4},{7,5},{8,10},{9,11},{10,... | collective-permute-start | bytes 483848 | tf_op jit(solution)/shard_map/ppermute | solution.py:18
  5.5 14.6 %collective-permute-start = (f32[56,720]{1,0:T(8,128)S(1)}, f32[56,720]{1,0:T(8,128)S(1)}, u32[]{:S(2)}, u32[]{:S(2)}) collective-permute-start(f32[56,720]{1,0:T(8,128)S(1)} %pad_maximum_fusion.21), channel_id=1, source_target_pairs={{0,1},{1,2},{2,3},{3,0},{4,5},{5,6},{6,7},{7,4},{8,9},{9,10},{10,1... | collective-permute-start | bytes 483848 | tf_op jit(solution)/shard_map/ppermute | solution.py:18
  22.6 4.2 %collective-permute-start.3 = (f32[4,16,720]{2,1,0:T(8,128)S(1)}, f32[4,16,720]{2,1,0:T(8,128)S(1)}, u32[]{:S(2)}, u32[]{:S(2)}) collective-permute-start(f32[4,16,720]{2,1,0:T(8,128)S(1)} %get-tuple-element.56), channel_id=1, source_target_pairs={{0,4},{4,0},{8,12},{12,8},{16,20},{20,16},{24,28},{28,24},{1,5},{5... | collective-permute-start | bytes 552968 | tf_op jit(solution)/shard_map/ppermute | solution.py:252
  23.6 9.4 %collective-permute-start.4 = (f32[4,16,720]{2,1,0:T(8,128)S(1)}, f32[4,16,720]{2,1,0:T(8,128)S(1)}, u32[]{:S(2)}, u32[]{:S(2)}) collective-permute-start(f32[4,16,720]{2,1,0:T(8,128)S(1)} %get-tuple-element.55), channel_id=1, source_target_pairs={{4,8},{8,4},{12,16},{16,12},{20,24},{24,20},{5,9},{9,5},{13,17},{1... | collective-permute-start | bytes 552968 | tf_op jit(solution)/shard_map/ppermute | solution.py:255
  35.3 1.6 %copy-start.1 = (f32[4,180,720]{2,1,0:T(8,128)S(1)}, f32[4,180,720]{2,1,0:T(8,128)}, u32[]{:S(2)}) copy-start(f32[4,180,720]{2,1,0:T(8,128)} %copy.139) | copy-start | bytes 6220804
  43.2 8.2 %collective-permute-start.5 = (f32[4,15,720]{2,0,1:T(4,128)S(1)}, f32[4,15,720]{2,0,1:T(4,128)S(1)}, u32[]{:S(2)}, u32[]{:S(2)}) collective-permute-start(f32[4,15,720]{2,0,1:T(4,128)S(1)} %bitcast.120), channel_id=1, source_target_pairs={{4,8},{8,4},{12,16},{16,12},{20,24},{24,20},{5,9},{9,5},{13,17},{1... | collective-permute-start | bytes 518408 | tf_op jit(solution)/shard_map/ppermute | solution.py:255
  46.8 4.6 %collective-permute-start.6 = (f32[4,15,720]{2,0,1:T(4,128)S(1)}, f32[4,15,720]{2,0,1:T(4,128)S(1)}, u32[]{:S(2)}, u32[]{:S(2)}) collective-permute-start(f32[4,15,720]{2,0,1:T(4,128)S(1)} %bitcast.121), channel_id=1, source_target_pairs={{0,4},{4,0},{8,12},{12,8},{16,20},{20,16},{24,28},{28,24},{1,5},{5... | collective-permute-start | bytes 518408 | tf_op jit(solution)/shard_map/ppermute | solution.py:252
  58.6 7.0 %collective-permute-start.7 = (f32[5,8,720]{2,1,0:T(8,128)S(1)}, f32[5,8,720]{2,1,0:T(8,128)S(1)}, u32[]{:S(2)}, u32[]{:S(2)}) collective-permute-start(f32[5,8,720]{2,1,0:T(8,128)S(1)} %get-tuple-element.34), channel_id=1, source_target_pairs={{0,3},{1,2},{2,1},{3,0},{4,7},{5,6},{6,5},{7,4},{8,11},{9,10},{10,... | collective-permute-start | bytes 345608 | tf_op jit(solution)/shard_map/ppermute | solution.py:298
  59.2 11.3 %collective-permute-start.8 = (f32[5,8,720]{2,1,0:T(8,128)S(1)}, f32[5,8,720]{2,1,0:T(8,128)S(1)}, u32[]{:S(2)}, u32[]{:S(2)}) collective-permute-start(f32[5,8,720]{2,1,0:T(8,128)S(1)} %get-tuple-element.33), channel_id=1, source_target_pairs={{0,2},{1,3},{2,0},{3,1},{4,6},{5,7},{6,4},{7,5},{8,10},{9,11},{10,... | collective-permute-start | bytes 345608 | tf_op jit(solution)/shard_map/ppermute | solution.py:298
  61.4 9.2 %collective-permute-start.9 = (f32[5,8,720]{2,1,0:T(8,128)S(1)}, f32[5,8,720]{2,1,0:T(8,128)S(1)}, u32[]{:S(2)}, u32[]{:S(2)}) collective-permute-start(f32[5,8,720]{2,1,0:T(8,128)S(1)} %get-tuple-element.32), channel_id=1, source_target_pairs={{0,1},{1,0},{2,3},{3,2},{4,5},{5,4},{6,7},{7,6},{8,9},{9,8},{10,11... | collective-permute-start | bytes 345608 | tf_op jit(solution)/shard_map/ppermute | solution.py:298

commit v15 on v13

--- a/solution.py
+++ b/solution.py
@@ -291,9 +291,9 @@
         rows = filter_rows(rows, basis, roots, weights, polar, 0, True)
         state = rows.reshape(lon_devices, tracer_count, lat_rows, lon_cols)
 
-    back = [state[0]] + [
-        shift(state[(lon_devices - by) % lon_devices], "lon", by, True) for by in range(1, lon_devices)
-    ]
+    back = [state[0]]
+    for by in range(1, lon_devices):
+        back.append(shift(state[(lon_devices - by) % lon_devices], "lon", by, True))
     levels = []
     for level in range(level_count):
         pick = back[0]

time: 71.7 us -> 71.7 us (level)
  no operation moved by 1% of the time
where the time goes in v15:
time: 71.7 us; the launch traced here: 71.4 us
  waiting for transfers between devices  21.5 us (30%)
  starting transfers between devices  15.8 us (22%)
  other arithmetic  15.1 us (21%)
  local copies, waits for them, and re-layouts  10.7 us (15%)
  matrix products  7.76 us (11%)
    ppermute x6, waiting for transfers between devices, shift(): return lax.ppermute(x, axis, pairs)  10.9 us
    ppermute x2, waiting for transfers between devices, transposed_path(): lax.ppermute(jnp.where(is_even, bottom, top), 'lat', [(i, i + (1 if i % 2...  10.6 us
    ppermute x6, starting transfers between devices, shift(): return lax.ppermute(x, axis, pairs)  8.05 us
    ppermute x2, starting transfers between devices, transposed_path(): lax.ppermute(jnp.where(is_even, bottom, top), 'lat', [(i, i + (1 if i % 2...  6.77 us
    dot_general x2, matrix products, filter_rows(): lax.dot_general(z, basis, (((2,), (q_axis,)), ((0,), (0,))), precision=MA...  4.14 us
    dot_general x2, matrix products, filter_rows(): lax.dot_general(spec, basis, (((2,), (m_axis,)), ((0,), (0,))), precision...  3.62 us
    sub x1, local copies, waits for them, and re-layouts, product_basis(): cos_qk = (ca * cb - sa * sb).reshape(tiles, per_class, cols)  3.3 us
    sub x1, other arithmetic, product_basis(): cos_qk = (ca * cb - sa * sb).reshape(tiles, per_class, cols)  3.25 us
  transfers between devices with their start and end apart: 10, of which 5 were waited for; matrix products, arithmetic and copies ran while one was open for 16% of the time, Pallas kernels for 0%

profile of v15, /device:TPU:3, one launch (start us, length us, event | category | flops | bytes accessed | tf_op | source)
XLA Modules:
  0.0 71.4 jit_solution(13987896325762916660)
XLA Ops:
  0.0 1.1 %dynamic-slice_bitcast_fusion.3 = (f32[40,720]{1,0:T(8,128)S(1)}, f32[40,720]{1,0:T(8,128)S(1)}, f32[40,720]{1,0:T(8,128)S(1)}, f32[40,720]{1,0:T(8,128)S(1)}) fusion(f32[5,4,8,720]{3,2,1,0:T(8,128)} %param.4, s32[]{:T(128)S(6)} %select_n.418, s32[]{:T(128)S(6)} %select_n.422, s32[]{:T(128)S(6)} %select_n.420, s32[]{:T(128)S(6)} %select_n.424), kind=kLoop, calls=%fused_computation.211 | loop fusion | bytes 921616 | tf_op jit(solution)/shard_map/reshape | solution.py:215
  1.1 0.9 %dynamic-slice_bitcast_fusion.10 = (f32[8,720]{1,0:T(8,128)S(1)}, f32[8,720]{1,0:T(8,128)S(1)}, f32[8,720]{1,0:T(8,128)S(1)}, f32[8,720]{1,0:T(8,128)S(1)}, f32[...) fusion(f32[4,8,720]{2,1,0:T(8,128)} %param.6, s32[]{:T(128)S(6)} %select_n.418, ...), kind=kLoop, calls=%fused_computation.237 | loop fusion | bytes 368656 | tf_op jit(solution)/shard_map/jit(dynamic_index_in_dim)/squeeze | solution.py:217
  2.0 3.4 %collective-permute-start.2 = (f32[56,720]{1,0:T(8,128)S(1)}, f32[56,720]{1,0:T(8,128)S(1)}, u32[]{:S(2)}, u32[]{:S(2)}) collective-permute-start(f32[56,720]{1,0:T(8,128)S(1)} %pad_maximum_fusion.23), channel_id=1, source_target_pairs={{0,3},{1,0},{2,1},{3,2},{4,7},{5,4},{6,5},{7,6},{8,11},{9,8},{10,9... | collective-permute-start | bytes 483848 | tf_op jit(solution)/shard_map/ppermute | solution.py:18
  5.5 0.5 collective-permute-start
  6.2 0.4 fusion.121
  6.6 0.6 fusion.114
  7.3 0.8 %gather_fusion = s32[40]{0:T(128)S(1)} fusion(s32[64]{0:T(128)S(1)} %copy-done, s32[1024]{0:T(1024)S(1)} %pad_clamp_fusion), kind=kCustom, calls=%fused_computation | custom fusion | bytes 480 | tf_op jit(solution)/shard_map/jit(_take)/gather | solution.py:233
  8.1 3.3 %multiply_subtract_fusion = (f32[4,180,30,24]{1,3,2,0:T(8,128)}, f32[4,180,30,24]{1,3,2,0:T(8,128)}) fusion(f32[4,180,24]{1,2,0:T(8,128)S(1)} %get-tuple-element.81, f32[4,180,30]{1,2,0:T(8,128)S(1)} %get-tuple-element.79, f32[4,180,24]{1,2,0:T(8,128)S(1)} %get-tuple-element.80, f32[4,180,30]{1,2,0:T(8,128)S(1)} %get-tuple-element.78), kind=kLoop, calls=%fused_computation.3 | loop fusion | flops 3110400 | bytes 4458240 | tf_op jit(solution)/shard_map/sub | solution.py:34
  11.4 2.3 %copy.118 = f32[4,180,720]{2,1,0:T(8,128)S(1)} copy(f32[4,180,720]{1,2,0:T(8,128)} %bitcast.104) | data formatting | bytes 4147200 | tf_op jit(solution)/shard_map/add | solution.py:35
  13.7 3.3 %copy.117 = f32[4,180,720]{2,1,0:T(8,128)} copy(f32[4,180,720]{1,2,0:T(8,128)} %bitcast.103) | data formatting | bytes 4147200 | tf_op jit(solution)/shard_map/sub | solution.py:34
  17.0 3.1 %collective-permute-done.1 = f32[56,720]{1,0:T(8,128)S(1)} collective-permute-done((f32[56,720]{1,0:T(8,128)S(1)}, f32[56,720]{1,0:T(8,128)S(1)}, u32[]{:S(2)}, u32[]{:S(2)}) %collective-permute-start.1) | collective-permute-done | bytes 161312 | tf_op jit(solution)/shard_map/ppermute | solution.py:18
  20.9 0.2 maximum_maximum_fusion
  21.1 0.5 fusion.86
  21.6 0.5 fusion.79
  22.1 0.2 slice_subtract_fusion.3
  22.6 0.9 %collective-permute-start.3 = (f32[4,16,720]{2,1,0:T(8,128)S(1)}, f32[4,16,720]{2,1,0:T(8,128)S(1)}, u32[]{:S(2)}, u32[]{:S(2)}) collective-permute-start(f32[4,16,720]{2,1,0:T(8,128)S(1)} %get-tuple-element.55), channel_id=1, source_target_pairs={{0,4},{4,0},{8,12},{12,8},{16,20},{20,16},{24,28},{28,24},{1,5},{5... | collective-permute-start | bytes 552968 | tf_op jit(solution)/shard_map/ppermute | solution.py:252
  23.6 3.2 %collective-permute-start.4 = (f32[4,16,720]{2,1,0:T(8,128)S(1)}, f32[4,16,720]{2,1,0:T(8,128)S(1)}, u32[]{:S(2)}, u32[]{:S(2)}) collective-permute-start(f32[4,16,720]{2,1,0:T(8,128)S(1)} %get-tuple-element.54), channel_id=1, source_target_pairs={{4,8},{8,4},{12,16},{16,12},{20,24},{24,20},{5,9},{9,5},{13,17},{1... | collective-permute-start | bytes 552968 | tf_op jit(solution)/shard_map/ppermute | solution.py:255
  26.8 6.1 %collective-permute-done.4 = f32[4,16,720]{2,1,0:T(8,128)S(1)} collective-permute-done((f32[4,16,720]{2,1,0:T(8,128)S(1)}, f32[4,16,720]{2,1,0:T(8,128)S(1)}, u32[]{:S(2)}, u32[]{:S(2)}) %collective-permute-start.4) | collective-permute-done | bytes 184352 | tf_op jit(solution)/shard_map/ppermute | solution.py:255
  33.4 0.2 copy_select_fusion.3
  33.6 0.2 pad_maximum_fusion.9
  33.8 0.4 fusion.43
  34.3 1.0 %fusion.30 = f32[4,5,9,720]{3,2,1,0:T(8,128)S(1)} fusion(f32[4,5,8,720]{3,2,1,0:T(8,128)S(1)} %slice_bitcast_fusion, f32[4,5,3,720]{3,2,1,0:T(4,128)S(1)} %get-tuple-element.63, f32[4,5,3,720]{3,2,1,0:T(4,128)S(1)} %get-tuple-element.62, f32[4,5,11,720]{3,2,1,0:T(8,128)S(1)} %fusion.43, f32[9]{0:T(128)S(1)} %or_select_fusion, ...), kind=kLoop, calls=%fused_computation.52 | loop fusion | flops 2980800 | bytes 3216996 | tf_op jit(solution)/shard_map/mul | solution.py:287
  35.4 0.4 multiply_reduce_fusion.3
  35.9 1.0 %copy-done.1 = f32[4,180,720]{2,1,0:T(8,128)S(1)} copy-done((f32[4,180,720]{2,1,0:T(8,128)S(1)}, f32[4,180,720]{2,1,0:T(8,128)}, u32[]{:S(2)}) %copy-start.1) | copy-done | bytes 2073624
  36.9 2.1 %fusion.3 = f32[4,80,360]{2,1,0:T(8,128)S(1)} fusion(f32[4,180,720]{2,1,0:T(8,128)S(1)} %copy.118, f32[4,180,720]{2,1,0:T(8,128)S(1)} %copy-done.1, f32[4,40,720]{2,1,0:T(8,128)S(1)} %neg.12, f32[4,40,720]{2,1,0:T(8,128)S(1)} %get-tuple-element.7), kind=kOutput, calls=%fused_computation.13 | convolution fusion | flops 498931200 | bytes 5529600 | tf_op jit(solution)/shard_map/dot_general | solution.py:95
  39.1 1.8 %fusion.2 = f32[4,80,720]{2,1,0:T(8,128)S(1)} fusion(f32[4,180,720]{2,1,0:T(8,128)S(1)} %copy.118, f32[4,180,720]{2,1,0:T(8,128)S(1)} %copy-done.1, f32[4,40,180]{2,1,0:T(8,128)S(1)} %get-tuple-element.30, f32[4,40,180]{2,1,0:T(8,128)S(1)} %get-tuple-element.14, f32[4,40,180]{2,1,0:T(8,128)S(1)} %get-tuple-element.15), kind=kOutput, calls=%fused_computation.12 | convolution fusion | flops 499046400 | bytes 5414400 | tf_op jit(solution)/shard_map/dot_general | solution.py:104
  41.0 0.3 subtract_reduce_fusion.1
  41.8 0.2 maximum_maximum_fusion.2
  42.0 0.5 fusion.69
  42.5 0.5 fusion.62
  42.9 0.2 slice_subtract_fusion.1
  43.2 3.6 %collective-permute-start.5 = (f32[4,15,720]{2,0,1:T(4,128)S(1)}, f32[4,15,720]{2,0,1:T(4,128)S(1)}, u32[]{:S(2)}, u32[]{:S(2)}) collective-permute-start(f32[4,15,720]{2,0,1:T(4,128)S(1)} %bitcast.124), channel_id=1, source_target_pairs={{4,8},{8,4},{12,16},{16,12},{20,24},{24,20},{5,9},{9,5},{13,17},{1... | collective-permute-start | bytes 518408 | tf_op jit(solution)/shard_map/ppermute | solution.py:255
  47.0 4.5 %collective-permute-done.5 = f32[4,15,720]{2,0,1:T(4,128)S(1)} collective-permute-done((f32[4,15,720]{2,0,1:T(4,128)S(1)}, f32[4,15,720]{2,0,1:T(4,128)S(1)}, u32[]{:S(2)}, u32[]{:S(2)}) %collective-permute-start.5) | collective-permute-done | bytes 172832 | tf_op jit(solution)/shard_map/ppermute | solution.py:255
  51.5 0.2 copy_select_fusion.1
  51.7 0.2 pad_maximum_fusion.10
  51.9 0.4 fusion.40
  52.4 1.0 %fusion.13 = f32[4,5,9,720]{3,2,1,0:T(8,128)S(1)} fusion(f32[4,5,8,720]{3,2,1,0:T(8,128)S(1)} %bitcast_select_fusion, f32[4,5,3,720]{3,2,1,0:T(4,128)S(1)} %get-tuple-element.59, f32[4,5,3,720]{3,2,1,0:T(4,128)S(1)} %get-tuple-element.58, f32[4,5,11,720]{3,2,1,0:T(8,128)S(1)} %fusion.40, f32[9]{0:T(128)S(1)} %or_select_fusion, ...), kind=kLoop, calls=%fused_computation.35 | loop fusion | flops 2980800 | bytes 3216996 | tf_op jit(solution)/shard_map/mul | solution.py:287
  53.3 0.2 fusion.55
  53.5 0.4 multiply_reduce_fusion.1
  54.0 2.1 %fusion.1 = f32[4,80,360]{2,1,0:T(8,128)S(1)} fusion(f32[4,180,720]{2,1,0:T(8,128)S(1)} %copy.118, f32[4,180,720]{2,1,0:T(8,128)S(1)} %copy-done.1, f32[4,40,720]{2,1,0:T(8,128)S(1)} %neg.14, f32[4,40,720]{2,1,0:T(8,128)S(1)} %get-tuple-element.5), kind=kOutput, calls=%fused_computation.11 | convolution fusion | flops 498931200 | bytes 5529600 | tf_op jit(solution)/shard_map/dot_general | solution.py:95
  56.2 1.8 %fusion = f32[4,80,720]{2,1,0:T(8,128)S(1)} fusion(f32[4,180,720]{2,1,0:T(8,128)S(1)} %copy.118, f32[4,180,720]{2,1,0:T(8,128)S(1)} %copy-done.1, f32[4,40,180]{2,1,0:T(8,128)S(1)} %get-tuple-element.29, f32[4,40,180]{2,1,0:T(8,128)S(1)} %get-tuple-element.9, f32[4,40,180]{2,1,0:T(8,128)S(1)} %get-tuple-element.10), kind=kOutput, calls=%fused_computation.10 | convolution fusion | flops 499046400 | bytes 5414400 | tf_op jit(solution)/shard_map/dot_general | solution.py:104
  58.1 0.3 subtract_reduce_fusion
  58.6 0.6 collective-permute-start.7
  59.2 2.1 %collective-permute-start.8 = (f32[5,8,720]{2,1,0:T(8,128)S(1)}, f32[5,8,720]{2,1,0:T(8,128)S(1)}, u32[]{:S(2)}, u32[]{:S(2)}) collective-permute-start(f32[5,8,720]{2,1,0:T(8,128)S(1)} %get-tuple-element.32), channel_id=1, source_target_pairs={{0,2},{1,3},{2,0},{3,1},{4,6},{5,7},{6,4},{7,5},{8,10},{9,11},{10,... | collective-permute-start | bytes 345608 | tf_op jit(solution)/shard_map/ppermute | solution.py:18
  61.4 1.4 %collective-permute-start.9 = (f32[5,8,720]{2,1,0:T(8,128)S(1)}, f32[5,8,720]{2,1,0:T(8,128)S(1)}, u32[]{:S(2)}, u32[]{:S(2)}) collective-permute-start(f32[5,8,720]{2,1,0:T(8,128)S(1)} %get-tuple-element.31), channel_id=1, source_target_pairs={{0,1},{1,2},{2,3},{3,0},{4,5},{5,6},{6,7},{7,4},{8,9},{9,10},{10,1... | collective-permute-start | bytes 345608 | tf_op jit(solution)/shard_map/ppermute | solution.py:18
  62.7 1.2 %collective-permute-done.7 = f32[5,8,720]{2,1,0:T(8,128)S(1)} collective-permute-done((f32[5,8,720]{2,1,0:T(8,128)S(1)}, f32[5,8,720]{2,1,0:T(8,128)S(1)}, u32[]{:S(2)}, u32[]{:S(2)}) %collective-permute-start.7) | collective-permute-done | bytes 115232 | tf_op jit(solution)/shard_map/ppermute | solution.py:18
  64.0 6.6 %collective-permute-done.8 = f32[5,8,720]{2,1,0:T(8,128)S(1)} collective-permute-done((f32[5,8,720]{2,1,0:T(8,128)S(1)}, f32[5,8,720]{2,1,0:T(8,128)S(1)}, u32[]{:S(2)}, u32[]{:S(2)}) %collective-permute-start.8) | collective-permute-done | bytes 115232 | tf_op jit(solution)/shard_map/ppermute | solution.py:18
  70.6 0.8 %pad_maximum_fusion.14 = f32[5,4,8,720]{3,2,1,0:T(8,128)} fusion(f32[5,1,8,720]{3,2,1,0:T(8,128)S(1)} %get-tuple-element.24, f32[5,1,8,720]{3,2,1,0:T(8,128)S(1)} %get-tuple-element.25, f32[5,1,8,720]{3,2,1,0:T(8,128)S(1)} %get-tuple-element.26, f32[5,1,8,720]{3,2,1,0:T(8,128)S(1)} %get-tuple-element.23), kind=kLoop, calls=%fused_computation.145 | loop fusion | flops 345600 | bytes 921600 | tf_op jit(solution)/shard_map/stack | solution.py:303
  (73 shorter events, 3.4 us)
Async XLA Ops:
  0.0 7.3 %copy-start = (s32[64]{0:T(128)S(1)}, s32[64]{0:T(128)}, u32[]{:S(2)}) copy-start(s32[64]{0:T(128)} %param.7) | copy-start | bytes 772
  2.0 15.0 %collective-permute-start.2 = (f32[56,720]{1,0:T(8,128)S(1)}, f32[56,720]{1,0:T(8,128)S(1)}, u32[]{:S(2)}, u32[]{:S(2)}) collective-permute-start(f32[56,720]{1,0:T(8,128)S(1)} %pad_maximum_fusion.23), channel_id=1, source_target_pairs={{0,3},{1,0},{2,1},{3,2},{4,7},{5,4},{6,5},{7,6},{8,11},{9,8},{10,9... | collective-permute-start | bytes 483848 | tf_op jit(solution)/shard_map/ppermute | solution.py:18
  5.4 14.7 %collective-permute-start.1 = (f32[56,720]{1,0:T(8,128)S(1)}, f32[56,720]{1,0:T(8,128)S(1)}, u32[]{:S(2)}, u32[]{:S(2)}) collective-permute-start(f32[56,720]{1,0:T(8,128)S(1)} %pad_maximum_fusion.22), channel_id=1, source_target_pairs={{0,2},{1,3},{2,0},{3,1},{4,6},{5,7},{6,4},{7,5},{8,10},{9,11},{10,... | collective-permute-start | bytes 483848 | tf_op jit(solution)/shard_map/ppermute | solution.py:18
  5.5 14.6 %collective-permute-start = (f32[56,720]{1,0:T(8,128)S(1)}, f32[56,720]{1,0:T(8,128)S(1)}, u32[]{:S(2)}, u32[]{:S(2)}) collective-permute-start(f32[56,720]{1,0:T(8,128)S(1)} %pad_maximum_fusion.21), channel_id=1, source_target_pairs={{0,1},{1,2},{2,3},{3,0},{4,5},{5,6},{6,7},{7,4},{8,9},{9,10},{10,1... | collective-permute-start | bytes 483848 | tf_op jit(solution)/shard_map/ppermute | solution.py:18
  22.6 4.2 %collective-permute-start.3 = (f32[4,16,720]{2,1,0:T(8,128)S(1)}, f32[4,16,720]{2,1,0:T(8,128)S(1)}, u32[]{:S(2)}, u32[]{:S(2)}) collective-permute-start(f32[4,16,720]{2,1,0:T(8,128)S(1)} %get-tuple-element.55), channel_id=1, source_target_pairs={{0,4},{4,0},{8,12},{12,8},{16,20},{20,16},{24,28},{28,24},{1,5},{5... | collective-permute-start | bytes 552968 | tf_op jit(solution)/shard_map/ppermute | solution.py:252
  23.6 9.4 %collective-permute-start.4 = (f32[4,16,720]{2,1,0:T(8,128)S(1)}, f32[4,16,720]{2,1,0:T(8,128)S(1)}, u32[]{:S(2)}, u32[]{:S(2)}) collective-permute-start(f32[4,16,720]{2,1,0:T(8,128)S(1)} %get-tuple-element.54), channel_id=1, source_target_pairs={{4,8},{8,4},{12,16},{16,12},{20,24},{24,20},{5,9},{9,5},{13,17},{1... | collective-permute-start | bytes 552968 | tf_op jit(solution)/shard_map/ppermute | solution.py:255
  35.3 1.6 %copy-start.1 = (f32[4,180,720]{2,1,0:T(8,128)S(1)}, f32[4,180,720]{2,1,0:T(8,128)}, u32[]{:S(2)}) copy-start(f32[4,180,720]{2,1,0:T(8,128)} %copy.117) | copy-start | bytes 6220804
  43.2 8.2 %collective-permute-start.5 = (f32[4,15,720]{2,0,1:T(4,128)S(1)}, f32[4,15,720]{2,0,1:T(4,128)S(1)}, u32[]{:S(2)}, u32[]{:S(2)}) collective-permute-start(f32[4,15,720]{2,0,1:T(4,128)S(1)} %bitcast.124), channel_id=1, source_target_pairs={{4,8},{8,4},{12,16},{16,12},{20,24},{24,20},{5,9},{9,5},{13,17},{1... | collective-permute-start | bytes 518408 | tf_op jit(solution)/shard_map/ppermute | solution.py:255
  46.8 4.6 %collective-permute-start.6 = (f32[4,15,720]{2,0,1:T(4,128)S(1)}, f32[4,15,720]{2,0,1:T(4,128)S(1)}, u32[]{:S(2)}, u32[]{:S(2)}) collective-permute-start(f32[4,15,720]{2,0,1:T(4,128)S(1)} %bitcast.125), channel_id=1, source_target_pairs={{0,4},{4,0},{8,12},{12,8},{16,20},{20,16},{24,28},{28,24},{1,5},{5... | collective-permute-start | bytes 518408 | tf_op jit(solution)/shard_map/ppermute | solution.py:252
  58.6 5.3 %collective-permute-start.7 = (f32[5,8,720]{2,1,0:T(8,128)S(1)}, f32[5,8,720]{2,1,0:T(8,128)S(1)}, u32[]{:S(2)}, u32[]{:S(2)}) collective-permute-start(f32[5,8,720]{2,1,0:T(8,128)S(1)} %get-tuple-element.33), channel_id=1, source_target_pairs={{0,3},{1,0},{2,1},{3,2},{4,7},{5,4},{6,5},{7,6},{8,11},{9,8},{10,9... | collective-permute-start | bytes 345608 | tf_op jit(solution)/shard_map/ppermute | solution.py:18
  59.2 11.3 %collective-permute-start.8 = (f32[5,8,720]{2,1,0:T(8,128)S(1)}, f32[5,8,720]{2,1,0:T(8,128)S(1)}, u32[]{:S(2)}, u32[]{:S(2)}) collective-permute-start(f32[5,8,720]{2,1,0:T(8,128)S(1)} %get-tuple-element.32), channel_id=1, source_target_pairs={{0,2},{1,3},{2,0},{3,1},{4,6},{5,7},{6,4},{7,5},{8,10},{9,11},{10,... | collective-permute-start | bytes 345608 | tf_op jit(solution)/shard_map/ppermute | solution.py:18
  61.4 9.2 %collective-permute-start.9 = (f32[5,8,720]{2,1,0:T(8,128)S(1)}, f32[5,8,720]{2,1,0:T(8,128)S(1)}, u32[]{:S(2)}, u32[]{:S(2)}) collective-permute-start(f32[5,8,720]{2,1,0:T(8,128)S(1)} %get-tuple-element.31), channel_id=1, source_target_pairs={{0,1},{1,2},{2,3},{3,0},{4,5},{5,6},{6,7},{7,4},{8,9},{9,10},{10,1... | collective-permute-start | bytes 345608 | tf_op jit(solution)/shard_map/ppermute | solution.py:18
